TPU v7x, 32 devices: a whole 2x2x4 slice. The times are simulated.
32 devices in a mesh: groups: 2 (over x), rows: 16 (over z, y, core).
Axes of the slice: x: 2, y: 2, z: 4, core: 2. Of those that a mesh axis runs over, the one named last changes fastest.
Arguments:
- inputs: bfloat16 [256, 512, 128], P(('groups', 'rows')), parts along dimension 0, may hold values from -6 to 6
- cotangent: bfloat16 [256, 512, 128], P(('groups', 'rows')), parts along dimension 0, may hold values from -48 to 48
- first_kernel: bfloat16 [9, 128, 128], replicated, may hold values from -0.1875 to 0.1875
- second_kernel: bfloat16 [9, 128, 128], replicated, may hold values from -0.1875 to 0.1875
- level_table: float32 [16, 2, 128], replicated, may hold values from -3 to 3
- level_index: int32 [2], P('groups'), parts along dimension 0, may hold values from 0 to 15
Outputs:
- outputs: bfloat16 [256, 512, 128], P(('groups', 'rows')), parts along dimension 0
- input_grad: bfloat16 [256, 512, 128], P(('groups', 'rows')), parts along dimension 0
- first_grad: float32 [18, 128, 128], P('groups'), parts along dimension 0
- second_grad: float32 [18, 128, 128], P('groups'), parts along dimension 0
- level_grad: float32 [4, 128], P('groups'), parts along dimension 0
There are 2 independent parts, one for each index of `groups`. A program takes and returns all parts, laid end to end along the dimension named above; an argument that names none is the same for every part. Nothing has to cross between parts.
All inputs are finite; a program needn't handle non-finite values.
Results may differ from a plain program's by a relative error of at most 0.0036.
Values may be sent and summed in bfloat16 or wider, within the bound.
No kernel may reach another device: no remote copies, remote signals or barrier semaphores. Data moves between devices by JAX's collectives and lax.ppermute only.
A program may use at most 128 MiB of HBM per device.

v0:
```python
import math

import jax
import jax.numpy as jnp
from jax import lax
from jax.experimental import pallas as pl
from jax.experimental.pallas import tpu as pltpu
from jax.sharding import PartitionSpec as P


def forward_matrix(kernel):
    c, o = kernel.shape[1], kernel.shape[2]
    return kernel.reshape(3, 3, c, o).transpose(0, 2, 1, 3).reshape(3 * c, 3 * o)


def back_matrix(kernel):
    c, o = kernel.shape[1], kernel.shape[2]
    flipped = kernel.reshape(3, 3, c, o)[::-1, ::-1]
    return flipped.transpose(0, 3, 1, 2).reshape(3 * o, 3 * c)


def taps_from_matrix(matrix, c, o):
    return matrix.reshape(3, c, 3, o).transpose(0, 2, 1, 3).reshape(9, c, o)


def section_kernel(edge_ref, ss_ref, x_ref, c_ref, k1f_ref, k2f_ref, k2b_ref, k1b_ref,
                   out_ref, ig_ref, g1_ref, g2_ref, lv_ref, hid_ref, bf_ref):
    count = out_ref.shape[0]
    width = out_ref.shape[1]
    ch = out_ref.shape[2]
    col = lax.broadcasted_iota(jnp.int32, (width, ch), 0)
    not_first = col > 0
    not_last = col < width - 1
    scale = ss_ref[0:1, :]
    shift = ss_ref[1:2, :]
    top = edge_ref[0] > 0
    bottom = edge_ref[1] > 0

    def combine(y):
        left = pltpu.roll(y[:, 0:ch], 1, 0)
        right = pltpu.roll(y[:, 2 * ch:3 * ch], width - 1, 0)
        return y[:, ch:2 * ch] + jnp.where(not_first, left, 0.0) + jnp.where(not_last, right, 0.0)

    def conv_row(ref, r, matrix_ref):
        rows = jnp.concatenate([ref[r], ref[r + 1], ref[r + 2]], axis=1)
        y = jnp.dot(rows, matrix_ref[...], preferred_element_type=jnp.float32)
        return combine(y)

    def shifted(g):
        g32 = g.astype(jnp.float32)
        g0 = jnp.where(not_last, pltpu.roll(g32, width - 1, 0), 0.0)
        g2 = jnp.where(not_first, pltpu.roll(g32, 1, 0), 0.0)
        return jnp.concatenate([g0.astype(g.dtype), g, g2.astype(g.dtype)], axis=1)

    def phase_one(r, carry):
        lv0, lv1 = carry
        valid = jnp.logical_and(jnp.logical_or(r > 0, top), jnp.logical_or(r < count + 1, bottom))
        first = conv_row(x_ref, r, k1f_ref)
        mixed = first * scale + shift
        sig = 1.0 / (1.0 + jnp.exp(-mixed))
        hid_ref[r] = jnp.where(valid, mixed * sig, 0.0).astype(hid_ref.dtype)
        back_hidden = conv_row(c_ref, r, k2b_ref)
        back_mixed = back_hidden * (sig * (1.0 + mixed * (1.0 - sig)))
        bf_ref[r] = jnp.where(valid, back_mixed * scale, 0.0).astype(bf_ref.dtype)
        own = jnp.logical_and(r >= 1, r <= count)
        lv0 = lv0 + jnp.where(own, jnp.sum(back_mixed * first, axis=0, keepdims=True), 0.0)
        lv1 = lv1 + jnp.where(own, jnp.sum(back_mixed, axis=0, keepdims=True), 0.0)
        return lv0, lv1

    zero = jnp.zeros((1, ch), jnp.float32)
    lv0, lv1 = lax.fori_loop(0, count + 2, phase_one, (zero, zero))
    lv_ref[0:1, :] = lv0
    lv_ref[1:2, :] = lv1
    g1_ref[...] = jnp.zeros_like(g1_ref)
    g2_ref[...] = jnp.zeros_like(g2_ref)

    def phase_two(i, carry):
        out_ref[i] = (x_ref[i + 2].astype(jnp.float32) + conv_row(hid_ref, i, k2f_ref)).astype(out_ref.dtype)
        ig_ref[i] = (c_ref[i + 2].astype(jnp.float32) + conv_row(bf_ref, i, k1b_ref)).astype(ig_ref.dtype)
        xs = jnp.concatenate([x_ref[i + 1], x_ref[i + 2], x_ref[i + 3]], axis=1)
        gs = shifted(bf_ref[i + 1])
        g1_ref[...] += lax.dot_general(xs, gs, (((0,), (0,)), ((), ())), preferred_element_type=jnp.float32)
        hs = jnp.concatenate([hid_ref[i], hid_ref[i + 1], hid_ref[i + 2]], axis=1)
        cs = shifted(c_ref[i + 2])
        g2_ref[...] += lax.dot_general(hs, cs, (((0,), (0,)), ((), ())), preferred_element_type=jnp.float32)
        return carry

    lax.fori_loop(0, count, phase_two, 0)


def section(edge, ss, x12, c12, k1f, k2f, k2b, k1b):
    ext, width, ch = x12.shape
    count = ext - 4
    vmem = pltpu.MemorySpace.VMEM if hasattr(pltpu, "MemorySpace") else pltpu.VMEM
    spec = pl.BlockSpec(memory_space=vmem)
    flops = 2 * (count + 2) * width * (3 * ch) * (3 * ch) * 2 + 4 * count * width * (3 * ch) * (3 * ch) * 2
    return pl.pallas_call(
        section_kernel,
        out_shape=(
            jax.ShapeDtypeStruct((count, width, ch), jnp.bfloat16),
            jax.ShapeDtypeStruct((count, width, ch), jnp.bfloat16),
            jax.ShapeDtypeStruct((3 * ch, 3 * ch), jnp.float32),
            jax.ShapeDtypeStruct((3 * ch, 3 * ch), jnp.float32),
            jax.ShapeDtypeStruct((2, ch), jnp.float32),
        ),
        in_specs=[pl.BlockSpec(memory_space=pltpu.SMEM)] + [spec] * 7,
        out_specs=(spec,) * 5,
        scratch_shapes=[
            pltpu.VMEM((count + 2, width, ch), jnp.bfloat16),
            pltpu.VMEM((count + 2, width, ch), jnp.bfloat16),
        ],
        compiler_params=pltpu.CompilerParams(vmem_limit_bytes=60 * 1024 * 1024),
        cost_estimate=pl.CostEstimate(
            flops=flops, transcendentals=(count + 2) * width * ch, bytes_accessed=8 * ext * width * ch
        ),
    )(edge, ss, x12, c12, k1f, k2f, k2b, k1b)


def butterfly_sum(block):
    n = lax.axis_size("rows")
    me = lax.axis_index("rows")
    steps = []
    k = 1
    while k < n:
        steps.append(k)
        k *= 2
    piece = block
    for k in steps:
        half = piece.shape[0] // 2
        low = (me // k) % 2 == 0
        lo, hi = piece[:half], piece[half:]
        keep = jnp.where(low, lo, hi)
        send = jnp.where(low, hi, lo)
        got = lax.ppermute(send, "rows", [(i, i ^ k) for i in range(n)])
        piece = keep + got
    for k in reversed(steps):
        low = (me // k) % 2 == 0
        got = lax.ppermute(piece, "rows", [(i, i ^ k) for i in range(n)])
        piece = jnp.where(low, jnp.concatenate([piece, got]), jnp.concatenate([got, piece]))
    return piece


def local(inputs, cotangent, first_kernel, second_kernel, level_table, level_index):
    count = inputs.shape[0]
    width = inputs.shape[1]
    ch = inputs.shape[2]
    size = lax.axis_size("rows")
    me = lax.axis_index("rows")
    total_rows = count * size
    selected = lax.dynamic_index_in_dim(level_table, level_index[0], 0, keepdims=False)
    ss = jnp.stack([1.0 + selected[0], selected[1]])

    up = [(i, i + 1) for i in range(size - 1)]
    down = [(i + 1, i) for i in range(size - 1)]
    before = lax.ppermute(jnp.concatenate([inputs[-2:], cotangent[-2:]]), "rows", up)
    after = lax.ppermute(jnp.concatenate([inputs[:2], cotangent[:2]]), "rows", down)
    x12 = jnp.concatenate([before[:2], inputs, after[:2]])
    c12 = jnp.concatenate([before[2:], cotangent, after[2:]])
    edge = jnp.stack([me > 0, me < size - 1]).astype(jnp.int32)

    outputs, input_grad, g1, g2, lv = section(
        edge, ss, x12, c12,
        forward_matrix(first_kernel), forward_matrix(second_kernel),
        back_matrix(second_kernel), back_matrix(first_kernel),
    )
    used = 2 * (g1.size // ch) + 2
    pad = jnp.zeros((-used % size, ch), jnp.float32)
    packed = jnp.concatenate([g1.reshape(-1, ch), g2.reshape(-1, ch), lv, pad])
    total = butterfly_sum(packed)
    norm = 1.0 / math.sqrt(total_rows * width)
    n1 = g1.size // ch
    first_sum = taps_from_matrix(total[:n1].reshape(g1.shape), ch, ch)
    second_sum = taps_from_matrix(total[n1 : 2 * n1].reshape(g2.shape), ch, ch)
    level_sum = total[2 * n1 : 2 * n1 + 2]
    return (outputs, input_grad, first_sum * norm, second_sum * norm, level_sum * norm)


def solution(mesh):
    return jax.shard_map(
        local,
        mesh=mesh,
        in_specs=(
            P(("groups", "rows"), None, None),
            P(("groups", "rows"), None, None),
            P(),
            P(),
            P(),
            P("groups"),
        ),
        out_specs=(
            P(("groups", "rows"), None, None),
            P(("groups", "rows"), None, None),
            P("groups", None, None),
            P("groups", None, None),
            P("groups", None),
        ),
        check_vma=False,
    )
```

profile of v0, /device:TPU:0, one launch (start us, length us, event | category | flops | bytes accessed | tf_op | source)
XLA Modules:
  0.0 89.5 jit_solution(17992754530113325513)
XLA Ops:
  0.6 1.3 %fusion = (bf16[2,512,128]{2,1,0:T(8,128)(2,1)S(1)}, bf16[2,512,128]{2,1,0:T(8,128)(2,1)S(1)}, bf16[2,512,128]{2,1,0:T(8,128)(2,1)S(1)}, bf16[2,512,128]{2,1,0:T(8,128)(2,1)S(1)}) fusion(bf16[8,512,128]{2,1,0:T(8,128)(2,1)} %param.6, bf16[8,512,128]{2,1,0:T(8,128)(2,1)} %param.7), kind=kLoop, calls=%fused_computation.29 | loop fusion | bytes 2097152 | tf_op jit(solution)/shard_map/slice | solution.py:155
  2.0 1.4 %collective-permute-start.1 = (bf16[4,512,128]{2,1,0:T(8,128)(2,1)S(1)}, bf16[4,512,128]{2,1,0:T(8,128)(2,1)S(1)}, u32[]{:S(2)}, u32[]{:S(2)}) collective-permute-start(bf16[4,512,128]{2,1,0:T(8,128)(2,1)S(1)} %pad_maximum_fusion.4), channel_id=1, source_target_pairs={{1,0},{2,1},{3,2},{4,3},{5,4},{6,5},{7,6},{8,7},{9,8},{10,9},{11,1... | collective-permute-start | bytes 1572872 | tf_op jit(solution)/shard_map/ppermute | solution.py:156
  3.4 0.8 pad_maximum_fusion.3
  4.3 3.1 %collective-permute-start = (bf16[4,512,128]{2,1,0:T(8,128)(2,1)}, bf16[4,512,128]{2,1,0:T(8,128)(2,1)S(1)}, u32[]{:S(2)}, u32[]{:S(2)}) collective-permute-start(bf16[4,512,128]{2,1,0:T(8,128)(2,1)} %pad_maximum_fusion.3), channel_id=1, source_target_pairs={{0,1},{1,2},{2,3},{3,4},{4,5},{5,6},{6,7},{7,8},{8,9},{9,10},{10,1... | collective-permute-start | bytes 1572872 | tf_op jit(solution)/shard_map/ppermute | solution.py:155
  8.6 0.9 %copy_bitcast_fusion.2 = (bf16[384,384]{1,0:T(8,128)(2,1)}, bf16[384,384]{1,0:T(8,128)(2,1)}) fusion(bf16[48,8,3,128]{3,2,1,0:T(4,128)(2,1)S(1)} %bitcast.40, bf16[48,8,3,128]{3,2,1,0:T(4,128)(2,1)S(1)} %bitcast.41), kind=kLoop, calls=%fused_computation.15 | loop fusion | bytes 1179648 | tf_op jit(solution)/shard_map/reshape | solution.py:13
  9.5 0.6 pad_maximum_fusion.5.ss_ref
  10.0 0.6 add_convert_fusion.edge_ref
  11.2 1.8 %rev.7 = bf16[3,3,128,128]{2,1,3,0:T(4,128)(2,1)S(1)} reverse(bf16[3,3,128,128]{2,1,3,0:T(4,128)(2,1)S(1)} %copy.24), dimensions={0,1} | reverse | bytes 589824 | tf_op jit(solution)/shard_map/rev | solution.py:18
  13.0 1.8 %rev.6 = bf16[3,3,128,128]{2,1,3,0:T(4,128)(2,1)S(1)} reverse(bf16[3,3,128,128]{2,1,3,0:T(4,128)(2,1)S(1)} %copy.23), dimensions={0,1} | reverse | bytes 589824 | tf_op jit(solution)/shard_map/rev | solution.py:18
  14.8 0.9 copy_bitcast_fusion
  16.2 1.3 %pad_maximum_fusion.x_ref = bf16[12,512,128]{2,1,0:T(8,128)(2,1)} fusion(bf16[2,512,128]{2,1,0:T(8,128)(2,1)S(1)} %get-tuple-element.24, bf16[8,512,128]{2,1,0:T(8,128)(2,1)S(1)} %copy-done.1, bf16[2,512,128]{2,1,0:T(8,128)(2,1)S(1)} %get-tuple-element.22), kind=kLoop, calls=%fused_computation | loop fusion | flops 1572864 | bytes 3145728 | tf_op jit(solution)/shard_map/concatenate | solution.py:157
  17.7 1.3 %pad_maximum_fusion.1.c_ref = bf16[12,512,128]{2,1,0:T(8,128)(2,1)} fusion(bf16[2,512,128]{2,1,0:T(8,128)(2,1)S(1)} %get-tuple-element.23, bf16[8,512,128]{2,1,0:T(8,128)(2,1)S(1)} %copy-done.2, bf16[2,512,128]{2,1,0:T(8,128)(2,1)S(1)} %get-tuple-element.21), kind=kLoop, calls=%fused_computation.1 | loop fusion | flops 1572864 | bytes 3145728 | tf_op jit(solution)/shard_map/concatenate | solution.py:158
  19.1 19.2 %shard_map.101 = (bf16[8,512,128]{2,1,0:T(8,128)(2,1)}, bf16[8,512,128]{2,1,0:T(8,128)(2,1)}, f32[384,384]{1,0:T(8,128)}, f32[384,384]{1,0:T(8,128)}, f32[2,128]{1,0:T(2,128)}) custom-call(s32[2]{0:T(128)} %add_convert_fusion.edge_ref, f32[2,128]{1,0:T(2,128)} %pad_maximum_fusion.5.ss_ref, bf16[12,512,128]{2,1,0:T(8,128)(2,1)} %pad_maximum_fusion.x_ref, ...), custom_call_target="tpu_custom_call" | custom-call | flops 7851737088 | bytes 6291456 | tf_op jit(solution)/shard_map/pallas_call | solution.py:97
  38.3 1.2 %reshape.68 = f32[1152,128]{1,0:T(8,128)S(1)} reshape(f32[384,384]{1,0:T(8,128)} %get-tuple-element.13) | data formatting | bytes 1179648 | tf_op jit(solution)/shard_map/reshape | solution.py:168
  40.0 3.7 %collective-permute-start.2 = (f32[1160,128]{1,0:T(8,128)S(1)}, f32[1160,128]{1,0:T(8,128)S(1)}, u32[]{:S(2)}, u32[]{:S(2)}) collective-permute-start(f32[1160,128]{1,0:T(8,128)S(1)} %slice_select_fusion), channel_id=1, source_target_pairs={{0,1},{1,0},{2,3},{3,2},{4,5},{5,4},{6,7},{7,6},{8,9},{9,8},{10,11... | collective-permute-start | bytes 1781768 | tf_op jit(solution)/shard_map/ppermute | solution.py:134
  43.7 1.6 %collective-permute-done.2 = f32[1160,128]{1,0:T(8,128)S(1)} collective-permute-done((f32[1160,128]{1,0:T(8,128)S(1)}, f32[1160,128]{1,0:T(8,128)S(1)}, u32[]{:S(2)}, u32[]{:S(2)}) %collective-permute-start.2) | collective-permute-done | bytes 593952 | tf_op jit(solution)/shard_map/ppermute | solution.py:134
  45.6 2.7 %collective-permute-start.3 = (f32[580,128]{1,0:T(8,128)S(1)}, f32[580,128]{1,0:T(8,128)S(1)}, u32[]{:S(2)}, u32[]{:S(2)}) collective-permute-start(f32[580,128]{1,0:T(8,128)S(1)} %slice_select_fusion.1), channel_id=1, source_target_pairs={{0,2},{1,3},{2,0},{3,1},{4,6},{5,7},{6,4},{7,5},{8,10},{9,11},{10,... | collective-permute-start | bytes 890888 | tf_op jit(solution)/shard_map/ppermute | solution.py:134
  48.3 7.4 %collective-permute-done.3 = f32[580,128]{1,0:T(8,128)S(1)} collective-permute-done((f32[580,128]{1,0:T(8,128)S(1)}, f32[580,128]{1,0:T(8,128)S(1)}, u32[]{:S(2)}, u32[]{:S(2)}) %collective-permute-start.3) | collective-permute-done | bytes 296992 | tf_op jit(solution)/shard_map/ppermute | solution.py:134
  55.7 1.6 %collective-permute-start.4 = (f32[290,128]{1,0:T(8,128)S(1)}, f32[290,128]{1,0:T(8,128)S(1)}, u32[]{:S(2)}, u32[]{:S(2)}) collective-permute-start(f32[290,128]{1,0:T(8,128)S(1)} %slice_select_fusion.2), channel_id=1, source_target_pairs={{0,4},{1,5},{2,6},{3,7},{4,0},{5,1},{6,2},{7,3},{8,12},{9,13},{10,... | collective-permute-start | bytes 445448 | tf_op jit(solution)/shard_map/ppermute | solution.py:134
  57.4 3.9 %collective-permute-done.4 = f32[290,128]{1,0:T(8,128)S(1)} collective-permute-done((f32[290,128]{1,0:T(8,128)S(1)}, f32[290,128]{1,0:T(8,128)S(1)}, u32[]{:S(2)}, u32[]{:S(2)}) %collective-permute-start.4) | collective-permute-done | bytes 148512 | tf_op jit(solution)/shard_map/ppermute | solution.py:134
  61.3 2.6 %collective-permute-start.5 = (f32[145,128]{1,0:T(8,128)S(1)}, f32[145,128]{1,0:T(8,128)S(1)}, u32[]{:S(2)}, u32[]{:S(2)}) collective-permute-start(f32[145,128]{1,0:T(8,128)S(1)} %slice_select_fusion.3), channel_id=1, source_target_pairs={{0,8},{1,9},{2,10},{3,11},{4,12},{5,13},{6,14},{7,15},{8,0},{9,1},... | collective-permute-start | bytes 222728 | tf_op jit(solution)/shard_map/ppermute | solution.py:134
  64.0 2.7 %collective-permute-done.5 = f32[145,128]{1,0:T(8,128)S(1)} collective-permute-done((f32[145,128]{1,0:T(8,128)S(1)}, f32[145,128]{1,0:T(8,128)S(1)}, u32[]{:S(2)}, u32[]{:S(2)}) %collective-permute-start.5) | collective-permute-done | bytes 74272 | tf_op jit(solution)/shard_map/ppermute | solution.py:134
  66.7 2.7 %collective-permute-start.6 = (f32[145,128]{1,0:T(8,128)S(1)}, f32[145,128]{1,0:T(8,128)S(1)}, u32[]{:S(2)}, u32[]{:S(2)}) collective-permute-start(f32[145,128]{1,0:T(8,128)S(1)} %select_add_fusion.3), channel_id=1, source_target_pairs={{0,8},{1,9},{2,10},{3,11},{4,12},{5,13},{6,14},{7,15},{8,0},{9,1},... | collective-permute-start | bytes 222728 | tf_op jit(solution)/shard_map/ppermute | solution.py:138
  69.4 2.8 %collective-permute-done.6 = f32[145,128]{1,0:T(8,128)S(1)} collective-permute-done((f32[145,128]{1,0:T(8,128)S(1)}, f32[145,128]{1,0:T(8,128)S(1)}, u32[]{:S(2)}, u32[]{:S(2)}) %collective-permute-start.6) | collective-permute-done | bytes 74272 | tf_op jit(solution)/shard_map/ppermute | solution.py:138
  72.2 1.5 %collective-permute-start.7 = (f32[290,128]{1,0:T(8,128)S(1)}, f32[290,128]{1,0:T(8,128)S(1)}, u32[]{:S(2)}, u32[]{:S(2)}) collective-permute-start(f32[290,128]{1,0:T(8,128)S(1)} %maximum_select_fusion.3), channel_id=1, source_target_pairs={{0,4},{1,5},{2,6},{3,7},{4,0},{5,1},{6,2},{7,3},{8,12},{9,13},{10,... | collective-permute-start | bytes 445448 | tf_op jit(solution)/shard_map/ppermute | solution.py:138
  73.7 3.7 %collective-permute-done.7 = f32[290,128]{1,0:T(8,128)S(1)} collective-permute-done((f32[290,128]{1,0:T(8,128)S(1)}, f32[290,128]{1,0:T(8,128)S(1)}, u32[]{:S(2)}, u32[]{:S(2)}) %collective-permute-start.7) | collective-permute-done | bytes 148512 | tf_op jit(solution)/shard_map/ppermute | solution.py:138
  77.5 1.4 %collective-permute-start.8 = (f32[580,128]{1,0:T(8,128)S(1)}, f32[580,128]{1,0:T(8,128)S(1)}, u32[]{:S(2)}, u32[]{:S(2)}) collective-permute-start(f32[580,128]{1,0:T(8,128)S(1)} %maximum_select_fusion.2), channel_id=1, source_target_pairs={{0,2},{1,3},{2,0},{3,1},{4,6},{5,7},{6,4},{7,5},{8,10},{9,11},{10,... | collective-permute-start | bytes 890888 | tf_op jit(solution)/shard_map/ppermute | solution.py:138
  78.9 5.4 %collective-permute-done.8 = f32[580,128]{1,0:T(8,128)S(1)} collective-permute-done((f32[580,128]{1,0:T(8,128)S(1)}, f32[580,128]{1,0:T(8,128)S(1)}, u32[]{:S(2)}, u32[]{:S(2)}) %collective-permute-start.8) | collective-permute-done | bytes 296992 | tf_op jit(solution)/shard_map/ppermute | solution.py:138
  84.5 2.0 %collective-permute-done.9 = f32[1160,128]{1,0:T(8,128)S(1)} collective-permute-done((f32[1160,128]{1,0:T(8,128)S(1)}, f32[1160,128]{1,0:T(8,128)S(1)}, u32[]{:S(2)}, u32[]{:S(2)}) %collective-permute-start.9) | collective-permute-done | bytes 593952 | tf_op jit(solution)/shard_map/ppermute | solution.py:138
  86.7 0.6 slice_multiply_fusion.2
  87.5 0.9 copy.25
  88.6 0.9 copy.26
  (44 shorter events, 3.5 us)
Async XLA Ops:
  0.6 7.9 %copy-start = (f32[16,2,128]{2,1,0:T(2,128)S(1)}, f32[16,2,128]{2,1,0:T(2,128)}, u32[]{:S(2)}) copy-start(f32[16,2,128]{2,1,0:T(2,128)} %param.10) | copy-start | bytes 49156
  1.9 6.1 %copy-start.4 = (bf16[9,128,128]{2,1,0:T(8,128)(2,1)S(1)}, bf16[9,128,128]{2,1,0:T(8,128)(2,1)}, u32[]{:S(2)}) copy-start(bf16[9,128,128]{2,1,0:T(8,128)(2,1)} %param.9) | copy-start | bytes 884740
  1.9 6.3 %copy-start.3 = (bf16[9,128,128]{2,1,0:T(8,128)(2,1)S(1)}, bf16[9,128,128]{2,1,0:T(8,128)(2,1)}, u32[]{:S(2)}) copy-start(bf16[9,128,128]{2,1,0:T(8,128)(2,1)} %param.8) | copy-start | bytes 884740
  2.0 13.7 %collective-permute-start.1 = (bf16[4,512,128]{2,1,0:T(8,128)(2,1)S(1)}, bf16[4,512,128]{2,1,0:T(8,128)(2,1)S(1)}, u32[]{:S(2)}, u32[]{:S(2)}) collective-permute-start(bf16[4,512,128]{2,1,0:T(8,128)(2,1)S(1)} %pad_maximum_fusion.4), channel_id=1, source_target_pairs={{1,0},{2,1},{3,2},{4,3},{5,4},{6,5},{7,6},{8,7},{9,8},{10,9},{11,1... | collective-permute-start | bytes 1572872 | tf_op jit(solution)/shard_map/ppermute | solution.py:156
  4.3 11.5 %collective-permute-start = (bf16[4,512,128]{2,1,0:T(8,128)(2,1)}, bf16[4,512,128]{2,1,0:T(8,128)(2,1)S(1)}, u32[]{:S(2)}, u32[]{:S(2)}) collective-permute-start(bf16[4,512,128]{2,1,0:T(8,128)(2,1)} %pad_maximum_fusion.3), channel_id=1, source_target_pairs={{0,1},{1,2},{2,3},{3,4},{4,5},{5,6},{6,7},{7,8},{8,9},{9,10},{10,1... | collective-permute-start | bytes 1572872 | tf_op jit(solution)/shard_map/ppermute | solution.py:155
  14.8 1.4 %copy-start.1 = (bf16[8,512,128]{2,1,0:T(8,128)(2,1)S(1)}, bf16[8,512,128]{2,1,0:T(8,128)(2,1)}, u32[]{:S(2)}) copy-start(bf16[8,512,128]{2,1,0:T(8,128)(2,1)} %param.6) | copy-start | bytes 3145732
  16.2 1.5 %copy-start.2 = (bf16[8,512,128]{2,1,0:T(8,128)(2,1)S(1)}, bf16[8,512,128]{2,1,0:T(8,128)(2,1)}, u32[]{:S(2)}) copy-start(bf16[8,512,128]{2,1,0:T(8,128)(2,1)} %param.7) | copy-start | bytes 3145732
  38.3 1.2 %copy-start.5 = (f32[384,384]{1,0:T(8,128)S(1)}, f32[384,384]{1,0:T(8,128)}, u32[]{:S(2)}) copy-start(f32[384,384]{1,0:T(8,128)} %get-tuple-element.12) | copy-start | bytes 1769476
  38.3 1.3 %copy-start.6 = (f32[2,128]{1,0:T(2,128)S(1)}, f32[2,128]{1,0:T(2,128)}, u32[]{:S(2)}) copy-start(f32[2,128]{1,0:T(2,128)} %get-tuple-element.14) | copy-start | bytes 3076
  40.0 5.4 %collective-permute-start.2 = (f32[1160,128]{1,0:T(8,128)S(1)}, f32[1160,128]{1,0:T(8,128)S(1)}, u32[]{:S(2)}, u32[]{:S(2)}) collective-permute-start(f32[1160,128]{1,0:T(8,128)S(1)} %slice_select_fusion), channel_id=1, source_target_pairs={{0,1},{1,0},{2,3},{3,2},{4,5},{5,4},{6,7},{7,6},{8,9},{9,8},{10,11... | collective-permute-start | bytes 1781768 | tf_op jit(solution)/shard_map/ppermute | solution.py:134
  45.6 10.1 %collective-permute-start.3 = (f32[580,128]{1,0:T(8,128)S(1)}, f32[580,128]{1,0:T(8,128)S(1)}, u32[]{:S(2)}, u32[]{:S(2)}) collective-permute-start(f32[580,128]{1,0:T(8,128)S(1)} %slice_select_fusion.1), channel_id=1, source_target_pairs={{0,2},{1,3},{2,0},{3,1},{4,6},{5,7},{6,4},{7,5},{8,10},{9,11},{10,... | collective-permute-start | bytes 890888 | tf_op jit(solution)/shard_map/ppermute | solution.py:134
  55.7 5.5 %collective-permute-start.4 = (f32[290,128]{1,0:T(8,128)S(1)}, f32[290,128]{1,0:T(8,128)S(1)}, u32[]{:S(2)}, u32[]{:S(2)}) collective-permute-start(f32[290,128]{1,0:T(8,128)S(1)} %slice_select_fusion.2), channel_id=1, source_target_pairs={{0,4},{1,5},{2,6},{3,7},{4,0},{5,1},{6,2},{7,3},{8,12},{9,13},{10,... | collective-permute-start | bytes 445448 | tf_op jit(solution)/shard_map/ppermute | solution.py:134
  61.3 5.4 %collective-permute-start.5 = (f32[145,128]{1,0:T(8,128)S(1)}, f32[145,128]{1,0:T(8,128)S(1)}, u32[]{:S(2)}, u32[]{:S(2)}) collective-permute-start(f32[145,128]{1,0:T(8,128)S(1)} %slice_select_fusion.3), channel_id=1, source_target_pairs={{0,8},{1,9},{2,10},{3,11},{4,12},{5,13},{6,14},{7,15},{8,0},{9,1},... | collective-permute-start | bytes 222728 | tf_op jit(solution)/shard_map/ppermute | solution.py:134
  66.7 5.5 %collective-permute-start.6 = (f32[145,128]{1,0:T(8,128)S(1)}, f32[145,128]{1,0:T(8,128)S(1)}, u32[]{:S(2)}, u32[]{:S(2)}) collective-permute-start(f32[145,128]{1,0:T(8,128)S(1)} %select_add_fusion.3), channel_id=1, source_target_pairs={{0,8},{1,9},{2,10},{3,11},{4,12},{5,13},{6,14},{7,15},{8,0},{9,1},... | collective-permute-start | bytes 222728 | tf_op jit(solution)/shard_map/ppermute | solution.py:138
  72.2 5.3 %collective-permute-start.7 = (f32[290,128]{1,0:T(8,128)S(1)}, f32[290,128]{1,0:T(8,128)S(1)}, u32[]{:S(2)}, u32[]{:S(2)}) collective-permute-start(f32[290,128]{1,0:T(8,128)S(1)} %maximum_select_fusion.3), channel_id=1, source_target_pairs={{0,4},{1,5},{2,6},{3,7},{4,0},{5,1},{6,2},{7,3},{8,12},{9,13},{10,... | collective-permute-start | bytes 445448 | tf_op jit(solution)/shard_map/ppermute | solution.py:138
  77.5 6.8 %collective-permute-start.8 = (f32[580,128]{1,0:T(8,128)S(1)}, f32[580,128]{1,0:T(8,128)S(1)}, u32[]{:S(2)}, u32[]{:S(2)}) collective-permute-start(f32[580,128]{1,0:T(8,128)S(1)} %maximum_select_fusion.2), channel_id=1, source_target_pairs={{0,2},{1,3},{2,0},{3,1},{4,6},{5,7},{6,4},{7,5},{8,10},{9,11},{10,... | collective-permute-start | bytes 890888 | tf_op jit(solution)/shard_map/ppermute | solution.py:138
  84.4 2.1 %collective-permute-start.9 = (f32[1160,128]{1,0:T(8,128)S(1)}, f32[1160,128]{1,0:T(8,128)S(1)}, u32[]{:S(2)}, u32[]{:S(2)}) collective-permute-start(f32[1160,128]{1,0:T(8,128)S(1)} %maximum_select_fusion.1), channel_id=1, source_target_pairs={{0,1},{1,0},{2,3},{3,2},{4,5},{5,4},{6,7},{7,6},{8,9},{9,8},{10,11... | collective-permute-start | bytes 1781768 | tf_op jit(solution)/shard_map/ppermute | solution.py:138
where the time goes:
time: 89.8 us; the launch traced here: 89.5 us
  waiting for transfers between devices  29.6 us (33%)
  starting transfers between devices  20.9 us (23%)
  Pallas kernels  19.2 us (21%)
  local copies, waits for them, and re-layouts  12.1 us (13%)
  other arithmetic  6.12 us (7%)
  between operations  1.58 us (2%)
    pallas_call x1, Pallas kernels, section(): pl.pallas_call(section_kernel, out_shape=(jax.ShapeDtypeStruct((count, wi...  19.2 us
    ppermute x4, waiting for transfers between devices, butterfly_sum(): got = lax.ppermute(send, 'rows', [(i, i ^ k) for i in range(n)])  15.6 us
    ppermute x4, waiting for transfers between devices, butterfly_sum(): got = lax.ppermute(piece, 'rows', [(i, i ^ k) for i in range(n)])  13.9 us
    ppermute x4, starting transfers between devices, butterfly_sum(): got = lax.ppermute(send, 'rows', [(i, i ^ k) for i in range(n)])  10.7 us
    ppermute x4, starting transfers between devices, butterfly_sum(): got = lax.ppermute(piece, 'rows', [(i, i ^ k) for i in range(n)])  5.69 us
    rev x2, local copies, waits for them, and re-layouts, back_matrix(): flipped = kernel.reshape(3, 3, c, o)[::-1, ::-1]  3.56 us
    ppermute x1, starting transfers between devices, local(): lax.ppermute(jnp.concatenate([inputs[-2:], cotangent[-2:]]), 'rows', up)  3.05 us
    reshape x5, local copies, waits for them, and re-layouts, forward_matrix(): kernel.reshape(3, 3, c, o).transpose(0, 2, 1, 3).reshape(3 * c, 3 * o)  1.92 us
  transfers between devices with their start and end apart: 10, of which 8 were waited for; matrix products, arithmetic and copies ran while one was open for 9% of the time, Pallas kernels for 0%

commit v1 on v0

v1 whole, which is shorter than its diff:
```python
import functools
import math

import jax
import jax.numpy as jnp
from jax import lax
from jax.experimental import pallas as pl
from jax.experimental.pallas import tpu as pltpu
from jax.sharding import PartitionSpec as P


def section_kernel(norm, idx_ref, lt_ref, x_hbm, c_hbm, before_hbm, after_hbm, k1_ref, k2_ref,
                   out_ref, ig_ref, grad_ref,
                   x_ref, c_ref, hid_ref, bf_ref, k1f_ref, k2f_ref, k2b_ref, k1b_ref, acc1, acc2, sems):
    count = out_ref.shape[0]
    width = out_ref.shape[1]
    ch = out_ref.shape[2]
    copies = [
        pltpu.make_async_copy(before_hbm.at[0:2], x_ref.at[0:2], sems.at[0]),
        pltpu.make_async_copy(x_hbm, x_ref.at[2 : count + 2], sems.at[1]),
        pltpu.make_async_copy(after_hbm.at[0:2], x_ref.at[count + 2 : count + 4], sems.at[2]),
        pltpu.make_async_copy(before_hbm.at[2:4], c_ref.at[0:2], sems.at[3]),
        pltpu.make_async_copy(c_hbm, c_ref.at[2 : count + 2], sems.at[4]),
        pltpu.make_async_copy(after_hbm.at[2:4], c_ref.at[count + 2 : count + 4], sems.at[5]),
    ]
    for cp in copies:
        cp.start()

    for a in range(3):
        for b in range(3):
            rows = slice(a * ch, (a + 1) * ch)
            cols = slice(b * ch, (b + 1) * ch)
            k1f_ref[rows, cols] = k1_ref[3 * a + b]
            k2f_ref[rows, cols] = k2_ref[3 * a + b]
            flip = 3 * (2 - a) + (2 - b)
            k2b_ref[rows, cols] = k2_ref[flip].astype(jnp.float32).T.astype(k2b_ref.dtype)
            k1b_ref[rows, cols] = k1_ref[flip].astype(jnp.float32).T.astype(k1b_ref.dtype)

    me = lax.axis_index("rows")
    size = lax.axis_size("rows")
    top = me > 0
    bottom = me < size - 1
    level = lt_ref[idx_ref[0]]
    scale = level[0:1, :] + 1.0
    shift = level[1:2, :]
    col = lax.broadcasted_iota(jnp.int32, (width, ch), 0)
    not_first = col > 0
    not_last = col < width - 1

    def combine(y):
        left = pltpu.roll(y[:, 0:ch], 1, 0)
        right = pltpu.roll(y[:, 2 * ch:3 * ch], width - 1, 0)
        return y[:, ch:2 * ch] + jnp.where(not_first, left, 0.0) + jnp.where(not_last, right, 0.0)

    def conv_row(ref, r, matrix_ref):
        rows = jnp.concatenate([ref[r], ref[r + 1], ref[r + 2]], axis=1)
        y = jnp.dot(rows, matrix_ref[...], preferred_element_type=jnp.float32)
        return combine(y)

    def shifted(g):
        g32 = g.astype(jnp.float32)
        g0 = jnp.where(not_last, pltpu.roll(g32, width - 1, 0), 0.0)
        g2 = jnp.where(not_first, pltpu.roll(g32, 1, 0), 0.0)
        return jnp.concatenate([g0.astype(g.dtype), g, g2.astype(g.dtype)], axis=1)

    for cp in copies:
        cp.wait()

    def phase_one(r, carry):
        lv0, lv1 = carry
        valid = jnp.logical_and(jnp.logical_or(r > 0, top), jnp.logical_or(r < count + 1, bottom))
        first = conv_row(x_ref, r, k1f_ref)
        mixed = first * scale + shift
        sig = 1.0 / (1.0 + jnp.exp(-mixed))
        hid_ref[r] = jnp.where(valid, mixed * sig, 0.0).astype(hid_ref.dtype)
        back_hidden = conv_row(c_ref, r, k2b_ref)
        back_mixed = back_hidden * (sig * (1.0 + mixed * (1.0 - sig)))
        bf_ref[r] = jnp.where(valid, back_mixed * scale, 0.0).astype(bf_ref.dtype)
        own = jnp.logical_and(r >= 1, r <= count)
        lv0 = lv0 + jnp.where(own, jnp.sum(back_mixed * first, axis=0, keepdims=True), 0.0)
        lv1 = lv1 + jnp.where(own, jnp.sum(back_mixed, axis=0, keepdims=True), 0.0)
        return lv0, lv1

    zero = jnp.zeros((1, ch), jnp.float32)
    lv0, lv1 = lax.fori_loop(0, count + 2, phase_one, (zero, zero))
    acc1[...] = jnp.zeros_like(acc1)
    acc2[...] = jnp.zeros_like(acc2)

    def phase_two(i, carry):
        out_ref[i] = (x_ref[i + 2].astype(jnp.float32) + conv_row(hid_ref, i, k2f_ref)).astype(out_ref.dtype)
        ig_ref[i] = (c_ref[i + 2].astype(jnp.float32) + conv_row(bf_ref, i, k1b_ref)).astype(ig_ref.dtype)
        xs = jnp.concatenate([x_ref[i + 1], x_ref[i + 2], x_ref[i + 3]], axis=1)
        gs = shifted(bf_ref[i + 1])
        acc1[...] += lax.dot_general(xs, gs, (((0,), (0,)), ((), ())), preferred_element_type=jnp.float32)
        hs = jnp.concatenate([hid_ref[i], hid_ref[i + 1], hid_ref[i + 2]], axis=1)
        cs = shifted(c_ref[i + 2])
        acc2[...] += lax.dot_general(hs, cs, (((0,), (0,)), ((), ())), preferred_element_type=jnp.float32)
        return carry

    lax.fori_loop(0, count, phase_two, 0)

    for a in range(3):
        for b in range(3):
            t = 3 * a + b
            blk = (slice(a * ch, (a + 1) * ch), slice(b * ch, (b + 1) * ch))
            grad_ref[t * ch : (t + 1) * ch, :] = acc1[blk] * norm
            grad_ref[(9 + t) * ch : (10 + t) * ch, :] = acc2[blk] * norm
    base = 18 * ch
    tail = grad_ref.shape[0] - base
    grad_ref[base:, :] = jnp.zeros((tail, ch), jnp.float32)
    grad_ref[base : base + 1, :] = lv0 * norm
    grad_ref[base + 1 : base + 2, :] = lv1 * norm


def section(norm, packed_rows, level_index, level_table, inputs, cotangent, before, after, k1, k2):
    count, width, ch = inputs.shape
    vmem = pltpu.MemorySpace.VMEM if hasattr(pltpu, "MemorySpace") else pltpu.VMEM
    spec = pl.BlockSpec(memory_space=vmem)
    anywhere = pl.BlockSpec(memory_space=pl.ANY)
    big = 3 * ch
    flops = 2 * (count + 2) * width * big * big * 2 + 4 * count * width * big * big * 2
    return pl.pallas_call(
        functools.partial(section_kernel, norm),
        out_shape=(
            jax.ShapeDtypeStruct((count, width, ch), jnp.bfloat16),
            jax.ShapeDtypeStruct((count, width, ch), jnp.bfloat16),
            jax.ShapeDtypeStruct((packed_rows, ch), jnp.float32),
        ),
        in_specs=[pl.BlockSpec(memory_space=pltpu.SMEM), spec] + [anywhere] * 4 + [spec] * 2,
        out_specs=(spec,) * 3,
        scratch_shapes=[
            pltpu.VMEM((count + 4, width, ch), jnp.bfloat16),
            pltpu.VMEM((count + 4, width, ch), jnp.bfloat16),
            pltpu.VMEM((count + 2, width, ch), jnp.bfloat16),
            pltpu.VMEM((count + 2, width, ch), jnp.bfloat16),
            pltpu.VMEM((big, big), jnp.bfloat16),
            pltpu.VMEM((big, big), jnp.bfloat16),
            pltpu.VMEM((big, big), jnp.bfloat16),
            pltpu.VMEM((big, big), jnp.bfloat16),
            pltpu.VMEM((big, big), jnp.float32),
            pltpu.VMEM((big, big), jnp.float32),
            pltpu.SemaphoreType.DMA((6,)),
        ],
        compiler_params=pltpu.CompilerParams(vmem_limit_bytes=60 * 1024 * 1024),
        cost_estimate=pl.CostEstimate(
            flops=flops, transcendentals=(count + 2) * width * ch, bytes_accessed=6 * count * width * ch
        ),
    )(level_index, level_table, inputs, cotangent, before, after, k1, k2)


def butterfly_sum(block):
    n = lax.axis_size("rows")
    me = lax.axis_index("rows")
    steps = []
    k = 1
    while k < n:
        steps.append(k)
        k *= 2
    if len(steps) > 2:
        steps = steps[:1] + steps[2:] + steps[1:2]
    piece = block
    for k in steps:
        half = piece.shape[0] // 2
        low = (me // k) % 2 == 0
        lo, hi = piece[:half], piece[half:]
        keep = jnp.where(low, lo, hi)
        send = jnp.where(low, hi, lo)
        got = lax.ppermute(send, "rows", [(i, i ^ k) for i in range(n)])
        piece = keep + got
    for k in reversed(steps):
        low = (me // k) % 2 == 0
        got = lax.ppermute(piece, "rows", [(i, i ^ k) for i in range(n)])
        piece = jnp.where(low, jnp.concatenate([piece, got]), jnp.concatenate([got, piece]))
    return piece


def local(inputs, cotangent, first_kernel, second_kernel, level_table, level_index):
    count = inputs.shape[0]
    width = inputs.shape[1]
    ch = inputs.shape[2]
    size = lax.axis_size("rows")
    total_rows = count * size
    norm = 1.0 / math.sqrt(total_rows * width)

    up = [(i, i + 1) for i in range(size - 1)]
    down = [(i + 1, i) for i in range(size - 1)]
    before = lax.ppermute(jnp.concatenate([inputs[-2:], cotangent[-2:]]), "rows", up)
    after = lax.ppermute(jnp.concatenate([inputs[:2], cotangent[:2]]), "rows", down)

    used = 18 * ch + 2
    packed_rows = used + (-used % size)
    outputs, input_grad, packed = section(
        norm, packed_rows, level_index, level_table, inputs, cotangent, before, after,
        first_kernel, second_kernel,
    )
    total = butterfly_sum(packed)
    first_sum = total[: 9 * ch].reshape(9, ch, ch)
    second_sum = total[9 * ch : 18 * ch].reshape(9, ch, ch)
    level_sum = total[18 * ch : 18 * ch + 2]
    return (outputs, input_grad, first_sum, second_sum, level_sum)


def solution(mesh):
    return jax.shard_map(
        local,
        mesh=mesh,
        in_specs=(
            P(("groups", "rows"), None, None),
            P(("groups", "rows"), None, None),
            P(),
            P(),
            P(),
            P("groups"),
        ),
        out_specs=(
            P(("groups", "rows"), None, None),
            P(("groups", "rows"), None, None),
            P("groups", None, None),
            P("groups", None, None),
            P("groups", None),
        ),
        check_vma=False,
    )
```

time: 89.8 us -> 91.6 us (1.020)
  waiting for transfers between devices: 29.6 us -> 42.8 us
  local copies, waits for them, and re-layouts: 12.1 us -> 3.72 us
  other arithmetic: 6.12 us -> 2.09 us
    ppermute x4, waiting for transfers between devices: 13.9 us -> 19.5 us  [butterfly_sum(): got = lax.ppermute(piece, 'rows', [(i, i ^ k) for i in range(n)])]
    ppermute x4, starting transfers between devices: 10.7 us -> 15.9 us  [butterfly_sum(): got = lax.ppermute(send, 'rows', [(i, i ^ k) for i in range(n)])]
    reshape x8 -> x0, local copies, waits for them, and re-layouts: 4.02 us -> none  [the longest x5 1.92 us: forward_matrix(): kernel.reshape(3, 3, c, o).transpose(0, 2, 1, 3).reshape(3 * c, 3 * o)]
    ppermute x4, starting transfers between devices: 5.69 us -> 1.68 us  [butterfly_sum(): got = lax.ppermute(piece, 'rows', [(i, i ^ k) for i in range(n)])]
    ppermute x1, waiting for transfers between devices: 0.01 us -> 3.92 us  [local(): lax.ppermute(jnp.concatenate([inputs[:2], cotangent[:2]]), 'rows', down)]
    ppermute x4, waiting for transfers between devices: 15.6 us -> 19.3 us  [butterfly_sum(): got = lax.ppermute(send, 'rows', [(i, i ^ k) for i in range(n)])]
    rev x2 -> x0, local copies, waits for them, and re-layouts: 3.56 us -> none  [back_matrix(): flipped = kernel.reshape(3, 3, c, o)[::-1, ::-1]]
    concatenate x2 -> x0, other arithmetic: 2.68 us -> none  [the longest x1 1.34 us: local(): x12 = jnp.concatenate([before[:2], inputs, after[:2]])]
  transfers between devices with their start and end apart: 10 -> 10, of which waited for: 8 -> 9; matrix products, arithmetic and copies ran while one was open for 9% -> 0% of each run, Pallas kernels for 0% -> 0%
where the time goes in v1:
time: 91.6 us; the launch traced here: 91.3 us
  waiting for transfers between devices  42.8 us (47%)
  starting transfers between devices  21.3 us (23%)
  Pallas kernels  20 us (22%)
  local copies, waits for them, and re-layouts  3.72 us (4%)
  other arithmetic  2.09 us (2%)
  between operations  1.44 us (2%)
    pallas_call x1, Pallas kernels, section(): pl.pallas_call(functools.partial(section_kernel, norm), out_shape=(jax.Sh...  20 us
    ppermute x4, waiting for transfers between devices, butterfly_sum(): got = lax.ppermute(piece, 'rows', [(i, i ^ k) for i in range(n)])  19.5 us
    ppermute x4, waiting for transfers between devices, butterfly_sum(): got = lax.ppermute(send, 'rows', [(i, i ^ k) for i in range(n)])  19.3 us
    ppermute x4, starting transfers between devices, butterfly_sum(): got = lax.ppermute(send, 'rows', [(i, i ^ k) for i in range(n)])  15.9 us
    ppermute x1, waiting for transfers between devices, local(): lax.ppermute(jnp.concatenate([inputs[:2], cotangent[:2]]), 'rows', down)  3.92 us
    ppermute x1, starting transfers between devices, local(): lax.ppermute(jnp.concatenate([inputs[-2:], cotangent[-2:]]), 'rows', up)  2.39 us
  transfers between devices with their start and end apart: 10, of which 9 were waited for; matrix products, arithmetic and copies ran while one was open for 0% of the time, Pallas kernels for 0%

profile of v1, /device:TPU:0, one launch (start us, length us, event | category | flops | bytes accessed | tf_op | source)
XLA Modules:
  0.0 91.3 jit_solution(5180166374314386681)
XLA Ops:
  0.6 1.3 %fusion.1 = (bf16[2,512,128]{2,1,0:T(8,128)(2,1)S(1)}, bf16[2,512,128]{2,1,0:T(8,128)(2,1)S(1)}, bf16[2,512,128]{2,1,0:T(8,128)(2,1)S(1)}, bf16[2,512,128]{2,1,0:T(8,128)(2,1)S(1)}) fusion(bf16[8,512,128]{2,1,0:T(8,128)(2,1)} %x_hbm.1, bf16[8,512,128]{2,1,0:T(8,128)(2,1)} %c_hbm.1), kind=kLoop, calls=%fused_computation.15 | loop fusion | bytes 2097152 | tf_op jit(solution)/shard_map/slice | solution.py:188
  2.0 2.4 %collective-permute-start = (bf16[4,512,128]{2,1,0:T(8,128)(2,1)S(1)}, bf16[4,512,128]{2,1,0:T(8,128)(2,1)S(1)}, u32[]{:S(2)}, u32[]{:S(2)}) collective-permute-start(bf16[4,512,128]{2,1,0:T(8,128)(2,1)S(1)} %pad_maximum_fusion), channel_id=1, source_target_pairs={{0,1},{1,2},{2,3},{3,4},{4,5},{5,6},{6,7},{7,8},{8,9},{9,10},{10,1... | collective-permute-start | bytes 1572872 | tf_op jit(solution)/shard_map/ppermute | solution.py:187
  4.4 1.3 %collective-permute-start.1 = (bf16[4,512,128]{2,1,0:T(8,128)(2,1)S(1)}, bf16[4,512,128]{2,1,0:T(8,128)(2,1)S(1)}, u32[]{:S(2)}, u32[]{:S(2)}) collective-permute-start(bf16[4,512,128]{2,1,0:T(8,128)(2,1)S(1)} %pad_maximum_fusion.1), channel_id=1, source_target_pairs={{1,0},{2,1},{3,2},{4,3},{5,4},{6,5},{7,6},{8,7},{9,8},{10,9},{11,1... | collective-permute-start | bytes 1572872 | tf_op jit(solution)/shard_map/ppermute | solution.py:188
  6.4 0.0 collective-permute-done.before_hbm
  6.4 0.0 copy-start.1
  6.4 3.9 %collective-permute-done.1.after_hbm = bf16[4,512,128]{2,1,0:T(8,128)(2,1)S(1)} collective-permute-done((bf16[4,512,128]{2,1,0:T(8,128)(2,1)S(1)}, bf16[4,512,128]{2,1,0:T(8,128)(2,1)S(1)}, u32[]{:S(2)}, u32[]{:S(2)}) %collective-permute-start.1) | collective-permute-done | bytes 524320 | tf_op jit(solution)/shard_map/ppermute | solution.py:188
  10.3 0.0 copy-done.1
  10.3 0.8 copy-done.2
  11.1 20.0 %shard_map.101 = (bf16[8,512,128]{2,1,0:T(8,128)(2,1)}, bf16[8,512,128]{2,1,0:T(8,128)(2,1)}, f32[2320,128]{1,0:T(8,128)}) custom-call(s32[1]{0:T(128)S(6)} %copy.11.idx_ref, f32[16,2,128]{2,1,0:T(2,128)} %lt_ref.1, bf16[8,512,128]{2,1,0:T(8,128)(2,1)} %x_hbm.1, bf16[8,512,128]{2,1,0:T(8,128)(2,1)} %c_hbm.1, bf16[4,512,128]{2,1,0:T(8,128)(2,1)} %copy-done.1, ...), custom_call_target="tpu_custom_call" | custom-call | flops 7851737088 | bytes 3145728 | tf_op jit(solution)/shard_map/pallas_call | solution.py:122
  31.2 1.4 %slice_select_fusion = f32[1160,128]{1,0:T(8,128)S(1)} fusion(f32[2320,128]{1,0:T(8,128)} %get-tuple-element.10, pred[]{:T(512)S(6)} %eq.25), kind=kLoop, calls=%fused_computation.3 | loop fusion | flops 148480 | bytes 1781761 | tf_op jit(solution)/shard_map/jit(_where)/select_n | solution.py:167
  32.6 9.2 %collective-permute-start.2 = (f32[1160,128]{1,0:T(8,128)S(1)}, f32[1160,128]{1,0:T(8,128)S(1)}, u32[]{:S(2)}, u32[]{:S(2)}) collective-permute-start(f32[1160,128]{1,0:T(8,128)S(1)} %slice_select_fusion), channel_id=1, source_target_pairs={{0,1},{1,0},{2,3},{3,2},{4,5},{5,4},{6,7},{7,6},{8,9},{9,8},{10,11... | collective-permute-start | bytes 1781768 | tf_op jit(solution)/shard_map/ppermute | solution.py:168
  41.8 1.6 %collective-permute-done.2 = f32[1160,128]{1,0:T(8,128)S(1)} collective-permute-done((f32[1160,128]{1,0:T(8,128)S(1)}, f32[1160,128]{1,0:T(8,128)S(1)}, u32[]{:S(2)}, u32[]{:S(2)}) %collective-permute-start.2) | collective-permute-done | bytes 593952 | tf_op jit(solution)/shard_map/ppermute | solution.py:168
  43.4 0.1 select_add_fusion
  43.6 2.4 %collective-permute-start.3 = (f32[580,128]{1,0:T(8,128)S(1)}, f32[580,128]{1,0:T(8,128)S(1)}, u32[]{:S(2)}, u32[]{:S(2)}) collective-permute-start(f32[580,128]{1,0:T(8,128)S(1)} %slice_select_fusion.1), channel_id=1, source_target_pairs={{0,4},{1,5},{2,6},{3,7},{4,0},{5,1},{6,2},{7,3},{8,12},{9,13},{10,... | collective-permute-start | bytes 890888 | tf_op jit(solution)/shard_map/ppermute | solution.py:168
  46.0 7.6 %collective-permute-done.3 = f32[580,128]{1,0:T(8,128)S(1)} collective-permute-done((f32[580,128]{1,0:T(8,128)S(1)}, f32[580,128]{1,0:T(8,128)S(1)}, u32[]{:S(2)}, u32[]{:S(2)}) %collective-permute-start.3) | collective-permute-done | bytes 296992 | tf_op jit(solution)/shard_map/ppermute | solution.py:168
  53.6 0.1 select_add_fusion.1
  53.7 2.8 %collective-permute-start.4 = (f32[290,128]{1,0:T(8,128)S(1)}, f32[290,128]{1,0:T(8,128)S(1)}, u32[]{:S(2)}, u32[]{:S(2)}) collective-permute-start(f32[290,128]{1,0:T(8,128)S(1)} %slice_select_fusion.2), channel_id=1, source_target_pairs={{0,8},{1,9},{2,10},{3,11},{4,12},{5,13},{6,14},{7,15},{8,0},{9,1},... | collective-permute-start | bytes 445448 | tf_op jit(solution)/shard_map/ppermute | solution.py:168
  56.6 7.0 %collective-permute-done.4 = f32[290,128]{1,0:T(8,128)S(1)} collective-permute-done((f32[290,128]{1,0:T(8,128)S(1)}, f32[290,128]{1,0:T(8,128)S(1)}, u32[]{:S(2)}, u32[]{:S(2)}) %collective-permute-start.4) | collective-permute-done | bytes 148512 | tf_op jit(solution)/shard_map/ppermute | solution.py:168
  63.6 1.5 %collective-permute-start.5 = (f32[145,128]{1,0:T(8,128)S(1)}, f32[145,128]{1,0:T(8,128)S(1)}, u32[]{:S(2)}, u32[]{:S(2)}) collective-permute-start(f32[145,128]{1,0:T(8,128)S(1)} %slice_select_fusion.3), channel_id=1, source_target_pairs={{0,2},{1,3},{2,0},{3,1},{4,6},{5,7},{6,4},{7,5},{8,10},{9,11},{10,... | collective-permute-start | bytes 222728 | tf_op jit(solution)/shard_map/ppermute | solution.py:168
  65.1 3.0 %collective-permute-done.5 = f32[145,128]{1,0:T(8,128)S(1)} collective-permute-done((f32[145,128]{1,0:T(8,128)S(1)}, f32[145,128]{1,0:T(8,128)S(1)}, u32[]{:S(2)}, u32[]{:S(2)}) %collective-permute-start.5) | collective-permute-done | bytes 74272 | tf_op jit(solution)/shard_map/ppermute | solution.py:168
  68.1 1.5 %collective-permute-start.6 = (f32[145,128]{1,0:T(8,128)S(1)}, f32[145,128]{1,0:T(8,128)S(1)}, u32[]{:S(2)}, u32[]{:S(2)}) collective-permute-start(f32[145,128]{1,0:T(8,128)S(1)} %select_add_fusion.3), channel_id=1, source_target_pairs={{0,2},{1,3},{2,0},{3,1},{4,6},{5,7},{6,4},{7,5},{8,10},{9,11},{10,... | collective-permute-start | bytes 222728 | tf_op jit(solution)/shard_map/ppermute | solution.py:172
  69.6 3.0 %collective-permute-done.6 = f32[145,128]{1,0:T(8,128)S(1)} collective-permute-done((f32[145,128]{1,0:T(8,128)S(1)}, f32[145,128]{1,0:T(8,128)S(1)}, u32[]{:S(2)}, u32[]{:S(2)}) %collective-permute-start.6) | collective-permute-done | bytes 74272 | tf_op jit(solution)/shard_map/ppermute | solution.py:172
  72.6 0.1 collective-permute-start.7
  72.7 7.8 %collective-permute-done.7 = f32[290,128]{1,0:T(8,128)S(1)} collective-permute-done((f32[290,128]{1,0:T(8,128)S(1)}, f32[290,128]{1,0:T(8,128)S(1)}, u32[]{:S(2)}, u32[]{:S(2)}) %collective-permute-start.7) | collective-permute-done | bytes 148512 | tf_op jit(solution)/shard_map/ppermute | solution.py:172
  80.5 0.1 collective-permute-start.8
  80.6 6.8 %collective-permute-done.8 = f32[580,128]{1,0:T(8,128)S(1)} collective-permute-done((f32[580,128]{1,0:T(8,128)S(1)}, f32[580,128]{1,0:T(8,128)S(1)}, u32[]{:S(2)}, u32[]{:S(2)}) %collective-permute-start.8) | collective-permute-done | bytes 296992 | tf_op jit(solution)/shard_map/ppermute | solution.py:172
  87.4 0.1 maximum_select_fusion.1
  87.5 0.1 collective-permute-start.9
  87.5 2.0 %collective-permute-done.9 = f32[1160,128]{1,0:T(8,128)S(1)} collective-permute-done((f32[1160,128]{1,0:T(8,128)S(1)}, f32[1160,128]{1,0:T(8,128)S(1)}, u32[]{:S(2)}, u32[]{:S(2)}) %collective-permute-start.9) | collective-permute-done | bytes 593952 | tf_op jit(solution)/shard_map/ppermute | solution.py:172
  89.5 0.1 maximum_select_fusion
  89.7 0.6 slice.68
  90.2 1.1 %fusion = (f32[1152,128]{1,0:T(8,128)}, f32[1152,128]{1,0:T(8,128)}) fusion(f32[2320,128]{1,0:T(8,128)S(1)} %maximum_select_fusion), kind=kLoop, calls=%fused_computation.14 | loop fusion | bytes 2359296 | tf_op jit(solution)/shard_map/slice | solution.py:198
  (12 shorter events, 0.3 us)
Async XLA Ops:
  2.0 4.4 %collective-permute-start = (bf16[4,512,128]{2,1,0:T(8,128)(2,1)S(1)}, bf16[4,512,128]{2,1,0:T(8,128)(2,1)S(1)}, u32[]{:S(2)}, u32[]{:S(2)}) collective-permute-start(bf16[4,512,128]{2,1,0:T(8,128)(2,1)S(1)} %pad_maximum_fusion), channel_id=1, source_target_pairs={{0,1},{1,2},{2,3},{3,4},{4,5},{5,6},{6,7},{7,8},{8,9},{9,10},{10,1... | collective-permute-start | bytes 1572872 | tf_op jit(solution)/shard_map/ppermute | solution.py:187
  4.4 5.9 %collective-permute-start.1 = (bf16[4,512,128]{2,1,0:T(8,128)(2,1)S(1)}, bf16[4,512,128]{2,1,0:T(8,128)(2,1)S(1)}, u32[]{:S(2)}, u32[]{:S(2)}) collective-permute-start(bf16[4,512,128]{2,1,0:T(8,128)(2,1)S(1)} %pad_maximum_fusion.1), channel_id=1, source_target_pairs={{1,0},{2,1},{3,2},{4,3},{5,4},{6,5},{7,6},{8,7},{9,8},{10,9},{11,1... | collective-permute-start | bytes 1572872 | tf_op jit(solution)/shard_map/ppermute | solution.py:188
  6.4 3.9 %copy-start.1 = (bf16[4,512,128]{2,1,0:T(8,128)(2,1)}, bf16[4,512,128]{2,1,0:T(8,128)(2,1)S(1)}, u32[]{:S(2)}) copy-start(bf16[4,512,128]{2,1,0:T(8,128)(2,1)S(1)} %collective-permute-done.before_hbm) | copy-start | bytes 1572868
  10.3 0.8 copy-start.2
  31.2 12.3 %copy-start = (f32[2320,128]{1,0:T(8,128)S(1)}, f32[2320,128]{1,0:T(8,128)}, u32[]{:S(2)}) copy-start(f32[2320,128]{1,0:T(8,128)} %get-tuple-element.10) | copy-start | bytes 3563524
  32.6 10.9 %collective-permute-start.2 = (f32[1160,128]{1,0:T(8,128)S(1)}, f32[1160,128]{1,0:T(8,128)S(1)}, u32[]{:S(2)}, u32[]{:S(2)}) collective-permute-start(f32[1160,128]{1,0:T(8,128)S(1)} %slice_select_fusion), channel_id=1, source_target_pairs={{0,1},{1,0},{2,3},{3,2},{4,5},{5,4},{6,7},{7,6},{8,9},{9,8},{10,11... | collective-permute-start | bytes 1781768 | tf_op jit(solution)/shard_map/ppermute | solution.py:168
  43.6 10.1 %collective-permute-start.3 = (f32[580,128]{1,0:T(8,128)S(1)}, f32[580,128]{1,0:T(8,128)S(1)}, u32[]{:S(2)}, u32[]{:S(2)}) collective-permute-start(f32[580,128]{1,0:T(8,128)S(1)} %slice_select_fusion.1), channel_id=1, source_target_pairs={{0,4},{1,5},{2,6},{3,7},{4,0},{5,1},{6,2},{7,3},{8,12},{9,13},{10,... | collective-permute-start | bytes 890888 | tf_op jit(solution)/shard_map/ppermute | solution.py:168
  53.7 9.9 %collective-permute-start.4 = (f32[290,128]{1,0:T(8,128)S(1)}, f32[290,128]{1,0:T(8,128)S(1)}, u32[]{:S(2)}, u32[]{:S(2)}) collective-permute-start(f32[290,128]{1,0:T(8,128)S(1)} %slice_select_fusion.2), channel_id=1, source_target_pairs={{0,8},{1,9},{2,10},{3,11},{4,12},{5,13},{6,14},{7,15},{8,0},{9,1},... | collective-permute-start | bytes 445448 | tf_op jit(solution)/shard_map/ppermute | solution.py:168
  63.6 4.5 %collective-permute-start.5 = (f32[145,128]{1,0:T(8,128)S(1)}, f32[145,128]{1,0:T(8,128)S(1)}, u32[]{:S(2)}, u32[]{:S(2)}) collective-permute-start(f32[145,128]{1,0:T(8,128)S(1)} %slice_select_fusion.3), channel_id=1, source_target_pairs={{0,2},{1,3},{2,0},{3,1},{4,6},{5,7},{6,4},{7,5},{8,10},{9,11},{10,... | collective-permute-start | bytes 222728 | tf_op jit(solution)/shard_map/ppermute | solution.py:168
  68.1 4.5 %collective-permute-start.6 = (f32[145,128]{1,0:T(8,128)S(1)}, f32[145,128]{1,0:T(8,128)S(1)}, u32[]{:S(2)}, u32[]{:S(2)}) collective-permute-start(f32[145,128]{1,0:T(8,128)S(1)} %select_add_fusion.3), channel_id=1, source_target_pairs={{0,2},{1,3},{2,0},{3,1},{4,6},{5,7},{6,4},{7,5},{8,10},{9,11},{10,... | collective-permute-start | bytes 222728 | tf_op jit(solution)/shard_map/ppermute | solution.py:172
  72.6 7.9 %collective-permute-start.7 = (f32[290,128]{1,0:T(8,128)S(1)}, f32[290,128]{1,0:T(8,128)S(1)}, u32[]{:S(2)}, u32[]{:S(2)}) collective-permute-start(f32[290,128]{1,0:T(8,128)S(1)} %maximum_select_fusion.3), channel_id=1, source_target_pairs={{0,8},{1,9},{2,10},{3,11},{4,12},{5,13},{6,14},{7,15},{8,0},{9,1},... | collective-permute-start | bytes 445448 | tf_op jit(solution)/shard_map/ppermute | solution.py:172
  80.5 6.8 %collective-permute-start.8 = (f32[580,128]{1,0:T(8,128)S(1)}, f32[580,128]{1,0:T(8,128)S(1)}, u32[]{:S(2)}, u32[]{:S(2)}) collective-permute-start(f32[580,128]{1,0:T(8,128)S(1)} %maximum_select_fusion.2), channel_id=1, source_target_pairs={{0,4},{1,5},{2,6},{3,7},{4,0},{5,1},{6,2},{7,3},{8,12},{9,13},{10,... | collective-permute-start | bytes 890888 | tf_op jit(solution)/shard_map/ppermute | solution.py:172
  87.5 2.1 %collective-permute-start.9 = (f32[1160,128]{1,0:T(8,128)S(1)}, f32[1160,128]{1,0:T(8,128)S(1)}, u32[]{:S(2)}, u32[]{:S(2)}) collective-permute-start(f32[1160,128]{1,0:T(8,128)S(1)} %maximum_select_fusion.1), channel_id=1, source_target_pairs={{0,1},{1,0},{2,3},{3,2},{4,5},{5,4},{6,7},{7,6},{8,9},{9,8},{10,11... | collective-permute-start | bytes 1781768 | tf_op jit(solution)/shard_map/ppermute | solution.py:172

commit v2 on v1

--- a/solution.py
+++ b/solution.py
@@ -151,25 +151,34 @@
 def butterfly_sum(block):
     n = lax.axis_size("rows")
     me = lax.axis_index("rows")
-    steps = []
+    bits = []
     k = 1
     while k < n:
-        steps.append(k)
+        bits.append(k)
         k *= 2
-    if len(steps) > 2:
-        steps = steps[:1] + steps[2:] + steps[1:2]
+    other = list(bits)
+    if len(bits) > 2:
+        other[1], other[2] = bits[2], bits[1]
+    orders = list(zip(bits, other))
+    even = me % 2 == 0
+
+    def step_of(k0, k1):
+        perm = [(i, i ^ (k0 if i % 2 == 0 else k1)) for i in range(n)]
+        low = jnp.where(even, (me // k0) % 2, (me // k1) % 2) == 0
+        return perm, low
+
     piece = block
-    for k in steps:
+    for k0, k1 in orders:
+        perm, low = step_of(k0, k1)
         half = piece.shape[0] // 2
-        low = (me // k) % 2 == 0
         lo, hi = piece[:half], piece[half:]
         keep = jnp.where(low, lo, hi)
         send = jnp.where(low, hi, lo)
-        got = lax.ppermute(send, "rows", [(i, i ^ k) for i in range(n)])
+        got = lax.ppermute(send, "rows", perm)
         piece = keep + got
-    for k in reversed(steps):
-        low = (me // k) % 2 == 0
-        got = lax.ppermute(piece, "rows", [(i, i ^ k) for i in range(n)])
+    for k0, k1 in reversed(orders):
+        perm, low = step_of(k0, k1)
+        got = lax.ppermute(piece, "rows", perm)
         piece = jnp.where(low, jnp.concatenate([piece, got]), jnp.concatenate([got, piece]))
     return piece
 

time: 91.6 us -> 85 us (0.928)
  waiting for transfers between devices: 42.8 us -> 30.2 us
  starting transfers between devices: 21.3 us -> 27.3 us
    ppermute x8, waiting for transfers between devices: 38.8 us -> 26.2 us  [the longest x4 13.6 us: butterfly_sum(): got = lax.ppermute(piece, 'rows', perm)]
    ppermute x8, starting transfers between devices: 17.6 us -> 23.6 us  [the longest x4 16.4 us: butterfly_sum(): got = lax.ppermute(send, 'rows', perm)]
where the time goes in v2:
time: 85 us; the launch traced here: 84.7 us
  waiting for transfers between devices  30.2 us (36%)
  starting transfers between devices  27.3 us (32%)
  Pallas kernels  20 us (24%)
  local copies, waits for them, and re-layouts  3.72 us (4%)
  other arithmetic  2.09 us (2%)
  between operations  1.43 us (2%)
    pallas_call x1, Pallas kernels, section(): pl.pallas_call(functools.partial(section_kernel, norm), out_shape=(jax.Sh...  20 us
    ppermute x4, starting transfers between devices, butterfly_sum(): got = lax.ppermute(send, 'rows', perm)  16.4 us
    ppermute x4, waiting for transfers between devices, butterfly_sum(): got = lax.ppermute(piece, 'rows', perm)  13.6 us
    ppermute x4, waiting for transfers between devices, butterfly_sum(): got = lax.ppermute(send, 'rows', perm)  12.6 us
    ppermute x4, starting transfers between devices, butterfly_sum(): got = lax.ppermute(piece, 'rows', perm)  7.19 us
    ppermute x1, waiting for transfers between devices, local(): lax.ppermute(jnp.concatenate([inputs[:2], cotangent[:2]]), 'rows', down)  3.92 us
    ppermute x1, starting transfers between devices, local(): lax.ppermute(jnp.concatenate([inputs[-2:], cotangent[-2:]]), 'rows', up)  2.39 us
  transfers between devices with their start and end apart: 10, of which 9 were waited for; matrix products, arithmetic and copies ran while one was open for 0% of the time, Pallas kernels for 0%

profile of v2, /device:TPU:0, one launch (start us, length us, event | category | flops | bytes accessed | tf_op | source)
XLA Modules:
  0.0 84.7 jit_solution(17011290667720278082)
XLA Ops:
  0.6 1.3 %fusion.1 = (bf16[2,512,128]{2,1,0:T(8,128)(2,1)S(1)}, bf16[2,512,128]{2,1,0:T(8,128)(2,1)S(1)}, bf16[2,512,128]{2,1,0:T(8,128)(2,1)S(1)}, bf16[2,512,128]{2,1,0:T(8,128)(2,1)S(1)}) fusion(bf16[8,512,128]{2,1,0:T(8,128)(2,1)} %x_hbm.1, bf16[8,512,128]{2,1,0:T(8,128)(2,1)} %c_hbm.1), kind=kLoop, calls=%fused_computation.15 | loop fusion | bytes 2097152 | tf_op jit(solution)/shard_map/slice | solution.py:197
  2.0 2.4 %collective-permute-start = (bf16[4,512,128]{2,1,0:T(8,128)(2,1)S(1)}, bf16[4,512,128]{2,1,0:T(8,128)(2,1)S(1)}, u32[]{:S(2)}, u32[]{:S(2)}) collective-permute-start(bf16[4,512,128]{2,1,0:T(8,128)(2,1)S(1)} %pad_maximum_fusion), channel_id=1, source_target_pairs={{0,1},{1,2},{2,3},{3,4},{4,5},{5,6},{6,7},{7,8},{8,9},{9,10},{10,1... | collective-permute-start | bytes 1572872 | tf_op jit(solution)/shard_map/ppermute | solution.py:196
  4.4 1.3 %collective-permute-start.1 = (bf16[4,512,128]{2,1,0:T(8,128)(2,1)S(1)}, bf16[4,512,128]{2,1,0:T(8,128)(2,1)S(1)}, u32[]{:S(2)}, u32[]{:S(2)}) collective-permute-start(bf16[4,512,128]{2,1,0:T(8,128)(2,1)S(1)} %pad_maximum_fusion.1), channel_id=1, source_target_pairs={{1,0},{2,1},{3,2},{4,3},{5,4},{6,5},{7,6},{8,7},{9,8},{10,9},{11,1... | collective-permute-start | bytes 1572872 | tf_op jit(solution)/shard_map/ppermute | solution.py:197
  6.4 0.0 collective-permute-done.before_hbm
  6.4 0.0 copy-start.1
  6.4 3.9 %collective-permute-done.1.after_hbm = bf16[4,512,128]{2,1,0:T(8,128)(2,1)S(1)} collective-permute-done((bf16[4,512,128]{2,1,0:T(8,128)(2,1)S(1)}, bf16[4,512,128]{2,1,0:T(8,128)(2,1)S(1)}, u32[]{:S(2)}, u32[]{:S(2)}) %collective-permute-start.1) | collective-permute-done | bytes 524320 | tf_op jit(solution)/shard_map/ppermute | solution.py:197
  10.3 0.0 copy-done.1
  10.3 0.8 copy-done.2
  11.1 20.0 %shard_map.101 = (bf16[8,512,128]{2,1,0:T(8,128)(2,1)}, bf16[8,512,128]{2,1,0:T(8,128)(2,1)}, f32[2320,128]{1,0:T(8,128)}) custom-call(s32[1]{0:T(128)S(6)} %copy.11.idx_ref, f32[16,2,128]{2,1,0:T(2,128)} %lt_ref.1, bf16[8,512,128]{2,1,0:T(8,128)(2,1)} %x_hbm.1, bf16[8,512,128]{2,1,0:T(8,128)(2,1)} %c_hbm.1, bf16[4,512,128]{2,1,0:T(8,128)(2,1)} %copy-done.1, ...), custom_call_target="tpu_custom_call" | custom-call | flops 7851737088 | bytes 3145728 | tf_op jit(solution)/shard_map/pallas_call | solution.py:122
  31.2 1.4 %slice_select_fusion = f32[1160,128]{1,0:T(8,128)S(1)} fusion(f32[2320,128]{1,0:T(8,128)} %get-tuple-element.10, pred[]{:T(512)S(6)} %eq.35), kind=kLoop, calls=%fused_computation.3 | loop fusion | flops 148480 | bytes 1781761 | tf_op jit(solution)/shard_map/jit(_where)/select_n | solution.py:176
  32.6 9.2 %collective-permute-start.2 = (f32[1160,128]{1,0:T(8,128)S(1)}, f32[1160,128]{1,0:T(8,128)S(1)}, u32[]{:S(2)}, u32[]{:S(2)}) collective-permute-start(f32[1160,128]{1,0:T(8,128)S(1)} %slice_select_fusion), channel_id=1, source_target_pairs={{0,1},{1,0},{2,3},{3,2},{4,5},{5,4},{6,7},{7,6},{8,9},{9,8},{10,11... | collective-permute-start | bytes 1781768 | tf_op jit(solution)/shard_map/ppermute | solution.py:177
  41.8 1.6 %collective-permute-done.2 = f32[1160,128]{1,0:T(8,128)S(1)} collective-permute-done((f32[1160,128]{1,0:T(8,128)S(1)}, f32[1160,128]{1,0:T(8,128)S(1)}, u32[]{:S(2)}, u32[]{:S(2)}) %collective-permute-start.2) | collective-permute-done | bytes 593952 | tf_op jit(solution)/shard_map/ppermute | solution.py:177
  43.4 0.1 select_add_fusion
  43.6 2.8 %collective-permute-start.3 = (f32[580,128]{1,0:T(8,128)S(1)}, f32[580,128]{1,0:T(8,128)S(1)}, u32[]{:S(2)}, u32[]{:S(2)}) collective-permute-start(f32[580,128]{1,0:T(8,128)S(1)} %slice_select_fusion.1), channel_id=1, source_target_pairs={{0,2},{1,5},{2,0},{3,7},{4,6},{5,1},{6,4},{7,3},{8,10},{9,13},{10,... | collective-permute-start | bytes 890888 | tf_op jit(solution)/shard_map/ppermute | solution.py:177
  46.4 4.7 %collective-permute-done.3 = f32[580,128]{1,0:T(8,128)S(1)} collective-permute-done((f32[580,128]{1,0:T(8,128)S(1)}, f32[580,128]{1,0:T(8,128)S(1)}, u32[]{:S(2)}, u32[]{:S(2)}) %collective-permute-start.3) | collective-permute-done | bytes 296992 | tf_op jit(solution)/shard_map/ppermute | solution.py:177
  51.1 0.1 select_add_fusion.1
  51.2 1.7 %collective-permute-start.4 = (f32[290,128]{1,0:T(8,128)S(1)}, f32[290,128]{1,0:T(8,128)S(1)}, u32[]{:S(2)}, u32[]{:S(2)}) collective-permute-start(f32[290,128]{1,0:T(8,128)S(1)} %slice_select_fusion.2), channel_id=1, source_target_pairs={{0,4},{1,3},{2,6},{3,1},{4,0},{5,7},{6,2},{7,5},{8,12},{9,11},{10,... | collective-permute-start | bytes 445448 | tf_op jit(solution)/shard_map/ppermute | solution.py:177
  52.9 3.6 %collective-permute-done.4 = f32[290,128]{1,0:T(8,128)S(1)} collective-permute-done((f32[290,128]{1,0:T(8,128)S(1)}, f32[290,128]{1,0:T(8,128)S(1)}, u32[]{:S(2)}, u32[]{:S(2)}) %collective-permute-start.4) | collective-permute-done | bytes 148512 | tf_op jit(solution)/shard_map/ppermute | solution.py:177
  56.5 2.7 %collective-permute-start.5 = (f32[145,128]{1,0:T(8,128)S(1)}, f32[145,128]{1,0:T(8,128)S(1)}, u32[]{:S(2)}, u32[]{:S(2)}) collective-permute-start(f32[145,128]{1,0:T(8,128)S(1)} %slice_select_fusion.3), channel_id=1, source_target_pairs={{0,8},{1,9},{2,10},{3,11},{4,12},{5,13},{6,14},{7,15},{8,0},{9,1},... | collective-permute-start | bytes 222728 | tf_op jit(solution)/shard_map/ppermute | solution.py:177
  59.3 2.6 %collective-permute-done.5 = f32[145,128]{1,0:T(8,128)S(1)} collective-permute-done((f32[145,128]{1,0:T(8,128)S(1)}, f32[145,128]{1,0:T(8,128)S(1)}, u32[]{:S(2)}, u32[]{:S(2)}) %collective-permute-start.5) | collective-permute-done | bytes 74272 | tf_op jit(solution)/shard_map/ppermute | solution.py:177
  61.9 2.8 %collective-permute-start.6 = (f32[145,128]{1,0:T(8,128)S(1)}, f32[145,128]{1,0:T(8,128)S(1)}, u32[]{:S(2)}, u32[]{:S(2)}) collective-permute-start(f32[145,128]{1,0:T(8,128)S(1)} %select_add_fusion.3), channel_id=1, source_target_pairs={{0,8},{1,9},{2,10},{3,11},{4,12},{5,13},{6,14},{7,15},{8,0},{9,1},... | collective-permute-start | bytes 222728 | tf_op jit(solution)/shard_map/ppermute | solution.py:181
  64.7 2.6 %collective-permute-done.6 = f32[145,128]{1,0:T(8,128)S(1)} collective-permute-done((f32[145,128]{1,0:T(8,128)S(1)}, f32[145,128]{1,0:T(8,128)S(1)}, u32[]{:S(2)}, u32[]{:S(2)}) %collective-permute-start.6) | collective-permute-done | bytes 74272 | tf_op jit(solution)/shard_map/ppermute | solution.py:181
  67.3 2.1 %collective-permute-start.7 = (f32[290,128]{1,0:T(8,128)S(1)}, f32[290,128]{1,0:T(8,128)S(1)}, u32[]{:S(2)}, u32[]{:S(2)}) collective-permute-start(f32[290,128]{1,0:T(8,128)S(1)} %maximum_select_fusion.3), channel_id=1, source_target_pairs={{0,4},{1,3},{2,6},{3,1},{4,0},{5,7},{6,2},{7,5},{8,12},{9,11},{10,... | collective-permute-start | bytes 445448 | tf_op jit(solution)/shard_map/ppermute | solution.py:181
  69.4 4.3 %collective-permute-done.7 = f32[290,128]{1,0:T(8,128)S(1)} collective-permute-done((f32[290,128]{1,0:T(8,128)S(1)}, f32[290,128]{1,0:T(8,128)S(1)}, u32[]{:S(2)}, u32[]{:S(2)}) %collective-permute-start.7) | collective-permute-done | bytes 148512 | tf_op jit(solution)/shard_map/ppermute | solution.py:181
  73.8 2.2 %collective-permute-start.8 = (f32[580,128]{1,0:T(8,128)S(1)}, f32[580,128]{1,0:T(8,128)S(1)}, u32[]{:S(2)}, u32[]{:S(2)}) collective-permute-start(f32[580,128]{1,0:T(8,128)S(1)} %maximum_select_fusion.2), channel_id=1, source_target_pairs={{0,2},{1,5},{2,0},{3,7},{4,6},{5,1},{6,4},{7,3},{8,10},{9,13},{10,... | collective-permute-start | bytes 890888 | tf_op jit(solution)/shard_map/ppermute | solution.py:181
  76.0 4.7 %collective-permute-done.8 = f32[580,128]{1,0:T(8,128)S(1)} collective-permute-done((f32[580,128]{1,0:T(8,128)S(1)}, f32[580,128]{1,0:T(8,128)S(1)}, u32[]{:S(2)}, u32[]{:S(2)}) %collective-permute-start.8) | collective-permute-done | bytes 296992 | tf_op jit(solution)/shard_map/ppermute | solution.py:181
  80.8 0.1 maximum_select_fusion.1
  80.8 0.1 collective-permute-start.9
  80.9 2.0 %collective-permute-done.9 = f32[1160,128]{1,0:T(8,128)S(1)} collective-permute-done((f32[1160,128]{1,0:T(8,128)S(1)}, f32[1160,128]{1,0:T(8,128)S(1)}, u32[]{:S(2)}, u32[]{:S(2)}) %collective-permute-start.9) | collective-permute-done | bytes 593952 | tf_op jit(solution)/shard_map/ppermute | solution.py:181
  82.9 0.1 maximum_select_fusion
  83.1 0.6 slice.68
  83.6 1.1 %fusion = (f32[1152,128]{1,0:T(8,128)}, f32[1152,128]{1,0:T(8,128)}) fusion(f32[2320,128]{1,0:T(8,128)S(1)} %maximum_select_fusion), kind=kLoop, calls=%fused_computation.14 | loop fusion | bytes 2359296 | tf_op jit(solution)/shard_map/slice | solution.py:207
  (12 shorter events, 0.3 us)
Async XLA Ops:
  2.0 4.4 %collective-permute-start = (bf16[4,512,128]{2,1,0:T(8,128)(2,1)S(1)}, bf16[4,512,128]{2,1,0:T(8,128)(2,1)S(1)}, u32[]{:S(2)}, u32[]{:S(2)}) collective-permute-start(bf16[4,512,128]{2,1,0:T(8,128)(2,1)S(1)} %pad_maximum_fusion), channel_id=1, source_target_pairs={{0,1},{1,2},{2,3},{3,4},{4,5},{5,6},{6,7},{7,8},{8,9},{9,10},{10,1... | collective-permute-start | bytes 1572872 | tf_op jit(solution)/shard_map/ppermute | solution.py:196
  4.4 5.9 %collective-permute-start.1 = (bf16[4,512,128]{2,1,0:T(8,128)(2,1)S(1)}, bf16[4,512,128]{2,1,0:T(8,128)(2,1)S(1)}, u32[]{:S(2)}, u32[]{:S(2)}) collective-permute-start(bf16[4,512,128]{2,1,0:T(8,128)(2,1)S(1)} %pad_maximum_fusion.1), channel_id=1, source_target_pairs={{1,0},{2,1},{3,2},{4,3},{5,4},{6,5},{7,6},{8,7},{9,8},{10,9},{11,1... | collective-permute-start | bytes 1572872 | tf_op jit(solution)/shard_map/ppermute | solution.py:197
  6.4 3.9 %copy-start.1 = (bf16[4,512,128]{2,1,0:T(8,128)(2,1)}, bf16[4,512,128]{2,1,0:T(8,128)(2,1)S(1)}, u32[]{:S(2)}) copy-start(bf16[4,512,128]{2,1,0:T(8,128)(2,1)S(1)} %collective-permute-done.before_hbm) | copy-start | bytes 1572868
  10.3 0.8 copy-start.2
  31.2 12.3 %copy-start = (f32[2320,128]{1,0:T(8,128)S(1)}, f32[2320,128]{1,0:T(8,128)}, u32[]{:S(2)}) copy-start(f32[2320,128]{1,0:T(8,128)} %get-tuple-element.10) | copy-start | bytes 3563524
  32.6 10.9 %collective-permute-start.2 = (f32[1160,128]{1,0:T(8,128)S(1)}, f32[1160,128]{1,0:T(8,128)S(1)}, u32[]{:S(2)}, u32[]{:S(2)}) collective-permute-start(f32[1160,128]{1,0:T(8,128)S(1)} %slice_select_fusion), channel_id=1, source_target_pairs={{0,1},{1,0},{2,3},{3,2},{4,5},{5,4},{6,7},{7,6},{8,9},{9,8},{10,11... | collective-permute-start | bytes 1781768 | tf_op jit(solution)/shard_map/ppermute | solution.py:177
  43.6 7.6 %collective-permute-start.3 = (f32[580,128]{1,0:T(8,128)S(1)}, f32[580,128]{1,0:T(8,128)S(1)}, u32[]{:S(2)}, u32[]{:S(2)}) collective-permute-start(f32[580,128]{1,0:T(8,128)S(1)} %slice_select_fusion.1), channel_id=1, source_target_pairs={{0,2},{1,5},{2,0},{3,7},{4,6},{5,1},{6,4},{7,3},{8,10},{9,13},{10,... | collective-permute-start | bytes 890888 | tf_op jit(solution)/shard_map/ppermute | solution.py:177
  51.2 5.3 %collective-permute-start.4 = (f32[290,128]{1,0:T(8,128)S(1)}, f32[290,128]{1,0:T(8,128)S(1)}, u32[]{:S(2)}, u32[]{:S(2)}) collective-permute-start(f32[290,128]{1,0:T(8,128)S(1)} %slice_select_fusion.2), channel_id=1, source_target_pairs={{0,4},{1,3},{2,6},{3,1},{4,0},{5,7},{6,2},{7,5},{8,12},{9,11},{10,... | collective-permute-start | bytes 445448 | tf_op jit(solution)/shard_map/ppermute | solution.py:177
  56.5 5.4 %collective-permute-start.5 = (f32[145,128]{1,0:T(8,128)S(1)}, f32[145,128]{1,0:T(8,128)S(1)}, u32[]{:S(2)}, u32[]{:S(2)}) collective-permute-start(f32[145,128]{1,0:T(8,128)S(1)} %slice_select_fusion.3), channel_id=1, source_target_pairs={{0,8},{1,9},{2,10},{3,11},{4,12},{5,13},{6,14},{7,15},{8,0},{9,1},... | collective-permute-start | bytes 222728 | tf_op jit(solution)/shard_map/ppermute | solution.py:177
  61.9 5.4 %collective-permute-start.6 = (f32[145,128]{1,0:T(8,128)S(1)}, f32[145,128]{1,0:T(8,128)S(1)}, u32[]{:S(2)}, u32[]{:S(2)}) collective-permute-start(f32[145,128]{1,0:T(8,128)S(1)} %select_add_fusion.3), channel_id=1, source_target_pairs={{0,8},{1,9},{2,10},{3,11},{4,12},{5,13},{6,14},{7,15},{8,0},{9,1},... | collective-permute-start | bytes 222728 | tf_op jit(solution)/shard_map/ppermute | solution.py:181
  67.3 6.4 %collective-permute-start.7 = (f32[290,128]{1,0:T(8,128)S(1)}, f32[290,128]{1,0:T(8,128)S(1)}, u32[]{:S(2)}, u32[]{:S(2)}) collective-permute-start(f32[290,128]{1,0:T(8,128)S(1)} %maximum_select_fusion.3), channel_id=1, source_target_pairs={{0,4},{1,3},{2,6},{3,1},{4,0},{5,7},{6,2},{7,5},{8,12},{9,11},{10,... | collective-permute-start | bytes 445448 | tf_op jit(solution)/shard_map/ppermute | solution.py:181
  73.8 7.0 %collective-permute-start.8 = (f32[580,128]{1,0:T(8,128)S(1)}, f32[580,128]{1,0:T(8,128)S(1)}, u32[]{:S(2)}, u32[]{:S(2)}) collective-permute-start(f32[580,128]{1,0:T(8,128)S(1)} %maximum_select_fusion.2), channel_id=1, source_target_pairs={{0,2},{1,5},{2,0},{3,7},{4,6},{5,1},{6,4},{7,3},{8,10},{9,13},{10,... | collective-permute-start | bytes 890888 | tf_op jit(solution)/shard_map/ppermute | solution.py:181
  80.8 2.1 %collective-permute-start.9 = (f32[1160,128]{1,0:T(8,128)S(1)}, f32[1160,128]{1,0:T(8,128)S(1)}, u32[]{:S(2)}, u32[]{:S(2)}) collective-permute-start(f32[1160,128]{1,0:T(8,128)S(1)} %maximum_select_fusion.1), channel_id=1, source_target_pairs={{0,1},{1,0},{2,3},{3,2},{4,5},{5,4},{6,7},{7,6},{8,9},{9,8},{10,11... | collective-permute-start | bytes 1781768 | tf_op jit(solution)/shard_map/ppermute | solution.py:181

commit v3 on v2

--- a/solution.py
+++ b/solution.py
@@ -11,7 +11,7 @@
 
 def section_kernel(norm, idx_ref, lt_ref, x_hbm, c_hbm, before_hbm, after_hbm, k1_ref, k2_ref,
                    out_ref, ig_ref, grad_ref,
-                   x_ref, c_ref, hid_ref, bf_ref, k1f_ref, k2f_ref, k2b_ref, k1b_ref, acc1, acc2, sems):
+                   x_ref, c_ref, hid_ref, bf_ref, xt_ref, hidt_ref, k1f_ref, k2f_ref, k2b_ref, k1b_ref, acc1, acc2, sems):
     count = out_ref.shape[0]
     width = out_ref.shape[1]
     ch = out_ref.shape[2]
@@ -71,8 +71,10 @@
         valid = jnp.logical_and(jnp.logical_or(r > 0, top), jnp.logical_or(r < count + 1, bottom))
         first = conv_row(x_ref, r, k1f_ref)
         mixed = first * scale + shift
-        sig = 1.0 / (1.0 + jnp.exp(-mixed))
-        hid_ref[r] = jnp.where(valid, mixed * sig, 0.0).astype(hid_ref.dtype)
+        sig = 0.5 + 0.5 * jnp.tanh(0.5 * mixed)
+        hidden = jnp.where(valid, mixed * sig, 0.0)
+        hid_ref[r] = hidden.astype(hid_ref.dtype)
+        hidt_ref[r] = hidden.T.astype(hidt_ref.dtype)
         back_hidden = conv_row(c_ref, r, k2b_ref)
         back_mixed = back_hidden * (sig * (1.0 + mixed * (1.0 - sig)))
         bf_ref[r] = jnp.where(valid, back_mixed * scale, 0.0).astype(bf_ref.dtype)
@@ -83,18 +85,24 @@
 
     zero = jnp.zeros((1, ch), jnp.float32)
     lv0, lv1 = lax.fori_loop(0, count + 2, phase_one, (zero, zero))
+
+    def transpose_rows(r, carry):
+        xt_ref[r] = x_ref[r].astype(jnp.float32).T.astype(xt_ref.dtype)
+        return carry
+
+    lax.fori_loop(1, count + 3, transpose_rows, 0)
     acc1[...] = jnp.zeros_like(acc1)
     acc2[...] = jnp.zeros_like(acc2)
 
     def phase_two(i, carry):
         out_ref[i] = (x_ref[i + 2].astype(jnp.float32) + conv_row(hid_ref, i, k2f_ref)).astype(out_ref.dtype)
         ig_ref[i] = (c_ref[i + 2].astype(jnp.float32) + conv_row(bf_ref, i, k1b_ref)).astype(ig_ref.dtype)
-        xs = jnp.concatenate([x_ref[i + 1], x_ref[i + 2], x_ref[i + 3]], axis=1)
+        xs = jnp.concatenate([xt_ref[i + 1], xt_ref[i + 2], xt_ref[i + 3]], axis=0)
         gs = shifted(bf_ref[i + 1])
-        acc1[...] += lax.dot_general(xs, gs, (((0,), (0,)), ((), ())), preferred_element_type=jnp.float32)
-        hs = jnp.concatenate([hid_ref[i], hid_ref[i + 1], hid_ref[i + 2]], axis=1)
+        acc1[...] += jnp.dot(xs, gs, preferred_element_type=jnp.float32)
+        hs = jnp.concatenate([hidt_ref[i], hidt_ref[i + 1], hidt_ref[i + 2]], axis=0)
         cs = shifted(c_ref[i + 2])
-        acc2[...] += lax.dot_general(hs, cs, (((0,), (0,)), ((), ())), preferred_element_type=jnp.float32)
+        acc2[...] += jnp.dot(hs, cs, preferred_element_type=jnp.float32)
         return carry
 
     lax.fori_loop(0, count, phase_two, 0)
@@ -133,6 +141,8 @@
             pltpu.VMEM((count + 4, width, ch), jnp.bfloat16),
             pltpu.VMEM((count + 2, width, ch), jnp.bfloat16),
             pltpu.VMEM((count + 2, width, ch), jnp.bfloat16),
+            pltpu.VMEM((count + 4, ch, width), jnp.bfloat16),
+            pltpu.VMEM((count + 2, ch, width), jnp.bfloat16),
             pltpu.VMEM((big, big), jnp.bfloat16),
             pltpu.VMEM((big, big), jnp.bfloat16),
             pltpu.VMEM((big, big), jnp.bfloat16),

time: 85 us -> 86 us (1.012)
  Pallas kernels: 20 us -> 21.1 us
    pallas_call x1, Pallas kernels: 20 us -> 21.1 us  [section(): pl.pallas_call(functools.partial(section_kernel, norm), out_shape=(jax.Sh...]
where the time goes in v3:
time: 86 us; the launch traced here: 85.8 us
  waiting for transfers between devices  30.2 us (35%)
  starting transfers between devices  27.3 us (32%)
  Pallas kernels  21.1 us (25%)
  local copies, waits for them, and re-layouts  3.72 us (4%)
  other arithmetic  2.09 us (2%)
  between operations  1.43 us (2%)
    pallas_call x1, Pallas kernels, section(): pl.pallas_call(functools.partial(section_kernel, norm), out_shape=(jax.Sh...  21.1 us
    ppermute x4, starting transfers between devices, butterfly_sum(): got = lax.ppermute(send, 'rows', perm)  16.4 us
    ppermute x4, waiting for transfers between devices, butterfly_sum(): got = lax.ppermute(piece, 'rows', perm)  13.6 us
    ppermute x4, waiting for transfers between devices, butterfly_sum(): got = lax.ppermute(send, 'rows', perm)  12.6 us
    ppermute x4, starting transfers between devices, butterfly_sum(): got = lax.ppermute(piece, 'rows', perm)  7.19 us
    ppermute x1, waiting for transfers between devices, local(): lax.ppermute(jnp.concatenate([inputs[:2], cotangent[:2]]), 'rows', down)  3.92 us
    ppermute x1, starting transfers between devices, local(): lax.ppermute(jnp.concatenate([inputs[-2:], cotangent[-2:]]), 'rows', up)  2.39 us
  transfers between devices with their start and end apart: 10, of which 9 were waited for; matrix products, arithmetic and copies ran while one was open for 0% of the time, Pallas kernels for 0%

profile of v3, /device:TPU:0, one launch (start us, length us, event | category | flops | bytes accessed | tf_op | source)
XLA Modules:
  0.0 85.8 jit_solution(12851766139142545981)
XLA Ops:
  0.6 1.3 %fusion.1 = (bf16[2,512,128]{2,1,0:T(8,128)(2,1)S(1)}, bf16[2,512,128]{2,1,0:T(8,128)(2,1)S(1)}, bf16[2,512,128]{2,1,0:T(8,128)(2,1)S(1)}, bf16[2,512,128]{2,1,0:T(8,128)(2,1)S(1)}) fusion(bf16[8,512,128]{2,1,0:T(8,128)(2,1)} %x_hbm.1, bf16[8,512,128]{2,1,0:T(8,128)(2,1)} %c_hbm.1), kind=kLoop, calls=%fused_computation.15 | loop fusion | bytes 2097152 | tf_op jit(solution)/shard_map/slice | solution.py:207
  2.0 2.4 %collective-permute-start = (bf16[4,512,128]{2,1,0:T(8,128)(2,1)S(1)}, bf16[4,512,128]{2,1,0:T(8,128)(2,1)S(1)}, u32[]{:S(2)}, u32[]{:S(2)}) collective-permute-start(bf16[4,512,128]{2,1,0:T(8,128)(2,1)S(1)} %pad_maximum_fusion), channel_id=1, source_target_pairs={{0,1},{1,2},{2,3},{3,4},{4,5},{5,6},{6,7},{7,8},{8,9},{9,10},{10,1... | collective-permute-start | bytes 1572872 | tf_op jit(solution)/shard_map/ppermute | solution.py:206
  4.4 1.3 %collective-permute-start.1 = (bf16[4,512,128]{2,1,0:T(8,128)(2,1)S(1)}, bf16[4,512,128]{2,1,0:T(8,128)(2,1)S(1)}, u32[]{:S(2)}, u32[]{:S(2)}) collective-permute-start(bf16[4,512,128]{2,1,0:T(8,128)(2,1)S(1)} %pad_maximum_fusion.1), channel_id=1, source_target_pairs={{1,0},{2,1},{3,2},{4,3},{5,4},{6,5},{7,6},{8,7},{9,8},{10,9},{11,1... | collective-permute-start | bytes 1572872 | tf_op jit(solution)/shard_map/ppermute | solution.py:207
  6.4 0.0 collective-permute-done.before_hbm
  6.4 0.0 copy-start.1
  6.4 3.9 %collective-permute-done.1.after_hbm = bf16[4,512,128]{2,1,0:T(8,128)(2,1)S(1)} collective-permute-done((bf16[4,512,128]{2,1,0:T(8,128)(2,1)S(1)}, bf16[4,512,128]{2,1,0:T(8,128)(2,1)S(1)}, u32[]{:S(2)}, u32[]{:S(2)}) %collective-permute-start.1) | collective-permute-done | bytes 524320 | tf_op jit(solution)/shard_map/ppermute | solution.py:207
  10.3 0.8 copy-done.2
  11.1 21.1 %shard_map.101 = (bf16[8,512,128]{2,1,0:T(8,128)(2,1)}, bf16[8,512,128]{2,1,0:T(8,128)(2,1)}, f32[2320,128]{1,0:T(8,128)}) custom-call(s32[1]{0:T(128)S(6)} %copy.11.idx_ref, f32[16,2,128]{2,1,0:T(2,128)} %lt_ref.1, bf16[8,512,128]{2,1,0:T(8,128)(2,1)} %x_hbm.1, bf16[8,512,128]{2,1,0:T(8,128)(2,1)} %c_hbm.1, bf16[4,512,128]{2,1,0:T(8,128)(2,1)} %copy-done.1, ...), custom_call_target="tpu_custom_call" | custom-call | flops 7851737088 | bytes 3145728 | tf_op jit(solution)/shard_map/pallas_call | solution.py:130
  32.2 0.0 copy-start
  32.2 1.4 %slice_select_fusion = f32[1160,128]{1,0:T(8,128)S(1)} fusion(f32[2320,128]{1,0:T(8,128)} %get-tuple-element.10, pred[]{:T(512)S(6)} %eq.35), kind=kLoop, calls=%fused_computation.3 | loop fusion | flops 148480 | bytes 1781761 | tf_op jit(solution)/shard_map/jit(_where)/select_n | solution.py:186
  33.6 9.2 %collective-permute-start.2 = (f32[1160,128]{1,0:T(8,128)S(1)}, f32[1160,128]{1,0:T(8,128)S(1)}, u32[]{:S(2)}, u32[]{:S(2)}) collective-permute-start(f32[1160,128]{1,0:T(8,128)S(1)} %slice_select_fusion), channel_id=1, source_target_pairs={{0,1},{1,0},{2,3},{3,2},{4,5},{5,4},{6,7},{7,6},{8,9},{9,8},{10,11... | collective-permute-start | bytes 1781768 | tf_op jit(solution)/shard_map/ppermute | solution.py:187
  42.9 1.6 %collective-permute-done.2 = f32[1160,128]{1,0:T(8,128)S(1)} collective-permute-done((f32[1160,128]{1,0:T(8,128)S(1)}, f32[1160,128]{1,0:T(8,128)S(1)}, u32[]{:S(2)}, u32[]{:S(2)}) %collective-permute-start.2) | collective-permute-done | bytes 593952 | tf_op jit(solution)/shard_map/ppermute | solution.py:187
  44.5 0.1 select_add_fusion
  44.7 2.8 %collective-permute-start.3 = (f32[580,128]{1,0:T(8,128)S(1)}, f32[580,128]{1,0:T(8,128)S(1)}, u32[]{:S(2)}, u32[]{:S(2)}) collective-permute-start(f32[580,128]{1,0:T(8,128)S(1)} %slice_select_fusion.1), channel_id=1, source_target_pairs={{0,2},{1,5},{2,0},{3,7},{4,6},{5,1},{6,4},{7,3},{8,10},{9,13},{10,... | collective-permute-start | bytes 890888 | tf_op jit(solution)/shard_map/ppermute | solution.py:187
  47.5 4.7 %collective-permute-done.3 = f32[580,128]{1,0:T(8,128)S(1)} collective-permute-done((f32[580,128]{1,0:T(8,128)S(1)}, f32[580,128]{1,0:T(8,128)S(1)}, u32[]{:S(2)}, u32[]{:S(2)}) %collective-permute-start.3) | collective-permute-done | bytes 296992 | tf_op jit(solution)/shard_map/ppermute | solution.py:187
  52.2 0.1 select_add_fusion.1
  52.3 1.7 %collective-permute-start.4 = (f32[290,128]{1,0:T(8,128)S(1)}, f32[290,128]{1,0:T(8,128)S(1)}, u32[]{:S(2)}, u32[]{:S(2)}) collective-permute-start(f32[290,128]{1,0:T(8,128)S(1)} %slice_select_fusion.2), channel_id=1, source_target_pairs={{0,4},{1,3},{2,6},{3,1},{4,0},{5,7},{6,2},{7,5},{8,12},{9,11},{10,... | collective-permute-start | bytes 445448 | tf_op jit(solution)/shard_map/ppermute | solution.py:187
  54.0 3.6 %collective-permute-done.4 = f32[290,128]{1,0:T(8,128)S(1)} collective-permute-done((f32[290,128]{1,0:T(8,128)S(1)}, f32[290,128]{1,0:T(8,128)S(1)}, u32[]{:S(2)}, u32[]{:S(2)}) %collective-permute-start.4) | collective-permute-done | bytes 148512 | tf_op jit(solution)/shard_map/ppermute | solution.py:187
  57.6 2.7 %collective-permute-start.5 = (f32[145,128]{1,0:T(8,128)S(1)}, f32[145,128]{1,0:T(8,128)S(1)}, u32[]{:S(2)}, u32[]{:S(2)}) collective-permute-start(f32[145,128]{1,0:T(8,128)S(1)} %slice_select_fusion.3), channel_id=1, source_target_pairs={{0,8},{1,9},{2,10},{3,11},{4,12},{5,13},{6,14},{7,15},{8,0},{9,1},... | collective-permute-start | bytes 222728 | tf_op jit(solution)/shard_map/ppermute | solution.py:187
  60.3 2.6 %collective-permute-done.5 = f32[145,128]{1,0:T(8,128)S(1)} collective-permute-done((f32[145,128]{1,0:T(8,128)S(1)}, f32[145,128]{1,0:T(8,128)S(1)}, u32[]{:S(2)}, u32[]{:S(2)}) %collective-permute-start.5) | collective-permute-done | bytes 74272 | tf_op jit(solution)/shard_map/ppermute | solution.py:187
  63.0 2.8 %collective-permute-start.6 = (f32[145,128]{1,0:T(8,128)S(1)}, f32[145,128]{1,0:T(8,128)S(1)}, u32[]{:S(2)}, u32[]{:S(2)}) collective-permute-start(f32[145,128]{1,0:T(8,128)S(1)} %select_add_fusion.3), channel_id=1, source_target_pairs={{0,8},{1,9},{2,10},{3,11},{4,12},{5,13},{6,14},{7,15},{8,0},{9,1},... | collective-permute-start | bytes 222728 | tf_op jit(solution)/shard_map/ppermute | solution.py:191
  65.8 2.6 %collective-permute-done.6 = f32[145,128]{1,0:T(8,128)S(1)} collective-permute-done((f32[145,128]{1,0:T(8,128)S(1)}, f32[145,128]{1,0:T(8,128)S(1)}, u32[]{:S(2)}, u32[]{:S(2)}) %collective-permute-start.6) | collective-permute-done | bytes 74272 | tf_op jit(solution)/shard_map/ppermute | solution.py:191
  68.4 2.1 %collective-permute-start.7 = (f32[290,128]{1,0:T(8,128)S(1)}, f32[290,128]{1,0:T(8,128)S(1)}, u32[]{:S(2)}, u32[]{:S(2)}) collective-permute-start(f32[290,128]{1,0:T(8,128)S(1)} %maximum_select_fusion.3), channel_id=1, source_target_pairs={{0,4},{1,3},{2,6},{3,1},{4,0},{5,7},{6,2},{7,5},{8,12},{9,11},{10,... | collective-permute-start | bytes 445448 | tf_op jit(solution)/shard_map/ppermute | solution.py:191
  70.5 4.3 %collective-permute-done.7 = f32[290,128]{1,0:T(8,128)S(1)} collective-permute-done((f32[290,128]{1,0:T(8,128)S(1)}, f32[290,128]{1,0:T(8,128)S(1)}, u32[]{:S(2)}, u32[]{:S(2)}) %collective-permute-start.7) | collective-permute-done | bytes 148512 | tf_op jit(solution)/shard_map/ppermute | solution.py:191
  74.8 2.2 %collective-permute-start.8 = (f32[580,128]{1,0:T(8,128)S(1)}, f32[580,128]{1,0:T(8,128)S(1)}, u32[]{:S(2)}, u32[]{:S(2)}) collective-permute-start(f32[580,128]{1,0:T(8,128)S(1)} %maximum_select_fusion.2), channel_id=1, source_target_pairs={{0,2},{1,5},{2,0},{3,7},{4,6},{5,1},{6,4},{7,3},{8,10},{9,13},{10,... | collective-permute-start | bytes 890888 | tf_op jit(solution)/shard_map/ppermute | solution.py:191
  77.1 4.7 %collective-permute-done.8 = f32[580,128]{1,0:T(8,128)S(1)} collective-permute-done((f32[580,128]{1,0:T(8,128)S(1)}, f32[580,128]{1,0:T(8,128)S(1)}, u32[]{:S(2)}, u32[]{:S(2)}) %collective-permute-start.8) | collective-permute-done | bytes 296992 | tf_op jit(solution)/shard_map/ppermute | solution.py:191
  81.8 0.1 maximum_select_fusion.1
  81.9 0.1 collective-permute-start.9
  82.0 2.0 %collective-permute-done.9 = f32[1160,128]{1,0:T(8,128)S(1)} collective-permute-done((f32[1160,128]{1,0:T(8,128)S(1)}, f32[1160,128]{1,0:T(8,128)S(1)}, u32[]{:S(2)}, u32[]{:S(2)}) %collective-permute-start.9) | collective-permute-done | bytes 593952 | tf_op jit(solution)/shard_map/ppermute | solution.py:191
  84.0 0.1 maximum_select_fusion
  84.1 0.6 slice.68
  84.7 1.1 %fusion = (f32[1152,128]{1,0:T(8,128)}, f32[1152,128]{1,0:T(8,128)}) fusion(f32[2320,128]{1,0:T(8,128)S(1)} %maximum_select_fusion), kind=kLoop, calls=%fused_computation.14 | loop fusion | bytes 2359296 | tf_op jit(solution)/shard_map/slice | solution.py:217
  (12 shorter events, 0.3 us)
Async XLA Ops:
  2.0 4.4 %collective-permute-start = (bf16[4,512,128]{2,1,0:T(8,128)(2,1)S(1)}, bf16[4,512,128]{2,1,0:T(8,128)(2,1)S(1)}, u32[]{:S(2)}, u32[]{:S(2)}) collective-permute-start(bf16[4,512,128]{2,1,0:T(8,128)(2,1)S(1)} %pad_maximum_fusion), channel_id=1, source_target_pairs={{0,1},{1,2},{2,3},{3,4},{4,5},{5,6},{6,7},{7,8},{8,9},{9,10},{10,1... | collective-permute-start | bytes 1572872 | tf_op jit(solution)/shard_map/ppermute | solution.py:206
  4.4 5.9 %collective-permute-start.1 = (bf16[4,512,128]{2,1,0:T(8,128)(2,1)S(1)}, bf16[4,512,128]{2,1,0:T(8,128)(2,1)S(1)}, u32[]{:S(2)}, u32[]{:S(2)}) collective-permute-start(bf16[4,512,128]{2,1,0:T(8,128)(2,1)S(1)} %pad_maximum_fusion.1), channel_id=1, source_target_pairs={{1,0},{2,1},{3,2},{4,3},{5,4},{6,5},{7,6},{8,7},{9,8},{10,9},{11,1... | collective-permute-start | bytes 1572872 | tf_op jit(solution)/shard_map/ppermute | solution.py:207
  6.4 3.9 %copy-start.1 = (bf16[4,512,128]{2,1,0:T(8,128)(2,1)}, bf16[4,512,128]{2,1,0:T(8,128)(2,1)S(1)}, u32[]{:S(2)}) copy-start(bf16[4,512,128]{2,1,0:T(8,128)(2,1)S(1)} %collective-permute-done.before_hbm) | copy-start | bytes 1572868
  10.3 0.8 copy-start.2
  32.2 12.3 %copy-start = (f32[2320,128]{1,0:T(8,128)S(1)}, f32[2320,128]{1,0:T(8,128)}, u32[]{:S(2)}) copy-start(f32[2320,128]{1,0:T(8,128)} %get-tuple-element.10) | copy-start | bytes 3563524
  33.6 10.9 %collective-permute-start.2 = (f32[1160,128]{1,0:T(8,128)S(1)}, f32[1160,128]{1,0:T(8,128)S(1)}, u32[]{:S(2)}, u32[]{:S(2)}) collective-permute-start(f32[1160,128]{1,0:T(8,128)S(1)} %slice_select_fusion), channel_id=1, source_target_pairs={{0,1},{1,0},{2,3},{3,2},{4,5},{5,4},{6,7},{7,6},{8,9},{9,8},{10,11... | collective-permute-start | bytes 1781768 | tf_op jit(solution)/shard_map/ppermute | solution.py:187
  44.7 7.6 %collective-permute-start.3 = (f32[580,128]{1,0:T(8,128)S(1)}, f32[580,128]{1,0:T(8,128)S(1)}, u32[]{:S(2)}, u32[]{:S(2)}) collective-permute-start(f32[580,128]{1,0:T(8,128)S(1)} %slice_select_fusion.1), channel_id=1, source_target_pairs={{0,2},{1,5},{2,0},{3,7},{4,6},{5,1},{6,4},{7,3},{8,10},{9,13},{10,... | collective-permute-start | bytes 890888 | tf_op jit(solution)/shard_map/ppermute | solution.py:187
  52.3 5.3 %collective-permute-start.4 = (f32[290,128]{1,0:T(8,128)S(1)}, f32[290,128]{1,0:T(8,128)S(1)}, u32[]{:S(2)}, u32[]{:S(2)}) collective-permute-start(f32[290,128]{1,0:T(8,128)S(1)} %slice_select_fusion.2), channel_id=1, source_target_pairs={{0,4},{1,3},{2,6},{3,1},{4,0},{5,7},{6,2},{7,5},{8,12},{9,11},{10,... | collective-permute-start | bytes 445448 | tf_op jit(solution)/shard_map/ppermute | solution.py:187
  57.6 5.4 %collective-permute-start.5 = (f32[145,128]{1,0:T(8,128)S(1)}, f32[145,128]{1,0:T(8,128)S(1)}, u32[]{:S(2)}, u32[]{:S(2)}) collective-permute-start(f32[145,128]{1,0:T(8,128)S(1)} %slice_select_fusion.3), channel_id=1, source_target_pairs={{0,8},{1,9},{2,10},{3,11},{4,12},{5,13},{6,14},{7,15},{8,0},{9,1},... | collective-permute-start | bytes 222728 | tf_op jit(solution)/shard_map/ppermute | solution.py:187
  63.0 5.4 %collective-permute-start.6 = (f32[145,128]{1,0:T(8,128)S(1)}, f32[145,128]{1,0:T(8,128)S(1)}, u32[]{:S(2)}, u32[]{:S(2)}) collective-permute-start(f32[145,128]{1,0:T(8,128)S(1)} %select_add_fusion.3), channel_id=1, source_target_pairs={{0,8},{1,9},{2,10},{3,11},{4,12},{5,13},{6,14},{7,15},{8,0},{9,1},... | collective-permute-start | bytes 222728 | tf_op jit(solution)/shard_map/ppermute | solution.py:191
  68.4 6.4 %collective-permute-start.7 = (f32[290,128]{1,0:T(8,128)S(1)}, f32[290,128]{1,0:T(8,128)S(1)}, u32[]{:S(2)}, u32[]{:S(2)}) collective-permute-start(f32[290,128]{1,0:T(8,128)S(1)} %maximum_select_fusion.3), channel_id=1, source_target_pairs={{0,4},{1,3},{2,6},{3,1},{4,0},{5,7},{6,2},{7,5},{8,12},{9,11},{10,... | collective-permute-start | bytes 445448 | tf_op jit(solution)/shard_map/ppermute | solution.py:191
  74.8 7.0 %collective-permute-start.8 = (f32[580,128]{1,0:T(8,128)S(1)}, f32[580,128]{1,0:T(8,128)S(1)}, u32[]{:S(2)}, u32[]{:S(2)}) collective-permute-start(f32[580,128]{1,0:T(8,128)S(1)} %maximum_select_fusion.2), channel_id=1, source_target_pairs={{0,2},{1,5},{2,0},{3,7},{4,6},{5,1},{6,4},{7,3},{8,10},{9,13},{10,... | collective-permute-start | bytes 890888 | tf_op jit(solution)/shard_map/ppermute | solution.py:191
  81.9 2.1 %collective-permute-start.9 = (f32[1160,128]{1,0:T(8,128)S(1)}, f32[1160,128]{1,0:T(8,128)S(1)}, u32[]{:S(2)}, u32[]{:S(2)}) collective-permute-start(f32[1160,128]{1,0:T(8,128)S(1)} %maximum_select_fusion.1), channel_id=1, source_target_pairs={{0,1},{1,0},{2,3},{3,2},{4,5},{5,4},{6,7},{7,6},{8,9},{9,8},{10,11... | collective-permute-start | bytes 1781768 | tf_op jit(solution)/shard_map/ppermute | solution.py:191

commit v4 on v3

v4 whole, which is shorter than its diff:
```python
import functools
import math

import jax
import jax.numpy as jnp
from jax import lax
from jax.experimental import pallas as pl
from jax.experimental.pallas import tpu as pltpu
from jax.sharding import PartitionSpec as P


def row_ops(width, ch, scale, shift, top, bottom, count):
    col = lax.broadcasted_iota(jnp.int32, (width, ch), 0)
    not_first = col > 0
    not_last = col < width - 1

    def combine(y):
        left = pltpu.roll(y[:, 0:ch], 1, 0)
        right = pltpu.roll(y[:, 2 * ch:3 * ch], width - 1, 0)
        return y[:, ch:2 * ch] + jnp.where(not_first, left, 0.0) + jnp.where(not_last, right, 0.0)

    def conv_row(ref, r, matrix_ref):
        rows = jnp.concatenate([ref[r], ref[r + 1], ref[r + 2]], axis=1)
        y = jnp.dot(rows, matrix_ref[...], preferred_element_type=jnp.float32)
        return combine(y)

    def shifted(g):
        g32 = g.astype(jnp.float32)
        g0 = jnp.where(not_last, pltpu.roll(g32, width - 1, 0), 0.0)
        g2 = jnp.where(not_first, pltpu.roll(g32, 1, 0), 0.0)
        return jnp.concatenate([g0.astype(g.dtype), g, g2.astype(g.dtype)], axis=1)

    def phase_one(r, x_ref, c_ref, hid_ref, hidt_ref, bf_ref, k1f_ref, k2b_ref, carry):
        lv0, lv1 = carry
        valid = jnp.logical_and(jnp.logical_or(r > 0, top), jnp.logical_or(r < count + 1, bottom))
        first = conv_row(x_ref, r, k1f_ref)
        mixed = first * scale + shift
        sig = 0.5 + 0.5 * jnp.tanh(0.5 * mixed)
        hidden = jnp.where(valid, mixed * sig, 0.0)
        hid_ref[r] = hidden.astype(hid_ref.dtype)
        hidt_ref[r] = hidden.T.astype(hidt_ref.dtype)
        back_hidden = conv_row(c_ref, r, k2b_ref)
        back_mixed = back_hidden * (sig * (1.0 + mixed * (1.0 - sig)))
        bf_ref[r] = jnp.where(valid, back_mixed * scale, 0.0).astype(bf_ref.dtype)
        own = jnp.logical_and(r >= 1, r <= count)
        lv0 = lv0 + jnp.where(own, jnp.sum(back_mixed * first, axis=0, keepdims=True), 0.0)
        lv1 = lv1 + jnp.where(own, jnp.sum(back_mixed, axis=0, keepdims=True), 0.0)
        return lv0, lv1

    def out_row(i, x_ref, c_ref, hid_ref, bf_ref, k2f_ref, k1b_ref, out_ref, ig_ref):
        out_ref[i] = (x_ref[i + 2].astype(jnp.float32) + conv_row(hid_ref, i, k2f_ref)).astype(out_ref.dtype)
        ig_ref[i] = (c_ref[i + 2].astype(jnp.float32) + conv_row(bf_ref, i, k1b_ref)).astype(ig_ref.dtype)

    def g1_row(i, xt_ref, bf_ref, acc1):
        xs = jnp.concatenate([xt_ref[i + 1], xt_ref[i + 2], xt_ref[i + 3]], axis=0)
        acc1[...] += jnp.dot(xs, shifted(bf_ref[i + 1]), preferred_element_type=jnp.float32)

    def g2_row(i, hidt_ref, c_ref, acc2):
        hs = jnp.concatenate([hidt_ref[i], hidt_ref[i + 1], hidt_ref[i + 2]], axis=0)
        acc2[...] += jnp.dot(hs, shifted(c_ref[i + 2]), preferred_element_type=jnp.float32)

    return phase_one, out_row, g1_row, g2_row


def level_and_edges(idx_ref, lt_ref):
    me = lax.axis_index("rows")
    size = lax.axis_size("rows")
    level = lt_ref[idx_ref[0]]
    return level[0:1, :] + 1.0, level[1:2, :], me > 0, me < size - 1


def interior_kernel(idx_ref, lt_ref, x_hbm, c_hbm, k1_ref, k2_ref,
                    out_ref, ig_ref, hid_ref, bf_ref, hidt_ref, acc1, acc2, lv_ref, mats_ref,
                    x_ref, c_ref, xt_ref, sems):
    count, width, ch = out_ref.shape
    copies = [
        pltpu.make_async_copy(x_hbm, x_ref.at[2 : count + 2], sems.at[0]),
        pltpu.make_async_copy(c_hbm, c_ref.at[2 : count + 2], sems.at[1]),
    ]
    for cp in copies:
        cp.start()
    for a in range(3):
        for b in range(3):
            rows = slice(a * ch, (a + 1) * ch)
            cols = slice(b * ch, (b + 1) * ch)
            flip = 3 * (2 - a) + (2 - b)
            mats_ref[0, rows, cols] = k1_ref[3 * a + b]
            mats_ref[1, rows, cols] = k2_ref[3 * a + b]
            mats_ref[2, rows, cols] = k2_ref[flip].astype(jnp.float32).T.astype(mats_ref.dtype)
            mats_ref[3, rows, cols] = k1_ref[flip].astype(jnp.float32).T.astype(mats_ref.dtype)
    scale, shift, top, bottom = level_and_edges(idx_ref, lt_ref)
    phase_one, out_row, g1_row, g2_row = row_ops(width, ch, scale, shift, top, bottom, count)
    k1f, k2f, k2b, k1b = (mats_ref.at[t] for t in range(4))
    for cp in copies:
        cp.wait()

    zero = jnp.zeros((1, ch), jnp.float32)
    lv0, lv1 = lax.fori_loop(
        2, count, lambda r, cr: phase_one(r, x_ref, c_ref, hid_ref, hidt_ref, bf_ref, k1f, k2b, cr), (zero, zero)
    )
    lv_ref[0:1, :] = lv0
    lv_ref[1:2, :] = lv1

    def transpose_rows(r, carry):
        xt_ref[r] = x_ref[r].astype(jnp.float32).T.astype(xt_ref.dtype)
        return carry

    lax.fori_loop(2, count + 2, transpose_rows, 0)
    acc1[...] = jnp.zeros_like(acc1)
    acc2[...] = jnp.zeros_like(acc2)

    def middle(i, carry):
        out_row(i, x_ref, c_ref, hid_ref, bf_ref, k2f, k1b, out_ref, ig_ref)
        g2_row(i, hidt_ref, c_ref, acc2)
        return carry

    lax.fori_loop(2, count - 2, middle, 0)

    def g1_middle(i, carry):
        g1_row(i, xt_ref, bf_ref, acc1)
        return carry

    lax.fori_loop(1, count - 1, g1_middle, 0)


def edge_kernel(norm, idx_ref, lt_ref, x_hbm, c_hbm, before_hbm, after_hbm, hida_hbm, bfa_hbm, hidta_hbm,
                acc1a_ref, acc2a_ref, lva_ref, mats_ref, outa_ref, iga_ref,
                out_ref, ig_ref, grad_ref,
                x_ref, c_ref, hid_ref, bf_ref, hidt_ref, xt_ref, acc1, acc2, sems):
    count, width, ch = out_ref.shape
    out_ref[2 : count - 2] = outa_ref[2 : count - 2]
    ig_ref[2 : count - 2] = iga_ref[2 : count - 2]
    copies = [
        pltpu.make_async_copy(before_hbm.at[0:2], x_ref.at[0:2], sems.at[0]),
        pltpu.make_async_copy(x_hbm, x_ref.at[2 : count + 2], sems.at[1]),
        pltpu.make_async_copy(after_hbm.at[0:2], x_ref.at[count + 2 : count + 4], sems.at[2]),
        pltpu.make_async_copy(before_hbm.at[2:4], c_ref.at[0:2], sems.at[3]),
        pltpu.make_async_copy(c_hbm, c_ref.at[2 : count + 2], sems.at[4]),
        pltpu.make_async_copy(after_hbm.at[2:4], c_ref.at[count + 2 : count + 4], sems.at[5]),
        pltpu.make_async_copy(hida_hbm, hid_ref, sems.at[6]),
        pltpu.make_async_copy(bfa_hbm, bf_ref, sems.at[7]),
        pltpu.make_async_copy(hidta_hbm, hidt_ref, sems.at[8]),
    ]
    for cp in copies:
        cp.start()
    scale, shift, top, bottom = level_and_edges(idx_ref, lt_ref)
    phase_one, out_row, g1_row, g2_row = row_ops(width, ch, scale, shift, top, bottom, count)
    k1f, k2f, k2b, k1b = (mats_ref.at[t] for t in range(4))
    acc1[...] = acc1a_ref[...]
    acc2[...] = acc2a_ref[...]
    for cp in copies:
        cp.wait()

    carry = (lva_ref[0:1, :], lva_ref[1:2, :])
    for r in (0, 1, count, count + 1):
        carry = phase_one(r, x_ref, c_ref, hid_ref, hidt_ref, bf_ref, k1f, k2b, carry)
    lv0, lv1 = carry
    for r in (1, 2, 3, count, count + 1, count + 2):
        xt_ref[r] = x_ref[r].astype(jnp.float32).T.astype(xt_ref.dtype)
    for i in (0, 1, count - 2, count - 1):
        out_row(i, x_ref, c_ref, hid_ref, bf_ref, k2f, k1b, out_ref, ig_ref)
        g2_row(i, hidt_ref, c_ref, acc2)
    for i in (0, count - 1):
        g1_row(i, xt_ref, bf_ref, acc1)

    for a in range(3):
        for b in range(3):
            t = 3 * a + b
            blk = (slice(a * ch, (a + 1) * ch), slice(b * ch, (b + 1) * ch))
            grad_ref[t * ch : (t + 1) * ch, :] = acc1[blk] * norm
            grad_ref[(9 + t) * ch : (10 + t) * ch, :] = acc2[blk] * norm
    base = 18 * ch
    tail = grad_ref.shape[0] - base
    grad_ref[base:, :] = jnp.zeros((tail, ch), jnp.float32)
    grad_ref[base : base + 1, :] = lv0 * norm
    grad_ref[base + 1 : base + 2, :] = lv1 * norm


def section(norm, packed_rows, level_index, level_table, inputs, cotangent, before_fn, k1, k2):
    count, width, ch = inputs.shape
    vmem = pltpu.MemorySpace.VMEM if hasattr(pltpu, "MemorySpace") else pltpu.VMEM
    spec = pl.BlockSpec(memory_space=vmem)
    anywhere = pl.BlockSpec(memory_space=pl.ANY)
    smem = pl.BlockSpec(memory_space=pltpu.SMEM)
    big = 3 * ch
    unit = width * big * big * 2
    field = jax.ShapeDtypeStruct((count, width, ch), jnp.bfloat16)
    frame = jax.ShapeDtypeStruct((count + 2, width, ch), jnp.bfloat16)
    frame_t = jax.ShapeDtypeStruct((count + 2, ch, width), jnp.bfloat16)
    square = jax.ShapeDtypeStruct((big, big), jnp.float32)
    params = pltpu.CompilerParams(vmem_limit_bytes=60 * 1024 * 1024)
    out, ig, hid, bf, hidt, acc1, acc2, lv, mats = pl.pallas_call(
        interior_kernel,
        out_shape=(field, field, frame, frame, frame_t, square, square,
                   jax.ShapeDtypeStruct((2, ch), jnp.float32), jax.ShapeDtypeStruct((4, big, big), jnp.bfloat16)),
        in_specs=[smem, spec, anywhere, anywhere, spec, spec],
        out_specs=(spec,) * 9,
        scratch_shapes=[
            pltpu.VMEM((count + 4, width, ch), jnp.bfloat16),
            pltpu.VMEM((count + 4, width, ch), jnp.bfloat16),
            pltpu.VMEM((count + 4, ch, width), jnp.bfloat16),
            pltpu.SemaphoreType.DMA((2,)),
        ],
        compiler_params=params,
        cost_estimate=pl.CostEstimate(
            flops=(5 * count - 8) * unit, transcendentals=count * width * ch, bytes_accessed=8 * count * width * ch
        ),
    )(level_index, level_table, inputs, cotangent, k1, k2)
    before, after = before_fn()
    return pl.pallas_call(
        functools.partial(edge_kernel, norm),
        out_shape=(field, field, jax.ShapeDtypeStruct((packed_rows, ch), jnp.float32)),
        in_specs=[smem, spec] + [anywhere] * 7 + [spec] * 6,
        out_specs=(spec,) * 3,
        scratch_shapes=[
            pltpu.VMEM((count + 4, width, ch), jnp.bfloat16),
            pltpu.VMEM((count + 4, width, ch), jnp.bfloat16),
            pltpu.VMEM((count + 2, width, ch), jnp.bfloat16),
            pltpu.VMEM((count + 2, width, ch), jnp.bfloat16),
            pltpu.VMEM((count + 2, ch, width), jnp.bfloat16),
            pltpu.VMEM((count + 4, ch, width), jnp.bfloat16),
            pltpu.VMEM((big, big), jnp.float32),
            pltpu.VMEM((big, big), jnp.float32),
            pltpu.SemaphoreType.DMA((9,)),
        ],
        compiler_params=params,
        cost_estimate=pl.CostEstimate(
            flops=22 * unit, transcendentals=4 * width * ch, bytes_accessed=10 * count * width * ch
        ),
    )(level_index, level_table, inputs, cotangent, before, after, hid, bf, hidt, acc1, acc2, lv, mats, out, ig)


def butterfly_sum(block):
    n = lax.axis_size("rows")
    me = lax.axis_index("rows")
    bits = []
    k = 1
    while k < n:
        bits.append(k)
        k *= 2
    other = list(bits)
    if len(bits) > 2:
        other[1], other[2] = bits[2], bits[1]
    orders = list(zip(bits, other))
    even = me % 2 == 0

    def step_of(k0, k1):
        perm = [(i, i ^ (k0 if i % 2 == 0 else k1)) for i in range(n)]
        low = jnp.where(even, (me // k0) % 2, (me // k1) % 2) == 0
        return perm, low

    piece = block
    for k0, k1 in orders:
        perm, low = step_of(k0, k1)
        half = piece.shape[0] // 2
        lo, hi = piece[:half], piece[half:]
        keep = jnp.where(low, lo, hi)
        send = jnp.where(low, hi, lo)
        got = lax.ppermute(send, "rows", perm)
        piece = keep + got
    for k0, k1 in reversed(orders):
        perm, low = step_of(k0, k1)
        got = lax.ppermute(piece, "rows", perm)
        piece = jnp.where(low, jnp.concatenate([piece, got]), jnp.concatenate([got, piece]))
    return piece


def local(inputs, cotangent, first_kernel, second_kernel, level_table, level_index):
    count = inputs.shape[0]
    width = inputs.shape[1]
    ch = inputs.shape[2]
    size = lax.axis_size("rows")
    total_rows = count * size
    norm = 1.0 / math.sqrt(total_rows * width)

    up = [(i, i + 1) for i in range(size - 1)]
    down = [(i + 1, i) for i in range(size - 1)]
    before = lax.ppermute(jnp.concatenate([inputs[-2:], cotangent[-2:]]), "rows", up)
    after = lax.ppermute(jnp.concatenate([inputs[:2], cotangent[:2]]), "rows", down)
    halo = lambda: (before, after)

    used = 18 * ch + 2
    packed_rows = used + (-used % size)
    outputs, input_grad, packed = section(
        norm, packed_rows, level_index, level_table, inputs, cotangent, halo,
        first_kernel, second_kernel,
    )
    total = butterfly_sum(packed)
    first_sum = total[: 9 * ch].reshape(9, ch, ch)
    second_sum = total[9 * ch : 18 * ch].reshape(9, ch, ch)
    level_sum = total[18 * ch : 18 * ch + 2]
    return (outputs, input_grad, first_sum, second_sum, level_sum)


def solution(mesh):
    return jax.shard_map(
        local,
        mesh=mesh,
        in_specs=(
            P(("groups", "rows"), None, None),
            P(("groups", "rows"), None, None),
            P(),
            P(),
            P(),
            P("groups"),
        ),
        out_specs=(
            P(("groups", "rows"), None, None),
            P(("groups", "rows"), None, None),
            P("groups", None, None),
            P("groups", None, None),
            P("groups", None),
        ),
        check_vma=False,
    )
```

time: 86 us -> 85.6 us (level)
  Pallas kernels: 21.1 us -> 28.5 us
  starting transfers between devices: 27.3 us -> 22.1 us
  waiting for transfers between devices: 30.2 us -> 27.3 us
    pallas_call x1 -> x2, Pallas kernels: 21.1 us -> 28.5 us  [the longest x1 16.7 us: section(): pl.pallas_call(interior_kernel, out_shape=(field, field, frame, frame, fr...]
    ppermute x4, starting transfers between devices: 16.4 us -> 11.5 us  [butterfly_sum(): got = lax.ppermute(send, 'rows', perm)]
    ppermute x1, waiting for transfers between devices: 3.92 us -> 0.01 us  [local(): lax.ppermute(jnp.concatenate([inputs[:2], cotangent[:2]]), 'rows', down)]
    ppermute x4, waiting for transfers between devices: 13.6 us -> 15.3 us  [butterfly_sum(): got = lax.ppermute(piece, 'rows', perm)]
  transfers between devices with their start and end apart: 10 -> 10, of which waited for: 9 -> 8; matrix products, arithmetic and copies ran while one was open for 0% -> 0% of each run, Pallas kernels for 0% -> 20%
where the time goes in v4:
time: 85.6 us; the launch traced here: 85.3 us
  Pallas kernels  28.5 us (33%)
  waiting for transfers between devices  27.3 us (32%)
  starting transfers between devices  22.1 us (26%)
  local copies, waits for them, and re-layouts  3.94 us (5%)
  other arithmetic  2.09 us (2%)
  between operations  1.45 us (2%)
    pallas_call x1, Pallas kernels, section(): pl.pallas_call(interior_kernel, out_shape=(field, field, frame, frame, fr...  16.7 us
    ppermute x4, waiting for transfers between devices, butterfly_sum(): got = lax.ppermute(piece, 'rows', perm)  15.3 us
    ppermute x4, waiting for transfers between devices, butterfly_sum(): got = lax.ppermute(send, 'rows', perm)  11.9 us
    pallas_call x1, Pallas kernels, section(): pl.pallas_call(functools.partial(edge_kernel, norm), out_shape=(field, fi...  11.7 us
    ppermute x4, starting transfers between devices, butterfly_sum(): got = lax.ppermute(send, 'rows', perm)  11.5 us
    ppermute x4, starting transfers between devices, butterfly_sum(): got = lax.ppermute(piece, 'rows', perm)  6.97 us
    ppermute x1, starting transfers between devices, local(): lax.ppermute(jnp.concatenate([inputs[-2:], cotangent[-2:]]), 'rows', up)  2.39 us
  transfers between devices with their start and end apart: 10, of which 8 were waited for; matrix products, arithmetic and copies ran while one was open for 0% of the time, Pallas kernels for 20%

profile of v4, /device:TPU:0, one launch (start us, length us, event | category | flops | bytes accessed | tf_op | source)
XLA Modules:
  0.0 85.3 jit_solution(2067241525456301516)
XLA Ops:
  0.6 1.3 %fusion.1 = (bf16[2,512,128]{2,1,0:T(8,128)(2,1)S(1)}, bf16[2,512,128]{2,1,0:T(8,128)(2,1)S(1)}, bf16[2,512,128]{2,1,0:T(8,128)(2,1)S(1)}, bf16[2,512,128]{2,1,0:T(8,128)(2,1)S(1)}) fusion(bf16[8,512,128]{2,1,0:T(8,128)(2,1)} %x_hbm.3, bf16[8,512,128]{2,1,0:T(8,128)(2,1)} %c_hbm.3), kind=kLoop, calls=%fused_computation.15 | loop fusion | bytes 2097152 | tf_op jit(solution)/shard_map/slice | solution.py:279
  2.0 2.4 %collective-permute-start = (bf16[4,512,128]{2,1,0:T(8,128)(2,1)S(1)}, bf16[4,512,128]{2,1,0:T(8,128)(2,1)S(1)}, u32[]{:S(2)}, u32[]{:S(2)}) collective-permute-start(bf16[4,512,128]{2,1,0:T(8,128)(2,1)S(1)} %pad_maximum_fusion), channel_id=1, source_target_pairs={{0,1},{1,2},{2,3},{3,4},{4,5},{5,6},{6,7},{7,8},{8,9},{9,10},{10,1... | collective-permute-start | bytes 1572872 | tf_op jit(solution)/shard_map/ppermute | solution.py:278
  4.4 1.3 %collective-permute-start.1 = (bf16[4,512,128]{2,1,0:T(8,128)(2,1)S(1)}, bf16[4,512,128]{2,1,0:T(8,128)(2,1)S(1)}, u32[]{:S(2)}, u32[]{:S(2)}) collective-permute-start(bf16[4,512,128]{2,1,0:T(8,128)(2,1)S(1)} %pad_maximum_fusion.1), channel_id=1, source_target_pairs={{1,0},{2,1},{3,2},{4,3},{5,4},{6,5},{7,6},{8,7},{9,8},{10,9},{11,1... | collective-permute-start | bytes 1572872 | tf_op jit(solution)/shard_map/ppermute | solution.py:279
  6.4 16.7 %shard_map.101 = (bf16[8,512,128]{2,1,0:T(8,128)(2,1)}, bf16[8,512,128]{2,1,0:T(8,128)(2,1)}, bf16[10,512,128]{2,1,0:T(8,128)(2,1)}, bf16[10,512,128]{2,1,0:T(8,...) custom-call(s32[1]{0:T(128)S(6)} %copy.11.idx_ref, ...), custom_call_target="tpu_custom_call" | custom-call | flops 4831838208 | bytes 4194304 | tf_op jit(solution)/shard_map/pallas_call | solution.py:192
  23.1 0.0 collective-permute-done.before_hbm
  23.1 0.0 collective-permute-done.1.after_hbm
  23.1 0.8 copy-done.1
  24.0 0.2 copy-done.2
  24.2 11.7 %shard_map.102 = (bf16[8,512,128]{2,1,0:T(8,128)(2,1)}, bf16[8,512,128]{2,1,0:T(8,128)(2,1)}, f32[2320,128]{1,0:T(8,128)}) custom-call(s32[1]{0:T(128)S(6)} %copy.11.idx_ref, f32[16,2,128]{2,1,0:T(2,128)} %lt_ref.3, bf16[8,512,128]{2,1,0:T(8,128)(2,1)} %x_hbm.3, bf16[8,512,128]{2,1,0:T(8,128)(2,1)} %c_hbm.3, bf16[4,512,128]{2,1,0:T(8,128)(2,1)} %copy-done.1, ...), custom_call_target="tpu_custom_call" | custom-call | flops 3321888768 | bytes 5242880 | tf_op jit(solution)/shard_map/pallas_call | solution.py:210
  35.9 1.4 %slice_select_fusion = f32[1160,128]{1,0:T(8,128)S(1)} fusion(f32[2320,128]{1,0:T(8,128)} %get-tuple-element.28, pred[]{:T(512)S(6)} %eq.35), kind=kLoop, calls=%fused_computation.3 | loop fusion | flops 148480 | bytes 1781761 | tf_op jit(solution)/shard_map/jit(_where)/select_n | solution.py:258
  37.3 3.3 %collective-permute-start.2 = (f32[1160,128]{1,0:T(8,128)S(1)}, f32[1160,128]{1,0:T(8,128)S(1)}, u32[]{:S(2)}, u32[]{:S(2)}) collective-permute-start(f32[1160,128]{1,0:T(8,128)S(1)} %slice_select_fusion), channel_id=1, source_target_pairs={{0,1},{1,0},{2,3},{3,2},{4,5},{5,4},{6,7},{7,6},{8,9},{9,8},{10,11... | collective-permute-start | bytes 1781768 | tf_op jit(solution)/shard_map/ppermute | solution.py:259
  40.6 1.6 %collective-permute-done.2 = f32[1160,128]{1,0:T(8,128)S(1)} collective-permute-done((f32[1160,128]{1,0:T(8,128)S(1)}, f32[1160,128]{1,0:T(8,128)S(1)}, u32[]{:S(2)}, u32[]{:S(2)}) %collective-permute-start.2) | collective-permute-done | bytes 593952 | tf_op jit(solution)/shard_map/ppermute | solution.py:259
  42.3 0.1 select_add_fusion
  42.4 2.1 %collective-permute-start.3 = (f32[580,128]{1,0:T(8,128)S(1)}, f32[580,128]{1,0:T(8,128)S(1)}, u32[]{:S(2)}, u32[]{:S(2)}) collective-permute-start(f32[580,128]{1,0:T(8,128)S(1)} %slice_select_fusion.1), channel_id=1, source_target_pairs={{0,2},{1,5},{2,0},{3,7},{4,6},{5,1},{6,4},{7,3},{8,10},{9,13},{10,... | collective-permute-start | bytes 890888 | tf_op jit(solution)/shard_map/ppermute | solution.py:259
  44.5 4.8 %collective-permute-done.3 = f32[580,128]{1,0:T(8,128)S(1)} collective-permute-done((f32[580,128]{1,0:T(8,128)S(1)}, f32[580,128]{1,0:T(8,128)S(1)}, u32[]{:S(2)}, u32[]{:S(2)}) %collective-permute-start.3) | collective-permute-done | bytes 296992 | tf_op jit(solution)/shard_map/ppermute | solution.py:259
  49.3 0.1 select_add_fusion.1
  49.4 3.0 %collective-permute-start.4 = (f32[290,128]{1,0:T(8,128)S(1)}, f32[290,128]{1,0:T(8,128)S(1)}, u32[]{:S(2)}, u32[]{:S(2)}) collective-permute-start(f32[290,128]{1,0:T(8,128)S(1)} %slice_select_fusion.2), channel_id=1, source_target_pairs={{0,4},{1,3},{2,6},{3,1},{4,0},{5,7},{6,2},{7,5},{8,12},{9,11},{10,... | collective-permute-start | bytes 445448 | tf_op jit(solution)/shard_map/ppermute | solution.py:259
  52.4 3.2 %collective-permute-done.4 = f32[290,128]{1,0:T(8,128)S(1)} collective-permute-done((f32[290,128]{1,0:T(8,128)S(1)}, f32[290,128]{1,0:T(8,128)S(1)}, u32[]{:S(2)}, u32[]{:S(2)}) %collective-permute-start.4) | collective-permute-done | bytes 148512 | tf_op jit(solution)/shard_map/ppermute | solution.py:259
  55.6 3.1 %collective-permute-start.5 = (f32[145,128]{1,0:T(8,128)S(1)}, f32[145,128]{1,0:T(8,128)S(1)}, u32[]{:S(2)}, u32[]{:S(2)}) collective-permute-start(f32[145,128]{1,0:T(8,128)S(1)} %slice_select_fusion.3), channel_id=1, source_target_pairs={{0,8},{1,9},{2,10},{3,11},{4,12},{5,13},{6,14},{7,15},{8,0},{9,1},... | collective-permute-start | bytes 222728 | tf_op jit(solution)/shard_map/ppermute | solution.py:259
  58.7 2.4 %collective-permute-done.5 = f32[145,128]{1,0:T(8,128)S(1)} collective-permute-done((f32[145,128]{1,0:T(8,128)S(1)}, f32[145,128]{1,0:T(8,128)S(1)}, u32[]{:S(2)}, u32[]{:S(2)}) %collective-permute-start.5) | collective-permute-done | bytes 74272 | tf_op jit(solution)/shard_map/ppermute | solution.py:259
  61.1 3.1 %collective-permute-start.6 = (f32[145,128]{1,0:T(8,128)S(1)}, f32[145,128]{1,0:T(8,128)S(1)}, u32[]{:S(2)}, u32[]{:S(2)}) collective-permute-start(f32[145,128]{1,0:T(8,128)S(1)} %select_add_fusion.3), channel_id=1, source_target_pairs={{0,8},{1,9},{2,10},{3,11},{4,12},{5,13},{6,14},{7,15},{8,0},{9,1},... | collective-permute-start | bytes 222728 | tf_op jit(solution)/shard_map/ppermute | solution.py:263
  64.1 2.4 %collective-permute-done.6 = f32[145,128]{1,0:T(8,128)S(1)} collective-permute-done((f32[145,128]{1,0:T(8,128)S(1)}, f32[145,128]{1,0:T(8,128)S(1)}, u32[]{:S(2)}, u32[]{:S(2)}) %collective-permute-start.6) | collective-permute-done | bytes 74272 | tf_op jit(solution)/shard_map/ppermute | solution.py:263
  66.5 3.2 %collective-permute-start.7 = (f32[290,128]{1,0:T(8,128)S(1)}, f32[290,128]{1,0:T(8,128)S(1)}, u32[]{:S(2)}, u32[]{:S(2)}) collective-permute-start(f32[290,128]{1,0:T(8,128)S(1)} %maximum_select_fusion.3), channel_id=1, source_target_pairs={{0,4},{1,3},{2,6},{3,1},{4,0},{5,7},{6,2},{7,5},{8,12},{9,11},{10,... | collective-permute-start | bytes 445448 | tf_op jit(solution)/shard_map/ppermute | solution.py:263
  69.7 4.8 %collective-permute-done.7 = f32[290,128]{1,0:T(8,128)S(1)} collective-permute-done((f32[290,128]{1,0:T(8,128)S(1)}, f32[290,128]{1,0:T(8,128)S(1)}, u32[]{:S(2)}, u32[]{:S(2)}) %collective-permute-start.7) | collective-permute-done | bytes 148512 | tf_op jit(solution)/shard_map/ppermute | solution.py:263
  74.5 0.7 collective-permute-start.8
  75.2 6.1 %collective-permute-done.8 = f32[580,128]{1,0:T(8,128)S(1)} collective-permute-done((f32[580,128]{1,0:T(8,128)S(1)}, f32[580,128]{1,0:T(8,128)S(1)}, u32[]{:S(2)}, u32[]{:S(2)}) %collective-permute-start.8) | collective-permute-done | bytes 296992 | tf_op jit(solution)/shard_map/ppermute | solution.py:263
  81.4 0.1 maximum_select_fusion.1
  81.4 0.1 collective-permute-start.9
  81.5 2.0 %collective-permute-done.9 = f32[1160,128]{1,0:T(8,128)S(1)} collective-permute-done((f32[1160,128]{1,0:T(8,128)S(1)}, f32[1160,128]{1,0:T(8,128)S(1)}, u32[]{:S(2)}, u32[]{:S(2)}) %collective-permute-start.9) | collective-permute-done | bytes 593952 | tf_op jit(solution)/shard_map/ppermute | solution.py:263
  83.5 0.1 maximum_select_fusion
  83.7 1.1 %fusion = (f32[1152,128]{1,0:T(8,128)}, f32[1152,128]{1,0:T(8,128)}) fusion(f32[2320,128]{1,0:T(8,128)S(1)} %maximum_select_fusion), kind=kLoop, calls=%fused_computation.14 | loop fusion | bytes 2359296 | tf_op jit(solution)/shard_map/slice | solution.py:290
  84.8 0.6 slice.68
  (13 shorter events, 0.3 us)
Async XLA Ops:
  2.0 21.1 %collective-permute-start = (bf16[4,512,128]{2,1,0:T(8,128)(2,1)S(1)}, bf16[4,512,128]{2,1,0:T(8,128)(2,1)S(1)}, u32[]{:S(2)}, u32[]{:S(2)}) collective-permute-start(bf16[4,512,128]{2,1,0:T(8,128)(2,1)S(1)} %pad_maximum_fusion), channel_id=1, source_target_pairs={{0,1},{1,2},{2,3},{3,4},{4,5},{5,6},{6,7},{7,8},{8,9},{9,10},{10,1... | collective-permute-start | bytes 1572872 | tf_op jit(solution)/shard_map/ppermute | solution.py:278
  4.4 18.7 %collective-permute-start.1 = (bf16[4,512,128]{2,1,0:T(8,128)(2,1)S(1)}, bf16[4,512,128]{2,1,0:T(8,128)(2,1)S(1)}, u32[]{:S(2)}, u32[]{:S(2)}) collective-permute-start(bf16[4,512,128]{2,1,0:T(8,128)(2,1)S(1)} %pad_maximum_fusion.1), channel_id=1, source_target_pairs={{1,0},{2,1},{3,2},{4,3},{5,4},{6,5},{7,6},{8,7},{9,8},{10,9},{11,1... | collective-permute-start | bytes 1572872 | tf_op jit(solution)/shard_map/ppermute | solution.py:279
  23.1 0.8 copy-start.1
  23.1 1.0 %copy-start.2 = (bf16[4,512,128]{2,1,0:T(8,128)(2,1)}, bf16[4,512,128]{2,1,0:T(8,128)(2,1)S(1)}, u32[]{:S(2)}) copy-start(bf16[4,512,128]{2,1,0:T(8,128)(2,1)S(1)} %collective-permute-done.1.after_hbm) | copy-start | bytes 1572868
  35.9 6.3 %copy-start = (f32[2320,128]{1,0:T(8,128)S(1)}, f32[2320,128]{1,0:T(8,128)}, u32[]{:S(2)}) copy-start(f32[2320,128]{1,0:T(8,128)} %get-tuple-element.28) | copy-start | bytes 3563524
  37.3 4.9 %collective-permute-start.2 = (f32[1160,128]{1,0:T(8,128)S(1)}, f32[1160,128]{1,0:T(8,128)S(1)}, u32[]{:S(2)}, u32[]{:S(2)}) collective-permute-start(f32[1160,128]{1,0:T(8,128)S(1)} %slice_select_fusion), channel_id=1, source_target_pairs={{0,1},{1,0},{2,3},{3,2},{4,5},{5,4},{6,7},{7,6},{8,9},{9,8},{10,11... | collective-permute-start | bytes 1781768 | tf_op jit(solution)/shard_map/ppermute | solution.py:259
  42.4 6.8 %collective-permute-start.3 = (f32[580,128]{1,0:T(8,128)S(1)}, f32[580,128]{1,0:T(8,128)S(1)}, u32[]{:S(2)}, u32[]{:S(2)}) collective-permute-start(f32[580,128]{1,0:T(8,128)S(1)} %slice_select_fusion.1), channel_id=1, source_target_pairs={{0,2},{1,5},{2,0},{3,7},{4,6},{5,1},{6,4},{7,3},{8,10},{9,13},{10,... | collective-permute-start | bytes 890888 | tf_op jit(solution)/shard_map/ppermute | solution.py:259
  49.4 6.2 %collective-permute-start.4 = (f32[290,128]{1,0:T(8,128)S(1)}, f32[290,128]{1,0:T(8,128)S(1)}, u32[]{:S(2)}, u32[]{:S(2)}) collective-permute-start(f32[290,128]{1,0:T(8,128)S(1)} %slice_select_fusion.2), channel_id=1, source_target_pairs={{0,4},{1,3},{2,6},{3,1},{4,0},{5,7},{6,2},{7,5},{8,12},{9,11},{10,... | collective-permute-start | bytes 445448 | tf_op jit(solution)/shard_map/ppermute | solution.py:259
  55.6 5.5 %collective-permute-start.5 = (f32[145,128]{1,0:T(8,128)S(1)}, f32[145,128]{1,0:T(8,128)S(1)}, u32[]{:S(2)}, u32[]{:S(2)}) collective-permute-start(f32[145,128]{1,0:T(8,128)S(1)} %slice_select_fusion.3), channel_id=1, source_target_pairs={{0,8},{1,9},{2,10},{3,11},{4,12},{5,13},{6,14},{7,15},{8,0},{9,1},... | collective-permute-start | bytes 222728 | tf_op jit(solution)/shard_map/ppermute | solution.py:259
  61.1 5.4 %collective-permute-start.6 = (f32[145,128]{1,0:T(8,128)S(1)}, f32[145,128]{1,0:T(8,128)S(1)}, u32[]{:S(2)}, u32[]{:S(2)}) collective-permute-start(f32[145,128]{1,0:T(8,128)S(1)} %select_add_fusion.3), channel_id=1, source_target_pairs={{0,8},{1,9},{2,10},{3,11},{4,12},{5,13},{6,14},{7,15},{8,0},{9,1},... | collective-permute-start | bytes 222728 | tf_op jit(solution)/shard_map/ppermute | solution.py:263
  66.5 7.9 %collective-permute-start.7 = (f32[290,128]{1,0:T(8,128)S(1)}, f32[290,128]{1,0:T(8,128)S(1)}, u32[]{:S(2)}, u32[]{:S(2)}) collective-permute-start(f32[290,128]{1,0:T(8,128)S(1)} %maximum_select_fusion.3), channel_id=1, source_target_pairs={{0,4},{1,3},{2,6},{3,1},{4,0},{5,7},{6,2},{7,5},{8,12},{9,11},{10,... | collective-permute-start | bytes 445448 | tf_op jit(solution)/shard_map/ppermute | solution.py:263
  74.5 6.8 %collective-permute-start.8 = (f32[580,128]{1,0:T(8,128)S(1)}, f32[580,128]{1,0:T(8,128)S(1)}, u32[]{:S(2)}, u32[]{:S(2)}) collective-permute-start(f32[580,128]{1,0:T(8,128)S(1)} %maximum_select_fusion.2), channel_id=1, source_target_pairs={{0,2},{1,5},{2,0},{3,7},{4,6},{5,1},{6,4},{7,3},{8,10},{9,13},{10,... | collective-permute-start | bytes 890888 | tf_op jit(solution)/shard_map/ppermute | solution.py:263
  81.4 2.1 %collective-permute-start.9 = (f32[1160,128]{1,0:T(8,128)S(1)}, f32[1160,128]{1,0:T(8,128)S(1)}, u32[]{:S(2)}, u32[]{:S(2)}) collective-permute-start(f32[1160,128]{1,0:T(8,128)S(1)} %maximum_select_fusion.1), channel_id=1, source_target_pairs={{0,1},{1,0},{2,3},{3,2},{4,5},{5,4},{6,7},{7,6},{8,9},{9,8},{10,11... | collective-permute-start | bytes 1781768 | tf_op jit(solution)/shard_map/ppermute | solution.py:263

commit v5 on v4

--- a/solution.py
+++ b/solution.py
@@ -70,9 +70,10 @@
 
 
 def interior_kernel(idx_ref, lt_ref, x_hbm, c_hbm, k1_ref, k2_ref,
-                    out_ref, ig_ref, hid_ref, bf_ref, hidt_ref, acc1, acc2, lv_ref, mats_ref,
+                    hid_ref, bf_ref, hidt_ref, acc1, acc2, lv_ref, k1f, k2f, k2b, k1b,
                     x_ref, c_ref, xt_ref, sems):
-    count, width, ch = out_ref.shape
+    count = hid_ref.shape[0] - 2
+    width, ch = hid_ref.shape[1], hid_ref.shape[2]
     copies = [
         pltpu.make_async_copy(x_hbm, x_ref.at[2 : count + 2], sems.at[0]),
         pltpu.make_async_copy(c_hbm, c_ref.at[2 : count + 2], sems.at[1]),
@@ -84,13 +85,12 @@
             rows = slice(a * ch, (a + 1) * ch)
             cols = slice(b * ch, (b + 1) * ch)
             flip = 3 * (2 - a) + (2 - b)
-            mats_ref[0, rows, cols] = k1_ref[3 * a + b]
-            mats_ref[1, rows, cols] = k2_ref[3 * a + b]
-            mats_ref[2, rows, cols] = k2_ref[flip].astype(jnp.float32).T.astype(mats_ref.dtype)
-            mats_ref[3, rows, cols] = k1_ref[flip].astype(jnp.float32).T.astype(mats_ref.dtype)
+            k1f[rows, cols] = k1_ref[3 * a + b]
+            k2f[rows, cols] = k2_ref[3 * a + b]
+            k2b[rows, cols] = k2_ref[flip].astype(jnp.float32).T.astype(k2b.dtype)
+            k1b[rows, cols] = k1_ref[flip].astype(jnp.float32).T.astype(k1b.dtype)
     scale, shift, top, bottom = level_and_edges(idx_ref, lt_ref)
     phase_one, out_row, g1_row, g2_row = row_ops(width, ch, scale, shift, top, bottom, count)
-    k1f, k2f, k2b, k1b = (mats_ref.at[t] for t in range(4))
     for cp in copies:
         cp.wait()
 
@@ -110,7 +110,6 @@
     acc2[...] = jnp.zeros_like(acc2)
 
     def middle(i, carry):
-        out_row(i, x_ref, c_ref, hid_ref, bf_ref, k2f, k1b, out_ref, ig_ref)
         g2_row(i, hidt_ref, c_ref, acc2)
         return carry
 
@@ -124,12 +123,11 @@
 
 
 def edge_kernel(norm, idx_ref, lt_ref, x_hbm, c_hbm, before_hbm, after_hbm, hida_hbm, bfa_hbm, hidta_hbm,
-                acc1a_ref, acc2a_ref, lva_ref, mats_ref, outa_ref, iga_ref,
-                out_ref, ig_ref, grad_ref,
-                x_ref, c_ref, hid_ref, bf_ref, hidt_ref, xt_ref, acc1, acc2, sems):
-    count, width, ch = out_ref.shape
-    out_ref[2 : count - 2] = outa_ref[2 : count - 2]
-    ig_ref[2 : count - 2] = iga_ref[2 : count - 2]
+                acc1a_ref, acc2a_ref, lva_ref, k1f, k2b,
+                grad_ref, hid_ref, bf_ref,
+                x_ref, c_ref, hidt_ref, xt_ref, acc1, acc2, sems):
+    count = hid_ref.shape[0] - 2
+    width, ch = hid_ref.shape[1], hid_ref.shape[2]
     copies = [
         pltpu.make_async_copy(before_hbm.at[0:2], x_ref.at[0:2], sems.at[0]),
         pltpu.make_async_copy(x_hbm, x_ref.at[2 : count + 2], sems.at[1]),
@@ -145,7 +143,6 @@
         cp.start()
     scale, shift, top, bottom = level_and_edges(idx_ref, lt_ref)
     phase_one, out_row, g1_row, g2_row = row_ops(width, ch, scale, shift, top, bottom, count)
-    k1f, k2f, k2b, k1b = (mats_ref.at[t] for t in range(4))
     acc1[...] = acc1a_ref[...]
     acc2[...] = acc2a_ref[...]
     for cp in copies:
@@ -158,7 +155,6 @@
     for r in (1, 2, 3, count, count + 1, count + 2):
         xt_ref[r] = x_ref[r].astype(jnp.float32).T.astype(xt_ref.dtype)
     for i in (0, 1, count - 2, count - 1):
-        out_row(i, x_ref, c_ref, hid_ref, bf_ref, k2f, k1b, out_ref, ig_ref)
         g2_row(i, hidt_ref, c_ref, acc2)
     for i in (0, count - 1):
         g1_row(i, xt_ref, bf_ref, acc1)
@@ -174,6 +170,25 @@
     grad_ref[base:, :] = jnp.zeros((tail, ch), jnp.float32)
     grad_ref[base : base + 1, :] = lv0 * norm
     grad_ref[base + 1 : base + 2, :] = lv1 * norm
+
+
+def out_kernel(first_row, x_hbm, c_hbm, hid_hbm, bf_hbm, k2f, k1b, out_ref, ig_ref,
+               x_ref, c_ref, hid_ref, bf_ref, sems):
+    n, width, ch = out_ref.shape
+    copies = [
+        pltpu.make_async_copy(x_hbm.at[first_row : first_row + n], x_ref.at[2 : n + 2], sems.at[0]),
+        pltpu.make_async_copy(c_hbm.at[first_row : first_row + n], c_ref.at[2 : n + 2], sems.at[1]),
+        pltpu.make_async_copy(hid_hbm.at[first_row : first_row + n + 2], hid_ref, sems.at[2]),
+        pltpu.make_async_copy(bf_hbm.at[first_row : first_row + n + 2], bf_ref, sems.at[3]),
+    ]
+    for cp in copies:
+        cp.start()
+    one = jnp.ones((1, ch), jnp.float32)
+    out_row = row_ops(width, ch, one, one, True, True, n)[1]
+    for cp in copies:
+        cp.wait()
+    for i in range(n):
+        out_row(i, x_ref, c_ref, hid_ref, bf_ref, k2f, k1b, out_ref, ig_ref)
 
 
 def section(norm, packed_rows, level_index, level_table, inputs, cotangent, before_fn, k1, k2):
@@ -189,12 +204,13 @@
     frame_t = jax.ShapeDtypeStruct((count + 2, ch, width), jnp.bfloat16)
     square = jax.ShapeDtypeStruct((big, big), jnp.float32)
     params = pltpu.CompilerParams(vmem_limit_bytes=60 * 1024 * 1024)
-    out, ig, hid, bf, hidt, acc1, acc2, lv, mats = pl.pallas_call(
+    matrix = jax.ShapeDtypeStruct((big, big), jnp.bfloat16)
+    hid, bf, hidt, acc1, acc2, lv, k1f, k2f, k2b, k1b = pl.pallas_call(
         interior_kernel,
-        out_shape=(field, field, frame, frame, frame_t, square, square,
-                   jax.ShapeDtypeStruct((2, ch), jnp.float32), jax.ShapeDtypeStruct((4, big, big), jnp.bfloat16)),
+        out_shape=(frame, frame, frame_t, square, square,
+                   jax.ShapeDtypeStruct((2, ch), jnp.float32), matrix, matrix, matrix, matrix),
         in_specs=[smem, spec, anywhere, anywhere, spec, spec],
-        out_specs=(spec,) * 9,
+        out_specs=(spec,) * 10,
         scratch_shapes=[
             pltpu.VMEM((count + 4, width, ch), jnp.bfloat16),
             pltpu.VMEM((count + 4, width, ch), jnp.bfloat16),
@@ -203,20 +219,18 @@
         ],
         compiler_params=params,
         cost_estimate=pl.CostEstimate(
-            flops=(5 * count - 8) * unit, transcendentals=count * width * ch, bytes_accessed=8 * count * width * ch
+            flops=(4 * count - 6) * unit, transcendentals=count * width * ch, bytes_accessed=8 * count * width * ch
         ),
     )(level_index, level_table, inputs, cotangent, k1, k2)
     before, after = before_fn()
-    return pl.pallas_call(
+    packed, hid, bf = pl.pallas_call(
         functools.partial(edge_kernel, norm),
-        out_shape=(field, field, jax.ShapeDtypeStruct((packed_rows, ch), jnp.float32)),
-        in_specs=[smem, spec] + [anywhere] * 7 + [spec] * 6,
-        out_specs=(spec,) * 3,
+        out_shape=(jax.ShapeDtypeStruct((packed_rows, ch), jnp.float32), frame, frame),
+        in_specs=[smem, spec] + [anywhere] * 7 + [spec] * 5,
+        out_specs=(spec, spec, spec),
         scratch_shapes=[
             pltpu.VMEM((count + 4, width, ch), jnp.bfloat16),
             pltpu.VMEM((count + 4, width, ch), jnp.bfloat16),
-            pltpu.VMEM((count + 2, width, ch), jnp.bfloat16),
-            pltpu.VMEM((count + 2, width, ch), jnp.bfloat16),
             pltpu.VMEM((count + 2, ch, width), jnp.bfloat16),
             pltpu.VMEM((count + 4, ch, width), jnp.bfloat16),
             pltpu.VMEM((big, big), jnp.float32),
@@ -225,12 +239,35 @@
         ],
         compiler_params=params,
         cost_estimate=pl.CostEstimate(
-            flops=22 * unit, transcendentals=4 * width * ch, bytes_accessed=10 * count * width * ch
+            flops=14 * unit, transcendentals=4 * width * ch, bytes_accessed=10 * count * width * ch
         ),
-    )(level_index, level_table, inputs, cotangent, before, after, hid, bf, hidt, acc1, acc2, lv, mats, out, ig)
-
-
-def butterfly_sum(block):
+    )(level_index, level_table, inputs, cotangent, before, after, hid, bf, hidt, acc1, acc2, lv, k1f, k2b)
+    step = 2 if count % 2 == 0 else 1
+    chunk = jax.ShapeDtypeStruct((step, width, ch), jnp.bfloat16)
+    outs, igs = [], []
+    for first_row in range(0, count, step):
+        o, g = pl.pallas_call(
+            functools.partial(out_kernel, first_row),
+            out_shape=(chunk, chunk),
+            in_specs=[anywhere] * 4 + [spec] * 2,
+            out_specs=(spec, spec),
+            scratch_shapes=[
+                pltpu.VMEM((step + 2, width, ch), jnp.bfloat16),
+                pltpu.VMEM((step + 2, width, ch), jnp.bfloat16),
+                pltpu.VMEM((step + 2, width, ch), jnp.bfloat16),
+                pltpu.VMEM((step + 2, width, ch), jnp.bfloat16),
+                pltpu.SemaphoreType.DMA((4,)),
+            ],
+            compiler_params=params,
+            cost_estimate=pl.CostEstimate(
+                flops=2 * step * unit, transcendentals=0, bytes_accessed=8 * step * width * ch
+            ),
+        )(inputs, cotangent, hid, bf, k2f, k1b)
+        outs.append((o, g))
+    return outs, packed
+
+
+def butterfly_sum(block, riders=()):
     n = lax.axis_size("rows")
     me = lax.axis_index("rows")
     bits = []
@@ -249,6 +286,8 @@
         low = jnp.where(even, (me // k0) % 2, (me // k1) % 2) == 0
         return perm, low
 
+    riders = list(riders)
+    tied = []
     piece = block
     for k0, k1 in orders:
         perm, low = step_of(k0, k1)
@@ -257,12 +296,18 @@
         keep = jnp.where(low, lo, hi)
         send = jnp.where(low, hi, lo)
         got = lax.ppermute(send, "rows", perm)
+        if riders:
+            got, rider = lax.optimization_barrier((got, riders.pop(0)))
+            tied.append(rider)
         piece = keep + got
     for k0, k1 in reversed(orders):
         perm, low = step_of(k0, k1)
         got = lax.ppermute(piece, "rows", perm)
+        if riders:
+            got, rider = lax.optimization_barrier((got, riders.pop(0)))
+            tied.append(rider)
         piece = jnp.where(low, jnp.concatenate([piece, got]), jnp.concatenate([got, piece]))
-    return piece
+    return piece, tied + riders
 
 
 def local(inputs, cotangent, first_kernel, second_kernel, level_table, level_index):
@@ -281,11 +326,13 @@
 
     used = 18 * ch + 2
     packed_rows = used + (-used % size)
-    outputs, input_grad, packed = section(
+    chunks, packed = section(
         norm, packed_rows, level_index, level_table, inputs, cotangent, halo,
         first_kernel, second_kernel,
     )
-    total = butterfly_sum(packed)
+    total, chunks = butterfly_sum(packed, chunks)
+    outputs = jnp.concatenate([o for o, _ in chunks])
+    input_grad = jnp.concatenate([g for _, g in chunks])
     first_sum = total[: 9 * ch].reshape(9, ch, ch)
     second_sum = total[9 * ch : 18 * ch].reshape(9, ch, ch)
     level_sum = total[18 * ch : 18 * ch + 2]

time: 85.6 us -> 84 us (0.981)
  Pallas kernels: 28.5 us -> 40.4 us
  waiting for transfers between devices: 27.3 us -> 15.8 us
  starting transfers between devices: 22.1 us -> 17.6 us
  other arithmetic: 2.09 us -> 4.21 us
    pallas_call x2 -> x6, Pallas kernels: 28.5 us -> 40.4 us  [the longest x4 17.2 us: section(): pl.pallas_call(functools.partial(out_kernel, first_row), out_shape=(chunk...]
    ppermute x4, waiting for transfers between devices: 11.9 us -> 0.45 us  [butterfly_sum(): got = lax.ppermute(send, 'rows', perm)]
    ppermute x4, starting transfers between devices: 6.97 us -> 4.2 us  [butterfly_sum(): got = lax.ppermute(piece, 'rows', perm)]
    ppermute x4, starting transfers between devices: 11.5 us -> 9 us  [butterfly_sum(): got = lax.ppermute(send, 'rows', perm)]
    concatenate x0 -> x2, other arithmetic: none -> 2.21 us  [the longest x1 1.1 us: local(): outputs = jnp.concatenate([o for o, _ in chunks])]
  transfers between devices with their start and end apart: 10 -> 10, of which waited for: 8 -> 4; matrix products, arithmetic and copies ran while one was open for 0% -> 3% of each run, Pallas kernels for 20% -> 38%
where the time goes in v5:
time: 84 us; the launch traced here: 83.5 us
  Pallas kernels  40.4 us (48%)
  starting transfers between devices  17.6 us (21%)
  waiting for transfers between devices  15.8 us (19%)
  other arithmetic  4.21 us (5%)
  local copies, waits for them, and re-layouts  3.9 us (5%)
  between operations  1.61 us (2%)
    pallas_call x4, Pallas kernels, section(): pl.pallas_call(functools.partial(out_kernel, first_row), out_shape=(chunk...  17.2 us
    ppermute x4, waiting for transfers between devices, butterfly_sum(): got = lax.ppermute(piece, 'rows', perm)  15.3 us
    pallas_call x1, Pallas kernels, section(): pl.pallas_call(interior_kernel, out_shape=(frame, frame, frame_t, square,...  14.2 us
    pallas_call x1, Pallas kernels, section(): pl.pallas_call(functools.partial(edge_kernel, norm), out_shape=(jax.Shape...  9.01 us
    ppermute x4, starting transfers between devices, butterfly_sum(): got = lax.ppermute(send, 'rows', perm)  9 us
    ppermute x4, starting transfers between devices, butterfly_sum(): got = lax.ppermute(piece, 'rows', perm)  4.2 us
    ppermute x1, starting transfers between devices, local(): lax.ppermute(jnp.concatenate([inputs[-2:], cotangent[-2:]]), 'rows', up)  3.06 us
  transfers between devices with their start and end apart: 10, of which 4 were waited for; matrix products, arithmetic and copies ran while one was open for 3% of the time, Pallas kernels for 38%

profile of v5, /device:TPU:0, one launch (start us, length us, event | category | flops | bytes accessed | tf_op | source)
XLA Modules:
  0.0 83.5 jit_solution(5558956561137801292)
XLA Ops:
  0.6 1.3 %fusion.1 = (bf16[2,512,128]{2,1,0:T(8,128)(2,1)S(1)}, bf16[2,512,128]{2,1,0:T(8,128)(2,1)S(1)}, bf16[2,512,128]{2,1,0:T(8,128)(2,1)S(1)}, bf16[2,512,128]{2,1,0:T(8,128)(2,1)S(1)}) fusion(bf16[8,512,128]{2,1,0:T(8,128)(2,1)} %x_hbm.11, bf16[8,512,128]{2,1,0:T(8,128)(2,1)} %c_hbm.11), kind=kLoop, calls=%fused_computation.17 | loop fusion | bytes 2097152 | tf_op jit(solution)/shard_map/slice | solution.py:324
  2.0 1.3 %collective-permute-start.1 = (bf16[4,512,128]{2,1,0:T(8,128)(2,1)S(1)}, bf16[4,512,128]{2,1,0:T(8,128)(2,1)S(1)}, u32[]{:S(2)}, u32[]{:S(2)}) collective-permute-start(bf16[4,512,128]{2,1,0:T(8,128)(2,1)S(1)} %pad_maximum_fusion.3), channel_id=1, source_target_pairs={{1,0},{2,1},{3,2},{4,3},{5,4},{6,5},{7,6},{8,7},{9,8},{10,9},{11,1... | collective-permute-start | bytes 1572872 | tf_op jit(solution)/shard_map/ppermute | solution.py:324
  3.3 3.1 %collective-permute-start = (bf16[4,512,128]{2,1,0:T(8,128)(2,1)S(1)}, bf16[4,512,128]{2,1,0:T(8,128)(2,1)S(1)}, u32[]{:S(2)}, u32[]{:S(2)}) collective-permute-start(bf16[4,512,128]{2,1,0:T(8,128)(2,1)S(1)} %pad_maximum_fusion.2), channel_id=1, source_target_pairs={{0,1},{1,2},{2,3},{3,4},{4,5},{5,6},{6,7},{7,8},{8,9},{9,10},{10,1... | collective-permute-start | bytes 1572872 | tf_op jit(solution)/shard_map/ppermute | solution.py:323
  7.0 14.2 %shard_map.101 = (bf16[10,512,128]{2,1,0:T(8,128)(2,1)}, bf16[10,512,128]{2,1,0:T(8,128)(2,1)}, bf16[10,128,512]{2,1,0:T(8,128)(2,1)}, f32[384,384]{1,0:T(8,128)...) custom-call(s32[1]{0:T(128)S(6)} %copy.11.idx_ref, ...), custom_call_target="tpu_custom_call" | custom-call | flops 3925868544 | bytes 4194304 | tf_op jit(solution)/shard_map/pallas_call | solution.py:208
  21.3 0.8 copy-done.1
  22.0 0.2 copy-done.2
  22.2 9.0 %shard_map.102 = (f32[2320,128]{1,0:T(8,128)}, bf16[10,512,128]{2,1,0:T(8,128)(2,1)}, bf16[10,512,128]{2,1,0:T(8,128)(2,1)}) custom-call(s32[1]{0:T(128)S(6)} %copy.11.idx_ref, f32[16,2,128]{2,1,0:T(2,128)} %lt_ref.3, bf16[8,512,128]{2,1,0:T(8,128)(2,1)} %x_hbm.11, bf16[8,512,128]{2,1,0:T(8,128)(2,1)} %c_hbm.11, bf16[4,512,128]{2,1,0:T(8,128)(2,1)} %copy-done.2, ...), custom_call_target="tpu_custom_call" | custom-call | flops 2113929216 | bytes 5242880 | tf_op jit(solution)/shard_map/pallas_call | solution.py:226
  31.2 1.3 %slice_select_fusion = f32[1160,128]{1,0:T(8,128)S(1)} fusion(f32[2320,128]{1,0:T(8,128)} %get-tuple-element.46, pred[]{:T(512)S(6)} %eq.35), kind=kLoop, calls=%fused_computation.5 | loop fusion | flops 148480 | bytes 1781761 | tf_op jit(solution)/shard_map/jit(_where)/select_n | solution.py:297
  32.5 2.6 %collective-permute-start.2 = (f32[1160,128]{1,0:T(8,128)S(1)}, f32[1160,128]{1,0:T(8,128)S(1)}, u32[]{:S(2)}, u32[]{:S(2)}) collective-permute-start(f32[1160,128]{1,0:T(8,128)S(1)} %slice_select_fusion), channel_id=1, source_target_pairs={{0,1},{1,0},{2,3},{3,2},{4,5},{5,4},{6,7},{7,6},{8,9},{9,8},{10,11... | collective-permute-start | bytes 1781768 | tf_op jit(solution)/shard_map/ppermute | solution.py:298
  35.2 4.4 %shard_map.103 = (bf16[2,512,128]{2,1,0:T(8,128)(2,1)}, bf16[2,512,128]{2,1,0:T(8,128)(2,1)}) custom-call(bf16[8,512,128]{2,1,0:T(8,128)(2,1)} %x_hbm.11, bf16[8,512,128]{2,1,0:T(8,128)(2,1)} %c_hbm.11, bf16[10,512,128]{2,1,0:T(8,128)(2,1)} %get-tuple-element.47.hid_hbm, bf16[10,512,128]{2,1,0:T(8,128)(2,1)} %get-tuple-element.48.bf_hbm, ...), custom_call_target="tpu_custom_call" | custom-call | flops 603979776 | bytes 1048576 | tf_op jit(solution)/shard_map/pallas_call | solution.py:249
  39.6 0.1 select_add_fusion
  39.7 2.4 %collective-permute-start.3 = (f32[580,128]{1,0:T(8,128)S(1)}, f32[580,128]{1,0:T(8,128)S(1)}, u32[]{:S(2)}, u32[]{:S(2)}) collective-permute-start(f32[580,128]{1,0:T(8,128)S(1)} %slice_select_fusion.1), channel_id=1, source_target_pairs={{0,2},{1,5},{2,0},{3,7},{4,6},{5,1},{6,4},{7,3},{8,10},{9,13},{10,... | collective-permute-start | bytes 890888 | tf_op jit(solution)/shard_map/ppermute | solution.py:298
  42.2 4.3 %shard_map.104 = (bf16[2,512,128]{2,1,0:T(8,128)(2,1)}, bf16[2,512,128]{2,1,0:T(8,128)(2,1)}) custom-call(bf16[8,512,128]{2,1,0:T(8,128)(2,1)} %x_hbm.11, bf16[8,512,128]{2,1,0:T(8,128)(2,1)} %c_hbm.11, bf16[10,512,128]{2,1,0:T(8,128)(2,1)} %get-tuple-element.47.hid_hbm, bf16[10,512,128]{2,1,0:T(8,128)(2,1)} %get-tuple-element.48.bf_hbm, ...), custom_call_target="tpu_custom_call" | custom-call | flops 603979776 | bytes 1048576 | tf_op jit(solution)/shard_map/pallas_call | solution.py:249
  46.5 0.4 collective-permute-done.3
  46.9 0.1 select_add_fusion.1
  47.0 1.6 %collective-permute-start.4 = (f32[290,128]{1,0:T(8,128)S(1)}, f32[290,128]{1,0:T(8,128)S(1)}, u32[]{:S(2)}, u32[]{:S(2)}) collective-permute-start(f32[290,128]{1,0:T(8,128)S(1)} %slice_select_fusion.2), channel_id=1, source_target_pairs={{0,4},{1,3},{2,6},{3,1},{4,0},{5,7},{6,2},{7,5},{8,12},{9,11},{10,... | collective-permute-start | bytes 445448 | tf_op jit(solution)/shard_map/ppermute | solution.py:298
  48.6 4.3 %shard_map.105 = (bf16[2,512,128]{2,1,0:T(8,128)(2,1)}, bf16[2,512,128]{2,1,0:T(8,128)(2,1)}) custom-call(bf16[8,512,128]{2,1,0:T(8,128)(2,1)} %x_hbm.11, bf16[8,512,128]{2,1,0:T(8,128)(2,1)} %c_hbm.11, bf16[10,512,128]{2,1,0:T(8,128)(2,1)} %get-tuple-element.47.hid_hbm, bf16[10,512,128]{2,1,0:T(8,128)(2,1)} %get-tuple-element.48.bf_hbm, ...), custom_call_target="tpu_custom_call" | custom-call | flops 603979776 | bytes 1048576 | tf_op jit(solution)/shard_map/pallas_call | solution.py:249
  53.0 2.3 %collective-permute-start.5 = (f32[145,128]{1,0:T(8,128)S(1)}, f32[145,128]{1,0:T(8,128)S(1)}, u32[]{:S(2)}, u32[]{:S(2)}) collective-permute-start(f32[145,128]{1,0:T(8,128)S(1)} %slice_select_fusion.3), channel_id=1, source_target_pairs={{0,8},{1,9},{2,10},{3,11},{4,12},{5,13},{6,14},{7,15},{8,0},{9,1},... | collective-permute-start | bytes 222728 | tf_op jit(solution)/shard_map/ppermute | solution.py:298
  55.3 4.3 %shard_map.106 = (bf16[2,512,128]{2,1,0:T(8,128)(2,1)}, bf16[2,512,128]{2,1,0:T(8,128)(2,1)}) custom-call(bf16[8,512,128]{2,1,0:T(8,128)(2,1)} %x_hbm.11, bf16[8,512,128]{2,1,0:T(8,128)(2,1)} %c_hbm.11, bf16[10,512,128]{2,1,0:T(8,128)(2,1)} %get-tuple-element.47.hid_hbm, bf16[10,512,128]{2,1,0:T(8,128)(2,1)} %get-tuple-element.48.bf_hbm, ...), custom_call_target="tpu_custom_call" | custom-call | flops 603979776 | bytes 1048576 | tf_op jit(solution)/shard_map/pallas_call | solution.py:249
  59.7 1.0 %collective-permute-start.6 = (f32[145,128]{1,0:T(8,128)S(1)}, f32[145,128]{1,0:T(8,128)S(1)}, u32[]{:S(2)}, u32[]{:S(2)}) collective-permute-start(f32[145,128]{1,0:T(8,128)S(1)} %select_add_fusion.3), channel_id=1, source_target_pairs={{0,8},{1,9},{2,10},{3,11},{4,12},{5,13},{6,14},{7,15},{8,0},{9,1},... | collective-permute-start | bytes 222728 | tf_op jit(solution)/shard_map/ppermute | solution.py:305
  60.7 5.1 %collective-permute-done.6 = f32[145,128]{1,0:T(8,128)S(1)} collective-permute-done((f32[145,128]{1,0:T(8,128)S(1)}, f32[145,128]{1,0:T(8,128)S(1)}, u32[]{:S(2)}, u32[]{:S(2)}) %collective-permute-start.6) | collective-permute-done | bytes 74272 | tf_op jit(solution)/shard_map/ppermute | solution.py:305
  65.9 0.2 collective-permute-start.7
  66.1 5.4 %collective-permute-done.7 = f32[290,128]{1,0:T(8,128)S(1)} collective-permute-done((f32[290,128]{1,0:T(8,128)S(1)}, f32[290,128]{1,0:T(8,128)S(1)}, u32[]{:S(2)}, u32[]{:S(2)}) %collective-permute-start.7) | collective-permute-done | bytes 148512 | tf_op jit(solution)/shard_map/ppermute | solution.py:305
  71.6 2.8 %collective-permute-start.8 = (f32[580,128]{1,0:T(8,128)S(1)}, f32[580,128]{1,0:T(8,128)S(1)}, u32[]{:S(2)}, u32[]{:S(2)}) collective-permute-start(f32[580,128]{1,0:T(8,128)S(1)} %maximum_select_fusion.2), channel_id=1, source_target_pairs={{0,2},{1,5},{2,0},{3,7},{4,6},{5,1},{6,4},{7,3},{8,10},{9,13},{10,... | collective-permute-start | bytes 890888 | tf_op jit(solution)/shard_map/ppermute | solution.py:305
  74.4 4.7 %collective-permute-done.8 = f32[580,128]{1,0:T(8,128)S(1)} collective-permute-done((f32[580,128]{1,0:T(8,128)S(1)}, f32[580,128]{1,0:T(8,128)S(1)}, u32[]{:S(2)}, u32[]{:S(2)}) %collective-permute-start.8) | collective-permute-done | bytes 296992 | tf_op jit(solution)/shard_map/ppermute | solution.py:305
  79.2 0.1 maximum_select_fusion.1
  79.3 0.1 collective-permute-start.9
  79.4 1.1 %pad_maximum_fusion.1 = bf16[8,512,128]{2,1,0:T(8,128)(2,1)} fusion(bf16[2,512,128]{2,1,0:T(8,128)(2,1)S(1)} %copy-done.10, bf16[2,512,128]{2,1,0:T(8,128)(2,1)S(1)} %copy-done.8, bf16[2,512,128]{2,1,0:T(8,128)(2,1)S(1)} %copy-done.6, bf16[2,512,128]{2,1,0:T(8,128)(2,1)S(1)} %copy-done.4), kind=kLoop, calls=%fused_computation.2 | loop fusion | flops 1572864 | bytes 2097152 | tf_op jit(solution)/shard_map/concatenate | solution.py:335
  80.5 1.1 %pad_maximum_fusion = bf16[8,512,128]{2,1,0:T(8,128)(2,1)} fusion(bf16[2,512,128]{2,1,0:T(8,128)(2,1)S(1)} %copy-done.9, bf16[2,512,128]{2,1,0:T(8,128)(2,1)S(1)} %copy-done.7, bf16[2,512,128]{2,1,0:T(8,128)(2,1)S(1)} %copy-done.5, bf16[2,512,128]{2,1,0:T(8,128)(2,1)S(1)} %copy-done.3), kind=kLoop, calls=%fused_computation.1 | loop fusion | flops 1572864 | bytes 2097152 | tf_op jit(solution)/shard_map/concatenate | solution.py:334
  81.7 0.1 maximum_select_fusion
  81.8 1.1 %fusion = (f32[1152,128]{1,0:T(8,128)}, f32[1152,128]{1,0:T(8,128)}) fusion(f32[2320,128]{1,0:T(8,128)S(1)} %maximum_select_fusion), kind=kLoop, calls=%fused_computation.16 | loop fusion | bytes 2359296 | tf_op jit(solution)/shard_map/slice | solution.py:337
  82.9 0.6 slice.68
  (35 shorter events, 0.3 us)
Async XLA Ops:
  2.0 19.3 %collective-permute-start.1 = (bf16[4,512,128]{2,1,0:T(8,128)(2,1)S(1)}, bf16[4,512,128]{2,1,0:T(8,128)(2,1)S(1)}, u32[]{:S(2)}, u32[]{:S(2)}) collective-permute-start(bf16[4,512,128]{2,1,0:T(8,128)(2,1)S(1)} %pad_maximum_fusion.3), channel_id=1, source_target_pairs={{1,0},{2,1},{3,2},{4,3},{5,4},{6,5},{7,6},{8,7},{9,8},{10,9},{11,1... | collective-permute-start | bytes 1572872 | tf_op jit(solution)/shard_map/ppermute | solution.py:324
  3.3 17.9 %collective-permute-start = (bf16[4,512,128]{2,1,0:T(8,128)(2,1)S(1)}, bf16[4,512,128]{2,1,0:T(8,128)(2,1)S(1)}, u32[]{:S(2)}, u32[]{:S(2)}) collective-permute-start(bf16[4,512,128]{2,1,0:T(8,128)(2,1)S(1)} %pad_maximum_fusion.2), channel_id=1, source_target_pairs={{0,1},{1,2},{2,3},{3,4},{4,5},{5,6},{6,7},{7,8},{8,9},{9,10},{10,1... | collective-permute-start | bytes 1572872 | tf_op jit(solution)/shard_map/ppermute | solution.py:323
  21.2 0.8 copy-start.1
  21.3 0.9 %copy-start.2 = (bf16[4,512,128]{2,1,0:T(8,128)(2,1)}, bf16[4,512,128]{2,1,0:T(8,128)(2,1)S(1)}, u32[]{:S(2)}) copy-start(bf16[4,512,128]{2,1,0:T(8,128)(2,1)S(1)} %collective-permute-done.before_hbm) | copy-start | bytes 1572868
  32.5 7.0 %collective-permute-start.2 = (f32[1160,128]{1,0:T(8,128)S(1)}, f32[1160,128]{1,0:T(8,128)S(1)}, u32[]{:S(2)}, u32[]{:S(2)}) collective-permute-start(f32[1160,128]{1,0:T(8,128)S(1)} %slice_select_fusion), channel_id=1, source_target_pairs={{0,1},{1,0},{2,3},{3,2},{4,5},{5,4},{6,7},{7,6},{8,9},{9,8},{10,11... | collective-permute-start | bytes 1781768 | tf_op jit(solution)/shard_map/ppermute | solution.py:298
  35.2 4.4 %copy-start = (f32[2320,128]{1,0:T(8,128)S(1)}, f32[2320,128]{1,0:T(8,128)}, u32[]{:S(2)}) copy-start(f32[2320,128]{1,0:T(8,128)} %get-tuple-element.46) | copy-start | bytes 3563524
  39.7 7.2 %collective-permute-start.3 = (f32[580,128]{1,0:T(8,128)S(1)}, f32[580,128]{1,0:T(8,128)S(1)}, u32[]{:S(2)}, u32[]{:S(2)}) collective-permute-start(f32[580,128]{1,0:T(8,128)S(1)} %slice_select_fusion.1), channel_id=1, source_target_pairs={{0,2},{1,5},{2,0},{3,7},{4,6},{5,1},{6,4},{7,3},{8,10},{9,13},{10,... | collective-permute-start | bytes 890888 | tf_op jit(solution)/shard_map/ppermute | solution.py:298
  47.0 5.9 %collective-permute-start.4 = (f32[290,128]{1,0:T(8,128)S(1)}, f32[290,128]{1,0:T(8,128)S(1)}, u32[]{:S(2)}, u32[]{:S(2)}) collective-permute-start(f32[290,128]{1,0:T(8,128)S(1)} %slice_select_fusion.2), channel_id=1, source_target_pairs={{0,4},{1,3},{2,6},{3,1},{4,0},{5,7},{6,2},{7,5},{8,12},{9,11},{10,... | collective-permute-start | bytes 445448 | tf_op jit(solution)/shard_map/ppermute | solution.py:298
  53.0 6.6 %collective-permute-start.5 = (f32[145,128]{1,0:T(8,128)S(1)}, f32[145,128]{1,0:T(8,128)S(1)}, u32[]{:S(2)}, u32[]{:S(2)}) collective-permute-start(f32[145,128]{1,0:T(8,128)S(1)} %slice_select_fusion.3), channel_id=1, source_target_pairs={{0,8},{1,9},{2,10},{3,11},{4,12},{5,13},{6,14},{7,15},{8,0},{9,1},... | collective-permute-start | bytes 222728 | tf_op jit(solution)/shard_map/ppermute | solution.py:298
  59.6 19.8 %copy-start.4 = (bf16[2,512,128]{2,1,0:T(8,128)(2,1)S(1)}, bf16[2,512,128]{2,1,0:T(8,128)(2,1)}, u32[]{:S(2)}) copy-start(bf16[2,512,128]{2,1,0:T(8,128)(2,1)} %get-tuple-element.66) | copy-start | bytes 786436
  59.6 19.8 %copy-start.6 = (bf16[2,512,128]{2,1,0:T(8,128)(2,1)S(1)}, bf16[2,512,128]{2,1,0:T(8,128)(2,1)}, u32[]{:S(2)}) copy-start(bf16[2,512,128]{2,1,0:T(8,128)(2,1)} %get-tuple-element.67) | copy-start | bytes 786436
  59.6 19.8 %copy-start.8 = (bf16[2,512,128]{2,1,0:T(8,128)(2,1)S(1)}, bf16[2,512,128]{2,1,0:T(8,128)(2,1)}, u32[]{:S(2)}) copy-start(bf16[2,512,128]{2,1,0:T(8,128)(2,1)} %get-tuple-element.68) | copy-start | bytes 786436
  59.6 19.8 %copy-start.10 = (bf16[2,512,128]{2,1,0:T(8,128)(2,1)S(1)}, bf16[2,512,128]{2,1,0:T(8,128)(2,1)}, u32[]{:S(2)}) copy-start(bf16[2,512,128]{2,1,0:T(8,128)(2,1)} %get-tuple-element.69) | copy-start | bytes 786436
  59.7 6.2 %collective-permute-start.6 = (f32[145,128]{1,0:T(8,128)S(1)}, f32[145,128]{1,0:T(8,128)S(1)}, u32[]{:S(2)}, u32[]{:S(2)}) collective-permute-start(f32[145,128]{1,0:T(8,128)S(1)} %select_add_fusion.3), channel_id=1, source_target_pairs={{0,8},{1,9},{2,10},{3,11},{4,12},{5,13},{6,14},{7,15},{8,0},{9,1},... | collective-permute-start | bytes 222728 | tf_op jit(solution)/shard_map/ppermute | solution.py:305
  65.9 5.7 %collective-permute-start.7 = (f32[290,128]{1,0:T(8,128)S(1)}, f32[290,128]{1,0:T(8,128)S(1)}, u32[]{:S(2)}, u32[]{:S(2)}) collective-permute-start(f32[290,128]{1,0:T(8,128)S(1)} %maximum_select_fusion.3), channel_id=1, source_target_pairs={{0,4},{1,3},{2,6},{3,1},{4,0},{5,7},{6,2},{7,5},{8,12},{9,11},{10,... | collective-permute-start | bytes 445448 | tf_op jit(solution)/shard_map/ppermute | solution.py:305
  71.6 7.6 %collective-permute-start.8 = (f32[580,128]{1,0:T(8,128)S(1)}, f32[580,128]{1,0:T(8,128)S(1)}, u32[]{:S(2)}, u32[]{:S(2)}) collective-permute-start(f32[580,128]{1,0:T(8,128)S(1)} %maximum_select_fusion.2), channel_id=1, source_target_pairs={{0,2},{1,5},{2,0},{3,7},{4,6},{5,1},{6,4},{7,3},{8,10},{9,13},{10,... | collective-permute-start | bytes 890888 | tf_op jit(solution)/shard_map/ppermute | solution.py:305
  79.3 1.3 %copy-start.3 = (bf16[2,512,128]{2,1,0:T(8,128)(2,1)S(1)}, bf16[2,512,128]{2,1,0:T(8,128)(2,1)}, u32[]{:S(2)}) copy-start(bf16[2,512,128]{2,1,0:T(8,128)(2,1)} %get-tuple-element.53) | copy-start | bytes 786436
  79.3 1.3 %copy-start.5 = (bf16[2,512,128]{2,1,0:T(8,128)(2,1)S(1)}, bf16[2,512,128]{2,1,0:T(8,128)(2,1)}, u32[]{:S(2)}) copy-start(bf16[2,512,128]{2,1,0:T(8,128)(2,1)} %get-tuple-element.57) | copy-start | bytes 786436
  79.3 1.3 %copy-start.7 = (bf16[2,512,128]{2,1,0:T(8,128)(2,1)S(1)}, bf16[2,512,128]{2,1,0:T(8,128)(2,1)}, u32[]{:S(2)}) copy-start(bf16[2,512,128]{2,1,0:T(8,128)(2,1)} %get-tuple-element.61) | copy-start | bytes 786436
  79.3 1.2 %copy-start.9 = (bf16[2,512,128]{2,1,0:T(8,128)(2,1)S(1)}, bf16[2,512,128]{2,1,0:T(8,128)(2,1)}, u32[]{:S(2)}) copy-start(bf16[2,512,128]{2,1,0:T(8,128)(2,1)} %get-tuple-element.65) | copy-start | bytes 786436
  79.3 2.3 %collective-permute-start.9 = (f32[1160,128]{1,0:T(8,128)S(1)}, f32[1160,128]{1,0:T(8,128)S(1)}, u32[]{:S(2)}, u32[]{:S(2)}) collective-permute-start(f32[1160,128]{1,0:T(8,128)S(1)} %maximum_select_fusion.1), channel_id=1, source_target_pairs={{0,1},{1,0},{2,3},{3,2},{4,5},{5,4},{6,7},{7,6},{8,9},{9,8},{10,11... | collective-permute-start | bytes 1781768 | tf_op jit(solution)/shard_map/ppermute | solution.py:305

commit v6 on v5

--- a/solution.py
+++ b/solution.py
@@ -172,9 +172,10 @@
     grad_ref[base + 1 : base + 2, :] = lv1 * norm
 
 
-def out_kernel(first_row, x_hbm, c_hbm, hid_hbm, bf_hbm, k2f, k1b, out_ref, ig_ref,
-               x_ref, c_ref, hid_ref, bf_ref, sems):
-    n, width, ch = out_ref.shape
+def out_kernel(first_row, x_hbm, c_hbm, hid_hbm, bf_hbm, k2f, k1b, outa_hbm, iga_hbm, out_hbm, ig_hbm,
+               x_ref, c_ref, hid_ref, bf_ref, o_ref, g_ref, sems):
+    del outa_hbm, iga_hbm
+    n, width, ch = o_ref.shape
     copies = [
         pltpu.make_async_copy(x_hbm.at[first_row : first_row + n], x_ref.at[2 : n + 2], sems.at[0]),
         pltpu.make_async_copy(c_hbm.at[first_row : first_row + n], c_ref.at[2 : n + 2], sems.at[1]),
@@ -188,7 +189,15 @@
     for cp in copies:
         cp.wait()
     for i in range(n):
-        out_row(i, x_ref, c_ref, hid_ref, bf_ref, k2f, k1b, out_ref, ig_ref)
+        out_row(i, x_ref, c_ref, hid_ref, bf_ref, k2f, k1b, o_ref, g_ref)
+    stores = [
+        pltpu.make_async_copy(o_ref, out_hbm.at[first_row : first_row + n], sems.at[4]),
+        pltpu.make_async_copy(g_ref, ig_hbm.at[first_row : first_row + n], sems.at[5]),
+    ]
+    for cp in stores:
+        cp.start()
+    for cp in stores:
+        cp.wait()
 
 
 def section(norm, packed_rows, level_index, level_table, inputs, cotangent, before_fn, k1, k2):
@@ -242,32 +251,39 @@
             flops=14 * unit, transcendentals=4 * width * ch, bytes_accessed=10 * count * width * ch
         ),
     )(level_index, level_table, inputs, cotangent, before, after, hid, bf, hidt, acc1, acc2, lv, k1f, k2b)
-    step = 2 if count % 2 == 0 else 1
-    chunk = jax.ShapeDtypeStruct((step, width, ch), jnp.bfloat16)
-    outs, igs = [], []
+    step = 1
+    whole = jax.ShapeDtypeStruct((count, width, ch), jnp.bfloat16)
+    out = jnp.zeros((count, width, ch), jnp.bfloat16)
+    ig = jnp.zeros((count, width, ch), jnp.bfloat16)
+    chunks = []
     for first_row in range(0, count, step):
-        o, g = pl.pallas_call(
-            functools.partial(out_kernel, first_row),
-            out_shape=(chunk, chunk),
-            in_specs=[anywhere] * 4 + [spec] * 2,
-            out_specs=(spec, spec),
-            scratch_shapes=[
-                pltpu.VMEM((step + 2, width, ch), jnp.bfloat16),
-                pltpu.VMEM((step + 2, width, ch), jnp.bfloat16),
-                pltpu.VMEM((step + 2, width, ch), jnp.bfloat16),
-                pltpu.VMEM((step + 2, width, ch), jnp.bfloat16),
-                pltpu.SemaphoreType.DMA((4,)),
-            ],
-            compiler_params=params,
-            cost_estimate=pl.CostEstimate(
-                flops=2 * step * unit, transcendentals=0, bytes_accessed=8 * step * width * ch
+        chunks.append(functools.partial(
+            pl.pallas_call(
+                functools.partial(out_kernel, first_row),
+                out_shape=(whole, whole),
+                in_specs=[anywhere] * 4 + [spec] * 2 + [anywhere] * 2,
+                out_specs=(anywhere, anywhere),
+                scratch_shapes=[
+                    pltpu.VMEM((step + 2, width, ch), jnp.bfloat16),
+                    pltpu.VMEM((step + 2, width, ch), jnp.bfloat16),
+                    pltpu.VMEM((step + 2, width, ch), jnp.bfloat16),
+                    pltpu.VMEM((step + 2, width, ch), jnp.bfloat16),
+                    pltpu.VMEM((step, width, ch), jnp.bfloat16),
+                    pltpu.VMEM((step, width, ch), jnp.bfloat16),
+                    pltpu.SemaphoreType.DMA((6,)),
+                ],
+                input_output_aliases={6: 0, 7: 1},
+                compiler_params=params,
+                cost_estimate=pl.CostEstimate(
+                    flops=2 * step * unit, transcendentals=0, bytes_accessed=8 * step * width * ch
+                ),
             ),
-        )(inputs, cotangent, hid, bf, k2f, k1b)
-        outs.append((o, g))
-    return outs, packed
-
-
-def butterfly_sum(block, riders=()):
+            inputs, cotangent, hid, bf, k2f, k1b,
+        ))
+    return (out, ig), chunks, packed
+
+
+def butterfly_sum(block, state, riders=()):
     n = lax.axis_size("rows")
     me = lax.axis_index("rows")
     bits = []
@@ -287,7 +303,6 @@
         return perm, low
 
     riders = list(riders)
-    tied = []
     piece = block
     for k0, k1 in orders:
         perm, low = step_of(k0, k1)
@@ -297,17 +312,17 @@
         send = jnp.where(low, hi, lo)
         got = lax.ppermute(send, "rows", perm)
         if riders:
-            got, rider = lax.optimization_barrier((got, riders.pop(0)))
-            tied.append(rider)
+            got, state = lax.optimization_barrier((got, riders.pop(0)(*state)))
         piece = keep + got
     for k0, k1 in reversed(orders):
         perm, low = step_of(k0, k1)
         got = lax.ppermute(piece, "rows", perm)
         if riders:
-            got, rider = lax.optimization_barrier((got, riders.pop(0)))
-            tied.append(rider)
+            got, state = lax.optimization_barrier((got, riders.pop(0)(*state)))
         piece = jnp.where(low, jnp.concatenate([piece, got]), jnp.concatenate([got, piece]))
-    return piece, tied + riders
+    for rider in riders:
+        state = rider(*state)
+    return piece, state
 
 
 def local(inputs, cotangent, first_kernel, second_kernel, level_table, level_index):
@@ -326,13 +341,11 @@
 
     used = 18 * ch + 2
     packed_rows = used + (-used % size)
-    chunks, packed = section(
+    state, chunks, packed = section(
         norm, packed_rows, level_index, level_table, inputs, cotangent, halo,
         first_kernel, second_kernel,
     )
-    total, chunks = butterfly_sum(packed, chunks)
-    outputs = jnp.concatenate([o for o, _ in chunks])
-    input_grad = jnp.concatenate([g for _, g in chunks])
+    total, (outputs, input_grad) = butterfly_sum(packed, state, chunks)
     first_sum = total[: 9 * ch].reshape(9, ch, ch)
     second_sum = total[9 * ch : 18 * ch].reshape(9, ch, ch)
     level_sum = total[18 * ch : 18 * ch + 2]

time: 84 us -> 86.3 us (1.027)
  Pallas kernels: 40.4 us -> 52.5 us
  waiting for transfers between devices: 15.8 us -> 4.41 us
  other arithmetic: 4.21 us -> 2 us
  local copies, waits for them, and re-layouts: 3.9 us -> 6.07 us
  starting transfers between devices: 17.6 us -> 19.1 us
    ppermute x4, waiting for transfers between devices: 15.3 us -> 3.11 us  [butterfly_sum(): got = lax.ppermute(piece, 'rows', perm)]
    pallas_call x4 -> x8, Pallas kernels: 17.2 us -> 29.3 us  [butterfly_sum(): got, state = lax.optimization_barrier((got, riders.pop(0)(*state)))]
    another operation x0 -> x2, local copies, waits for them, and re-layouts: none -> 2.21 us
    concatenate x2 -> x0, other arithmetic: 2.21 us -> none  [the longest x1 1.1 us: local(): outputs = jnp.concatenate([o for o, _ in chunks])]
    ppermute x4, starting transfers between devices: 4.2 us -> 5.44 us  [butterfly_sum(): got = lax.ppermute(piece, 'rows', perm)]
  transfers between devices with their start and end apart: 10 -> 10, of which waited for: 4 -> 5; matrix products, arithmetic and copies ran while one was open for 3% -> 3% of each run, Pallas kernels for 38% -> 51%
where the time goes in v6:
time: 86.3 us; the launch traced here: 85.6 us
  Pallas kernels  52.5 us (61%)
  starting transfers between devices  19.1 us (22%)
  local copies, waits for them, and re-layouts  6.07 us (7%)
  waiting for transfers between devices  4.41 us (5%)
  other arithmetic  2 us (2%)
  between operations  1.54 us (2%)
    pallas_call x8, Pallas kernels, butterfly_sum(): got, state = lax.optimization_barrier((got, riders.pop(0)(*state)))  29.3 us
    pallas_call x1, Pallas kernels, section(): pl.pallas_call(interior_kernel, out_shape=(frame, frame, frame_t, square,...  14.1 us
    ppermute x4, starting transfers between devices, butterfly_sum(): got = lax.ppermute(send, 'rows', perm)  9.28 us
    pallas_call x1, Pallas kernels, section(): pl.pallas_call(functools.partial(edge_kernel, norm), out_shape=(jax.Shape...  9.08 us
    ppermute x4, starting transfers between devices, butterfly_sum(): got = lax.ppermute(piece, 'rows', perm)  5.44 us
    ppermute x4, waiting for transfers between devices, butterfly_sum(): got = lax.ppermute(piece, 'rows', perm)  3.11 us
    ppermute x1, starting transfers between devices, local(): lax.ppermute(jnp.concatenate([inputs[-2:], cotangent[-2:]]), 'rows', up)  3.06 us
    another operation x2, local copies, waits for them, and re-layouts  2.21 us
  transfers between devices with their start and end apart: 10, of which 5 were waited for; matrix products, arithmetic and copies ran while one was open for 3% of the time, Pallas kernels for 51%

profile of v6, /device:TPU:0, one launch (start us, length us, event | category | flops | bytes accessed | tf_op | source)
XLA Modules:
  0.0 85.6 jit_solution(9749667163816874752)
XLA Ops:
  0.6 1.3 %fusion.1 = (bf16[2,512,128]{2,1,0:T(8,128)(2,1)S(1)}, bf16[2,512,128]{2,1,0:T(8,128)(2,1)S(1)}, bf16[2,512,128]{2,1,0:T(8,128)(2,1)S(1)}, bf16[2,512,128]{2,1,0:T(8,128)(2,1)S(1)}) fusion(bf16[8,512,128]{2,1,0:T(8,128)(2,1)} %x_hbm.19, bf16[8,512,128]{2,1,0:T(8,128)(2,1)} %c_hbm.19), kind=kLoop, calls=%fused_computation.15 | loop fusion | bytes 2097152 | tf_op jit(solution)/shard_map/slice | solution.py:339
  2.0 1.3 %collective-permute-start.1 = (bf16[4,512,128]{2,1,0:T(8,128)(2,1)S(1)}, bf16[4,512,128]{2,1,0:T(8,128)(2,1)S(1)}, u32[]{:S(2)}, u32[]{:S(2)}) collective-permute-start(bf16[4,512,128]{2,1,0:T(8,128)(2,1)S(1)} %pad_maximum_fusion.1), channel_id=1, source_target_pairs={{1,0},{2,1},{3,2},{4,3},{5,4},{6,5},{7,6},{8,7},{9,8},{10,9},{11,1... | collective-permute-start | bytes 1572872 | tf_op jit(solution)/shard_map/ppermute | solution.py:339
  3.3 3.1 %collective-permute-start = (bf16[4,512,128]{2,1,0:T(8,128)(2,1)S(1)}, bf16[4,512,128]{2,1,0:T(8,128)(2,1)S(1)}, u32[]{:S(2)}, u32[]{:S(2)}) collective-permute-start(bf16[4,512,128]{2,1,0:T(8,128)(2,1)S(1)} %pad_maximum_fusion), channel_id=1, source_target_pairs={{0,1},{1,2},{2,3},{3,4},{4,5},{5,6},{6,7},{7,8},{8,9},{9,10},{10,1... | collective-permute-start | bytes 1572872 | tf_op jit(solution)/shard_map/ppermute | solution.py:338
  7.0 14.1 %shard_map.101 = (bf16[10,512,128]{2,1,0:T(8,128)(2,1)}, bf16[10,512,128]{2,1,0:T(8,128)(2,1)}, bf16[10,128,512]{2,1,0:T(8,128)(2,1)}, f32[384,384]{1,0:T(8,128)...) custom-call(s32[1]{0:T(128)S(6)} %copy.43.idx_ref, ...), custom_call_target="tpu_custom_call" | custom-call | flops 3925868544 | bytes 4194304 | tf_op jit(solution)/shard_map/pallas_call | solution.py:217
  21.2 0.8 copy-done.1
  22.0 0.2 copy-done.2
  22.2 9.1 %shard_map.102 = (f32[2320,128]{1,0:T(8,128)}, bf16[10,512,128]{2,1,0:T(8,128)(2,1)}, bf16[10,512,128]{2,1,0:T(8,128)(2,1)}) custom-call(s32[1]{0:T(128)S(6)} %copy.43.idx_ref, f32[16,2,128]{2,1,0:T(2,128)} %lt_ref.3, bf16[8,512,128]{2,1,0:T(8,128)(2,1)} %x_hbm.19, bf16[8,512,128]{2,1,0:T(8,128)(2,1)} %c_hbm.19, bf16[4,512,128]{2,1,0:T(8,128)(2,1)} %copy-done.2, ...), custom_call_target="tpu_custom_call" | custom-call | flops 2113929216 | bytes 5242880 | tf_op jit(solution)/shard_map/pallas_call | solution.py:235
  31.3 1.3 %slice_select_fusion = f32[1160,128]{1,0:T(8,128)S(1)} fusion(f32[2320,128]{1,0:T(8,128)} %get-tuple-element.66, pred[]{:T(512)S(6)} %eq.35), kind=kLoop, calls=%fused_computation.3 | loop fusion | flops 148480 | bytes 1781761 | tf_op jit(solution)/shard_map/jit(_where)/select_n | solution.py:312
  32.6 2.6 %collective-permute-start.2 = (f32[1160,128]{1,0:T(8,128)S(1)}, f32[1160,128]{1,0:T(8,128)S(1)}, u32[]{:S(2)}, u32[]{:S(2)}) collective-permute-start(f32[1160,128]{1,0:T(8,128)S(1)} %slice_select_fusion), channel_id=1, source_target_pairs={{0,1},{1,0},{2,3},{3,2},{4,5},{5,4},{6,7},{7,6},{8,9},{9,8},{10,11... | collective-permute-start | bytes 1781768 | tf_op jit(solution)/shard_map/ppermute | solution.py:313
  35.2 1.1 %broadcast_1_outa_hbm_iga_hbm.2.outa_hbm = bf16[8,512,128]{2,1,0:T(8,128)(2,1)} broadcast(bf16[]{:T(256)} %constant.123.clone.1), dimensions={} | broadcast | bytes 1048578 | tf_op jit(solution)/shard_map/broadcast.1.outa_hbm.iga_hbm
  36.3 1.1 %broadcast_1_outa_hbm_iga_hbm.2.clone.iga_hbm = bf16[8,512,128]{2,1,0:T(8,128)(2,1)} broadcast(bf16[]{:T(256)} %constant.123.clone.1), dimensions={} | broadcast | bytes 1048578 | tf_op jit(solution)/shard_map/broadcast.1.outa_hbm.iga_hbm
  37.4 3.7 %shard_map.103 = (bf16[8,512,128]{2,1,0:T(8,128)(2,1)}, bf16[8,512,128]{2,1,0:T(8,128)(2,1)}) custom-call(bf16[8,512,128]{2,1,0:T(8,128)(2,1)} %x_hbm.19, bf16[8,512,128]{2,1,0:T(8,128)(2,1)} %c_hbm.19, bf16[10,512,128]{2,1,0:T(8,128)(2,1)} %get-tuple-element.67.hid_hbm, ...), custom_call_target="tpu_custom_call", output_to_operand_aliasing={{0}: (6, {}), {1}: (7, {})} | custom-call | flops 301989888 | bytes 524288 | tf_op jit(solution)/shard_map/pallas_call | solution.py:315
  41.4 2.4 %collective-permute-start.3 = (f32[580,128]{1,0:T(8,128)S(1)}, f32[580,128]{1,0:T(8,128)S(1)}, u32[]{:S(2)}, u32[]{:S(2)}) collective-permute-start(f32[580,128]{1,0:T(8,128)S(1)} %slice_select_fusion.1), channel_id=1, source_target_pairs={{0,2},{1,5},{2,0},{3,7},{4,6},{5,1},{6,4},{7,3},{8,10},{9,13},{10,... | collective-permute-start | bytes 890888 | tf_op jit(solution)/shard_map/ppermute | solution.py:313
  43.8 3.6 %shard_map.104 = (bf16[8,512,128]{2,1,0:T(8,128)(2,1)}, bf16[8,512,128]{2,1,0:T(8,128)(2,1)}) custom-call(bf16[8,512,128]{2,1,0:T(8,128)(2,1)} %x_hbm.19, bf16[8,512,128]{2,1,0:T(8,128)(2,1)} %c_hbm.19, bf16[10,512,128]{2,1,0:T(8,128)(2,1)} %get-tuple-element.67.hid_hbm, ...), custom_call_target="tpu_custom_call", output_to_operand_aliasing={{0}: (6, {}), {1}: (7, {})} | custom-call | flops 301989888 | bytes 524288 | tf_op jit(solution)/shard_map/pallas_call | solution.py:315
  47.4 1.1 %collective-permute-done.3 = f32[580,128]{1,0:T(8,128)S(1)} collective-permute-done((f32[580,128]{1,0:T(8,128)S(1)}, f32[580,128]{1,0:T(8,128)S(1)}, u32[]{:S(2)}, u32[]{:S(2)}) %collective-permute-start.3) | collective-permute-done | bytes 296992 | tf_op jit(solution)/shard_map/ppermute | solution.py:313
  48.6 1.6 %collective-permute-start.4 = (f32[290,128]{1,0:T(8,128)S(1)}, f32[290,128]{1,0:T(8,128)S(1)}, u32[]{:S(2)}, u32[]{:S(2)}) collective-permute-start(f32[290,128]{1,0:T(8,128)S(1)} %slice_select_fusion.2), channel_id=1, source_target_pairs={{0,4},{1,3},{2,6},{3,1},{4,0},{5,7},{6,2},{7,5},{8,12},{9,11},{10,... | collective-permute-start | bytes 445448 | tf_op jit(solution)/shard_map/ppermute | solution.py:313
  50.3 3.6 %shard_map.105 = (bf16[8,512,128]{2,1,0:T(8,128)(2,1)}, bf16[8,512,128]{2,1,0:T(8,128)(2,1)}) custom-call(bf16[8,512,128]{2,1,0:T(8,128)(2,1)} %x_hbm.19, bf16[8,512,128]{2,1,0:T(8,128)(2,1)} %c_hbm.19, bf16[10,512,128]{2,1,0:T(8,128)(2,1)} %get-tuple-element.67.hid_hbm, ...), custom_call_target="tpu_custom_call", output_to_operand_aliasing={{0}: (6, {}), {1}: (7, {})} | custom-call | flops 301989888 | bytes 524288 | tf_op jit(solution)/shard_map/pallas_call | solution.py:315
  54.0 2.6 %collective-permute-start.5 = (f32[145,128]{1,0:T(8,128)S(1)}, f32[145,128]{1,0:T(8,128)S(1)}, u32[]{:S(2)}, u32[]{:S(2)}) collective-permute-start(f32[145,128]{1,0:T(8,128)S(1)} %slice_select_fusion.3), channel_id=1, source_target_pairs={{0,8},{1,9},{2,10},{3,11},{4,12},{5,13},{6,14},{7,15},{8,0},{9,1},... | collective-permute-start | bytes 222728 | tf_op jit(solution)/shard_map/ppermute | solution.py:313
  56.6 3.6 %shard_map.106 = (bf16[8,512,128]{2,1,0:T(8,128)(2,1)}, bf16[8,512,128]{2,1,0:T(8,128)(2,1)}) custom-call(bf16[8,512,128]{2,1,0:T(8,128)(2,1)} %x_hbm.19, bf16[8,512,128]{2,1,0:T(8,128)(2,1)} %c_hbm.19, bf16[10,512,128]{2,1,0:T(8,128)(2,1)} %get-tuple-element.67.hid_hbm, ...), custom_call_target="tpu_custom_call", output_to_operand_aliasing={{0}: (6, {}), {1}: (7, {})} | custom-call | flops 301989888 | bytes 524288 | tf_op jit(solution)/shard_map/pallas_call | solution.py:315
  60.2 0.2 collective-permute-done.5
  60.5 1.6 %collective-permute-start.6 = (f32[145,128]{1,0:T(8,128)S(1)}, f32[145,128]{1,0:T(8,128)S(1)}, u32[]{:S(2)}, u32[]{:S(2)}) collective-permute-start(f32[145,128]{1,0:T(8,128)S(1)} %select_add_fusion.3), channel_id=1, source_target_pairs={{0,8},{1,9},{2,10},{3,11},{4,12},{5,13},{6,14},{7,15},{8,0},{9,1},... | collective-permute-start | bytes 222728 | tf_op jit(solution)/shard_map/ppermute | solution.py:319
  62.1 3.6 %shard_map.107 = (bf16[8,512,128]{2,1,0:T(8,128)(2,1)}, bf16[8,512,128]{2,1,0:T(8,128)(2,1)}) custom-call(bf16[8,512,128]{2,1,0:T(8,128)(2,1)} %x_hbm.19, bf16[8,512,128]{2,1,0:T(8,128)(2,1)} %c_hbm.19, bf16[10,512,128]{2,1,0:T(8,128)(2,1)} %get-tuple-element.67.hid_hbm, ...), custom_call_target="tpu_custom_call", output_to_operand_aliasing={{0}: (6, {}), {1}: (7, {})} | custom-call | flops 301989888 | bytes 524288 | tf_op jit(solution)/shard_map/pallas_call | solution.py:321
  65.7 0.9 %collective-permute-done.6 = f32[145,128]{1,0:T(8,128)S(1)} collective-permute-done((f32[145,128]{1,0:T(8,128)S(1)}, f32[145,128]{1,0:T(8,128)S(1)}, u32[]{:S(2)}, u32[]{:S(2)}) %collective-permute-start.6) | collective-permute-done | bytes 74272 | tf_op jit(solution)/shard_map/ppermute | solution.py:319
  66.7 1.1 %collective-permute-start.7 = (f32[290,128]{1,0:T(8,128)S(1)}, f32[290,128]{1,0:T(8,128)S(1)}, u32[]{:S(2)}, u32[]{:S(2)}) collective-permute-start(f32[290,128]{1,0:T(8,128)S(1)} %maximum_select_fusion.3), channel_id=1, source_target_pairs={{0,4},{1,3},{2,6},{3,1},{4,0},{5,7},{6,2},{7,5},{8,12},{9,11},{10,... | collective-permute-start | bytes 445448 | tf_op jit(solution)/shard_map/ppermute | solution.py:319
  67.8 3.6 %shard_map.108 = (bf16[8,512,128]{2,1,0:T(8,128)(2,1)}, bf16[8,512,128]{2,1,0:T(8,128)(2,1)}) custom-call(bf16[8,512,128]{2,1,0:T(8,128)(2,1)} %x_hbm.19, bf16[8,512,128]{2,1,0:T(8,128)(2,1)} %c_hbm.19, bf16[10,512,128]{2,1,0:T(8,128)(2,1)} %get-tuple-element.67.hid_hbm, ...), custom_call_target="tpu_custom_call", output_to_operand_aliasing={{0}: (6, {}), {1}: (7, {})} | custom-call | flops 301989888 | bytes 524288 | tf_op jit(solution)/shard_map/pallas_call | solution.py:321
  71.5 1.1 %collective-permute-done.7 = f32[290,128]{1,0:T(8,128)S(1)} collective-permute-done((f32[290,128]{1,0:T(8,128)S(1)}, f32[290,128]{1,0:T(8,128)S(1)}, u32[]{:S(2)}, u32[]{:S(2)}) %collective-permute-start.7) | collective-permute-done | bytes 148512 | tf_op jit(solution)/shard_map/ppermute | solution.py:319
  72.6 2.6 %collective-permute-start.8 = (f32[580,128]{1,0:T(8,128)S(1)}, f32[580,128]{1,0:T(8,128)S(1)}, u32[]{:S(2)}, u32[]{:S(2)}) collective-permute-start(f32[580,128]{1,0:T(8,128)S(1)} %maximum_select_fusion.2), channel_id=1, source_target_pairs={{0,2},{1,5},{2,0},{3,7},{4,6},{5,1},{6,4},{7,3},{8,10},{9,13},{10,... | collective-permute-start | bytes 890888 | tf_op jit(solution)/shard_map/ppermute | solution.py:319
  75.2 3.6 %shard_map.109 = (bf16[8,512,128]{2,1,0:T(8,128)(2,1)}, bf16[8,512,128]{2,1,0:T(8,128)(2,1)}) custom-call(bf16[8,512,128]{2,1,0:T(8,128)(2,1)} %x_hbm.19, bf16[8,512,128]{2,1,0:T(8,128)(2,1)} %c_hbm.19, bf16[10,512,128]{2,1,0:T(8,128)(2,1)} %get-tuple-element.67.hid_hbm, ...), custom_call_target="tpu_custom_call", output_to_operand_aliasing={{0}: (6, {}), {1}: (7, {})} | custom-call | flops 301989888 | bytes 524288 | tf_op jit(solution)/shard_map/pallas_call | solution.py:321
  78.9 1.1 %collective-permute-done.8 = f32[580,128]{1,0:T(8,128)S(1)} collective-permute-done((f32[580,128]{1,0:T(8,128)S(1)}, f32[580,128]{1,0:T(8,128)S(1)}, u32[]{:S(2)}, u32[]{:S(2)}) %collective-permute-start.8) | collective-permute-done | bytes 296992 | tf_op jit(solution)/shard_map/ppermute | solution.py:319
  80.1 3.7 %shard_map.110 = (bf16[8,512,128]{2,1,0:T(8,128)(2,1)}, bf16[8,512,128]{2,1,0:T(8,128)(2,1)}) custom-call(bf16[8,512,128]{2,1,0:T(8,128)(2,1)} %x_hbm.19, bf16[8,512,128]{2,1,0:T(8,128)(2,1)} %c_hbm.19, bf16[10,512,128]{2,1,0:T(8,128)(2,1)} %get-tuple-element.67.hid_hbm, ...), custom_call_target="tpu_custom_call", output_to_operand_aliasing={{0}: (6, {}), {1}: (7, {})} | custom-call | flops 301989888 | bytes 524288 | tf_op jit(solution)/shard_map/pallas_call | solution.py:321
  84.0 1.1 %fusion = (f32[1152,128]{1,0:T(8,128)}, f32[1152,128]{1,0:T(8,128)}) fusion(f32[2320,128]{1,0:T(8,128)S(1)} %maximum_select_fusion), kind=kLoop, calls=%fused_computation.14 | loop fusion | bytes 2359296 | tf_op jit(solution)/shard_map/slice | solution.py:350
  85.0 0.6 slice.68
  (23 shorter events, 0.8 us)
Async XLA Ops:
  2.0 19.2 %collective-permute-start.1 = (bf16[4,512,128]{2,1,0:T(8,128)(2,1)S(1)}, bf16[4,512,128]{2,1,0:T(8,128)(2,1)S(1)}, u32[]{:S(2)}, u32[]{:S(2)}) collective-permute-start(bf16[4,512,128]{2,1,0:T(8,128)(2,1)S(1)} %pad_maximum_fusion.1), channel_id=1, source_target_pairs={{1,0},{2,1},{3,2},{4,3},{5,4},{6,5},{7,6},{8,7},{9,8},{10,9},{11,1... | collective-permute-start | bytes 1572872 | tf_op jit(solution)/shard_map/ppermute | solution.py:339
  3.3 17.9 %collective-permute-start = (bf16[4,512,128]{2,1,0:T(8,128)(2,1)S(1)}, bf16[4,512,128]{2,1,0:T(8,128)(2,1)S(1)}, u32[]{:S(2)}, u32[]{:S(2)}) collective-permute-start(bf16[4,512,128]{2,1,0:T(8,128)(2,1)S(1)} %pad_maximum_fusion), channel_id=1, source_target_pairs={{0,1},{1,2},{2,3},{3,4},{4,5},{5,6},{6,7},{7,8},{8,9},{9,10},{10,1... | collective-permute-start | bytes 1572872 | tf_op jit(solution)/shard_map/ppermute | solution.py:338
  21.2 0.8 copy-start.1
  21.2 0.9 %copy-start.2 = (bf16[4,512,128]{2,1,0:T(8,128)(2,1)}, bf16[4,512,128]{2,1,0:T(8,128)(2,1)S(1)}, u32[]{:S(2)}) copy-start(bf16[4,512,128]{2,1,0:T(8,128)(2,1)S(1)} %collective-permute-done.before_hbm) | copy-start | bytes 1572868
  32.6 8.6 %collective-permute-start.2 = (f32[1160,128]{1,0:T(8,128)S(1)}, f32[1160,128]{1,0:T(8,128)S(1)}, u32[]{:S(2)}, u32[]{:S(2)}) collective-permute-start(f32[1160,128]{1,0:T(8,128)S(1)} %slice_select_fusion), channel_id=1, source_target_pairs={{0,1},{1,0},{2,3},{3,2},{4,5},{5,4},{6,7},{7,6},{8,9},{9,8},{10,11... | collective-permute-start | bytes 1781768 | tf_op jit(solution)/shard_map/ppermute | solution.py:313
  37.4 3.8 %copy-start = (f32[2320,128]{1,0:T(8,128)S(1)}, f32[2320,128]{1,0:T(8,128)}, u32[]{:S(2)}) copy-start(f32[2320,128]{1,0:T(8,128)} %get-tuple-element.66) | copy-start | bytes 3563524
  41.4 7.2 %collective-permute-start.3 = (f32[580,128]{1,0:T(8,128)S(1)}, f32[580,128]{1,0:T(8,128)S(1)}, u32[]{:S(2)}, u32[]{:S(2)}) collective-permute-start(f32[580,128]{1,0:T(8,128)S(1)} %slice_select_fusion.1), channel_id=1, source_target_pairs={{0,2},{1,5},{2,0},{3,7},{4,6},{5,1},{6,4},{7,3},{8,10},{9,13},{10,... | collective-permute-start | bytes 890888 | tf_op jit(solution)/shard_map/ppermute | solution.py:313
  48.6 5.3 %collective-permute-start.4 = (f32[290,128]{1,0:T(8,128)S(1)}, f32[290,128]{1,0:T(8,128)S(1)}, u32[]{:S(2)}, u32[]{:S(2)}) collective-permute-start(f32[290,128]{1,0:T(8,128)S(1)} %slice_select_fusion.2), channel_id=1, source_target_pairs={{0,4},{1,3},{2,6},{3,1},{4,0},{5,7},{6,2},{7,5},{8,12},{9,11},{10,... | collective-permute-start | bytes 445448 | tf_op jit(solution)/shard_map/ppermute | solution.py:313
  54.0 6.5 %collective-permute-start.5 = (f32[145,128]{1,0:T(8,128)S(1)}, f32[145,128]{1,0:T(8,128)S(1)}, u32[]{:S(2)}, u32[]{:S(2)}) collective-permute-start(f32[145,128]{1,0:T(8,128)S(1)} %slice_select_fusion.3), channel_id=1, source_target_pairs={{0,8},{1,9},{2,10},{3,11},{4,12},{5,13},{6,14},{7,15},{8,0},{9,1},... | collective-permute-start | bytes 222728 | tf_op jit(solution)/shard_map/ppermute | solution.py:313
  60.5 6.2 %collective-permute-start.6 = (f32[145,128]{1,0:T(8,128)S(1)}, f32[145,128]{1,0:T(8,128)S(1)}, u32[]{:S(2)}, u32[]{:S(2)}) collective-permute-start(f32[145,128]{1,0:T(8,128)S(1)} %select_add_fusion.3), channel_id=1, source_target_pairs={{0,8},{1,9},{2,10},{3,11},{4,12},{5,13},{6,14},{7,15},{8,0},{9,1},... | collective-permute-start | bytes 222728 | tf_op jit(solution)/shard_map/ppermute | solution.py:319
  66.7 5.9 %collective-permute-start.7 = (f32[290,128]{1,0:T(8,128)S(1)}, f32[290,128]{1,0:T(8,128)S(1)}, u32[]{:S(2)}, u32[]{:S(2)}) collective-permute-start(f32[290,128]{1,0:T(8,128)S(1)} %maximum_select_fusion.3), channel_id=1, source_target_pairs={{0,4},{1,3},{2,6},{3,1},{4,0},{5,7},{6,2},{7,5},{8,12},{9,11},{10,... | collective-permute-start | bytes 445448 | tf_op jit(solution)/shard_map/ppermute | solution.py:319
  72.6 7.4 %collective-permute-start.8 = (f32[580,128]{1,0:T(8,128)S(1)}, f32[580,128]{1,0:T(8,128)S(1)}, u32[]{:S(2)}, u32[]{:S(2)}) collective-permute-start(f32[580,128]{1,0:T(8,128)S(1)} %maximum_select_fusion.2), channel_id=1, source_target_pairs={{0,2},{1,5},{2,0},{3,7},{4,6},{5,1},{6,4},{7,3},{8,10},{9,13},{10,... | collective-permute-start | bytes 890888 | tf_op jit(solution)/shard_map/ppermute | solution.py:319
  80.1 3.7 %collective-permute-start.9 = (f32[1160,128]{1,0:T(8,128)S(1)}, f32[1160,128]{1,0:T(8,128)S(1)}, u32[]{:S(2)}, u32[]{:S(2)}) collective-permute-start(f32[1160,128]{1,0:T(8,128)S(1)} %maximum_select_fusion.1), channel_id=1, source_target_pairs={{0,1},{1,0},{2,3},{3,2},{4,5},{5,4},{6,7},{7,6},{8,9},{9,8},{10,11... | collective-permute-start | bytes 1781768 | tf_op jit(solution)/shard_map/ppermute | solution.py:319

commit v7 on v6

--- a/solution.py
+++ b/solution.py
@@ -172,9 +172,10 @@
     grad_ref[base + 1 : base + 2, :] = lv1 * norm
 
 
-def out_kernel(first_row, x_hbm, c_hbm, hid_hbm, bf_hbm, k2f, k1b, outa_hbm, iga_hbm, out_hbm, ig_hbm,
-               x_ref, c_ref, hid_ref, bf_ref, o_ref, g_ref, sems):
-    del outa_hbm, iga_hbm
+def out_kernel(first_row, aliased, x_hbm, c_hbm, hid_hbm, bf_hbm, k2f, k1b, *refs):
+    if aliased:
+        refs = refs[2:]
+    out_hbm, ig_hbm, x_ref, c_ref, hid_ref, bf_ref, o_ref, g_ref, sems = refs
     n, width, ch = o_ref.shape
     copies = [
         pltpu.make_async_copy(x_hbm.at[first_row : first_row + n], x_ref.at[2 : n + 2], sems.at[0]),
@@ -251,17 +252,16 @@
             flops=14 * unit, transcendentals=4 * width * ch, bytes_accessed=10 * count * width * ch
         ),
     )(level_index, level_table, inputs, cotangent, before, after, hid, bf, hidt, acc1, acc2, lv, k1f, k2b)
-    step = 1
+    step = count // 2 if count % 2 == 0 else count
     whole = jax.ShapeDtypeStruct((count, width, ch), jnp.bfloat16)
-    out = jnp.zeros((count, width, ch), jnp.bfloat16)
-    ig = jnp.zeros((count, width, ch), jnp.bfloat16)
     chunks = []
     for first_row in range(0, count, step):
+        aliased = first_row > 0
         chunks.append(functools.partial(
             pl.pallas_call(
-                functools.partial(out_kernel, first_row),
+                functools.partial(out_kernel, first_row, aliased),
                 out_shape=(whole, whole),
-                in_specs=[anywhere] * 4 + [spec] * 2 + [anywhere] * 2,
+                in_specs=[anywhere] * 4 + [spec] * 2 + [anywhere] * (2 if aliased else 0),
                 out_specs=(anywhere, anywhere),
                 scratch_shapes=[
                     pltpu.VMEM((step + 2, width, ch), jnp.bfloat16),
@@ -272,7 +272,7 @@
                     pltpu.VMEM((step, width, ch), jnp.bfloat16),
                     pltpu.SemaphoreType.DMA((6,)),
                 ],
-                input_output_aliases={6: 0, 7: 1},
+                input_output_aliases={6: 0, 7: 1} if aliased else {},
                 compiler_params=params,
                 cost_estimate=pl.CostEstimate(
                     flops=2 * step * unit, transcendentals=0, bytes_accessed=8 * step * width * ch
@@ -280,10 +280,10 @@
             ),
             inputs, cotangent, hid, bf, k2f, k1b,
         ))
-    return (out, ig), chunks, packed
-
-
-def butterfly_sum(block, state, riders=()):
+    return chunks, packed
+
+
+def butterfly_sum(block, riders):
     n = lax.axis_size("rows")
     me = lax.axis_index("rows")
     bits = []
@@ -302,7 +302,8 @@
         low = jnp.where(even, (me // k0) % 2, (me // k1) % 2) == 0
         return perm, low
 
-    riders = list(riders)
+    state = ()
+    count = 0
     piece = block
     for k0, k1 in orders:
         perm, low = step_of(k0, k1)
@@ -311,17 +312,17 @@
         keep = jnp.where(low, lo, hi)
         send = jnp.where(low, hi, lo)
         got = lax.ppermute(send, "rows", perm)
-        if riders:
-            got, state = lax.optimization_barrier((got, riders.pop(0)(*state)))
+        if count in riders:
+            got, state = lax.optimization_barrier((got, riders[count](*state)))
+        count += 1
         piece = keep + got
     for k0, k1 in reversed(orders):
         perm, low = step_of(k0, k1)
         got = lax.ppermute(piece, "rows", perm)
-        if riders:
-            got, state = lax.optimization_barrier((got, riders.pop(0)(*state)))
+        if count in riders:
+            got, state = lax.optimization_barrier((got, riders[count](*state)))
+        count += 1
         piece = jnp.where(low, jnp.concatenate([piece, got]), jnp.concatenate([got, piece]))
-    for rider in riders:
-        state = rider(*state)
     return piece, state
 
 
@@ -341,11 +342,13 @@
 
     used = 18 * ch + 2
     packed_rows = used + (-used % size)
-    state, chunks, packed = section(
+    chunks, packed = section(
         norm, packed_rows, level_index, level_table, inputs, cotangent, halo,
         first_kernel, second_kernel,
     )
-    total, (outputs, input_grad) = butterfly_sum(packed, state, chunks)
+    steps = 2 * (size.bit_length() - 1)
+    places = [1, steps - 2] if len(chunks) == 2 and steps >= 4 else list(range(len(chunks)))
+    total, (outputs, input_grad) = butterfly_sum(packed, dict(zip(places, chunks)))
     first_sum = total[: 9 * ch].reshape(9, ch, ch)
     second_sum = total[9 * ch : 18 * ch].reshape(9, ch, ch)
     level_sum = total[18 * ch : 18 * ch + 2]

time: 86.3 us -> 80.6 us (0.934)
  Pallas kernels: 52.5 us -> 34.6 us
  waiting for transfers between devices: 4.41 us -> 16.3 us
  starting transfers between devices: 19.1 us -> 21.9 us
  local copies, waits for them, and re-layouts: 6.07 us -> 3.86 us
    pallas_call x8 -> x2, Pallas kernels: 29.3 us -> 11.3 us  [butterfly_sum(): got, state = lax.optimization_barrier((got, riders[count](*state)))]
    ppermute x4, waiting for transfers between devices: 1.3 us -> 7.95 us  [butterfly_sum(): got = lax.ppermute(send, 'rows', perm)]
    ppermute x4, waiting for transfers between devices: 3.11 us -> 8.31 us  [butterfly_sum(): got = lax.ppermute(piece, 'rows', perm)]
    ppermute x4, starting transfers between devices: 5.44 us -> 8.2 us  [butterfly_sum(): got = lax.ppermute(piece, 'rows', perm)]
    another operation x2 -> x0, local copies, waits for them, and re-layouts: 2.21 us -> none
  transfers between devices with their start and end apart: 10 -> 10, of which waited for: 5 -> 6; matrix products, arithmetic and copies ran while one was open for 3% -> 0% of each run, Pallas kernels for 51% -> 32%
where the time goes in v7:
time: 80.6 us; the launch traced here: 80.2 us
  Pallas kernels  34.6 us (43%)
  starting transfers between devices  21.9 us (27%)
  waiting for transfers between devices  16.3 us (20%)
  local copies, waits for them, and re-layouts  3.86 us (5%)
  other arithmetic  2.09 us (3%)
  between operations  1.48 us (2%)
    pallas_call x1, Pallas kernels, section(): pl.pallas_call(interior_kernel, out_shape=(frame, frame, frame_t, square,...  14.2 us
    pallas_call x2, Pallas kernels, butterfly_sum(): got, state = lax.optimization_barrier((got, riders[count](*state)))  11.3 us
    ppermute x4, starting transfers between devices, butterfly_sum(): got = lax.ppermute(send, 'rows', perm)  9.34 us
    pallas_call x1, Pallas kernels, section(): pl.pallas_call(functools.partial(edge_kernel, norm), out_shape=(jax.Shape...  9.09 us
    ppermute x4, waiting for transfers between devices, butterfly_sum(): got = lax.ppermute(piece, 'rows', perm)  8.31 us
    ppermute x4, starting transfers between devices, butterfly_sum(): got = lax.ppermute(piece, 'rows', perm)  8.2 us
    ppermute x4, waiting for transfers between devices, butterfly_sum(): got = lax.ppermute(send, 'rows', perm)  7.95 us
    ppermute x1, starting transfers between devices, local(): lax.ppermute(jnp.concatenate([inputs[-2:], cotangent[-2:]]), 'rows', up)  3.06 us
  transfers between devices with their start and end apart: 10, of which 6 were waited for; matrix products, arithmetic and copies ran while one was open for 0% of the time, Pallas kernels for 32%

profile of v7, /device:TPU:0, one launch (start us, length us, event | category | flops | bytes accessed | tf_op | source)
XLA Modules:
  0.0 80.2 jit_solution(4255247772058060849)
XLA Ops:
  0.6 1.3 %fusion.1 = (bf16[2,512,128]{2,1,0:T(8,128)(2,1)S(1)}, bf16[2,512,128]{2,1,0:T(8,128)(2,1)S(1)}, bf16[2,512,128]{2,1,0:T(8,128)(2,1)S(1)}, bf16[2,512,128]{2,1,0:T(8,128)(2,1)S(1)}) fusion(bf16[8,512,128]{2,1,0:T(8,128)(2,1)} %x_hbm.7, bf16[8,512,128]{2,1,0:T(8,128)(2,1)} %c_hbm.7), kind=kLoop, calls=%fused_computation.15 | loop fusion | bytes 2097152 | tf_op jit(solution)/shard_map/slice | solution.py:340
  2.0 1.3 %collective-permute-start.1 = (bf16[4,512,128]{2,1,0:T(8,128)(2,1)S(1)}, bf16[4,512,128]{2,1,0:T(8,128)(2,1)S(1)}, u32[]{:S(2)}, u32[]{:S(2)}) collective-permute-start(bf16[4,512,128]{2,1,0:T(8,128)(2,1)S(1)} %pad_maximum_fusion.1), channel_id=1, source_target_pairs={{1,0},{2,1},{3,2},{4,3},{5,4},{6,5},{7,6},{8,7},{9,8},{10,9},{11,1... | collective-permute-start | bytes 1572872 | tf_op jit(solution)/shard_map/ppermute | solution.py:340
  3.3 3.1 %collective-permute-start = (bf16[4,512,128]{2,1,0:T(8,128)(2,1)S(1)}, bf16[4,512,128]{2,1,0:T(8,128)(2,1)S(1)}, u32[]{:S(2)}, u32[]{:S(2)}) collective-permute-start(bf16[4,512,128]{2,1,0:T(8,128)(2,1)S(1)} %pad_maximum_fusion), channel_id=1, source_target_pairs={{0,1},{1,2},{2,3},{3,4},{4,5},{5,6},{6,7},{7,8},{8,9},{9,10},{10,1... | collective-permute-start | bytes 1572872 | tf_op jit(solution)/shard_map/ppermute | solution.py:339
  7.0 14.2 %shard_map.101 = (bf16[10,512,128]{2,1,0:T(8,128)(2,1)}, bf16[10,512,128]{2,1,0:T(8,128)(2,1)}, bf16[10,128,512]{2,1,0:T(8,128)(2,1)}, f32[384,384]{1,0:T(8,128)...) custom-call(s32[1]{0:T(128)S(6)} %copy.15.idx_ref, ...), custom_call_target="tpu_custom_call" | custom-call | flops 3925868544 | bytes 4194304 | tf_op jit(solution)/shard_map/pallas_call | solution.py:218
  21.2 0.0 copy-start.1
  21.3 0.0 copy-start.2
  21.3 0.8 copy-done.1
  22.0 0.2 copy-done.2
  22.2 9.1 %shard_map.102 = (f32[2320,128]{1,0:T(8,128)}, bf16[10,512,128]{2,1,0:T(8,128)(2,1)}, bf16[10,512,128]{2,1,0:T(8,128)(2,1)}) custom-call(s32[1]{0:T(128)S(6)} %copy.15.idx_ref, f32[16,2,128]{2,1,0:T(2,128)} %lt_ref.3, bf16[8,512,128]{2,1,0:T(8,128)(2,1)} %x_hbm.7, bf16[8,512,128]{2,1,0:T(8,128)(2,1)} %c_hbm.7, bf16[4,512,128]{2,1,0:T(8,128)(2,1)} %copy-done.2, ...), custom_call_target="tpu_custom_call" | custom-call | flops 2113929216 | bytes 5242880 | tf_op jit(solution)/shard_map/pallas_call | solution.py:236
  31.3 1.4 %slice_select_fusion = f32[1160,128]{1,0:T(8,128)S(1)} fusion(f32[2320,128]{1,0:T(8,128)} %get-tuple-element.36, pred[]{:T(512)S(6)} %eq.35), kind=kLoop, calls=%fused_computation.3 | loop fusion | flops 148480 | bytes 1781761 | tf_op jit(solution)/shard_map/jit(_where)/select_n | solution.py:313
  32.7 2.6 %collective-permute-start.2 = (f32[1160,128]{1,0:T(8,128)S(1)}, f32[1160,128]{1,0:T(8,128)S(1)}, u32[]{:S(2)}, u32[]{:S(2)}) collective-permute-start(f32[1160,128]{1,0:T(8,128)S(1)} %slice_select_fusion), channel_id=1, source_target_pairs={{0,1},{1,0},{2,3},{3,2},{4,5},{5,4},{6,7},{7,6},{8,9},{9,8},{10,11... | collective-permute-start | bytes 1781768 | tf_op jit(solution)/shard_map/ppermute | solution.py:314
  35.3 1.6 %collective-permute-done.2 = f32[1160,128]{1,0:T(8,128)S(1)} collective-permute-done((f32[1160,128]{1,0:T(8,128)S(1)}, f32[1160,128]{1,0:T(8,128)S(1)}, u32[]{:S(2)}, u32[]{:S(2)}) %collective-permute-start.2) | collective-permute-done | bytes 593952 | tf_op jit(solution)/shard_map/ppermute | solution.py:314
  37.0 0.1 select_add_fusion
  37.1 2.4 %collective-permute-start.3 = (f32[580,128]{1,0:T(8,128)S(1)}, f32[580,128]{1,0:T(8,128)S(1)}, u32[]{:S(2)}, u32[]{:S(2)}) collective-permute-start(f32[580,128]{1,0:T(8,128)S(1)} %slice_select_fusion.1), channel_id=1, source_target_pairs={{0,2},{1,5},{2,0},{3,7},{4,6},{5,1},{6,4},{7,3},{8,10},{9,13},{10,... | collective-permute-start | bytes 890888 | tf_op jit(solution)/shard_map/ppermute | solution.py:314
  39.6 5.7 %shard_map.103 = (bf16[8,512,128]{2,1,0:T(8,128)(2,1)}, bf16[8,512,128]{2,1,0:T(8,128)(2,1)}) custom-call(bf16[8,512,128]{2,1,0:T(8,128)(2,1)} %x_hbm.7, bf16[8,512,128]{2,1,0:T(8,128)(2,1)} %c_hbm.7, bf16[10,512,128]{2,1,0:T(8,128)(2,1)} %get-tuple-element.37.hid_hbm, bf16[10,512,128]{2,1,0:T(8,128)(2,1)} %get-tuple-element.38.bf_hbm, ...), custom_call_target="tpu_custom_call" | custom-call | flops 1207959552 | bytes 2097152 | tf_op jit(solution)/shard_map/pallas_call | solution.py:316
  45.2 0.1 select_add_fusion.1
  45.3 1.6 %collective-permute-start.4 = (f32[290,128]{1,0:T(8,128)S(1)}, f32[290,128]{1,0:T(8,128)S(1)}, u32[]{:S(2)}, u32[]{:S(2)}) collective-permute-start(f32[290,128]{1,0:T(8,128)S(1)} %slice_select_fusion.2), channel_id=1, source_target_pairs={{0,4},{1,3},{2,6},{3,1},{4,0},{5,7},{6,2},{7,5},{8,12},{9,11},{10,... | collective-permute-start | bytes 445448 | tf_op jit(solution)/shard_map/ppermute | solution.py:314
  47.0 3.6 %collective-permute-done.4 = f32[290,128]{1,0:T(8,128)S(1)} collective-permute-done((f32[290,128]{1,0:T(8,128)S(1)}, f32[290,128]{1,0:T(8,128)S(1)}, u32[]{:S(2)}, u32[]{:S(2)}) %collective-permute-start.4) | collective-permute-done | bytes 148512 | tf_op jit(solution)/shard_map/ppermute | solution.py:314
  50.6 2.7 %collective-permute-start.5 = (f32[145,128]{1,0:T(8,128)S(1)}, f32[145,128]{1,0:T(8,128)S(1)}, u32[]{:S(2)}, u32[]{:S(2)}) collective-permute-start(f32[145,128]{1,0:T(8,128)S(1)} %slice_select_fusion.3), channel_id=1, source_target_pairs={{0,8},{1,9},{2,10},{3,11},{4,12},{5,13},{6,14},{7,15},{8,0},{9,1},... | collective-permute-start | bytes 222728 | tf_op jit(solution)/shard_map/ppermute | solution.py:314
  53.3 2.7 %collective-permute-done.5 = f32[145,128]{1,0:T(8,128)S(1)} collective-permute-done((f32[145,128]{1,0:T(8,128)S(1)}, f32[145,128]{1,0:T(8,128)S(1)}, u32[]{:S(2)}, u32[]{:S(2)}) %collective-permute-start.5) | collective-permute-done | bytes 74272 | tf_op jit(solution)/shard_map/ppermute | solution.py:314
  56.0 2.7 %collective-permute-start.6 = (f32[145,128]{1,0:T(8,128)S(1)}, f32[145,128]{1,0:T(8,128)S(1)}, u32[]{:S(2)}, u32[]{:S(2)}) collective-permute-start(f32[145,128]{1,0:T(8,128)S(1)} %select_add_fusion.3), channel_id=1, source_target_pairs={{0,8},{1,9},{2,10},{3,11},{4,12},{5,13},{6,14},{7,15},{8,0},{9,1},... | collective-permute-start | bytes 222728 | tf_op jit(solution)/shard_map/ppermute | solution.py:321
  58.7 2.7 %collective-permute-done.6 = f32[145,128]{1,0:T(8,128)S(1)} collective-permute-done((f32[145,128]{1,0:T(8,128)S(1)}, f32[145,128]{1,0:T(8,128)S(1)}, u32[]{:S(2)}, u32[]{:S(2)}) %collective-permute-start.6) | collective-permute-done | bytes 74272 | tf_op jit(solution)/shard_map/ppermute | solution.py:321
  61.4 1.6 %collective-permute-start.7 = (f32[290,128]{1,0:T(8,128)S(1)}, f32[290,128]{1,0:T(8,128)S(1)}, u32[]{:S(2)}, u32[]{:S(2)}) collective-permute-start(f32[290,128]{1,0:T(8,128)S(1)} %maximum_select_fusion.3), channel_id=1, source_target_pairs={{0,4},{1,3},{2,6},{3,1},{4,0},{5,7},{6,2},{7,5},{8,12},{9,11},{10,... | collective-permute-start | bytes 445448 | tf_op jit(solution)/shard_map/ppermute | solution.py:321
  63.0 3.6 %collective-permute-done.7 = f32[290,128]{1,0:T(8,128)S(1)} collective-permute-done((f32[290,128]{1,0:T(8,128)S(1)}, f32[290,128]{1,0:T(8,128)S(1)}, u32[]{:S(2)}, u32[]{:S(2)}) %collective-permute-start.7) | collective-permute-done | bytes 148512 | tf_op jit(solution)/shard_map/ppermute | solution.py:321
  66.7 3.8 %collective-permute-start.8 = (f32[580,128]{1,0:T(8,128)S(1)}, f32[580,128]{1,0:T(8,128)S(1)}, u32[]{:S(2)}, u32[]{:S(2)}) collective-permute-start(f32[580,128]{1,0:T(8,128)S(1)} %maximum_select_fusion.2), channel_id=1, source_target_pairs={{0,2},{1,5},{2,0},{3,7},{4,6},{5,1},{6,4},{7,3},{8,10},{9,13},{10,... | collective-permute-start | bytes 890888 | tf_op jit(solution)/shard_map/ppermute | solution.py:321
  70.5 5.7 %shard_map.104 = (bf16[8,512,128]{2,1,0:T(8,128)(2,1)}, bf16[8,512,128]{2,1,0:T(8,128)(2,1)}) custom-call(bf16[8,512,128]{2,1,0:T(8,128)(2,1)} %x_hbm.7, bf16[8,512,128]{2,1,0:T(8,128)(2,1)} %c_hbm.7, bf16[10,512,128]{2,1,0:T(8,128)(2,1)} %get-tuple-element.37.hid_hbm, ...), custom_call_target="tpu_custom_call", output_to_operand_aliasing={{0}: (6, {}), {1}: (7, {})} | custom-call | flops 1207959552 | bytes 2097152 | tf_op jit(solution)/shard_map/pallas_call | solution.py:323
  76.2 0.1 maximum_select_fusion.1
  76.3 0.1 collective-permute-start.9
  76.4 2.0 %collective-permute-done.9 = f32[1160,128]{1,0:T(8,128)S(1)} collective-permute-done((f32[1160,128]{1,0:T(8,128)S(1)}, f32[1160,128]{1,0:T(8,128)S(1)}, u32[]{:S(2)}, u32[]{:S(2)}) %collective-permute-start.9) | collective-permute-done | bytes 593952 | tf_op jit(solution)/shard_map/ppermute | solution.py:321
  78.4 0.1 maximum_select_fusion
  78.5 1.1 %fusion = (f32[1152,128]{1,0:T(8,128)}, f32[1152,128]{1,0:T(8,128)}) fusion(f32[2320,128]{1,0:T(8,128)S(1)} %maximum_select_fusion), kind=kLoop, calls=%fused_computation.14 | loop fusion | bytes 2359296 | tf_op jit(solution)/shard_map/slice | solution.py:353
  79.6 0.6 slice.68
  (15 shorter events, 0.3 us)
Async XLA Ops:
  2.0 19.3 %collective-permute-start.1 = (bf16[4,512,128]{2,1,0:T(8,128)(2,1)S(1)}, bf16[4,512,128]{2,1,0:T(8,128)(2,1)S(1)}, u32[]{:S(2)}, u32[]{:S(2)}) collective-permute-start(bf16[4,512,128]{2,1,0:T(8,128)(2,1)S(1)} %pad_maximum_fusion.1), channel_id=1, source_target_pairs={{1,0},{2,1},{3,2},{4,3},{5,4},{6,5},{7,6},{8,7},{9,8},{10,9},{11,1... | collective-permute-start | bytes 1572872 | tf_op jit(solution)/shard_map/ppermute | solution.py:340
  3.3 17.9 %collective-permute-start = (bf16[4,512,128]{2,1,0:T(8,128)(2,1)S(1)}, bf16[4,512,128]{2,1,0:T(8,128)(2,1)S(1)}, u32[]{:S(2)}, u32[]{:S(2)}) collective-permute-start(bf16[4,512,128]{2,1,0:T(8,128)(2,1)S(1)} %pad_maximum_fusion), channel_id=1, source_target_pairs={{0,1},{1,2},{2,3},{3,4},{4,5},{5,6},{6,7},{7,8},{8,9},{9,10},{10,1... | collective-permute-start | bytes 1572872 | tf_op jit(solution)/shard_map/ppermute | solution.py:339
  21.2 0.8 copy-start.1
  21.3 0.9 %copy-start.2 = (bf16[4,512,128]{2,1,0:T(8,128)(2,1)}, bf16[4,512,128]{2,1,0:T(8,128)(2,1)S(1)}, u32[]{:S(2)}) copy-start(bf16[4,512,128]{2,1,0:T(8,128)(2,1)S(1)} %collective-permute-done.before_hbm) | copy-start | bytes 1572868
  31.3 5.7 %copy-start = (f32[2320,128]{1,0:T(8,128)S(1)}, f32[2320,128]{1,0:T(8,128)}, u32[]{:S(2)}) copy-start(f32[2320,128]{1,0:T(8,128)} %get-tuple-element.36) | copy-start | bytes 3563524
  32.7 4.3 %collective-permute-start.2 = (f32[1160,128]{1,0:T(8,128)S(1)}, f32[1160,128]{1,0:T(8,128)S(1)}, u32[]{:S(2)}, u32[]{:S(2)}) collective-permute-start(f32[1160,128]{1,0:T(8,128)S(1)} %slice_select_fusion), channel_id=1, source_target_pairs={{0,1},{1,0},{2,3},{3,2},{4,5},{5,4},{6,7},{7,6},{8,9},{9,8},{10,11... | collective-permute-start | bytes 1781768 | tf_op jit(solution)/shard_map/ppermute | solution.py:314
  37.1 8.1 %collective-permute-start.3 = (f32[580,128]{1,0:T(8,128)S(1)}, f32[580,128]{1,0:T(8,128)S(1)}, u32[]{:S(2)}, u32[]{:S(2)}) collective-permute-start(f32[580,128]{1,0:T(8,128)S(1)} %slice_select_fusion.1), channel_id=1, source_target_pairs={{0,2},{1,5},{2,0},{3,7},{4,6},{5,1},{6,4},{7,3},{8,10},{9,13},{10,... | collective-permute-start | bytes 890888 | tf_op jit(solution)/shard_map/ppermute | solution.py:314
  45.3 5.3 %collective-permute-start.4 = (f32[290,128]{1,0:T(8,128)S(1)}, f32[290,128]{1,0:T(8,128)S(1)}, u32[]{:S(2)}, u32[]{:S(2)}) collective-permute-start(f32[290,128]{1,0:T(8,128)S(1)} %slice_select_fusion.2), channel_id=1, source_target_pairs={{0,4},{1,3},{2,6},{3,1},{4,0},{5,7},{6,2},{7,5},{8,12},{9,11},{10,... | collective-permute-start | bytes 445448 | tf_op jit(solution)/shard_map/ppermute | solution.py:314
  50.6 5.4 %collective-permute-start.5 = (f32[145,128]{1,0:T(8,128)S(1)}, f32[145,128]{1,0:T(8,128)S(1)}, u32[]{:S(2)}, u32[]{:S(2)}) collective-permute-start(f32[145,128]{1,0:T(8,128)S(1)} %slice_select_fusion.3), channel_id=1, source_target_pairs={{0,8},{1,9},{2,10},{3,11},{4,12},{5,13},{6,14},{7,15},{8,0},{9,1},... | collective-permute-start | bytes 222728 | tf_op jit(solution)/shard_map/ppermute | solution.py:314
  56.0 5.4 %collective-permute-start.6 = (f32[145,128]{1,0:T(8,128)S(1)}, f32[145,128]{1,0:T(8,128)S(1)}, u32[]{:S(2)}, u32[]{:S(2)}) collective-permute-start(f32[145,128]{1,0:T(8,128)S(1)} %select_add_fusion.3), channel_id=1, source_target_pairs={{0,8},{1,9},{2,10},{3,11},{4,12},{5,13},{6,14},{7,15},{8,0},{9,1},... | collective-permute-start | bytes 222728 | tf_op jit(solution)/shard_map/ppermute | solution.py:321
  61.4 5.3 %collective-permute-start.7 = (f32[290,128]{1,0:T(8,128)S(1)}, f32[290,128]{1,0:T(8,128)S(1)}, u32[]{:S(2)}, u32[]{:S(2)}) collective-permute-start(f32[290,128]{1,0:T(8,128)S(1)} %maximum_select_fusion.3), channel_id=1, source_target_pairs={{0,4},{1,3},{2,6},{3,1},{4,0},{5,7},{6,2},{7,5},{8,12},{9,11},{10,... | collective-permute-start | bytes 445448 | tf_op jit(solution)/shard_map/ppermute | solution.py:321
  66.7 9.5 %collective-permute-start.8 = (f32[580,128]{1,0:T(8,128)S(1)}, f32[580,128]{1,0:T(8,128)S(1)}, u32[]{:S(2)}, u32[]{:S(2)}) collective-permute-start(f32[580,128]{1,0:T(8,128)S(1)} %maximum_select_fusion.2), channel_id=1, source_target_pairs={{0,2},{1,5},{2,0},{3,7},{4,6},{5,1},{6,4},{7,3},{8,10},{9,13},{10,... | collective-permute-start | bytes 890888 | tf_op jit(solution)/shard_map/ppermute | solution.py:321
  76.3 2.1 %collective-permute-start.9 = (f32[1160,128]{1,0:T(8,128)S(1)}, f32[1160,128]{1,0:T(8,128)S(1)}, u32[]{:S(2)}, u32[]{:S(2)}) collective-permute-start(f32[1160,128]{1,0:T(8,128)S(1)} %maximum_select_fusion.1), channel_id=1, source_target_pairs={{0,1},{1,0},{2,3},{3,2},{4,5},{5,4},{6,7},{7,6},{8,9},{9,8},{10,11... | collective-permute-start | bytes 1781768 | tf_op jit(solution)/shard_map/ppermute | solution.py:321

commit v8 on v7

--- a/solution.py
+++ b/solution.py
@@ -252,7 +252,7 @@
             flops=14 * unit, transcendentals=4 * width * ch, bytes_accessed=10 * count * width * ch
         ),
     )(level_index, level_table, inputs, cotangent, before, after, hid, bf, hidt, acc1, acc2, lv, k1f, k2b)
-    step = count // 2 if count % 2 == 0 else count
+    step = 2 if count % 2 == 0 else count
     whole = jax.ShapeDtypeStruct((count, width, ch), jnp.bfloat16)
     chunks = []
     for first_row in range(0, count, step):
@@ -322,8 +322,9 @@
         if count in riders:
             got, state = lax.optimization_barrier((got, riders[count](*state)))
         count += 1
-        piece = jnp.where(low, jnp.concatenate([piece, got]), jnp.concatenate([got, piece]))
-    return piece, state
+        if count < 2 * len(orders):
+            piece = jnp.where(low, jnp.concatenate([piece, got]), jnp.concatenate([got, piece]))
+    return (jnp.where(low, piece, got), jnp.where(low, got, piece)), state
 
 
 def local(inputs, cotangent, first_kernel, second_kernel, level_table, level_index):
@@ -347,11 +348,26 @@
         first_kernel, second_kernel,
     )
     steps = 2 * (size.bit_length() - 1)
-    places = [1, steps - 2] if len(chunks) == 2 and steps >= 4 else list(range(len(chunks)))
-    total, (outputs, input_grad) = butterfly_sum(packed, dict(zip(places, chunks)))
-    first_sum = total[: 9 * ch].reshape(9, ch, ch)
-    second_sum = total[9 * ch : 18 * ch].reshape(9, ch, ch)
-    level_sum = total[18 * ch : 18 * ch + 2]
+    if len(chunks) == 4 and steps >= 8:
+        places = [1, 2, steps - 3, steps - 2]
+    elif len(chunks) == 2 and steps >= 4:
+        places = [1, steps - 2]
+    else:
+        places = list(range(len(chunks)))
+    (lower, upper), (outputs, input_grad) = butterfly_sum(packed, dict(zip(places, chunks)))
+    half = lower.shape[0]
+
+    def rows(a, b):
+        parts = []
+        if a < half:
+            parts.append(lower[a : min(b, half)])
+        if b > half:
+            parts.append(upper[max(a, half) - half : b - half])
+        return parts[0] if len(parts) == 1 else jnp.concatenate(parts)
+
+    first_sum = rows(0, 9 * ch).reshape(9, ch, ch)
+    second_sum = rows(9 * ch, 18 * ch).reshape(9, ch, ch)
+    level_sum = rows(18 * ch, 18 * ch + 2)
     return (outputs, input_grad, first_sum, second_sum, level_sum)
 
 

time: 80.6 us -> 81.4 us (level)
  Pallas kernels: 34.6 us -> 40.4 us
  starting transfers between devices: 21.9 us -> 16.3 us
    pallas_call x2 -> x4, Pallas kernels: 11.3 us -> 17.2 us  [butterfly_sum(): got, state = lax.optimization_barrier((got, riders[count](*state)))]
    ppermute x4, starting transfers between devices: 8.2 us -> 2.97 us  [butterfly_sum(): got = lax.ppermute(piece, 'rows', perm)]
    ppermute x4, waiting for transfers between devices: 7.95 us -> 6.52 us  [butterfly_sum(): got = lax.ppermute(send, 'rows', perm)]
    ppermute x4, waiting for transfers between devices: 8.31 us -> 9.6 us  [butterfly_sum(): got = lax.ppermute(piece, 'rows', perm)]
    concatenate x0 -> x1, other arithmetic: none -> 0.85 us  [rows(): return parts[0] if len(parts) == 1 else jnp.concatenate(parts)]
    slice x2 -> x4, local copies, waits for them, and re-layouts: 1.65 us -> 1.46 us  [the longest x2 0.86 us: rows(): parts.append(lower[a:min(b, half)])]
  transfers between devices with their start and end apart: 10 -> 10, of which waited for: 6 -> 7; matrix products, arithmetic and copies ran while one was open for 0% -> 0% of each run, Pallas kernels for 32% -> 39%
where the time goes in v8:
time: 81.4 us; the launch traced here: 80.9 us
  Pallas kernels  40.4 us (50%)
  starting transfers between devices  16.3 us (20%)
  waiting for transfers between devices  16.1 us (20%)
  local copies, waits for them, and re-layouts  3.67 us (5%)
  other arithmetic  2.88 us (4%)
  between operations  1.51 us (2%)
    pallas_call x4, Pallas kernels, butterfly_sum(): got, state = lax.optimization_barrier((got, riders[count](*state)))  17.2 us
    pallas_call x1, Pallas kernels, section(): pl.pallas_call(interior_kernel, out_shape=(frame, frame, frame_t, square,...  14.2 us
    ppermute x4, waiting for transfers between devices, butterfly_sum(): got = lax.ppermute(piece, 'rows', perm)  9.6 us
    pallas_call x1, Pallas kernels, section(): pl.pallas_call(functools.partial(edge_kernel, norm), out_shape=(jax.Shape...  9.09 us
    ppermute x4, starting transfers between devices, butterfly_sum(): got = lax.ppermute(send, 'rows', perm)  9 us
    ppermute x4, waiting for transfers between devices, butterfly_sum(): got = lax.ppermute(send, 'rows', perm)  6.52 us
    ppermute x1, starting transfers between devices, local(): lax.ppermute(jnp.concatenate([inputs[-2:], cotangent[-2:]]), 'rows', up)  3.06 us
    ppermute x4, starting transfers between devices, butterfly_sum(): got = lax.ppermute(piece, 'rows', perm)  2.97 us
  transfers between devices with their start and end apart: 10, of which 7 were waited for; matrix products, arithmetic and copies ran while one was open for 0% of the time, Pallas kernels for 39%

profile of v8, /device:TPU:0, one launch (start us, length us, event | category | flops | bytes accessed | tf_op | source)
XLA Modules:
  0.0 80.9 jit_solution(17207788072063363441)
XLA Ops:
  0.6 1.3 %fusion = (bf16[2,512,128]{2,1,0:T(8,128)(2,1)S(1)}, bf16[2,512,128]{2,1,0:T(8,128)(2,1)S(1)}, bf16[2,512,128]{2,1,0:T(8,128)(2,1)S(1)}, bf16[2,512,128]{2,1,0:T(8,128)(2,1)S(1)}) fusion(bf16[8,512,128]{2,1,0:T(8,128)(2,1)} %x_hbm.11, bf16[8,512,128]{2,1,0:T(8,128)(2,1)} %c_hbm.11), kind=kLoop, calls=%fused_computation.16 | loop fusion | bytes 2097152 | tf_op jit(solution)/shard_map/slice | solution.py:341
  2.0 1.3 %collective-permute-start.1 = (bf16[4,512,128]{2,1,0:T(8,128)(2,1)S(1)}, bf16[4,512,128]{2,1,0:T(8,128)(2,1)S(1)}, u32[]{:S(2)}, u32[]{:S(2)}) collective-permute-start(bf16[4,512,128]{2,1,0:T(8,128)(2,1)S(1)} %pad_maximum_fusion.2), channel_id=1, source_target_pairs={{1,0},{2,1},{3,2},{4,3},{5,4},{6,5},{7,6},{8,7},{9,8},{10,9},{11,1... | collective-permute-start | bytes 1572872 | tf_op jit(solution)/shard_map/ppermute | solution.py:341
  3.3 3.1 %collective-permute-start = (bf16[4,512,128]{2,1,0:T(8,128)(2,1)S(1)}, bf16[4,512,128]{2,1,0:T(8,128)(2,1)S(1)}, u32[]{:S(2)}, u32[]{:S(2)}) collective-permute-start(bf16[4,512,128]{2,1,0:T(8,128)(2,1)S(1)} %pad_maximum_fusion.1), channel_id=1, source_target_pairs={{0,1},{1,2},{2,3},{3,4},{4,5},{5,6},{6,7},{7,8},{8,9},{9,10},{10,1... | collective-permute-start | bytes 1572872 | tf_op jit(solution)/shard_map/ppermute | solution.py:340
  7.0 14.2 %shard_map.101 = (bf16[10,512,128]{2,1,0:T(8,128)(2,1)}, bf16[10,512,128]{2,1,0:T(8,128)(2,1)}, bf16[10,128,512]{2,1,0:T(8,128)(2,1)}, f32[384,384]{1,0:T(8,128)...) custom-call(s32[1]{0:T(128)S(6)} %copy.23.idx_ref, ...), custom_call_target="tpu_custom_call" | custom-call | flops 3925868544 | bytes 4194304 | tf_op jit(solution)/shard_map/pallas_call | solution.py:218
  21.3 0.8 copy-done.1
  22.0 0.2 copy-done.2
  22.2 9.1 %shard_map.102 = (f32[2320,128]{1,0:T(8,128)}, bf16[10,512,128]{2,1,0:T(8,128)(2,1)}, bf16[10,512,128]{2,1,0:T(8,128)(2,1)}) custom-call(s32[1]{0:T(128)S(6)} %copy.23.idx_ref, f32[16,2,128]{2,1,0:T(2,128)} %lt_ref.3, bf16[8,512,128]{2,1,0:T(8,128)(2,1)} %x_hbm.11, bf16[8,512,128]{2,1,0:T(8,128)(2,1)} %c_hbm.11, bf16[4,512,128]{2,1,0:T(8,128)(2,1)} %copy-done.2, ...), custom_call_target="tpu_custom_call" | custom-call | flops 2113929216 | bytes 5242880 | tf_op jit(solution)/shard_map/pallas_call | solution.py:236
  31.3 1.4 %slice_select_fusion = f32[1160,128]{1,0:T(8,128)S(1)} fusion(f32[2320,128]{1,0:T(8,128)} %get-tuple-element.46, pred[]{:T(512)S(6)} %eq.35), kind=kLoop, calls=%fused_computation.3 | loop fusion | flops 148480 | bytes 1781761 | tf_op jit(solution)/shard_map/jit(_where)/select_n | solution.py:313
  32.7 2.6 %collective-permute-start.2 = (f32[1160,128]{1,0:T(8,128)S(1)}, f32[1160,128]{1,0:T(8,128)S(1)}, u32[]{:S(2)}, u32[]{:S(2)}) collective-permute-start(f32[1160,128]{1,0:T(8,128)S(1)} %slice_select_fusion), channel_id=1, source_target_pairs={{0,1},{1,0},{2,3},{3,2},{4,5},{5,4},{6,7},{7,6},{8,9},{9,8},{10,11... | collective-permute-start | bytes 1781768 | tf_op jit(solution)/shard_map/ppermute | solution.py:314
  35.3 1.6 %collective-permute-done.2 = f32[1160,128]{1,0:T(8,128)S(1)} collective-permute-done((f32[1160,128]{1,0:T(8,128)S(1)}, f32[1160,128]{1,0:T(8,128)S(1)}, u32[]{:S(2)}, u32[]{:S(2)}) %collective-permute-start.2) | collective-permute-done | bytes 593952 | tf_op jit(solution)/shard_map/ppermute | solution.py:314
  37.0 0.1 select_add_fusion
  37.1 2.4 %collective-permute-start.3 = (f32[580,128]{1,0:T(8,128)S(1)}, f32[580,128]{1,0:T(8,128)S(1)}, u32[]{:S(2)}, u32[]{:S(2)}) collective-permute-start(f32[580,128]{1,0:T(8,128)S(1)} %slice_select_fusion.1), channel_id=1, source_target_pairs={{0,2},{1,5},{2,0},{3,7},{4,6},{5,1},{6,4},{7,3},{8,10},{9,13},{10,... | collective-permute-start | bytes 890888 | tf_op jit(solution)/shard_map/ppermute | solution.py:314
  39.5 4.3 %shard_map.103 = (bf16[8,512,128]{2,1,0:T(8,128)(2,1)}, bf16[8,512,128]{2,1,0:T(8,128)(2,1)}) custom-call(bf16[8,512,128]{2,1,0:T(8,128)(2,1)} %x_hbm.11, bf16[8,512,128]{2,1,0:T(8,128)(2,1)} %c_hbm.11, bf16[10,512,128]{2,1,0:T(8,128)(2,1)} %get-tuple-element.47.hid_hbm, bf16[10,512,128]{2,1,0:T(8,128)(2,1)} %get-tuple-element.48.bf_hbm, ...), custom_call_target="tpu_custom_call" | custom-call | flops 603979776 | bytes 1048576 | tf_op jit(solution)/shard_map/pallas_call | solution.py:316
  43.8 0.5 collective-permute-done.3
  44.4 1.6 %collective-permute-start.4 = (f32[290,128]{1,0:T(8,128)S(1)}, f32[290,128]{1,0:T(8,128)S(1)}, u32[]{:S(2)}, u32[]{:S(2)}) collective-permute-start(f32[290,128]{1,0:T(8,128)S(1)} %slice_select_fusion.2), channel_id=1, source_target_pairs={{0,4},{1,3},{2,6},{3,1},{4,0},{5,7},{6,2},{7,5},{8,12},{9,11},{10,... | collective-permute-start | bytes 445448 | tf_op jit(solution)/shard_map/ppermute | solution.py:314
  46.0 4.3 %shard_map.104 = (bf16[8,512,128]{2,1,0:T(8,128)(2,1)}, bf16[8,512,128]{2,1,0:T(8,128)(2,1)}) custom-call(bf16[8,512,128]{2,1,0:T(8,128)(2,1)} %x_hbm.11, bf16[8,512,128]{2,1,0:T(8,128)(2,1)} %c_hbm.11, bf16[10,512,128]{2,1,0:T(8,128)(2,1)} %get-tuple-element.47.hid_hbm, ...), custom_call_target="tpu_custom_call", output_to_operand_aliasing={{0}: (6, {}), {1}: (7, {})} | custom-call | flops 603979776 | bytes 1048576 | tf_op jit(solution)/shard_map/pallas_call | solution.py:316
  50.4 2.3 %collective-permute-start.5 = (f32[145,128]{1,0:T(8,128)S(1)}, f32[145,128]{1,0:T(8,128)S(1)}, u32[]{:S(2)}, u32[]{:S(2)}) collective-permute-start(f32[145,128]{1,0:T(8,128)S(1)} %slice_select_fusion.3), channel_id=1, source_target_pairs={{0,8},{1,9},{2,10},{3,11},{4,12},{5,13},{6,14},{7,15},{8,0},{9,1},... | collective-permute-start | bytes 222728 | tf_op jit(solution)/shard_map/ppermute | solution.py:314
  52.7 4.4 %collective-permute-done.5 = f32[145,128]{1,0:T(8,128)S(1)} collective-permute-done((f32[145,128]{1,0:T(8,128)S(1)}, f32[145,128]{1,0:T(8,128)S(1)}, u32[]{:S(2)}, u32[]{:S(2)}) %collective-permute-start.5) | collective-permute-done | bytes 74272 | tf_op jit(solution)/shard_map/ppermute | solution.py:314
  57.2 0.9 %collective-permute-start.6 = (f32[145,128]{1,0:T(8,128)S(1)}, f32[145,128]{1,0:T(8,128)S(1)}, u32[]{:S(2)}, u32[]{:S(2)}) collective-permute-start(f32[145,128]{1,0:T(8,128)S(1)} %select_add_fusion.3), channel_id=1, source_target_pairs={{0,8},{1,9},{2,10},{3,11},{4,12},{5,13},{6,14},{7,15},{8,0},{9,1},... | collective-permute-start | bytes 222728 | tf_op jit(solution)/shard_map/ppermute | solution.py:321
  58.1 4.8 %collective-permute-done.6 = f32[145,128]{1,0:T(8,128)S(1)} collective-permute-done((f32[145,128]{1,0:T(8,128)S(1)}, f32[145,128]{1,0:T(8,128)S(1)}, u32[]{:S(2)}, u32[]{:S(2)}) %collective-permute-start.6) | collective-permute-done | bytes 74272 | tf_op jit(solution)/shard_map/ppermute | solution.py:321
  63.0 4.3 %shard_map.105 = (bf16[8,512,128]{2,1,0:T(8,128)(2,1)}, bf16[8,512,128]{2,1,0:T(8,128)(2,1)}) custom-call(bf16[8,512,128]{2,1,0:T(8,128)(2,1)} %x_hbm.11, bf16[8,512,128]{2,1,0:T(8,128)(2,1)} %c_hbm.11, bf16[10,512,128]{2,1,0:T(8,128)(2,1)} %get-tuple-element.47.hid_hbm, ...), custom_call_target="tpu_custom_call", output_to_operand_aliasing={{0}: (6, {}), {1}: (7, {})} | custom-call | flops 603979776 | bytes 1048576 | tf_op jit(solution)/shard_map/pallas_call | solution.py:323
  67.3 2.2 %collective-permute-done.7 = f32[290,128]{1,0:T(8,128)S(1)} collective-permute-done((f32[290,128]{1,0:T(8,128)S(1)}, f32[290,128]{1,0:T(8,128)S(1)}, u32[]{:S(2)}, u32[]{:S(2)}) %collective-permute-start.7) | collective-permute-done | bytes 148512 | tf_op jit(solution)/shard_map/ppermute | solution.py:321
  69.5 1.9 %collective-permute-start.8 = (f32[580,128]{1,0:T(8,128)S(1)}, f32[580,128]{1,0:T(8,128)S(1)}, u32[]{:S(2)}, u32[]{:S(2)}) collective-permute-start(f32[580,128]{1,0:T(8,128)S(1)} %maximum_select_fusion.1), channel_id=1, source_target_pairs={{0,2},{1,5},{2,0},{3,7},{4,6},{5,1},{6,4},{7,3},{8,10},{9,13},{10,... | collective-permute-start | bytes 890888 | tf_op jit(solution)/shard_map/ppermute | solution.py:321
  71.4 4.3 %shard_map.106 = (bf16[8,512,128]{2,1,0:T(8,128)(2,1)}, bf16[8,512,128]{2,1,0:T(8,128)(2,1)}) custom-call(bf16[8,512,128]{2,1,0:T(8,128)(2,1)} %x_hbm.11, bf16[8,512,128]{2,1,0:T(8,128)(2,1)} %c_hbm.11, bf16[10,512,128]{2,1,0:T(8,128)(2,1)} %get-tuple-element.47.hid_hbm, ...), custom_call_target="tpu_custom_call", output_to_operand_aliasing={{0}: (6, {}), {1}: (7, {})} | custom-call | flops 603979776 | bytes 1048576 | tf_op jit(solution)/shard_map/pallas_call | solution.py:323
  75.7 0.6 collective-permute-done.8
  76.3 0.1 maximum_select_fusion
  76.4 0.1 collective-permute-start.9
  76.5 2.0 %collective-permute-done.9 = f32[1160,128]{1,0:T(8,128)S(1)} collective-permute-done((f32[1160,128]{1,0:T(8,128)S(1)}, f32[1160,128]{1,0:T(8,128)S(1)}, u32[]{:S(2)}, u32[]{:S(2)}) %collective-permute-start.9) | collective-permute-done | bytes 593952 | tf_op jit(solution)/shard_map/ppermute | solution.py:321
  78.5 0.1 broadcast_select_fusion
  78.6 0.9 %slice.70 = f32[1152,128]{1,0:T(8,128)} slice(f32[1160,128]{1,0:T(8,128)S(1)} %get-tuple-element.72), slice={[0:1152], [0:128]} | slice | bytes 1179648 | tf_op jit(solution)/shard_map/slice | solution.py:363
  79.5 0.6 slice.73
  80.1 0.9 %pad_maximum_fusion = f32[1152,128]{1,0:T(8,128)} fusion(f32[1144,128]{1,0:T(8,128)S(1)} %slice.72, f32[8,128]{1,0:T(8,128)S(1)} %slice.71), kind=kLoop, calls=%fused_computation.2 | loop fusion | flops 147456 | bytes 1179648 | tf_op jit(solution)/shard_map/concatenate | solution.py:366
  (20 shorter events, 0.5 us)
Async XLA Ops:
  2.0 19.3 %collective-permute-start.1 = (bf16[4,512,128]{2,1,0:T(8,128)(2,1)S(1)}, bf16[4,512,128]{2,1,0:T(8,128)(2,1)S(1)}, u32[]{:S(2)}, u32[]{:S(2)}) collective-permute-start(bf16[4,512,128]{2,1,0:T(8,128)(2,1)S(1)} %pad_maximum_fusion.2), channel_id=1, source_target_pairs={{1,0},{2,1},{3,2},{4,3},{5,4},{6,5},{7,6},{8,7},{9,8},{10,9},{11,1... | collective-permute-start | bytes 1572872 | tf_op jit(solution)/shard_map/ppermute | solution.py:341
  3.3 17.9 %collective-permute-start = (bf16[4,512,128]{2,1,0:T(8,128)(2,1)S(1)}, bf16[4,512,128]{2,1,0:T(8,128)(2,1)S(1)}, u32[]{:S(2)}, u32[]{:S(2)}) collective-permute-start(bf16[4,512,128]{2,1,0:T(8,128)(2,1)S(1)} %pad_maximum_fusion.1), channel_id=1, source_target_pairs={{0,1},{1,2},{2,3},{3,4},{4,5},{5,6},{6,7},{7,8},{8,9},{9,10},{10,1... | collective-permute-start | bytes 1572872 | tf_op jit(solution)/shard_map/ppermute | solution.py:340
  21.2 0.8 copy-start.1
  21.2 0.9 %copy-start.2 = (bf16[4,512,128]{2,1,0:T(8,128)(2,1)}, bf16[4,512,128]{2,1,0:T(8,128)(2,1)S(1)}, u32[]{:S(2)}) copy-start(bf16[4,512,128]{2,1,0:T(8,128)(2,1)S(1)} %collective-permute-done.before_hbm) | copy-start | bytes 1572868
  31.3 5.7 %copy-start = (f32[2320,128]{1,0:T(8,128)S(1)}, f32[2320,128]{1,0:T(8,128)}, u32[]{:S(2)}) copy-start(f32[2320,128]{1,0:T(8,128)} %get-tuple-element.46) | copy-start | bytes 3563524
  32.7 4.3 %collective-permute-start.2 = (f32[1160,128]{1,0:T(8,128)S(1)}, f32[1160,128]{1,0:T(8,128)S(1)}, u32[]{:S(2)}, u32[]{:S(2)}) collective-permute-start(f32[1160,128]{1,0:T(8,128)S(1)} %slice_select_fusion), channel_id=1, source_target_pairs={{0,1},{1,0},{2,3},{3,2},{4,5},{5,4},{6,7},{7,6},{8,9},{9,8},{10,11... | collective-permute-start | bytes 1781768 | tf_op jit(solution)/shard_map/ppermute | solution.py:314
  37.1 7.2 %collective-permute-start.3 = (f32[580,128]{1,0:T(8,128)S(1)}, f32[580,128]{1,0:T(8,128)S(1)}, u32[]{:S(2)}, u32[]{:S(2)}) collective-permute-start(f32[580,128]{1,0:T(8,128)S(1)} %slice_select_fusion.1), channel_id=1, source_target_pairs={{0,2},{1,5},{2,0},{3,7},{4,6},{5,1},{6,4},{7,3},{8,10},{9,13},{10,... | collective-permute-start | bytes 890888 | tf_op jit(solution)/shard_map/ppermute | solution.py:314
  44.4 5.9 %collective-permute-start.4 = (f32[290,128]{1,0:T(8,128)S(1)}, f32[290,128]{1,0:T(8,128)S(1)}, u32[]{:S(2)}, u32[]{:S(2)}) collective-permute-start(f32[290,128]{1,0:T(8,128)S(1)} %slice_select_fusion.2), channel_id=1, source_target_pairs={{0,4},{1,3},{2,6},{3,1},{4,0},{5,7},{6,2},{7,5},{8,12},{9,11},{10,... | collective-permute-start | bytes 445448 | tf_op jit(solution)/shard_map/ppermute | solution.py:314
  50.4 6.7 %collective-permute-start.5 = (f32[145,128]{1,0:T(8,128)S(1)}, f32[145,128]{1,0:T(8,128)S(1)}, u32[]{:S(2)}, u32[]{:S(2)}) collective-permute-start(f32[145,128]{1,0:T(8,128)S(1)} %slice_select_fusion.3), channel_id=1, source_target_pairs={{0,8},{1,9},{2,10},{3,11},{4,12},{5,13},{6,14},{7,15},{8,0},{9,1},... | collective-permute-start | bytes 222728 | tf_op jit(solution)/shard_map/ppermute | solution.py:314
  57.2 5.8 %collective-permute-start.6 = (f32[145,128]{1,0:T(8,128)S(1)}, f32[145,128]{1,0:T(8,128)S(1)}, u32[]{:S(2)}, u32[]{:S(2)}) collective-permute-start(f32[145,128]{1,0:T(8,128)S(1)} %select_add_fusion.3), channel_id=1, source_target_pairs={{0,8},{1,9},{2,10},{3,11},{4,12},{5,13},{6,14},{7,15},{8,0},{9,1},... | collective-permute-start | bytes 222728 | tf_op jit(solution)/shard_map/ppermute | solution.py:321
  62.9 6.5 %collective-permute-start.7 = (f32[290,128]{1,0:T(8,128)S(1)}, f32[290,128]{1,0:T(8,128)S(1)}, u32[]{:S(2)}, u32[]{:S(2)}) collective-permute-start(f32[290,128]{1,0:T(8,128)S(1)} %maximum_select_fusion.2), channel_id=1, source_target_pairs={{0,4},{1,3},{2,6},{3,1},{4,0},{5,7},{6,2},{7,5},{8,12},{9,11},{10,... | collective-permute-start | bytes 445448 | tf_op jit(solution)/shard_map/ppermute | solution.py:321
  69.5 6.8 %collective-permute-start.8 = (f32[580,128]{1,0:T(8,128)S(1)}, f32[580,128]{1,0:T(8,128)S(1)}, u32[]{:S(2)}, u32[]{:S(2)}) collective-permute-start(f32[580,128]{1,0:T(8,128)S(1)} %maximum_select_fusion.1), channel_id=1, source_target_pairs={{0,2},{1,5},{2,0},{3,7},{4,6},{5,1},{6,4},{7,3},{8,10},{9,13},{10,... | collective-permute-start | bytes 890888 | tf_op jit(solution)/shard_map/ppermute | solution.py:321
  76.4 2.1 %collective-permute-start.9 = (f32[1160,128]{1,0:T(8,128)S(1)}, f32[1160,128]{1,0:T(8,128)S(1)}, u32[]{:S(2)}, u32[]{:S(2)}) collective-permute-start(f32[1160,128]{1,0:T(8,128)S(1)} %maximum_select_fusion), channel_id=1, source_target_pairs={{0,1},{1,0},{2,3},{3,2},{4,5},{5,4},{6,7},{7,6},{8,9},{9,8},{10,11... | collective-permute-start | bytes 1781768 | tf_op jit(solution)/shard_map/ppermute | solution.py:321

commit v9 on v7

--- a/solution.py
+++ b/solution.py
@@ -96,7 +96,8 @@
 
     zero = jnp.zeros((1, ch), jnp.float32)
     lv0, lv1 = lax.fori_loop(
-        2, count, lambda r, cr: phase_one(r, x_ref, c_ref, hid_ref, hidt_ref, bf_ref, k1f, k2b, cr), (zero, zero)
+        2, count, lambda r, cr: phase_one(r, x_ref, c_ref, hid_ref, hidt_ref, bf_ref, k1f, k2b, cr), (zero, zero),
+        unroll=True,
     )
     lv_ref[0:1, :] = lv0
     lv_ref[1:2, :] = lv1
@@ -105,7 +106,7 @@
         xt_ref[r] = x_ref[r].astype(jnp.float32).T.astype(xt_ref.dtype)
         return carry
 
-    lax.fori_loop(2, count + 2, transpose_rows, 0)
+    lax.fori_loop(2, count + 2, transpose_rows, 0, unroll=True)
     acc1[...] = jnp.zeros_like(acc1)
     acc2[...] = jnp.zeros_like(acc2)
 
@@ -113,13 +114,13 @@
         g2_row(i, hidt_ref, c_ref, acc2)
         return carry
 
-    lax.fori_loop(2, count - 2, middle, 0)
+    lax.fori_loop(2, count - 2, middle, 0, unroll=True)
 
     def g1_middle(i, carry):
         g1_row(i, xt_ref, bf_ref, acc1)
         return carry
 
-    lax.fori_loop(1, count - 1, g1_middle, 0)
+    lax.fori_loop(1, count - 1, g1_middle, 0, unroll=True)
 
 
 def edge_kernel(norm, idx_ref, lt_ref, x_hbm, c_hbm, before_hbm, after_hbm, hida_hbm, bfa_hbm, hidta_hbm,

time: 80.6 us -> 74.6 us (0.926)
  Pallas kernels: 34.6 us -> 29.3 us
  starting transfers between devices: 21.9 us -> 20 us
  waiting for transfers between devices: 16.3 us -> 17.5 us
    pallas_call x1, Pallas kernels: 14.2 us -> 8.87 us  [section(): pl.pallas_call(interior_kernel, out_shape=(frame, frame, frame_t, square,...]
    ppermute x4, starting transfers between devices: 8.2 us -> 4.99 us  [butterfly_sum(): got = lax.ppermute(piece, 'rows', perm)]
    ppermute x4, starting transfers between devices: 9.34 us -> 10.6 us  [butterfly_sum(): got = lax.ppermute(send, 'rows', perm)]
    ppermute x4, waiting for transfers between devices: 8.31 us -> 9.57 us  [butterfly_sum(): got = lax.ppermute(piece, 'rows', perm)]
  transfers between devices with their start and end apart: 10 -> 10, of which waited for: 6 -> 7; matrix products, arithmetic and copies ran while one was open for 0% -> 0% of each run, Pallas kernels for 32% -> 27%
where the time goes in v9:
time: 74.6 us; the launch traced here: 74.2 us
  Pallas kernels  29.3 us (39%)
  starting transfers between devices  20 us (27%)
  waiting for transfers between devices  17.5 us (23%)
  local copies, waits for them, and re-layouts  3.86 us (5%)
  other arithmetic  2.09 us (3%)
  between operations  1.47 us (2%)
    pallas_call x2, Pallas kernels, butterfly_sum(): got, state = lax.optimization_barrier((got, riders[count](*state)))  11.3 us
    ppermute x4, starting transfers between devices, butterfly_sum(): got = lax.ppermute(send, 'rows', perm)  10.6 us
    ppermute x4, waiting for transfers between devices, butterfly_sum(): got = lax.ppermute(piece, 'rows', perm)  9.57 us
    pallas_call x1, Pallas kernels, section(): pl.pallas_call(functools.partial(edge_kernel, norm), out_shape=(jax.Shape...  9.1 us
    pallas_call x1, Pallas kernels, section(): pl.pallas_call(interior_kernel, out_shape=(frame, frame, frame_t, square,...  8.87 us
    ppermute x4, waiting for transfers between devices, butterfly_sum(): got = lax.ppermute(send, 'rows', perm)  7.96 us
    ppermute x4, starting transfers between devices, butterfly_sum(): got = lax.ppermute(piece, 'rows', perm)  4.99 us
    ppermute x1, starting transfers between devices, local(): lax.ppermute(jnp.concatenate([inputs[-2:], cotangent[-2:]]), 'rows', up)  3.06 us
  transfers between devices with their start and end apart: 10, of which 7 were waited for; matrix products, arithmetic and copies ran while one was open for 0% of the time, Pallas kernels for 27%

profile of v9, /device:TPU:0, one launch (start us, length us, event | category | flops | bytes accessed | tf_op | source)
XLA Modules:
  0.0 74.2 jit_solution(8924776952226471643)
XLA Ops:
  0.6 1.3 %fusion.1 = (bf16[2,512,128]{2,1,0:T(8,128)(2,1)S(1)}, bf16[2,512,128]{2,1,0:T(8,128)(2,1)S(1)}, bf16[2,512,128]{2,1,0:T(8,128)(2,1)S(1)}, bf16[2,512,128]{2,1,0:T(8,128)(2,1)S(1)}) fusion(bf16[8,512,128]{2,1,0:T(8,128)(2,1)} %x_hbm.7, bf16[8,512,128]{2,1,0:T(8,128)(2,1)} %c_hbm.7), kind=kLoop, calls=%fused_computation.15 | loop fusion | bytes 2097152 | tf_op jit(solution)/shard_map/slice | solution.py:341
  2.0 1.3 %collective-permute-start.1 = (bf16[4,512,128]{2,1,0:T(8,128)(2,1)S(1)}, bf16[4,512,128]{2,1,0:T(8,128)(2,1)S(1)}, u32[]{:S(2)}, u32[]{:S(2)}) collective-permute-start(bf16[4,512,128]{2,1,0:T(8,128)(2,1)S(1)} %pad_maximum_fusion.1), channel_id=1, source_target_pairs={{1,0},{2,1},{3,2},{4,3},{5,4},{6,5},{7,6},{8,7},{9,8},{10,9},{11,1... | collective-permute-start | bytes 1572872 | tf_op jit(solution)/shard_map/ppermute | solution.py:341
  3.3 3.1 %collective-permute-start = (bf16[4,512,128]{2,1,0:T(8,128)(2,1)S(1)}, bf16[4,512,128]{2,1,0:T(8,128)(2,1)S(1)}, u32[]{:S(2)}, u32[]{:S(2)}) collective-permute-start(bf16[4,512,128]{2,1,0:T(8,128)(2,1)S(1)} %pad_maximum_fusion), channel_id=1, source_target_pairs={{0,1},{1,2},{2,3},{3,4},{4,5},{5,6},{6,7},{7,8},{8,9},{9,10},{10,1... | collective-permute-start | bytes 1572872 | tf_op jit(solution)/shard_map/ppermute | solution.py:340
  7.0 8.9 %shard_map.101 = (bf16[10,512,128]{2,1,0:T(8,128)(2,1)}, bf16[10,512,128]{2,1,0:T(8,128)(2,1)}, bf16[10,128,512]{2,1,0:T(8,128)(2,1)}, f32[384,384]{1,0:T(8,128)...) custom-call(s32[1]{0:T(128)S(6)} %copy.15.idx_ref, ...), custom_call_target="tpu_custom_call" | custom-call | flops 3925868544 | bytes 4194304 | tf_op jit(solution)/shard_map/pallas_call | solution.py:219
  15.9 0.0 copy-start.1
  16.0 0.8 %copy-done.1 = bf16[4,512,128]{2,1,0:T(8,128)(2,1)} copy-done((bf16[4,512,128]{2,1,0:T(8,128)(2,1)}, bf16[4,512,128]{2,1,0:T(8,128)(2,1)S(1)}, u32[]{:S(2)}) %copy-start.1) | copy-done | bytes 524312
  16.7 0.2 copy-done.2
  16.9 9.1 %shard_map.102 = (f32[2320,128]{1,0:T(8,128)}, bf16[10,512,128]{2,1,0:T(8,128)(2,1)}, bf16[10,512,128]{2,1,0:T(8,128)(2,1)}) custom-call(s32[1]{0:T(128)S(6)} %copy.15.idx_ref, f32[16,2,128]{2,1,0:T(2,128)} %lt_ref.3, bf16[8,512,128]{2,1,0:T(8,128)(2,1)} %x_hbm.7, bf16[8,512,128]{2,1,0:T(8,128)(2,1)} %c_hbm.7, bf16[4,512,128]{2,1,0:T(8,128)(2,1)} %copy-done.2, ...), custom_call_target="tpu_custom_call" | custom-call | flops 2113929216 | bytes 5242880 | tf_op jit(solution)/shard_map/pallas_call | solution.py:237
  26.0 1.4 %slice_select_fusion = f32[1160,128]{1,0:T(8,128)S(1)} fusion(f32[2320,128]{1,0:T(8,128)} %get-tuple-element.36, pred[]{:T(512)S(6)} %eq.35), kind=kLoop, calls=%fused_computation.3 | loop fusion | flops 148480 | bytes 1781761 | tf_op jit(solution)/shard_map/jit(_where)/select_n | solution.py:314
  27.4 3.5 %collective-permute-start.2 = (f32[1160,128]{1,0:T(8,128)S(1)}, f32[1160,128]{1,0:T(8,128)S(1)}, u32[]{:S(2)}, u32[]{:S(2)}) collective-permute-start(f32[1160,128]{1,0:T(8,128)S(1)} %slice_select_fusion), channel_id=1, source_target_pairs={{0,1},{1,0},{2,3},{3,2},{4,5},{5,4},{6,7},{7,6},{8,9},{9,8},{10,11... | collective-permute-start | bytes 1781768 | tf_op jit(solution)/shard_map/ppermute | solution.py:315
  31.0 1.6 %collective-permute-done.2 = f32[1160,128]{1,0:T(8,128)S(1)} collective-permute-done((f32[1160,128]{1,0:T(8,128)S(1)}, f32[1160,128]{1,0:T(8,128)S(1)}, u32[]{:S(2)}, u32[]{:S(2)}) %collective-permute-start.2) | collective-permute-done | bytes 593952 | tf_op jit(solution)/shard_map/ppermute | solution.py:315
  32.6 0.1 select_add_fusion
  32.8 2.8 %collective-permute-start.3 = (f32[580,128]{1,0:T(8,128)S(1)}, f32[580,128]{1,0:T(8,128)S(1)}, u32[]{:S(2)}, u32[]{:S(2)}) collective-permute-start(f32[580,128]{1,0:T(8,128)S(1)} %slice_select_fusion.1), channel_id=1, source_target_pairs={{0,2},{1,5},{2,0},{3,7},{4,6},{5,1},{6,4},{7,3},{8,10},{9,13},{10,... | collective-permute-start | bytes 890888 | tf_op jit(solution)/shard_map/ppermute | solution.py:315
  35.6 5.7 %shard_map.103 = (bf16[8,512,128]{2,1,0:T(8,128)(2,1)}, bf16[8,512,128]{2,1,0:T(8,128)(2,1)}) custom-call(bf16[8,512,128]{2,1,0:T(8,128)(2,1)} %x_hbm.7, bf16[8,512,128]{2,1,0:T(8,128)(2,1)} %c_hbm.7, bf16[10,512,128]{2,1,0:T(8,128)(2,1)} %get-tuple-element.37.hid_hbm, bf16[10,512,128]{2,1,0:T(8,128)(2,1)} %get-tuple-element.38.bf_hbm, ...), custom_call_target="tpu_custom_call" | custom-call | flops 1207959552 | bytes 2097152 | tf_op jit(solution)/shard_map/pallas_call | solution.py:317
  41.3 0.1 select_add_fusion.1
  41.4 1.6 %collective-permute-start.4 = (f32[290,128]{1,0:T(8,128)S(1)}, f32[290,128]{1,0:T(8,128)S(1)}, u32[]{:S(2)}, u32[]{:S(2)}) collective-permute-start(f32[290,128]{1,0:T(8,128)S(1)} %slice_select_fusion.2), channel_id=1, source_target_pairs={{0,4},{1,3},{2,6},{3,1},{4,0},{5,7},{6,2},{7,5},{8,12},{9,11},{10,... | collective-permute-start | bytes 445448 | tf_op jit(solution)/shard_map/ppermute | solution.py:315
  43.0 3.6 %collective-permute-done.4 = f32[290,128]{1,0:T(8,128)S(1)} collective-permute-done((f32[290,128]{1,0:T(8,128)S(1)}, f32[290,128]{1,0:T(8,128)S(1)}, u32[]{:S(2)}, u32[]{:S(2)}) %collective-permute-start.4) | collective-permute-done | bytes 148512 | tf_op jit(solution)/shard_map/ppermute | solution.py:315
  46.7 2.6 %collective-permute-start.5 = (f32[145,128]{1,0:T(8,128)S(1)}, f32[145,128]{1,0:T(8,128)S(1)}, u32[]{:S(2)}, u32[]{:S(2)}) collective-permute-start(f32[145,128]{1,0:T(8,128)S(1)} %slice_select_fusion.3), channel_id=1, source_target_pairs={{0,8},{1,9},{2,10},{3,11},{4,12},{5,13},{6,14},{7,15},{8,0},{9,1},... | collective-permute-start | bytes 222728 | tf_op jit(solution)/shard_map/ppermute | solution.py:315
  49.3 2.7 %collective-permute-done.5 = f32[145,128]{1,0:T(8,128)S(1)} collective-permute-done((f32[145,128]{1,0:T(8,128)S(1)}, f32[145,128]{1,0:T(8,128)S(1)}, u32[]{:S(2)}, u32[]{:S(2)}) %collective-permute-start.5) | collective-permute-done | bytes 74272 | tf_op jit(solution)/shard_map/ppermute | solution.py:315
  52.0 2.6 %collective-permute-start.6 = (f32[145,128]{1,0:T(8,128)S(1)}, f32[145,128]{1,0:T(8,128)S(1)}, u32[]{:S(2)}, u32[]{:S(2)}) collective-permute-start(f32[145,128]{1,0:T(8,128)S(1)} %select_add_fusion.3), channel_id=1, source_target_pairs={{0,8},{1,9},{2,10},{3,11},{4,12},{5,13},{6,14},{7,15},{8,0},{9,1},... | collective-permute-start | bytes 222728 | tf_op jit(solution)/shard_map/ppermute | solution.py:322
  54.7 2.7 %collective-permute-done.6 = f32[145,128]{1,0:T(8,128)S(1)} collective-permute-done((f32[145,128]{1,0:T(8,128)S(1)}, f32[145,128]{1,0:T(8,128)S(1)}, u32[]{:S(2)}, u32[]{:S(2)}) %collective-permute-start.6) | collective-permute-done | bytes 74272 | tf_op jit(solution)/shard_map/ppermute | solution.py:322
  57.4 1.6 %collective-permute-start.7 = (f32[290,128]{1,0:T(8,128)S(1)}, f32[290,128]{1,0:T(8,128)S(1)}, u32[]{:S(2)}, u32[]{:S(2)}) collective-permute-start(f32[290,128]{1,0:T(8,128)S(1)} %maximum_select_fusion.3), channel_id=1, source_target_pairs={{0,4},{1,3},{2,6},{3,1},{4,0},{5,7},{6,2},{7,5},{8,12},{9,11},{10,... | collective-permute-start | bytes 445448 | tf_op jit(solution)/shard_map/ppermute | solution.py:322
  59.1 4.3 %collective-permute-done.7 = f32[290,128]{1,0:T(8,128)S(1)} collective-permute-done((f32[290,128]{1,0:T(8,128)S(1)}, f32[290,128]{1,0:T(8,128)S(1)}, u32[]{:S(2)}, u32[]{:S(2)}) %collective-permute-start.7) | collective-permute-done | bytes 148512 | tf_op jit(solution)/shard_map/ppermute | solution.py:322
  63.4 0.6 collective-permute-start.8
  64.1 5.7 %shard_map.104 = (bf16[8,512,128]{2,1,0:T(8,128)(2,1)}, bf16[8,512,128]{2,1,0:T(8,128)(2,1)}) custom-call(bf16[8,512,128]{2,1,0:T(8,128)(2,1)} %x_hbm.7, bf16[8,512,128]{2,1,0:T(8,128)(2,1)} %c_hbm.7, bf16[10,512,128]{2,1,0:T(8,128)(2,1)} %get-tuple-element.37.hid_hbm, ...), custom_call_target="tpu_custom_call", output_to_operand_aliasing={{0}: (6, {}), {1}: (7, {})} | custom-call | flops 1207959552 | bytes 2097152 | tf_op jit(solution)/shard_map/pallas_call | solution.py:324
  69.7 0.5 collective-permute-done.8
  70.3 0.1 maximum_select_fusion.1
  70.4 0.1 collective-permute-start.9
  70.4 2.0 %collective-permute-done.9 = f32[1160,128]{1,0:T(8,128)S(1)} collective-permute-done((f32[1160,128]{1,0:T(8,128)S(1)}, f32[1160,128]{1,0:T(8,128)S(1)}, u32[]{:S(2)}, u32[]{:S(2)}) %collective-permute-start.9) | collective-permute-done | bytes 593952 | tf_op jit(solution)/shard_map/ppermute | solution.py:322
  72.4 0.1 maximum_select_fusion
  72.6 1.1 %fusion = (f32[1152,128]{1,0:T(8,128)}, f32[1152,128]{1,0:T(8,128)}) fusion(f32[2320,128]{1,0:T(8,128)S(1)} %maximum_select_fusion), kind=kLoop, calls=%fused_computation.14 | loop fusion | bytes 2359296 | tf_op jit(solution)/shard_map/slice | solution.py:354
  73.7 0.6 slice.68
  (15 shorter events, 0.3 us)
Async XLA Ops:
  2.0 14.0 %collective-permute-start.1 = (bf16[4,512,128]{2,1,0:T(8,128)(2,1)S(1)}, bf16[4,512,128]{2,1,0:T(8,128)(2,1)S(1)}, u32[]{:S(2)}, u32[]{:S(2)}) collective-permute-start(bf16[4,512,128]{2,1,0:T(8,128)(2,1)S(1)} %pad_maximum_fusion.1), channel_id=1, source_target_pairs={{1,0},{2,1},{3,2},{4,3},{5,4},{6,5},{7,6},{8,7},{9,8},{10,9},{11,1... | collective-permute-start | bytes 1572872 | tf_op jit(solution)/shard_map/ppermute | solution.py:341
  3.3 12.6 %collective-permute-start = (bf16[4,512,128]{2,1,0:T(8,128)(2,1)S(1)}, bf16[4,512,128]{2,1,0:T(8,128)(2,1)S(1)}, u32[]{:S(2)}, u32[]{:S(2)}) collective-permute-start(bf16[4,512,128]{2,1,0:T(8,128)(2,1)S(1)} %pad_maximum_fusion), channel_id=1, source_target_pairs={{0,1},{1,2},{2,3},{3,4},{4,5},{5,6},{6,7},{7,8},{8,9},{9,10},{10,1... | collective-permute-start | bytes 1572872 | tf_op jit(solution)/shard_map/ppermute | solution.py:340
  15.9 0.8 %copy-start.1 = (bf16[4,512,128]{2,1,0:T(8,128)(2,1)}, bf16[4,512,128]{2,1,0:T(8,128)(2,1)S(1)}, u32[]{:S(2)}) copy-start(bf16[4,512,128]{2,1,0:T(8,128)(2,1)S(1)} %collective-permute-done.1.after_hbm) | copy-start | bytes 1572868
  16.0 0.9 %copy-start.2 = (bf16[4,512,128]{2,1,0:T(8,128)(2,1)}, bf16[4,512,128]{2,1,0:T(8,128)(2,1)S(1)}, u32[]{:S(2)}) copy-start(bf16[4,512,128]{2,1,0:T(8,128)(2,1)S(1)} %collective-permute-done.before_hbm) | copy-start | bytes 1572868
  26.0 6.6 %copy-start = (f32[2320,128]{1,0:T(8,128)S(1)}, f32[2320,128]{1,0:T(8,128)}, u32[]{:S(2)}) copy-start(f32[2320,128]{1,0:T(8,128)} %get-tuple-element.36) | copy-start | bytes 3563524
  27.4 5.2 %collective-permute-start.2 = (f32[1160,128]{1,0:T(8,128)S(1)}, f32[1160,128]{1,0:T(8,128)S(1)}, u32[]{:S(2)}, u32[]{:S(2)}) collective-permute-start(f32[1160,128]{1,0:T(8,128)S(1)} %slice_select_fusion), channel_id=1, source_target_pairs={{0,1},{1,0},{2,3},{3,2},{4,5},{5,4},{6,7},{7,6},{8,9},{9,8},{10,11... | collective-permute-start | bytes 1781768 | tf_op jit(solution)/shard_map/ppermute | solution.py:315
  32.8 8.5 %collective-permute-start.3 = (f32[580,128]{1,0:T(8,128)S(1)}, f32[580,128]{1,0:T(8,128)S(1)}, u32[]{:S(2)}, u32[]{:S(2)}) collective-permute-start(f32[580,128]{1,0:T(8,128)S(1)} %slice_select_fusion.1), channel_id=1, source_target_pairs={{0,2},{1,5},{2,0},{3,7},{4,6},{5,1},{6,4},{7,3},{8,10},{9,13},{10,... | collective-permute-start | bytes 890888 | tf_op jit(solution)/shard_map/ppermute | solution.py:315
  41.4 5.3 %collective-permute-start.4 = (f32[290,128]{1,0:T(8,128)S(1)}, f32[290,128]{1,0:T(8,128)S(1)}, u32[]{:S(2)}, u32[]{:S(2)}) collective-permute-start(f32[290,128]{1,0:T(8,128)S(1)} %slice_select_fusion.2), channel_id=1, source_target_pairs={{0,4},{1,3},{2,6},{3,1},{4,0},{5,7},{6,2},{7,5},{8,12},{9,11},{10,... | collective-permute-start | bytes 445448 | tf_op jit(solution)/shard_map/ppermute | solution.py:315
  46.7 5.4 %collective-permute-start.5 = (f32[145,128]{1,0:T(8,128)S(1)}, f32[145,128]{1,0:T(8,128)S(1)}, u32[]{:S(2)}, u32[]{:S(2)}) collective-permute-start(f32[145,128]{1,0:T(8,128)S(1)} %slice_select_fusion.3), channel_id=1, source_target_pairs={{0,8},{1,9},{2,10},{3,11},{4,12},{5,13},{6,14},{7,15},{8,0},{9,1},... | collective-permute-start | bytes 222728 | tf_op jit(solution)/shard_map/ppermute | solution.py:315
  52.0 5.4 %collective-permute-start.6 = (f32[145,128]{1,0:T(8,128)S(1)}, f32[145,128]{1,0:T(8,128)S(1)}, u32[]{:S(2)}, u32[]{:S(2)}) collective-permute-start(f32[145,128]{1,0:T(8,128)S(1)} %select_add_fusion.3), channel_id=1, source_target_pairs={{0,8},{1,9},{2,10},{3,11},{4,12},{5,13},{6,14},{7,15},{8,0},{9,1},... | collective-permute-start | bytes 222728 | tf_op jit(solution)/shard_map/ppermute | solution.py:322
  57.4 6.0 %collective-permute-start.7 = (f32[290,128]{1,0:T(8,128)S(1)}, f32[290,128]{1,0:T(8,128)S(1)}, u32[]{:S(2)}, u32[]{:S(2)}) collective-permute-start(f32[290,128]{1,0:T(8,128)S(1)} %maximum_select_fusion.3), channel_id=1, source_target_pairs={{0,4},{1,3},{2,6},{3,1},{4,0},{5,7},{6,2},{7,5},{8,12},{9,11},{10,... | collective-permute-start | bytes 445448 | tf_op jit(solution)/shard_map/ppermute | solution.py:322
  63.4 6.8 %collective-permute-start.8 = (f32[580,128]{1,0:T(8,128)S(1)}, f32[580,128]{1,0:T(8,128)S(1)}, u32[]{:S(2)}, u32[]{:S(2)}) collective-permute-start(f32[580,128]{1,0:T(8,128)S(1)} %maximum_select_fusion.2), channel_id=1, source_target_pairs={{0,2},{1,5},{2,0},{3,7},{4,6},{5,1},{6,4},{7,3},{8,10},{9,13},{10,... | collective-permute-start | bytes 890888 | tf_op jit(solution)/shard_map/ppermute | solution.py:322
  70.4 2.1 %collective-permute-start.9 = (f32[1160,128]{1,0:T(8,128)S(1)}, f32[1160,128]{1,0:T(8,128)S(1)}, u32[]{:S(2)}, u32[]{:S(2)}) collective-permute-start(f32[1160,128]{1,0:T(8,128)S(1)} %maximum_select_fusion.1), channel_id=1, source_target_pairs={{0,1},{1,0},{2,3},{3,2},{4,5},{5,4},{6,7},{7,6},{8,9},{9,8},{10,11... | collective-permute-start | bytes 1781768 | tf_op jit(solution)/shard_map/ppermute | solution.py:322

commit v10 on v9

--- a/solution.py
+++ b/solution.py
@@ -136,11 +136,13 @@
         pltpu.make_async_copy(before_hbm.at[2:4], c_ref.at[0:2], sems.at[3]),
         pltpu.make_async_copy(c_hbm, c_ref.at[2 : count + 2], sems.at[4]),
         pltpu.make_async_copy(after_hbm.at[2:4], c_ref.at[count + 2 : count + 4], sems.at[5]),
-        pltpu.make_async_copy(hida_hbm, hid_ref, sems.at[6]),
-        pltpu.make_async_copy(bfa_hbm, bf_ref, sems.at[7]),
-        pltpu.make_async_copy(hidta_hbm, hidt_ref, sems.at[8]),
-    ]
-    for cp in copies:
+    ]
+    inner = [
+        pltpu.make_async_copy(hida_hbm.at[2:count], hid_ref.at[2:count], sems.at[6]),
+        pltpu.make_async_copy(bfa_hbm.at[2:count], bf_ref.at[2:count], sems.at[7]),
+        pltpu.make_async_copy(hidta_hbm.at[2:count], hidt_ref.at[2:count], sems.at[8]),
+    ]
+    for cp in copies + inner:
         cp.start()
     scale, shift, top, bottom = level_and_edges(idx_ref, lt_ref)
     phase_one, out_row, g1_row, g2_row = row_ops(width, ch, scale, shift, top, bottom, count)
@@ -153,6 +155,8 @@
     for r in (0, 1, count, count + 1):
         carry = phase_one(r, x_ref, c_ref, hid_ref, hidt_ref, bf_ref, k1f, k2b, carry)
     lv0, lv1 = carry
+    for cp in inner:
+        cp.wait()
     for r in (1, 2, 3, count, count + 1, count + 2):
         xt_ref[r] = x_ref[r].astype(jnp.float32).T.astype(xt_ref.dtype)
     for i in (0, 1, count - 2, count - 1):

time: 74.6 us -> 73.6 us (0.987)
  Pallas kernels: 29.3 us -> 28.2 us
    pallas_call x1, Pallas kernels: 9.1 us -> 8.03 us  [section(): pl.pallas_call(functools.partial(edge_kernel, norm), out_shape=(jax.Shape...]
  transfers between devices with their start and end apart: 10 -> 10, of which waited for: 7 -> 7; matrix products, arithmetic and copies ran while one was open for 0% -> 0% of each run, Pallas kernels for 27% -> 28%
where the time goes in v10:
time: 73.6 us; the launch traced here: 73.2 us
  Pallas kernels  28.2 us (38%)
  starting transfers between devices  20 us (27%)
  waiting for transfers between devices  17.5 us (24%)
  local copies, waits for them, and re-layouts  3.86 us (5%)
  other arithmetic  2.09 us (3%)
  between operations  1.47 us (2%)
    pallas_call x2, Pallas kernels, butterfly_sum(): got, state = lax.optimization_barrier((got, riders[count](*state)))  11.3 us
    ppermute x4, starting transfers between devices, butterfly_sum(): got = lax.ppermute(send, 'rows', perm)  10.6 us
    ppermute x4, waiting for transfers between devices, butterfly_sum(): got = lax.ppermute(piece, 'rows', perm)  9.56 us
    pallas_call x1, Pallas kernels, section(): pl.pallas_call(interior_kernel, out_shape=(frame, frame, frame_t, square,...  8.87 us
    pallas_call x1, Pallas kernels, section(): pl.pallas_call(functools.partial(edge_kernel, norm), out_shape=(jax.Shape...  8.03 us
    ppermute x4, waiting for transfers between devices, butterfly_sum(): got = lax.ppermute(send, 'rows', perm)  7.95 us
    ppermute x4, starting transfers between devices, butterfly_sum(): got = lax.ppermute(piece, 'rows', perm)  4.99 us
    ppermute x1, starting transfers between devices, local(): lax.ppermute(jnp.concatenate([inputs[-2:], cotangent[-2:]]), 'rows', up)  3.06 us
  transfers between devices with their start and end apart: 10, of which 7 were waited for; matrix products, arithmetic and copies ran while one was open for 0% of the time, Pallas kernels for 28%

profile of v10, /device:TPU:0, one launch (start us, length us, event | category | flops | bytes accessed | tf_op | source)
XLA Modules:
  0.0 73.2 jit_solution(3633802836203665716)
XLA Ops:
  0.6 1.3 %fusion.1 = (bf16[2,512,128]{2,1,0:T(8,128)(2,1)S(1)}, bf16[2,512,128]{2,1,0:T(8,128)(2,1)S(1)}, bf16[2,512,128]{2,1,0:T(8,128)(2,1)S(1)}, bf16[2,512,128]{2,1,0:T(8,128)(2,1)S(1)}) fusion(bf16[8,512,128]{2,1,0:T(8,128)(2,1)} %x_hbm.7, bf16[8,512,128]{2,1,0:T(8,128)(2,1)} %c_hbm.7), kind=kLoop, calls=%fused_computation.15 | loop fusion | bytes 2097152 | tf_op jit(solution)/shard_map/slice | solution.py:345
  2.0 1.3 %collective-permute-start.1 = (bf16[4,512,128]{2,1,0:T(8,128)(2,1)S(1)}, bf16[4,512,128]{2,1,0:T(8,128)(2,1)S(1)}, u32[]{:S(2)}, u32[]{:S(2)}) collective-permute-start(bf16[4,512,128]{2,1,0:T(8,128)(2,1)S(1)} %pad_maximum_fusion.1), channel_id=1, source_target_pairs={{1,0},{2,1},{3,2},{4,3},{5,4},{6,5},{7,6},{8,7},{9,8},{10,9},{11,1... | collective-permute-start | bytes 1572872 | tf_op jit(solution)/shard_map/ppermute | solution.py:345
  3.3 3.1 %collective-permute-start = (bf16[4,512,128]{2,1,0:T(8,128)(2,1)S(1)}, bf16[4,512,128]{2,1,0:T(8,128)(2,1)S(1)}, u32[]{:S(2)}, u32[]{:S(2)}) collective-permute-start(bf16[4,512,128]{2,1,0:T(8,128)(2,1)S(1)} %pad_maximum_fusion), channel_id=1, source_target_pairs={{0,1},{1,2},{2,3},{3,4},{4,5},{5,6},{6,7},{7,8},{8,9},{9,10},{10,1... | collective-permute-start | bytes 1572872 | tf_op jit(solution)/shard_map/ppermute | solution.py:344
  7.0 8.9 %shard_map.101 = (bf16[10,512,128]{2,1,0:T(8,128)(2,1)}, bf16[10,512,128]{2,1,0:T(8,128)(2,1)}, bf16[10,128,512]{2,1,0:T(8,128)(2,1)}, f32[384,384]{1,0:T(8,128)...) custom-call(s32[1]{0:T(128)S(6)} %copy.15.idx_ref, ...), custom_call_target="tpu_custom_call" | custom-call | flops 3925868544 | bytes 4194304 | tf_op jit(solution)/shard_map/pallas_call | solution.py:223
  15.9 0.0 copy-start.1
  16.0 0.8 %copy-done.1 = bf16[4,512,128]{2,1,0:T(8,128)(2,1)} copy-done((bf16[4,512,128]{2,1,0:T(8,128)(2,1)}, bf16[4,512,128]{2,1,0:T(8,128)(2,1)S(1)}, u32[]{:S(2)}) %copy-start.1) | copy-done | bytes 524312
  16.7 0.2 copy-done.2
  16.9 8.0 %shard_map.102 = (f32[2320,128]{1,0:T(8,128)}, bf16[10,512,128]{2,1,0:T(8,128)(2,1)}, bf16[10,512,128]{2,1,0:T(8,128)(2,1)}) custom-call(s32[1]{0:T(128)S(6)} %copy.15.idx_ref, f32[16,2,128]{2,1,0:T(2,128)} %lt_ref.3, bf16[8,512,128]{2,1,0:T(8,128)(2,1)} %x_hbm.7, bf16[8,512,128]{2,1,0:T(8,128)(2,1)} %c_hbm.7, bf16[4,512,128]{2,1,0:T(8,128)(2,1)} %copy-done.2, ...), custom_call_target="tpu_custom_call" | custom-call | flops 2113929216 | bytes 5242880 | tf_op jit(solution)/shard_map/pallas_call | solution.py:241
  25.0 1.4 %slice_select_fusion = f32[1160,128]{1,0:T(8,128)S(1)} fusion(f32[2320,128]{1,0:T(8,128)} %get-tuple-element.36, pred[]{:T(512)S(6)} %eq.35), kind=kLoop, calls=%fused_computation.3 | loop fusion | flops 148480 | bytes 1781761 | tf_op jit(solution)/shard_map/jit(_where)/select_n | solution.py:318
  26.4 3.5 %collective-permute-start.2 = (f32[1160,128]{1,0:T(8,128)S(1)}, f32[1160,128]{1,0:T(8,128)S(1)}, u32[]{:S(2)}, u32[]{:S(2)}) collective-permute-start(f32[1160,128]{1,0:T(8,128)S(1)} %slice_select_fusion), channel_id=1, source_target_pairs={{0,1},{1,0},{2,3},{3,2},{4,5},{5,4},{6,7},{7,6},{8,9},{9,8},{10,11... | collective-permute-start | bytes 1781768 | tf_op jit(solution)/shard_map/ppermute | solution.py:319
  29.9 1.6 %collective-permute-done.2 = f32[1160,128]{1,0:T(8,128)S(1)} collective-permute-done((f32[1160,128]{1,0:T(8,128)S(1)}, f32[1160,128]{1,0:T(8,128)S(1)}, u32[]{:S(2)}, u32[]{:S(2)}) %collective-permute-start.2) | collective-permute-done | bytes 593952 | tf_op jit(solution)/shard_map/ppermute | solution.py:319
  31.5 0.1 select_add_fusion
  31.7 2.8 %collective-permute-start.3 = (f32[580,128]{1,0:T(8,128)S(1)}, f32[580,128]{1,0:T(8,128)S(1)}, u32[]{:S(2)}, u32[]{:S(2)}) collective-permute-start(f32[580,128]{1,0:T(8,128)S(1)} %slice_select_fusion.1), channel_id=1, source_target_pairs={{0,2},{1,5},{2,0},{3,7},{4,6},{5,1},{6,4},{7,3},{8,10},{9,13},{10,... | collective-permute-start | bytes 890888 | tf_op jit(solution)/shard_map/ppermute | solution.py:319
  34.5 5.7 %shard_map.103 = (bf16[8,512,128]{2,1,0:T(8,128)(2,1)}, bf16[8,512,128]{2,1,0:T(8,128)(2,1)}) custom-call(bf16[8,512,128]{2,1,0:T(8,128)(2,1)} %x_hbm.7, bf16[8,512,128]{2,1,0:T(8,128)(2,1)} %c_hbm.7, bf16[10,512,128]{2,1,0:T(8,128)(2,1)} %get-tuple-element.37.hid_hbm, bf16[10,512,128]{2,1,0:T(8,128)(2,1)} %get-tuple-element.38.bf_hbm, ...), custom_call_target="tpu_custom_call" | custom-call | flops 1207959552 | bytes 2097152 | tf_op jit(solution)/shard_map/pallas_call | solution.py:321
  40.2 0.1 select_add_fusion.1
  40.3 1.6 %collective-permute-start.4 = (f32[290,128]{1,0:T(8,128)S(1)}, f32[290,128]{1,0:T(8,128)S(1)}, u32[]{:S(2)}, u32[]{:S(2)}) collective-permute-start(f32[290,128]{1,0:T(8,128)S(1)} %slice_select_fusion.2), channel_id=1, source_target_pairs={{0,4},{1,3},{2,6},{3,1},{4,0},{5,7},{6,2},{7,5},{8,12},{9,11},{10,... | collective-permute-start | bytes 445448 | tf_op jit(solution)/shard_map/ppermute | solution.py:319
  41.9 3.6 %collective-permute-done.4 = f32[290,128]{1,0:T(8,128)S(1)} collective-permute-done((f32[290,128]{1,0:T(8,128)S(1)}, f32[290,128]{1,0:T(8,128)S(1)}, u32[]{:S(2)}, u32[]{:S(2)}) %collective-permute-start.4) | collective-permute-done | bytes 148512 | tf_op jit(solution)/shard_map/ppermute | solution.py:319
  45.6 2.7 %collective-permute-start.5 = (f32[145,128]{1,0:T(8,128)S(1)}, f32[145,128]{1,0:T(8,128)S(1)}, u32[]{:S(2)}, u32[]{:S(2)}) collective-permute-start(f32[145,128]{1,0:T(8,128)S(1)} %slice_select_fusion.3), channel_id=1, source_target_pairs={{0,8},{1,9},{2,10},{3,11},{4,12},{5,13},{6,14},{7,15},{8,0},{9,1},... | collective-permute-start | bytes 222728 | tf_op jit(solution)/shard_map/ppermute | solution.py:319
  48.3 2.7 %collective-permute-done.5 = f32[145,128]{1,0:T(8,128)S(1)} collective-permute-done((f32[145,128]{1,0:T(8,128)S(1)}, f32[145,128]{1,0:T(8,128)S(1)}, u32[]{:S(2)}, u32[]{:S(2)}) %collective-permute-start.5) | collective-permute-done | bytes 74272 | tf_op jit(solution)/shard_map/ppermute | solution.py:319
  51.0 2.7 %collective-permute-start.6 = (f32[145,128]{1,0:T(8,128)S(1)}, f32[145,128]{1,0:T(8,128)S(1)}, u32[]{:S(2)}, u32[]{:S(2)}) collective-permute-start(f32[145,128]{1,0:T(8,128)S(1)} %select_add_fusion.3), channel_id=1, source_target_pairs={{0,8},{1,9},{2,10},{3,11},{4,12},{5,13},{6,14},{7,15},{8,0},{9,1},... | collective-permute-start | bytes 222728 | tf_op jit(solution)/shard_map/ppermute | solution.py:326
  53.6 2.7 %collective-permute-done.6 = f32[145,128]{1,0:T(8,128)S(1)} collective-permute-done((f32[145,128]{1,0:T(8,128)S(1)}, f32[145,128]{1,0:T(8,128)S(1)}, u32[]{:S(2)}, u32[]{:S(2)}) %collective-permute-start.6) | collective-permute-done | bytes 74272 | tf_op jit(solution)/shard_map/ppermute | solution.py:326
  56.4 1.6 %collective-permute-start.7 = (f32[290,128]{1,0:T(8,128)S(1)}, f32[290,128]{1,0:T(8,128)S(1)}, u32[]{:S(2)}, u32[]{:S(2)}) collective-permute-start(f32[290,128]{1,0:T(8,128)S(1)} %maximum_select_fusion.3), channel_id=1, source_target_pairs={{0,4},{1,3},{2,6},{3,1},{4,0},{5,7},{6,2},{7,5},{8,12},{9,11},{10,... | collective-permute-start | bytes 445448 | tf_op jit(solution)/shard_map/ppermute | solution.py:326
  58.0 4.3 %collective-permute-done.7 = f32[290,128]{1,0:T(8,128)S(1)} collective-permute-done((f32[290,128]{1,0:T(8,128)S(1)}, f32[290,128]{1,0:T(8,128)S(1)}, u32[]{:S(2)}, u32[]{:S(2)}) %collective-permute-start.7) | collective-permute-done | bytes 148512 | tf_op jit(solution)/shard_map/ppermute | solution.py:326
  62.4 0.6 collective-permute-start.8
  63.0 5.7 %shard_map.104 = (bf16[8,512,128]{2,1,0:T(8,128)(2,1)}, bf16[8,512,128]{2,1,0:T(8,128)(2,1)}) custom-call(bf16[8,512,128]{2,1,0:T(8,128)(2,1)} %x_hbm.7, bf16[8,512,128]{2,1,0:T(8,128)(2,1)} %c_hbm.7, bf16[10,512,128]{2,1,0:T(8,128)(2,1)} %get-tuple-element.37.hid_hbm, ...), custom_call_target="tpu_custom_call", output_to_operand_aliasing={{0}: (6, {}), {1}: (7, {})} | custom-call | flops 1207959552 | bytes 2097152 | tf_op jit(solution)/shard_map/pallas_call | solution.py:328
  68.7 0.5 collective-permute-done.8
  69.2 0.1 maximum_select_fusion.1
  69.3 0.1 collective-permute-start.9
  69.4 2.0 %collective-permute-done.9 = f32[1160,128]{1,0:T(8,128)S(1)} collective-permute-done((f32[1160,128]{1,0:T(8,128)S(1)}, f32[1160,128]{1,0:T(8,128)S(1)}, u32[]{:S(2)}, u32[]{:S(2)}) %collective-permute-start.9) | collective-permute-done | bytes 593952 | tf_op jit(solution)/shard_map/ppermute | solution.py:326
  71.4 0.1 maximum_select_fusion
  71.5 1.1 %fusion = (f32[1152,128]{1,0:T(8,128)}, f32[1152,128]{1,0:T(8,128)}) fusion(f32[2320,128]{1,0:T(8,128)S(1)} %maximum_select_fusion), kind=kLoop, calls=%fused_computation.14 | loop fusion | bytes 2359296 | tf_op jit(solution)/shard_map/slice | solution.py:358
  72.6 0.6 slice.68
  (15 shorter events, 0.3 us)
Async XLA Ops:
  2.0 14.0 %collective-permute-start.1 = (bf16[4,512,128]{2,1,0:T(8,128)(2,1)S(1)}, bf16[4,512,128]{2,1,0:T(8,128)(2,1)S(1)}, u32[]{:S(2)}, u32[]{:S(2)}) collective-permute-start(bf16[4,512,128]{2,1,0:T(8,128)(2,1)S(1)} %pad_maximum_fusion.1), channel_id=1, source_target_pairs={{1,0},{2,1},{3,2},{4,3},{5,4},{6,5},{7,6},{8,7},{9,8},{10,9},{11,1... | collective-permute-start | bytes 1572872 | tf_op jit(solution)/shard_map/ppermute | solution.py:345
  3.3 12.6 %collective-permute-start = (bf16[4,512,128]{2,1,0:T(8,128)(2,1)S(1)}, bf16[4,512,128]{2,1,0:T(8,128)(2,1)S(1)}, u32[]{:S(2)}, u32[]{:S(2)}) collective-permute-start(bf16[4,512,128]{2,1,0:T(8,128)(2,1)S(1)} %pad_maximum_fusion), channel_id=1, source_target_pairs={{0,1},{1,2},{2,3},{3,4},{4,5},{5,6},{6,7},{7,8},{8,9},{9,10},{10,1... | collective-permute-start | bytes 1572872 | tf_op jit(solution)/shard_map/ppermute | solution.py:344
  15.9 0.8 %copy-start.1 = (bf16[4,512,128]{2,1,0:T(8,128)(2,1)}, bf16[4,512,128]{2,1,0:T(8,128)(2,1)S(1)}, u32[]{:S(2)}) copy-start(bf16[4,512,128]{2,1,0:T(8,128)(2,1)S(1)} %collective-permute-done.1.after_hbm) | copy-start | bytes 1572868
  16.0 0.9 %copy-start.2 = (bf16[4,512,128]{2,1,0:T(8,128)(2,1)}, bf16[4,512,128]{2,1,0:T(8,128)(2,1)S(1)}, u32[]{:S(2)}) copy-start(bf16[4,512,128]{2,1,0:T(8,128)(2,1)S(1)} %collective-permute-done.before_hbm) | copy-start | bytes 1572868
  25.0 6.6 %copy-start = (f32[2320,128]{1,0:T(8,128)S(1)}, f32[2320,128]{1,0:T(8,128)}, u32[]{:S(2)}) copy-start(f32[2320,128]{1,0:T(8,128)} %get-tuple-element.36) | copy-start | bytes 3563524
  26.4 5.2 %collective-permute-start.2 = (f32[1160,128]{1,0:T(8,128)S(1)}, f32[1160,128]{1,0:T(8,128)S(1)}, u32[]{:S(2)}, u32[]{:S(2)}) collective-permute-start(f32[1160,128]{1,0:T(8,128)S(1)} %slice_select_fusion), channel_id=1, source_target_pairs={{0,1},{1,0},{2,3},{3,2},{4,5},{5,4},{6,7},{7,6},{8,9},{9,8},{10,11... | collective-permute-start | bytes 1781768 | tf_op jit(solution)/shard_map/ppermute | solution.py:319
  31.7 8.5 %collective-permute-start.3 = (f32[580,128]{1,0:T(8,128)S(1)}, f32[580,128]{1,0:T(8,128)S(1)}, u32[]{:S(2)}, u32[]{:S(2)}) collective-permute-start(f32[580,128]{1,0:T(8,128)S(1)} %slice_select_fusion.1), channel_id=1, source_target_pairs={{0,2},{1,5},{2,0},{3,7},{4,6},{5,1},{6,4},{7,3},{8,10},{9,13},{10,... | collective-permute-start | bytes 890888 | tf_op jit(solution)/shard_map/ppermute | solution.py:319
  40.3 5.3 %collective-permute-start.4 = (f32[290,128]{1,0:T(8,128)S(1)}, f32[290,128]{1,0:T(8,128)S(1)}, u32[]{:S(2)}, u32[]{:S(2)}) collective-permute-start(f32[290,128]{1,0:T(8,128)S(1)} %slice_select_fusion.2), channel_id=1, source_target_pairs={{0,4},{1,3},{2,6},{3,1},{4,0},{5,7},{6,2},{7,5},{8,12},{9,11},{10,... | collective-permute-start | bytes 445448 | tf_op jit(solution)/shard_map/ppermute | solution.py:319
  45.6 5.4 %collective-permute-start.5 = (f32[145,128]{1,0:T(8,128)S(1)}, f32[145,128]{1,0:T(8,128)S(1)}, u32[]{:S(2)}, u32[]{:S(2)}) collective-permute-start(f32[145,128]{1,0:T(8,128)S(1)} %slice_select_fusion.3), channel_id=1, source_target_pairs={{0,8},{1,9},{2,10},{3,11},{4,12},{5,13},{6,14},{7,15},{8,0},{9,1},... | collective-permute-start | bytes 222728 | tf_op jit(solution)/shard_map/ppermute | solution.py:319
  51.0 5.4 %collective-permute-start.6 = (f32[145,128]{1,0:T(8,128)S(1)}, f32[145,128]{1,0:T(8,128)S(1)}, u32[]{:S(2)}, u32[]{:S(2)}) collective-permute-start(f32[145,128]{1,0:T(8,128)S(1)} %select_add_fusion.3), channel_id=1, source_target_pairs={{0,8},{1,9},{2,10},{3,11},{4,12},{5,13},{6,14},{7,15},{8,0},{9,1},... | collective-permute-start | bytes 222728 | tf_op jit(solution)/shard_map/ppermute | solution.py:326
  56.4 6.0 %collective-permute-start.7 = (f32[290,128]{1,0:T(8,128)S(1)}, f32[290,128]{1,0:T(8,128)S(1)}, u32[]{:S(2)}, u32[]{:S(2)}) collective-permute-start(f32[290,128]{1,0:T(8,128)S(1)} %maximum_select_fusion.3), channel_id=1, source_target_pairs={{0,4},{1,3},{2,6},{3,1},{4,0},{5,7},{6,2},{7,5},{8,12},{9,11},{10,... | collective-permute-start | bytes 445448 | tf_op jit(solution)/shard_map/ppermute | solution.py:326
  62.4 6.8 %collective-permute-start.8 = (f32[580,128]{1,0:T(8,128)S(1)}, f32[580,128]{1,0:T(8,128)S(1)}, u32[]{:S(2)}, u32[]{:S(2)}) collective-permute-start(f32[580,128]{1,0:T(8,128)S(1)} %maximum_select_fusion.2), channel_id=1, source_target_pairs={{0,2},{1,5},{2,0},{3,7},{4,6},{5,1},{6,4},{7,3},{8,10},{9,13},{10,... | collective-permute-start | bytes 890888 | tf_op jit(solution)/shard_map/ppermute | solution.py:326
  69.3 2.1 %collective-permute-start.9 = (f32[1160,128]{1,0:T(8,128)S(1)}, f32[1160,128]{1,0:T(8,128)S(1)}, u32[]{:S(2)}, u32[]{:S(2)}) collective-permute-start(f32[1160,128]{1,0:T(8,128)S(1)} %maximum_select_fusion.1), channel_id=1, source_target_pairs={{0,1},{1,0},{2,3},{3,2},{4,5},{5,4},{6,7},{7,6},{8,9},{9,8},{10,11... | collective-permute-start | bytes 1781768 | tf_op jit(solution)/shard_map/ppermute | solution.py:326

commit v11 on v10

--- a/solution.py
+++ b/solution.py
@@ -59,7 +59,7 @@
         hs = jnp.concatenate([hidt_ref[i], hidt_ref[i + 1], hidt_ref[i + 2]], axis=0)
         acc2[...] += jnp.dot(hs, shifted(c_ref[i + 2]), preferred_element_type=jnp.float32)
 
-    return phase_one, out_row, g1_row, g2_row
+    return phase_one, out_row, g1_row, g2_row, conv_row
 
 
 def level_and_edges(idx_ref, lt_ref):
@@ -90,7 +90,7 @@
             k2b[rows, cols] = k2_ref[flip].astype(jnp.float32).T.astype(k2b.dtype)
             k1b[rows, cols] = k1_ref[flip].astype(jnp.float32).T.astype(k1b.dtype)
     scale, shift, top, bottom = level_and_edges(idx_ref, lt_ref)
-    phase_one, out_row, g1_row, g2_row = row_ops(width, ch, scale, shift, top, bottom, count)
+    phase_one, out_row, g1_row, g2_row, _ = row_ops(width, ch, scale, shift, top, bottom, count)
     for cp in copies:
         cp.wait()
 
@@ -145,7 +145,7 @@
     for cp in copies + inner:
         cp.start()
     scale, shift, top, bottom = level_and_edges(idx_ref, lt_ref)
-    phase_one, out_row, g1_row, g2_row = row_ops(width, ch, scale, shift, top, bottom, count)
+    phase_one, out_row, g1_row, g2_row, _ = row_ops(width, ch, scale, shift, top, bottom, count)
     acc1[...] = acc1a_ref[...]
     acc2[...] = acc2a_ref[...]
     for cp in copies:
@@ -191,11 +191,15 @@
     for cp in copies:
         cp.start()
     one = jnp.ones((1, ch), jnp.float32)
-    out_row = row_ops(width, ch, one, one, True, True, n)[1]
-    for cp in copies:
-        cp.wait()
+    conv_row = row_ops(width, ch, one, one, True, True, n)[4]
+    copies[0].wait()
+    copies[2].wait()
     for i in range(n):
-        out_row(i, x_ref, c_ref, hid_ref, bf_ref, k2f, k1b, o_ref, g_ref)
+        o_ref[i] = (x_ref[i + 2].astype(jnp.float32) + conv_row(hid_ref, i, k2f)).astype(o_ref.dtype)
+    copies[1].wait()
+    copies[3].wait()
+    for i in range(n):
+        g_ref[i] = (c_ref[i + 2].astype(jnp.float32) + conv_row(bf_ref, i, k1b)).astype(g_ref.dtype)
     stores = [
         pltpu.make_async_copy(o_ref, out_hbm.at[first_row : first_row + n], sems.at[4]),
         pltpu.make_async_copy(g_ref, ig_hbm.at[first_row : first_row + n], sems.at[5]),
@@ -257,7 +261,7 @@
             flops=14 * unit, transcendentals=4 * width * ch, bytes_accessed=10 * count * width * ch
         ),
     )(level_index, level_table, inputs, cotangent, before, after, hid, bf, hidt, acc1, acc2, lv, k1f, k2b)
-    step = count // 2 if count % 2 == 0 else count
+    step = 2 if count % 2 == 0 else count
     whole = jax.ShapeDtypeStruct((count, width, ch), jnp.bfloat16)
     chunks = []
     for first_row in range(0, count, step):
@@ -352,7 +356,12 @@
         first_kernel, second_kernel,
     )
     steps = 2 * (size.bit_length() - 1)
-    places = [1, steps - 2] if len(chunks) == 2 and steps >= 4 else list(range(len(chunks)))
+    if len(chunks) == 4 and steps >= 8:
+        places = [1, 2, steps - 3, steps - 2]
+    elif len(chunks) == 2 and steps >= 4:
+        places = [1, steps - 2]
+    else:
+        places = list(range(len(chunks)))
     total, (outputs, input_grad) = butterfly_sum(packed, dict(zip(places, chunks)))
     first_sum = total[: 9 * ch].reshape(9, ch, ch)
     second_sum = total[9 * ch : 18 * ch].reshape(9, ch, ch)

time: 73.6 us -> 75.5 us (1.026)
  Pallas kernels: 28.2 us -> 34.1 us
  starting transfers between devices: 20 us -> 17.6 us
  waiting for transfers between devices: 17.5 us -> 15.9 us
    pallas_call x2 -> x4, Pallas kernels: 11.3 us -> 17.2 us  [butterfly_sum(): got, state = lax.optimization_barrier((got, riders[count](*state)))]
    ppermute x4, starting transfers between devices: 4.99 us -> 3.34 us  [butterfly_sum(): got = lax.ppermute(piece, 'rows', perm)]
    ppermute x4, waiting for transfers between devices: 7.95 us -> 6.65 us  [butterfly_sum(): got = lax.ppermute(send, 'rows', perm)]
  transfers between devices with their start and end apart: 10 -> 10, of which waited for: 7 -> 7; matrix products, arithmetic and copies ran while one was open for 0% -> 0% of each run, Pallas kernels for 28% -> 35%
where the time goes in v11:
time: 75.5 us; the launch traced here: 75.1 us
  Pallas kernels  34.1 us (45%)
  starting transfers between devices  17.6 us (23%)
  waiting for transfers between devices  15.9 us (21%)
  local copies, waits for them, and re-layouts  3.86 us (5%)
  other arithmetic  2.09 us (3%)
  between operations  1.5 us (2%)
    pallas_call x4, Pallas kernels, butterfly_sum(): got, state = lax.optimization_barrier((got, riders[count](*state)))  17.2 us
    ppermute x4, starting transfers between devices, butterfly_sum(): got = lax.ppermute(send, 'rows', perm)  9.94 us
    ppermute x4, waiting for transfers between devices, butterfly_sum(): got = lax.ppermute(piece, 'rows', perm)  9.23 us
    pallas_call x1, Pallas kernels, section(): pl.pallas_call(interior_kernel, out_shape=(frame, frame, frame_t, square,...  8.87 us
    pallas_call x1, Pallas kernels, section(): pl.pallas_call(functools.partial(edge_kernel, norm), out_shape=(jax.Shape...  8.02 us
    ppermute x4, waiting for transfers between devices, butterfly_sum(): got = lax.ppermute(send, 'rows', perm)  6.65 us
    ppermute x4, starting transfers between devices, butterfly_sum(): got = lax.ppermute(piece, 'rows', perm)  3.34 us
    ppermute x1, starting transfers between devices, local(): lax.ppermute(jnp.concatenate([inputs[-2:], cotangent[-2:]]), 'rows', up)  3.06 us
  transfers between devices with their start and end apart: 10, of which 7 were waited for; matrix products, arithmetic and copies ran while one was open for 0% of the time, Pallas kernels for 35%

profile of v11, /device:TPU:0, one launch (start us, length us, event | category | flops | bytes accessed | tf_op | source)
XLA Modules:
  0.0 75.1 jit_solution(5979591540795431180)
XLA Ops:
  0.6 1.3 %fusion.1 = (bf16[2,512,128]{2,1,0:T(8,128)(2,1)S(1)}, bf16[2,512,128]{2,1,0:T(8,128)(2,1)S(1)}, bf16[2,512,128]{2,1,0:T(8,128)(2,1)S(1)}, bf16[2,512,128]{2,1,0:T(8,128)(2,1)S(1)}) fusion(bf16[8,512,128]{2,1,0:T(8,128)(2,1)} %x_hbm.11, bf16[8,512,128]{2,1,0:T(8,128)(2,1)} %c_hbm.11), kind=kLoop, calls=%fused_computation.15 | loop fusion | bytes 2097152 | tf_op jit(solution)/shard_map/slice | solution.py:349
  2.0 1.3 %collective-permute-start.1 = (bf16[4,512,128]{2,1,0:T(8,128)(2,1)S(1)}, bf16[4,512,128]{2,1,0:T(8,128)(2,1)S(1)}, u32[]{:S(2)}, u32[]{:S(2)}) collective-permute-start(bf16[4,512,128]{2,1,0:T(8,128)(2,1)S(1)} %pad_maximum_fusion.1), channel_id=1, source_target_pairs={{1,0},{2,1},{3,2},{4,3},{5,4},{6,5},{7,6},{8,7},{9,8},{10,9},{11,1... | collective-permute-start | bytes 1572872 | tf_op jit(solution)/shard_map/ppermute | solution.py:349
  3.3 3.1 %collective-permute-start = (bf16[4,512,128]{2,1,0:T(8,128)(2,1)S(1)}, bf16[4,512,128]{2,1,0:T(8,128)(2,1)S(1)}, u32[]{:S(2)}, u32[]{:S(2)}) collective-permute-start(bf16[4,512,128]{2,1,0:T(8,128)(2,1)S(1)} %pad_maximum_fusion), channel_id=1, source_target_pairs={{0,1},{1,2},{2,3},{3,4},{4,5},{5,6},{6,7},{7,8},{8,9},{9,10},{10,1... | collective-permute-start | bytes 1572872 | tf_op jit(solution)/shard_map/ppermute | solution.py:348
  7.0 8.9 %shard_map.101 = (bf16[10,512,128]{2,1,0:T(8,128)(2,1)}, bf16[10,512,128]{2,1,0:T(8,128)(2,1)}, bf16[10,128,512]{2,1,0:T(8,128)(2,1)}, f32[384,384]{1,0:T(8,128)...) custom-call(s32[1]{0:T(128)S(6)} %copy.23.idx_ref, ...), custom_call_target="tpu_custom_call" | custom-call | flops 3925868544 | bytes 4194304 | tf_op jit(solution)/shard_map/pallas_call | solution.py:227
  16.0 0.8 %copy-done.1 = bf16[4,512,128]{2,1,0:T(8,128)(2,1)} copy-done((bf16[4,512,128]{2,1,0:T(8,128)(2,1)}, bf16[4,512,128]{2,1,0:T(8,128)(2,1)S(1)}, u32[]{:S(2)}) %copy-start.1) | copy-done | bytes 524312
  16.7 0.2 copy-done.2
  16.9 8.0 %shard_map.102 = (f32[2320,128]{1,0:T(8,128)}, bf16[10,512,128]{2,1,0:T(8,128)(2,1)}, bf16[10,512,128]{2,1,0:T(8,128)(2,1)}) custom-call(s32[1]{0:T(128)S(6)} %copy.23.idx_ref, f32[16,2,128]{2,1,0:T(2,128)} %lt_ref.3, bf16[8,512,128]{2,1,0:T(8,128)(2,1)} %x_hbm.11, bf16[8,512,128]{2,1,0:T(8,128)(2,1)} %c_hbm.11, bf16[4,512,128]{2,1,0:T(8,128)(2,1)} %copy-done.2, ...), custom_call_target="tpu_custom_call" | custom-call | flops 2113929216 | bytes 5242880 | tf_op jit(solution)/shard_map/pallas_call | solution.py:245
  24.9 1.4 %slice_select_fusion = f32[1160,128]{1,0:T(8,128)S(1)} fusion(f32[2320,128]{1,0:T(8,128)} %get-tuple-element.46, pred[]{:T(512)S(6)} %eq.35), kind=kLoop, calls=%fused_computation.3 | loop fusion | flops 148480 | bytes 1781761 | tf_op jit(solution)/shard_map/jit(_where)/select_n | solution.py:322
  26.4 3.5 %collective-permute-start.2 = (f32[1160,128]{1,0:T(8,128)S(1)}, f32[1160,128]{1,0:T(8,128)S(1)}, u32[]{:S(2)}, u32[]{:S(2)}) collective-permute-start(f32[1160,128]{1,0:T(8,128)S(1)} %slice_select_fusion), channel_id=1, source_target_pairs={{0,1},{1,0},{2,3},{3,2},{4,5},{5,4},{6,7},{7,6},{8,9},{9,8},{10,11... | collective-permute-start | bytes 1781768 | tf_op jit(solution)/shard_map/ppermute | solution.py:323
  29.9 1.6 %collective-permute-done.2 = f32[1160,128]{1,0:T(8,128)S(1)} collective-permute-done((f32[1160,128]{1,0:T(8,128)S(1)}, f32[1160,128]{1,0:T(8,128)S(1)}, u32[]{:S(2)}, u32[]{:S(2)}) %collective-permute-start.2) | collective-permute-done | bytes 593952 | tf_op jit(solution)/shard_map/ppermute | solution.py:323
  31.5 0.1 select_add_fusion
  31.7 2.8 %collective-permute-start.3 = (f32[580,128]{1,0:T(8,128)S(1)}, f32[580,128]{1,0:T(8,128)S(1)}, u32[]{:S(2)}, u32[]{:S(2)}) collective-permute-start(f32[580,128]{1,0:T(8,128)S(1)} %slice_select_fusion.1), channel_id=1, source_target_pairs={{0,2},{1,5},{2,0},{3,7},{4,6},{5,1},{6,4},{7,3},{8,10},{9,13},{10,... | collective-permute-start | bytes 890888 | tf_op jit(solution)/shard_map/ppermute | solution.py:323
  34.5 4.3 %shard_map.103 = (bf16[8,512,128]{2,1,0:T(8,128)(2,1)}, bf16[8,512,128]{2,1,0:T(8,128)(2,1)}) custom-call(bf16[8,512,128]{2,1,0:T(8,128)(2,1)} %x_hbm.11, bf16[8,512,128]{2,1,0:T(8,128)(2,1)} %c_hbm.11, bf16[10,512,128]{2,1,0:T(8,128)(2,1)} %get-tuple-element.47.hid_hbm, bf16[10,512,128]{2,1,0:T(8,128)(2,1)} %get-tuple-element.48.bf_hbm, ...), custom_call_target="tpu_custom_call" | custom-call | flops 603979776 | bytes 1048576 | tf_op jit(solution)/shard_map/pallas_call | solution.py:325
  38.8 0.4 collective-permute-done.3
  39.4 1.6 %collective-permute-start.4 = (f32[290,128]{1,0:T(8,128)S(1)}, f32[290,128]{1,0:T(8,128)S(1)}, u32[]{:S(2)}, u32[]{:S(2)}) collective-permute-start(f32[290,128]{1,0:T(8,128)S(1)} %slice_select_fusion.2), channel_id=1, source_target_pairs={{0,4},{1,3},{2,6},{3,1},{4,0},{5,7},{6,2},{7,5},{8,12},{9,11},{10,... | collective-permute-start | bytes 445448 | tf_op jit(solution)/shard_map/ppermute | solution.py:323
  41.0 4.3 %shard_map.104 = (bf16[8,512,128]{2,1,0:T(8,128)(2,1)}, bf16[8,512,128]{2,1,0:T(8,128)(2,1)}) custom-call(bf16[8,512,128]{2,1,0:T(8,128)(2,1)} %x_hbm.11, bf16[8,512,128]{2,1,0:T(8,128)(2,1)} %c_hbm.11, bf16[10,512,128]{2,1,0:T(8,128)(2,1)} %get-tuple-element.47.hid_hbm, ...), custom_call_target="tpu_custom_call", output_to_operand_aliasing={{0}: (6, {}), {1}: (7, {})} | custom-call | flops 603979776 | bytes 1048576 | tf_op jit(solution)/shard_map/pallas_call | solution.py:325
  45.4 2.0 %collective-permute-start.5 = (f32[145,128]{1,0:T(8,128)S(1)}, f32[145,128]{1,0:T(8,128)S(1)}, u32[]{:S(2)}, u32[]{:S(2)}) collective-permute-start(f32[145,128]{1,0:T(8,128)S(1)} %slice_select_fusion.3), channel_id=1, source_target_pairs={{0,8},{1,9},{2,10},{3,11},{4,12},{5,13},{6,14},{7,15},{8,0},{9,1},... | collective-permute-start | bytes 222728 | tf_op jit(solution)/shard_map/ppermute | solution.py:323
  47.3 4.6 %collective-permute-done.5 = f32[145,128]{1,0:T(8,128)S(1)} collective-permute-done((f32[145,128]{1,0:T(8,128)S(1)}, f32[145,128]{1,0:T(8,128)S(1)}, u32[]{:S(2)}, u32[]{:S(2)}) %collective-permute-start.5) | collective-permute-done | bytes 74272 | tf_op jit(solution)/shard_map/ppermute | solution.py:323
  51.9 0.9 %collective-permute-start.6 = (f32[145,128]{1,0:T(8,128)S(1)}, f32[145,128]{1,0:T(8,128)S(1)}, u32[]{:S(2)}, u32[]{:S(2)}) collective-permute-start(f32[145,128]{1,0:T(8,128)S(1)} %select_add_fusion.3), channel_id=1, source_target_pairs={{0,8},{1,9},{2,10},{3,11},{4,12},{5,13},{6,14},{7,15},{8,0},{9,1},... | collective-permute-start | bytes 222728 | tf_op jit(solution)/shard_map/ppermute | solution.py:330
  52.8 4.8 %collective-permute-done.6 = f32[145,128]{1,0:T(8,128)S(1)} collective-permute-done((f32[145,128]{1,0:T(8,128)S(1)}, f32[145,128]{1,0:T(8,128)S(1)}, u32[]{:S(2)}, u32[]{:S(2)}) %collective-permute-start.6) | collective-permute-done | bytes 74272 | tf_op jit(solution)/shard_map/ppermute | solution.py:330
  57.7 0.1 collective-permute-start.7
  57.8 4.3 %shard_map.105 = (bf16[8,512,128]{2,1,0:T(8,128)(2,1)}, bf16[8,512,128]{2,1,0:T(8,128)(2,1)}) custom-call(bf16[8,512,128]{2,1,0:T(8,128)(2,1)} %x_hbm.11, bf16[8,512,128]{2,1,0:T(8,128)(2,1)} %c_hbm.11, bf16[10,512,128]{2,1,0:T(8,128)(2,1)} %get-tuple-element.47.hid_hbm, ...), custom_call_target="tpu_custom_call", output_to_operand_aliasing={{0}: (6, {}), {1}: (7, {})} | custom-call | flops 603979776 | bytes 1048576 | tf_op jit(solution)/shard_map/pallas_call | solution.py:332
  62.1 1.9 %collective-permute-done.7 = f32[290,128]{1,0:T(8,128)S(1)} collective-permute-done((f32[290,128]{1,0:T(8,128)S(1)}, f32[290,128]{1,0:T(8,128)S(1)}, u32[]{:S(2)}, u32[]{:S(2)}) %collective-permute-start.7) | collective-permute-done | bytes 148512 | tf_op jit(solution)/shard_map/ppermute | solution.py:330
  64.1 2.3 %collective-permute-start.8 = (f32[580,128]{1,0:T(8,128)S(1)}, f32[580,128]{1,0:T(8,128)S(1)}, u32[]{:S(2)}, u32[]{:S(2)}) collective-permute-start(f32[580,128]{1,0:T(8,128)S(1)} %maximum_select_fusion.2), channel_id=1, source_target_pairs={{0,2},{1,5},{2,0},{3,7},{4,6},{5,1},{6,4},{7,3},{8,10},{9,13},{10,... | collective-permute-start | bytes 890888 | tf_op jit(solution)/shard_map/ppermute | solution.py:330
  66.3 4.3 %shard_map.106 = (bf16[8,512,128]{2,1,0:T(8,128)(2,1)}, bf16[8,512,128]{2,1,0:T(8,128)(2,1)}) custom-call(bf16[8,512,128]{2,1,0:T(8,128)(2,1)} %x_hbm.11, bf16[8,512,128]{2,1,0:T(8,128)(2,1)} %c_hbm.11, bf16[10,512,128]{2,1,0:T(8,128)(2,1)} %get-tuple-element.47.hid_hbm, ...), custom_call_target="tpu_custom_call", output_to_operand_aliasing={{0}: (6, {}), {1}: (7, {})} | custom-call | flops 603979776 | bytes 1048576 | tf_op jit(solution)/shard_map/pallas_call | solution.py:332
  70.7 0.4 collective-permute-done.8
  71.1 0.1 maximum_select_fusion.1
  71.2 0.1 collective-permute-start.9
  71.3 2.0 %collective-permute-done.9 = f32[1160,128]{1,0:T(8,128)S(1)} collective-permute-done((f32[1160,128]{1,0:T(8,128)S(1)}, f32[1160,128]{1,0:T(8,128)S(1)}, u32[]{:S(2)}, u32[]{:S(2)}) %collective-permute-start.9) | collective-permute-done | bytes 593952 | tf_op jit(solution)/shard_map/ppermute | solution.py:330
  73.3 0.1 maximum_select_fusion
  73.4 1.1 %fusion = (f32[1152,128]{1,0:T(8,128)}, f32[1152,128]{1,0:T(8,128)}) fusion(f32[2320,128]{1,0:T(8,128)S(1)} %maximum_select_fusion), kind=kLoop, calls=%fused_computation.14 | loop fusion | bytes 2359296 | tf_op jit(solution)/shard_map/slice | solution.py:367
  74.5 0.6 slice.68
  (17 shorter events, 0.4 us)
Async XLA Ops:
  2.0 14.0 %collective-permute-start.1 = (bf16[4,512,128]{2,1,0:T(8,128)(2,1)S(1)}, bf16[4,512,128]{2,1,0:T(8,128)(2,1)S(1)}, u32[]{:S(2)}, u32[]{:S(2)}) collective-permute-start(bf16[4,512,128]{2,1,0:T(8,128)(2,1)S(1)} %pad_maximum_fusion.1), channel_id=1, source_target_pairs={{1,0},{2,1},{3,2},{4,3},{5,4},{6,5},{7,6},{8,7},{9,8},{10,9},{11,1... | collective-permute-start | bytes 1572872 | tf_op jit(solution)/shard_map/ppermute | solution.py:349
  3.3 12.6 %collective-permute-start = (bf16[4,512,128]{2,1,0:T(8,128)(2,1)S(1)}, bf16[4,512,128]{2,1,0:T(8,128)(2,1)S(1)}, u32[]{:S(2)}, u32[]{:S(2)}) collective-permute-start(bf16[4,512,128]{2,1,0:T(8,128)(2,1)S(1)} %pad_maximum_fusion), channel_id=1, source_target_pairs={{0,1},{1,2},{2,3},{3,4},{4,5},{5,6},{6,7},{7,8},{8,9},{9,10},{10,1... | collective-permute-start | bytes 1572872 | tf_op jit(solution)/shard_map/ppermute | solution.py:348
  15.9 0.8 %copy-start.1 = (bf16[4,512,128]{2,1,0:T(8,128)(2,1)}, bf16[4,512,128]{2,1,0:T(8,128)(2,1)S(1)}, u32[]{:S(2)}) copy-start(bf16[4,512,128]{2,1,0:T(8,128)(2,1)S(1)} %collective-permute-done.1.after_hbm) | copy-start | bytes 1572868
  16.0 0.9 %copy-start.2 = (bf16[4,512,128]{2,1,0:T(8,128)(2,1)}, bf16[4,512,128]{2,1,0:T(8,128)(2,1)S(1)}, u32[]{:S(2)}) copy-start(bf16[4,512,128]{2,1,0:T(8,128)(2,1)S(1)} %collective-permute-done.before_hbm) | copy-start | bytes 1572868
  24.9 6.6 %copy-start = (f32[2320,128]{1,0:T(8,128)S(1)}, f32[2320,128]{1,0:T(8,128)}, u32[]{:S(2)}) copy-start(f32[2320,128]{1,0:T(8,128)} %get-tuple-element.46) | copy-start | bytes 3563524
  26.4 5.2 %collective-permute-start.2 = (f32[1160,128]{1,0:T(8,128)S(1)}, f32[1160,128]{1,0:T(8,128)S(1)}, u32[]{:S(2)}, u32[]{:S(2)}) collective-permute-start(f32[1160,128]{1,0:T(8,128)S(1)} %slice_select_fusion), channel_id=1, source_target_pairs={{0,1},{1,0},{2,3},{3,2},{4,5},{5,4},{6,7},{7,6},{8,9},{9,8},{10,11... | collective-permute-start | bytes 1781768 | tf_op jit(solution)/shard_map/ppermute | solution.py:323
  31.7 7.6 %collective-permute-start.3 = (f32[580,128]{1,0:T(8,128)S(1)}, f32[580,128]{1,0:T(8,128)S(1)}, u32[]{:S(2)}, u32[]{:S(2)}) collective-permute-start(f32[580,128]{1,0:T(8,128)S(1)} %slice_select_fusion.1), channel_id=1, source_target_pairs={{0,2},{1,5},{2,0},{3,7},{4,6},{5,1},{6,4},{7,3},{8,10},{9,13},{10,... | collective-permute-start | bytes 890888 | tf_op jit(solution)/shard_map/ppermute | solution.py:323
  39.4 5.9 %collective-permute-start.4 = (f32[290,128]{1,0:T(8,128)S(1)}, f32[290,128]{1,0:T(8,128)S(1)}, u32[]{:S(2)}, u32[]{:S(2)}) collective-permute-start(f32[290,128]{1,0:T(8,128)S(1)} %slice_select_fusion.2), channel_id=1, source_target_pairs={{0,4},{1,3},{2,6},{3,1},{4,0},{5,7},{6,2},{7,5},{8,12},{9,11},{10,... | collective-permute-start | bytes 445448 | tf_op jit(solution)/shard_map/ppermute | solution.py:323
  45.4 6.5 %collective-permute-start.5 = (f32[145,128]{1,0:T(8,128)S(1)}, f32[145,128]{1,0:T(8,128)S(1)}, u32[]{:S(2)}, u32[]{:S(2)}) collective-permute-start(f32[145,128]{1,0:T(8,128)S(1)} %slice_select_fusion.3), channel_id=1, source_target_pairs={{0,8},{1,9},{2,10},{3,11},{4,12},{5,13},{6,14},{7,15},{8,0},{9,1},... | collective-permute-start | bytes 222728 | tf_op jit(solution)/shard_map/ppermute | solution.py:323
  51.9 5.8 %collective-permute-start.6 = (f32[145,128]{1,0:T(8,128)S(1)}, f32[145,128]{1,0:T(8,128)S(1)}, u32[]{:S(2)}, u32[]{:S(2)}) collective-permute-start(f32[145,128]{1,0:T(8,128)S(1)} %select_add_fusion.3), channel_id=1, source_target_pairs={{0,8},{1,9},{2,10},{3,11},{4,12},{5,13},{6,14},{7,15},{8,0},{9,1},... | collective-permute-start | bytes 222728 | tf_op jit(solution)/shard_map/ppermute | solution.py:330
  57.7 6.3 %collective-permute-start.7 = (f32[290,128]{1,0:T(8,128)S(1)}, f32[290,128]{1,0:T(8,128)S(1)}, u32[]{:S(2)}, u32[]{:S(2)}) collective-permute-start(f32[290,128]{1,0:T(8,128)S(1)} %maximum_select_fusion.3), channel_id=1, source_target_pairs={{0,4},{1,3},{2,6},{3,1},{4,0},{5,7},{6,2},{7,5},{8,12},{9,11},{10,... | collective-permute-start | bytes 445448 | tf_op jit(solution)/shard_map/ppermute | solution.py:330
  64.1 7.0 %collective-permute-start.8 = (f32[580,128]{1,0:T(8,128)S(1)}, f32[580,128]{1,0:T(8,128)S(1)}, u32[]{:S(2)}, u32[]{:S(2)}) collective-permute-start(f32[580,128]{1,0:T(8,128)S(1)} %maximum_select_fusion.2), channel_id=1, source_target_pairs={{0,2},{1,5},{2,0},{3,7},{4,6},{5,1},{6,4},{7,3},{8,10},{9,13},{10,... | collective-permute-start | bytes 890888 | tf_op jit(solution)/shard_map/ppermute | solution.py:330
  71.2 2.1 %collective-permute-start.9 = (f32[1160,128]{1,0:T(8,128)S(1)}, f32[1160,128]{1,0:T(8,128)S(1)}, u32[]{:S(2)}, u32[]{:S(2)}) collective-permute-start(f32[1160,128]{1,0:T(8,128)S(1)} %maximum_select_fusion.1), channel_id=1, source_target_pairs={{0,1},{1,0},{2,3},{3,2},{4,5},{5,4},{6,7},{7,6},{8,9},{9,8},{10,11... | collective-permute-start | bytes 1781768 | tf_op jit(solution)/shard_map/ppermute | solution.py:330

commit v12 on v11

--- a/solution.py
+++ b/solution.py
@@ -196,18 +196,16 @@
     copies[2].wait()
     for i in range(n):
         o_ref[i] = (x_ref[i + 2].astype(jnp.float32) + conv_row(hid_ref, i, k2f)).astype(o_ref.dtype)
+    store_out = pltpu.make_async_copy(o_ref, out_hbm.at[first_row : first_row + n], sems.at[4])
+    store_out.start()
     copies[1].wait()
     copies[3].wait()
     for i in range(n):
         g_ref[i] = (c_ref[i + 2].astype(jnp.float32) + conv_row(bf_ref, i, k1b)).astype(g_ref.dtype)
-    stores = [
-        pltpu.make_async_copy(o_ref, out_hbm.at[first_row : first_row + n], sems.at[4]),
-        pltpu.make_async_copy(g_ref, ig_hbm.at[first_row : first_row + n], sems.at[5]),
-    ]
-    for cp in stores:
-        cp.start()
-    for cp in stores:
-        cp.wait()
+    store_ig = pltpu.make_async_copy(g_ref, ig_hbm.at[first_row : first_row + n], sems.at[5])
+    store_ig.start()
+    store_out.wait()
+    store_ig.wait()
 
 
 def section(norm, packed_rows, level_index, level_table, inputs, cotangent, before_fn, k1, k2):
@@ -261,7 +259,7 @@
             flops=14 * unit, transcendentals=4 * width * ch, bytes_accessed=10 * count * width * ch
         ),
     )(level_index, level_table, inputs, cotangent, before, after, hid, bf, hidt, acc1, acc2, lv, k1f, k2b)
-    step = 2 if count % 2 == 0 else count
+    step = count // 2 if count % 2 == 0 else count
     whole = jax.ShapeDtypeStruct((count, width, ch), jnp.bfloat16)
     chunks = []
     for first_row in range(0, count, step):
@@ -356,12 +354,7 @@
         first_kernel, second_kernel,
     )
     steps = 2 * (size.bit_length() - 1)
-    if len(chunks) == 4 and steps >= 8:
-        places = [1, 2, steps - 3, steps - 2]
-    elif len(chunks) == 2 and steps >= 4:
-        places = [1, steps - 2]
-    else:
-        places = list(range(len(chunks)))
+    places = [1, steps - 2] if len(chunks) == 2 and steps >= 4 else list(range(len(chunks)))
     total, (outputs, input_grad) = butterfly_sum(packed, dict(zip(places, chunks)))
     first_sum = total[: 9 * ch].reshape(9, ch, ch)
     second_sum = total[9 * ch : 18 * ch].reshape(9, ch, ch)

time: 75.5 us -> 73.5 us (0.974)
  Pallas kernels: 34.1 us -> 28.1 us
  starting transfers between devices: 17.6 us -> 20.1 us
  waiting for transfers between devices: 15.9 us -> 17.5 us
    pallas_call x4 -> x2, Pallas kernels: 17.2 us -> 11.2 us  [butterfly_sum(): got, state = lax.optimization_barrier((got, riders[count](*state)))]
    ppermute x4, starting transfers between devices: 3.34 us -> 5.13 us  [butterfly_sum(): got = lax.ppermute(piece, 'rows', perm)]
    ppermute x4, waiting for transfers between devices: 6.65 us -> 7.95 us  [butterfly_sum(): got = lax.ppermute(send, 'rows', perm)]
  transfers between devices with their start and end apart: 10 -> 10, of which waited for: 7 -> 7; matrix products, arithmetic and copies ran while one was open for 0% -> 0% of each run, Pallas kernels for 35% -> 27%
where the time goes in v12:
time: 73.5 us; the launch traced here: 73.1 us
  Pallas kernels  28.1 us (38%)
  starting transfers between devices  20.1 us (27%)
  waiting for transfers between devices  17.5 us (24%)
  local copies, waits for them, and re-layouts  3.86 us (5%)
  other arithmetic  2.09 us (3%)
  between operations  1.47 us (2%)
    pallas_call x2, Pallas kernels, butterfly_sum(): got, state = lax.optimization_barrier((got, riders[count](*state)))  11.2 us
    ppermute x4, starting transfers between devices, butterfly_sum(): got = lax.ppermute(send, 'rows', perm)  10.6 us
    ppermute x4, waiting for transfers between devices, butterfly_sum(): got = lax.ppermute(piece, 'rows', perm)  9.5 us
    pallas_call x1, Pallas kernels, section(): pl.pallas_call(interior_kernel, out_shape=(frame, frame, frame_t, square,...  8.87 us
    pallas_call x1, Pallas kernels, section(): pl.pallas_call(functools.partial(edge_kernel, norm), out_shape=(jax.Shape...  8.03 us
    ppermute x4, waiting for transfers between devices, butterfly_sum(): got = lax.ppermute(send, 'rows', perm)  7.95 us
    ppermute x4, starting transfers between devices, butterfly_sum(): got = lax.ppermute(piece, 'rows', perm)  5.13 us
    ppermute x1, starting transfers between devices, local(): lax.ppermute(jnp.concatenate([inputs[-2:], cotangent[-2:]]), 'rows', up)  3.06 us
  transfers between devices with their start and end apart: 10, of which 7 were waited for; matrix products, arithmetic and copies ran while one was open for 0% of the time, Pallas kernels for 27%

profile of v12, /device:TPU:0, one launch (start us, length us, event | category | flops | bytes accessed | tf_op | source)
XLA Modules:
  0.0 73.1 jit_solution(3125112620115882064)
XLA Ops:
  0.6 1.3 %fusion.1 = (bf16[2,512,128]{2,1,0:T(8,128)(2,1)S(1)}, bf16[2,512,128]{2,1,0:T(8,128)(2,1)S(1)}, bf16[2,512,128]{2,1,0:T(8,128)(2,1)S(1)}, bf16[2,512,128]{2,1,0:T(8,128)(2,1)S(1)}) fusion(bf16[8,512,128]{2,1,0:T(8,128)(2,1)} %x_hbm.7, bf16[8,512,128]{2,1,0:T(8,128)(2,1)} %c_hbm.7), kind=kLoop, calls=%fused_computation.15 | loop fusion | bytes 2097152 | tf_op jit(solution)/shard_map/slice | solution.py:347
  2.0 1.3 %collective-permute-start.1 = (bf16[4,512,128]{2,1,0:T(8,128)(2,1)S(1)}, bf16[4,512,128]{2,1,0:T(8,128)(2,1)S(1)}, u32[]{:S(2)}, u32[]{:S(2)}) collective-permute-start(bf16[4,512,128]{2,1,0:T(8,128)(2,1)S(1)} %pad_maximum_fusion.1), channel_id=1, source_target_pairs={{1,0},{2,1},{3,2},{4,3},{5,4},{6,5},{7,6},{8,7},{9,8},{10,9},{11,1... | collective-permute-start | bytes 1572872 | tf_op jit(solution)/shard_map/ppermute | solution.py:347
  3.3 3.1 %collective-permute-start = (bf16[4,512,128]{2,1,0:T(8,128)(2,1)S(1)}, bf16[4,512,128]{2,1,0:T(8,128)(2,1)S(1)}, u32[]{:S(2)}, u32[]{:S(2)}) collective-permute-start(bf16[4,512,128]{2,1,0:T(8,128)(2,1)S(1)} %pad_maximum_fusion), channel_id=1, source_target_pairs={{0,1},{1,2},{2,3},{3,4},{4,5},{5,6},{6,7},{7,8},{8,9},{9,10},{10,1... | collective-permute-start | bytes 1572872 | tf_op jit(solution)/shard_map/ppermute | solution.py:346
  7.0 8.9 %shard_map.101 = (bf16[10,512,128]{2,1,0:T(8,128)(2,1)}, bf16[10,512,128]{2,1,0:T(8,128)(2,1)}, bf16[10,128,512]{2,1,0:T(8,128)(2,1)}, f32[384,384]{1,0:T(8,128)...) custom-call(s32[1]{0:T(128)S(6)} %copy.15.idx_ref, ...), custom_call_target="tpu_custom_call" | custom-call | flops 3925868544 | bytes 4194304 | tf_op jit(solution)/shard_map/pallas_call | solution.py:225
  15.9 0.0 copy-start.1
  16.0 0.8 %copy-done.1 = bf16[4,512,128]{2,1,0:T(8,128)(2,1)} copy-done((bf16[4,512,128]{2,1,0:T(8,128)(2,1)}, bf16[4,512,128]{2,1,0:T(8,128)(2,1)S(1)}, u32[]{:S(2)}) %copy-start.1) | copy-done | bytes 524312
  16.7 0.2 copy-done.2
  16.9 8.0 %shard_map.102 = (f32[2320,128]{1,0:T(8,128)}, bf16[10,512,128]{2,1,0:T(8,128)(2,1)}, bf16[10,512,128]{2,1,0:T(8,128)(2,1)}) custom-call(s32[1]{0:T(128)S(6)} %copy.15.idx_ref, f32[16,2,128]{2,1,0:T(2,128)} %lt_ref.3, bf16[8,512,128]{2,1,0:T(8,128)(2,1)} %x_hbm.7, bf16[8,512,128]{2,1,0:T(8,128)(2,1)} %c_hbm.7, bf16[4,512,128]{2,1,0:T(8,128)(2,1)} %copy-done.2, ...), custom_call_target="tpu_custom_call" | custom-call | flops 2113929216 | bytes 5242880 | tf_op jit(solution)/shard_map/pallas_call | solution.py:243
  25.0 1.4 %slice_select_fusion = f32[1160,128]{1,0:T(8,128)S(1)} fusion(f32[2320,128]{1,0:T(8,128)} %get-tuple-element.36, pred[]{:T(512)S(6)} %eq.35), kind=kLoop, calls=%fused_computation.3 | loop fusion | flops 148480 | bytes 1781761 | tf_op jit(solution)/shard_map/jit(_where)/select_n | solution.py:320
  26.4 3.5 %collective-permute-start.2 = (f32[1160,128]{1,0:T(8,128)S(1)}, f32[1160,128]{1,0:T(8,128)S(1)}, u32[]{:S(2)}, u32[]{:S(2)}) collective-permute-start(f32[1160,128]{1,0:T(8,128)S(1)} %slice_select_fusion), channel_id=1, source_target_pairs={{0,1},{1,0},{2,3},{3,2},{4,5},{5,4},{6,7},{7,6},{8,9},{9,8},{10,11... | collective-permute-start | bytes 1781768 | tf_op jit(solution)/shard_map/ppermute | solution.py:321
  29.9 1.6 %collective-permute-done.2 = f32[1160,128]{1,0:T(8,128)S(1)} collective-permute-done((f32[1160,128]{1,0:T(8,128)S(1)}, f32[1160,128]{1,0:T(8,128)S(1)}, u32[]{:S(2)}, u32[]{:S(2)}) %collective-permute-start.2) | collective-permute-done | bytes 593952 | tf_op jit(solution)/shard_map/ppermute | solution.py:321
  31.5 0.1 select_add_fusion
  31.7 2.8 %collective-permute-start.3 = (f32[580,128]{1,0:T(8,128)S(1)}, f32[580,128]{1,0:T(8,128)S(1)}, u32[]{:S(2)}, u32[]{:S(2)}) collective-permute-start(f32[580,128]{1,0:T(8,128)S(1)} %slice_select_fusion.1), channel_id=1, source_target_pairs={{0,2},{1,5},{2,0},{3,7},{4,6},{5,1},{6,4},{7,3},{8,10},{9,13},{10,... | collective-permute-start | bytes 890888 | tf_op jit(solution)/shard_map/ppermute | solution.py:321
  34.5 5.6 %shard_map.103 = (bf16[8,512,128]{2,1,0:T(8,128)(2,1)}, bf16[8,512,128]{2,1,0:T(8,128)(2,1)}) custom-call(bf16[8,512,128]{2,1,0:T(8,128)(2,1)} %x_hbm.7, bf16[8,512,128]{2,1,0:T(8,128)(2,1)} %c_hbm.7, bf16[10,512,128]{2,1,0:T(8,128)(2,1)} %get-tuple-element.37.hid_hbm, bf16[10,512,128]{2,1,0:T(8,128)(2,1)} %get-tuple-element.38.bf_hbm, ...), custom_call_target="tpu_custom_call" | custom-call | flops 1207959552 | bytes 2097152 | tf_op jit(solution)/shard_map/pallas_call | solution.py:323
  40.1 0.1 select_add_fusion.1
  40.2 1.6 %collective-permute-start.4 = (f32[290,128]{1,0:T(8,128)S(1)}, f32[290,128]{1,0:T(8,128)S(1)}, u32[]{:S(2)}, u32[]{:S(2)}) collective-permute-start(f32[290,128]{1,0:T(8,128)S(1)} %slice_select_fusion.2), channel_id=1, source_target_pairs={{0,4},{1,3},{2,6},{3,1},{4,0},{5,7},{6,2},{7,5},{8,12},{9,11},{10,... | collective-permute-start | bytes 445448 | tf_op jit(solution)/shard_map/ppermute | solution.py:321
  41.9 3.6 %collective-permute-done.4 = f32[290,128]{1,0:T(8,128)S(1)} collective-permute-done((f32[290,128]{1,0:T(8,128)S(1)}, f32[290,128]{1,0:T(8,128)S(1)}, u32[]{:S(2)}, u32[]{:S(2)}) %collective-permute-start.4) | collective-permute-done | bytes 148512 | tf_op jit(solution)/shard_map/ppermute | solution.py:321
  45.5 2.7 %collective-permute-start.5 = (f32[145,128]{1,0:T(8,128)S(1)}, f32[145,128]{1,0:T(8,128)S(1)}, u32[]{:S(2)}, u32[]{:S(2)}) collective-permute-start(f32[145,128]{1,0:T(8,128)S(1)} %slice_select_fusion.3), channel_id=1, source_target_pairs={{0,8},{1,9},{2,10},{3,11},{4,12},{5,13},{6,14},{7,15},{8,0},{9,1},... | collective-permute-start | bytes 222728 | tf_op jit(solution)/shard_map/ppermute | solution.py:321
  48.2 2.7 %collective-permute-done.5 = f32[145,128]{1,0:T(8,128)S(1)} collective-permute-done((f32[145,128]{1,0:T(8,128)S(1)}, f32[145,128]{1,0:T(8,128)S(1)}, u32[]{:S(2)}, u32[]{:S(2)}) %collective-permute-start.5) | collective-permute-done | bytes 74272 | tf_op jit(solution)/shard_map/ppermute | solution.py:321
  50.9 2.7 %collective-permute-start.6 = (f32[145,128]{1,0:T(8,128)S(1)}, f32[145,128]{1,0:T(8,128)S(1)}, u32[]{:S(2)}, u32[]{:S(2)}) collective-permute-start(f32[145,128]{1,0:T(8,128)S(1)} %select_add_fusion.3), channel_id=1, source_target_pairs={{0,8},{1,9},{2,10},{3,11},{4,12},{5,13},{6,14},{7,15},{8,0},{9,1},... | collective-permute-start | bytes 222728 | tf_op jit(solution)/shard_map/ppermute | solution.py:328
  53.6 2.7 %collective-permute-done.6 = f32[145,128]{1,0:T(8,128)S(1)} collective-permute-done((f32[145,128]{1,0:T(8,128)S(1)}, f32[145,128]{1,0:T(8,128)S(1)}, u32[]{:S(2)}, u32[]{:S(2)}) %collective-permute-start.6) | collective-permute-done | bytes 74272 | tf_op jit(solution)/shard_map/ppermute | solution.py:328
  56.3 1.6 %collective-permute-start.7 = (f32[290,128]{1,0:T(8,128)S(1)}, f32[290,128]{1,0:T(8,128)S(1)}, u32[]{:S(2)}, u32[]{:S(2)}) collective-permute-start(f32[290,128]{1,0:T(8,128)S(1)} %maximum_select_fusion.3), channel_id=1, source_target_pairs={{0,4},{1,3},{2,6},{3,1},{4,0},{5,7},{6,2},{7,5},{8,12},{9,11},{10,... | collective-permute-start | bytes 445448 | tf_op jit(solution)/shard_map/ppermute | solution.py:328
  57.9 4.3 %collective-permute-done.7 = f32[290,128]{1,0:T(8,128)S(1)} collective-permute-done((f32[290,128]{1,0:T(8,128)S(1)}, f32[290,128]{1,0:T(8,128)S(1)}, u32[]{:S(2)}, u32[]{:S(2)}) %collective-permute-start.7) | collective-permute-done | bytes 148512 | tf_op jit(solution)/shard_map/ppermute | solution.py:328
  62.3 0.8 %collective-permute-start.8 = (f32[580,128]{1,0:T(8,128)S(1)}, f32[580,128]{1,0:T(8,128)S(1)}, u32[]{:S(2)}, u32[]{:S(2)}) collective-permute-start(f32[580,128]{1,0:T(8,128)S(1)} %maximum_select_fusion.2), channel_id=1, source_target_pairs={{0,2},{1,5},{2,0},{3,7},{4,6},{5,1},{6,4},{7,3},{8,10},{9,13},{10,... | collective-permute-start | bytes 890888 | tf_op jit(solution)/shard_map/ppermute | solution.py:328
  63.1 5.6 %shard_map.104 = (bf16[8,512,128]{2,1,0:T(8,128)(2,1)}, bf16[8,512,128]{2,1,0:T(8,128)(2,1)}) custom-call(bf16[8,512,128]{2,1,0:T(8,128)(2,1)} %x_hbm.7, bf16[8,512,128]{2,1,0:T(8,128)(2,1)} %c_hbm.7, bf16[10,512,128]{2,1,0:T(8,128)(2,1)} %get-tuple-element.37.hid_hbm, ...), custom_call_target="tpu_custom_call", output_to_operand_aliasing={{0}: (6, {}), {1}: (7, {})} | custom-call | flops 1207959552 | bytes 2097152 | tf_op jit(solution)/shard_map/pallas_call | solution.py:330
  68.7 0.5 collective-permute-done.8
  69.2 0.1 maximum_select_fusion.1
  69.2 0.1 collective-permute-start.9
  69.3 2.0 %collective-permute-done.9 = f32[1160,128]{1,0:T(8,128)S(1)} collective-permute-done((f32[1160,128]{1,0:T(8,128)S(1)}, f32[1160,128]{1,0:T(8,128)S(1)}, u32[]{:S(2)}, u32[]{:S(2)}) %collective-permute-start.9) | collective-permute-done | bytes 593952 | tf_op jit(solution)/shard_map/ppermute | solution.py:328
  71.3 0.1 maximum_select_fusion
  71.5 1.1 %fusion = (f32[1152,128]{1,0:T(8,128)}, f32[1152,128]{1,0:T(8,128)}) fusion(f32[2320,128]{1,0:T(8,128)S(1)} %maximum_select_fusion), kind=kLoop, calls=%fused_computation.14 | loop fusion | bytes 2359296 | tf_op jit(solution)/shard_map/slice | solution.py:360
  72.5 0.6 slice.68
  (15 shorter events, 0.3 us)
Async XLA Ops:
  2.0 14.0 %collective-permute-start.1 = (bf16[4,512,128]{2,1,0:T(8,128)(2,1)S(1)}, bf16[4,512,128]{2,1,0:T(8,128)(2,1)S(1)}, u32[]{:S(2)}, u32[]{:S(2)}) collective-permute-start(bf16[4,512,128]{2,1,0:T(8,128)(2,1)S(1)} %pad_maximum_fusion.1), channel_id=1, source_target_pairs={{1,0},{2,1},{3,2},{4,3},{5,4},{6,5},{7,6},{8,7},{9,8},{10,9},{11,1... | collective-permute-start | bytes 1572872 | tf_op jit(solution)/shard_map/ppermute | solution.py:347
  3.3 12.6 %collective-permute-start = (bf16[4,512,128]{2,1,0:T(8,128)(2,1)S(1)}, bf16[4,512,128]{2,1,0:T(8,128)(2,1)S(1)}, u32[]{:S(2)}, u32[]{:S(2)}) collective-permute-start(bf16[4,512,128]{2,1,0:T(8,128)(2,1)S(1)} %pad_maximum_fusion), channel_id=1, source_target_pairs={{0,1},{1,2},{2,3},{3,4},{4,5},{5,6},{6,7},{7,8},{8,9},{9,10},{10,1... | collective-permute-start | bytes 1572872 | tf_op jit(solution)/shard_map/ppermute | solution.py:346
  15.9 0.8 %copy-start.1 = (bf16[4,512,128]{2,1,0:T(8,128)(2,1)}, bf16[4,512,128]{2,1,0:T(8,128)(2,1)S(1)}, u32[]{:S(2)}) copy-start(bf16[4,512,128]{2,1,0:T(8,128)(2,1)S(1)} %collective-permute-done.1.after_hbm) | copy-start | bytes 1572868
  16.0 0.9 %copy-start.2 = (bf16[4,512,128]{2,1,0:T(8,128)(2,1)}, bf16[4,512,128]{2,1,0:T(8,128)(2,1)S(1)}, u32[]{:S(2)}) copy-start(bf16[4,512,128]{2,1,0:T(8,128)(2,1)S(1)} %collective-permute-done.before_hbm) | copy-start | bytes 1572868
  25.0 6.6 %copy-start = (f32[2320,128]{1,0:T(8,128)S(1)}, f32[2320,128]{1,0:T(8,128)}, u32[]{:S(2)}) copy-start(f32[2320,128]{1,0:T(8,128)} %get-tuple-element.36) | copy-start | bytes 3563524
  26.4 5.2 %collective-permute-start.2 = (f32[1160,128]{1,0:T(8,128)S(1)}, f32[1160,128]{1,0:T(8,128)S(1)}, u32[]{:S(2)}, u32[]{:S(2)}) collective-permute-start(f32[1160,128]{1,0:T(8,128)S(1)} %slice_select_fusion), channel_id=1, source_target_pairs={{0,1},{1,0},{2,3},{3,2},{4,5},{5,4},{6,7},{7,6},{8,9},{9,8},{10,11... | collective-permute-start | bytes 1781768 | tf_op jit(solution)/shard_map/ppermute | solution.py:321
  31.7 8.4 %collective-permute-start.3 = (f32[580,128]{1,0:T(8,128)S(1)}, f32[580,128]{1,0:T(8,128)S(1)}, u32[]{:S(2)}, u32[]{:S(2)}) collective-permute-start(f32[580,128]{1,0:T(8,128)S(1)} %slice_select_fusion.1), channel_id=1, source_target_pairs={{0,2},{1,5},{2,0},{3,7},{4,6},{5,1},{6,4},{7,3},{8,10},{9,13},{10,... | collective-permute-start | bytes 890888 | tf_op jit(solution)/shard_map/ppermute | solution.py:321
  40.2 5.3 %collective-permute-start.4 = (f32[290,128]{1,0:T(8,128)S(1)}, f32[290,128]{1,0:T(8,128)S(1)}, u32[]{:S(2)}, u32[]{:S(2)}) collective-permute-start(f32[290,128]{1,0:T(8,128)S(1)} %slice_select_fusion.2), channel_id=1, source_target_pairs={{0,4},{1,3},{2,6},{3,1},{4,0},{5,7},{6,2},{7,5},{8,12},{9,11},{10,... | collective-permute-start | bytes 445448 | tf_op jit(solution)/shard_map/ppermute | solution.py:321
  45.5 5.4 %collective-permute-start.5 = (f32[145,128]{1,0:T(8,128)S(1)}, f32[145,128]{1,0:T(8,128)S(1)}, u32[]{:S(2)}, u32[]{:S(2)}) collective-permute-start(f32[145,128]{1,0:T(8,128)S(1)} %slice_select_fusion.3), channel_id=1, source_target_pairs={{0,8},{1,9},{2,10},{3,11},{4,12},{5,13},{6,14},{7,15},{8,0},{9,1},... | collective-permute-start | bytes 222728 | tf_op jit(solution)/shard_map/ppermute | solution.py:321
  50.9 5.4 %collective-permute-start.6 = (f32[145,128]{1,0:T(8,128)S(1)}, f32[145,128]{1,0:T(8,128)S(1)}, u32[]{:S(2)}, u32[]{:S(2)}) collective-permute-start(f32[145,128]{1,0:T(8,128)S(1)} %select_add_fusion.3), channel_id=1, source_target_pairs={{0,8},{1,9},{2,10},{3,11},{4,12},{5,13},{6,14},{7,15},{8,0},{9,1},... | collective-permute-start | bytes 222728 | tf_op jit(solution)/shard_map/ppermute | solution.py:328
  56.3 6.0 %collective-permute-start.7 = (f32[290,128]{1,0:T(8,128)S(1)}, f32[290,128]{1,0:T(8,128)S(1)}, u32[]{:S(2)}, u32[]{:S(2)}) collective-permute-start(f32[290,128]{1,0:T(8,128)S(1)} %maximum_select_fusion.3), channel_id=1, source_target_pairs={{0,4},{1,3},{2,6},{3,1},{4,0},{5,7},{6,2},{7,5},{8,12},{9,11},{10,... | collective-permute-start | bytes 445448 | tf_op jit(solution)/shard_map/ppermute | solution.py:328
  62.3 6.8 %collective-permute-start.8 = (f32[580,128]{1,0:T(8,128)S(1)}, f32[580,128]{1,0:T(8,128)S(1)}, u32[]{:S(2)}, u32[]{:S(2)}) collective-permute-start(f32[580,128]{1,0:T(8,128)S(1)} %maximum_select_fusion.2), channel_id=1, source_target_pairs={{0,2},{1,5},{2,0},{3,7},{4,6},{5,1},{6,4},{7,3},{8,10},{9,13},{10,... | collective-permute-start | bytes 890888 | tf_op jit(solution)/shard_map/ppermute | solution.py:328
  69.2 2.1 %collective-permute-start.9 = (f32[1160,128]{1,0:T(8,128)S(1)}, f32[1160,128]{1,0:T(8,128)S(1)}, u32[]{:S(2)}, u32[]{:S(2)}) collective-permute-start(f32[1160,128]{1,0:T(8,128)S(1)} %maximum_select_fusion.1), channel_id=1, source_target_pairs={{0,1},{1,0},{2,3},{3,2},{4,5},{5,4},{6,7},{7,6},{8,9},{9,8},{10,11... | collective-permute-start | bytes 1781768 | tf_op jit(solution)/shard_map/ppermute | solution.py:328

commit v13 on v12

--- a/solution.py
+++ b/solution.py
@@ -354,7 +354,7 @@
         first_kernel, second_kernel,
     )
     steps = 2 * (size.bit_length() - 1)
-    places = [1, steps - 2] if len(chunks) == 2 and steps >= 4 else list(range(len(chunks)))
+    places = [1, steps - 3] if len(chunks) == 2 and steps >= 4 else list(range(len(chunks)))
     total, (outputs, input_grad) = butterfly_sum(packed, dict(zip(places, chunks)))
     first_sum = total[: 9 * ch].reshape(9, ch, ch)
     second_sum = total[9 * ch : 18 * ch].reshape(9, ch, ch)

time: 73.5 us -> 74.8 us (1.018)
  waiting for transfers between devices: 17.5 us -> 18.3 us
    ppermute x4, waiting for transfers between devices: 9.5 us -> 10.3 us  [butterfly_sum(): got = lax.ppermute(piece, 'rows', perm)]
  transfers between devices with their start and end apart: 10 -> 10, of which waited for: 7 -> 6; matrix products, arithmetic and copies ran while one was open for 0% -> 0% of each run, Pallas kernels for 27% -> 27%
where the time goes in v13:
time: 74.8 us; the launch traced here: 74.4 us
  Pallas kernels  28.1 us (38%)
  starting transfers between devices  20.6 us (28%)
  waiting for transfers between devices  18.3 us (24%)
  local copies, waits for them, and re-layouts  3.86 us (5%)
  other arithmetic  2.09 us (3%)
  between operations  1.48 us (2%)
    pallas_call x2, Pallas kernels, butterfly_sum(): got, state = lax.optimization_barrier((got, riders[count](*state)))  11.2 us
    ppermute x4, starting transfers between devices, butterfly_sum(): got = lax.ppermute(send, 'rows', perm)  10.6 us
    ppermute x4, waiting for transfers between devices, butterfly_sum(): got = lax.ppermute(piece, 'rows', perm)  10.3 us
    pallas_call x1, Pallas kernels, section(): pl.pallas_call(interior_kernel, out_shape=(frame, frame, frame_t, square,...  8.87 us
    pallas_call x1, Pallas kernels, section(): pl.pallas_call(functools.partial(edge_kernel, norm), out_shape=(jax.Shape...  8.03 us
    ppermute x4, waiting for transfers between devices, butterfly_sum(): got = lax.ppermute(send, 'rows', perm)  7.95 us
    ppermute x4, starting transfers between devices, butterfly_sum(): got = lax.ppermute(piece, 'rows', perm)  5.57 us
    ppermute x1, starting transfers between devices, local(): lax.ppermute(jnp.concatenate([inputs[-2:], cotangent[-2:]]), 'rows', up)  3.06 us
  transfers between devices with their start and end apart: 10, of which 6 were waited for; matrix products, arithmetic and copies ran while one was open for 0% of the time, Pallas kernels for 27%

profile of v13, /device:TPU:0, one launch (start us, length us, event | category | flops | bytes accessed | tf_op | source)
XLA Modules:
  0.0 74.4 jit_solution(2555559783258662153)
XLA Ops:
  0.6 1.3 %fusion.1 = (bf16[2,512,128]{2,1,0:T(8,128)(2,1)S(1)}, bf16[2,512,128]{2,1,0:T(8,128)(2,1)S(1)}, bf16[2,512,128]{2,1,0:T(8,128)(2,1)S(1)}, bf16[2,512,128]{2,1,0:T(8,128)(2,1)S(1)}) fusion(bf16[8,512,128]{2,1,0:T(8,128)(2,1)} %x_hbm.7, bf16[8,512,128]{2,1,0:T(8,128)(2,1)} %c_hbm.7), kind=kLoop, calls=%fused_computation.15 | loop fusion | bytes 2097152 | tf_op jit(solution)/shard_map/slice | solution.py:347
  2.0 1.3 %collective-permute-start.1 = (bf16[4,512,128]{2,1,0:T(8,128)(2,1)S(1)}, bf16[4,512,128]{2,1,0:T(8,128)(2,1)S(1)}, u32[]{:S(2)}, u32[]{:S(2)}) collective-permute-start(bf16[4,512,128]{2,1,0:T(8,128)(2,1)S(1)} %pad_maximum_fusion.1), channel_id=1, source_target_pairs={{1,0},{2,1},{3,2},{4,3},{5,4},{6,5},{7,6},{8,7},{9,8},{10,9},{11,1... | collective-permute-start | bytes 1572872 | tf_op jit(solution)/shard_map/ppermute | solution.py:347
  3.3 3.1 %collective-permute-start = (bf16[4,512,128]{2,1,0:T(8,128)(2,1)S(1)}, bf16[4,512,128]{2,1,0:T(8,128)(2,1)S(1)}, u32[]{:S(2)}, u32[]{:S(2)}) collective-permute-start(bf16[4,512,128]{2,1,0:T(8,128)(2,1)S(1)} %pad_maximum_fusion), channel_id=1, source_target_pairs={{0,1},{1,2},{2,3},{3,4},{4,5},{5,6},{6,7},{7,8},{8,9},{9,10},{10,1... | collective-permute-start | bytes 1572872 | tf_op jit(solution)/shard_map/ppermute | solution.py:346
  7.0 8.9 %shard_map.101 = (bf16[10,512,128]{2,1,0:T(8,128)(2,1)}, bf16[10,512,128]{2,1,0:T(8,128)(2,1)}, bf16[10,128,512]{2,1,0:T(8,128)(2,1)}, f32[384,384]{1,0:T(8,128)...) custom-call(s32[1]{0:T(128)S(6)} %copy.15.idx_ref, ...), custom_call_target="tpu_custom_call" | custom-call | flops 3925868544 | bytes 4194304 | tf_op jit(solution)/shard_map/pallas_call | solution.py:225
  15.9 0.0 copy-start.1
  16.0 0.0 copy-start.2
  16.0 0.8 %copy-done.1 = bf16[4,512,128]{2,1,0:T(8,128)(2,1)} copy-done((bf16[4,512,128]{2,1,0:T(8,128)(2,1)}, bf16[4,512,128]{2,1,0:T(8,128)(2,1)S(1)}, u32[]{:S(2)}) %copy-start.1) | copy-done | bytes 524312
  16.7 0.2 copy-done.2
  16.9 8.0 %shard_map.102 = (f32[2320,128]{1,0:T(8,128)}, bf16[10,512,128]{2,1,0:T(8,128)(2,1)}, bf16[10,512,128]{2,1,0:T(8,128)(2,1)}) custom-call(s32[1]{0:T(128)S(6)} %copy.15.idx_ref, f32[16,2,128]{2,1,0:T(2,128)} %lt_ref.3, bf16[8,512,128]{2,1,0:T(8,128)(2,1)} %x_hbm.7, bf16[8,512,128]{2,1,0:T(8,128)(2,1)} %c_hbm.7, bf16[4,512,128]{2,1,0:T(8,128)(2,1)} %copy-done.2, ...), custom_call_target="tpu_custom_call" | custom-call | flops 2113929216 | bytes 5242880 | tf_op jit(solution)/shard_map/pallas_call | solution.py:243
  25.0 1.4 %slice_select_fusion = f32[1160,128]{1,0:T(8,128)S(1)} fusion(f32[2320,128]{1,0:T(8,128)} %get-tuple-element.36, pred[]{:T(512)S(6)} %eq.36), kind=kLoop, calls=%fused_computation.3 | loop fusion | flops 148480 | bytes 1781761 | tf_op jit(solution)/shard_map/jit(_where)/select_n | solution.py:320
  26.4 3.5 %collective-permute-start.2 = (f32[1160,128]{1,0:T(8,128)S(1)}, f32[1160,128]{1,0:T(8,128)S(1)}, u32[]{:S(2)}, u32[]{:S(2)}) collective-permute-start(f32[1160,128]{1,0:T(8,128)S(1)} %slice_select_fusion), channel_id=1, source_target_pairs={{0,1},{1,0},{2,3},{3,2},{4,5},{5,4},{6,7},{7,6},{8,9},{9,8},{10,11... | collective-permute-start | bytes 1781768 | tf_op jit(solution)/shard_map/ppermute | solution.py:321
  29.9 1.6 %collective-permute-done.2 = f32[1160,128]{1,0:T(8,128)S(1)} collective-permute-done((f32[1160,128]{1,0:T(8,128)S(1)}, f32[1160,128]{1,0:T(8,128)S(1)}, u32[]{:S(2)}, u32[]{:S(2)}) %collective-permute-start.2) | collective-permute-done | bytes 593952 | tf_op jit(solution)/shard_map/ppermute | solution.py:321
  31.5 0.1 select_add_fusion
  31.7 2.8 %collective-permute-start.3 = (f32[580,128]{1,0:T(8,128)S(1)}, f32[580,128]{1,0:T(8,128)S(1)}, u32[]{:S(2)}, u32[]{:S(2)}) collective-permute-start(f32[580,128]{1,0:T(8,128)S(1)} %slice_select_fusion.1), channel_id=1, source_target_pairs={{0,2},{1,5},{2,0},{3,7},{4,6},{5,1},{6,4},{7,3},{8,10},{9,13},{10,... | collective-permute-start | bytes 890888 | tf_op jit(solution)/shard_map/ppermute | solution.py:321
  34.5 5.6 %shard_map.103 = (bf16[8,512,128]{2,1,0:T(8,128)(2,1)}, bf16[8,512,128]{2,1,0:T(8,128)(2,1)}) custom-call(bf16[8,512,128]{2,1,0:T(8,128)(2,1)} %x_hbm.7, bf16[8,512,128]{2,1,0:T(8,128)(2,1)} %c_hbm.7, bf16[10,512,128]{2,1,0:T(8,128)(2,1)} %get-tuple-element.37.hid_hbm, bf16[10,512,128]{2,1,0:T(8,128)(2,1)} %get-tuple-element.38.bf_hbm, ...), custom_call_target="tpu_custom_call" | custom-call | flops 1207959552 | bytes 2097152 | tf_op jit(solution)/shard_map/pallas_call | solution.py:323
  40.1 0.1 select_add_fusion.1
  40.2 1.6 %collective-permute-start.4 = (f32[290,128]{1,0:T(8,128)S(1)}, f32[290,128]{1,0:T(8,128)S(1)}, u32[]{:S(2)}, u32[]{:S(2)}) collective-permute-start(f32[290,128]{1,0:T(8,128)S(1)} %slice_select_fusion.2), channel_id=1, source_target_pairs={{0,4},{1,3},{2,6},{3,1},{4,0},{5,7},{6,2},{7,5},{8,12},{9,11},{10,... | collective-permute-start | bytes 445448 | tf_op jit(solution)/shard_map/ppermute | solution.py:321
  41.9 3.6 %collective-permute-done.4 = f32[290,128]{1,0:T(8,128)S(1)} collective-permute-done((f32[290,128]{1,0:T(8,128)S(1)}, f32[290,128]{1,0:T(8,128)S(1)}, u32[]{:S(2)}, u32[]{:S(2)}) %collective-permute-start.4) | collective-permute-done | bytes 148512 | tf_op jit(solution)/shard_map/ppermute | solution.py:321
  45.5 2.7 %collective-permute-start.5 = (f32[145,128]{1,0:T(8,128)S(1)}, f32[145,128]{1,0:T(8,128)S(1)}, u32[]{:S(2)}, u32[]{:S(2)}) collective-permute-start(f32[145,128]{1,0:T(8,128)S(1)} %slice_select_fusion.3), channel_id=1, source_target_pairs={{0,8},{1,9},{2,10},{3,11},{4,12},{5,13},{6,14},{7,15},{8,0},{9,1},... | collective-permute-start | bytes 222728 | tf_op jit(solution)/shard_map/ppermute | solution.py:321
  48.2 2.7 %collective-permute-done.5 = f32[145,128]{1,0:T(8,128)S(1)} collective-permute-done((f32[145,128]{1,0:T(8,128)S(1)}, f32[145,128]{1,0:T(8,128)S(1)}, u32[]{:S(2)}, u32[]{:S(2)}) %collective-permute-start.5) | collective-permute-done | bytes 74272 | tf_op jit(solution)/shard_map/ppermute | solution.py:321
  50.9 2.7 %collective-permute-start.6 = (f32[145,128]{1,0:T(8,128)S(1)}, f32[145,128]{1,0:T(8,128)S(1)}, u32[]{:S(2)}, u32[]{:S(2)}) collective-permute-start(f32[145,128]{1,0:T(8,128)S(1)} %select_add_fusion.3), channel_id=1, source_target_pairs={{0,8},{1,9},{2,10},{3,11},{4,12},{5,13},{6,14},{7,15},{8,0},{9,1},... | collective-permute-start | bytes 222728 | tf_op jit(solution)/shard_map/ppermute | solution.py:328
  53.6 2.7 %collective-permute-done.6 = f32[145,128]{1,0:T(8,128)S(1)} collective-permute-done((f32[145,128]{1,0:T(8,128)S(1)}, f32[145,128]{1,0:T(8,128)S(1)}, u32[]{:S(2)}, u32[]{:S(2)}) %collective-permute-start.6) | collective-permute-done | bytes 74272 | tf_op jit(solution)/shard_map/ppermute | solution.py:328
  56.3 1.6 %collective-permute-start.7 = (f32[290,128]{1,0:T(8,128)S(1)}, f32[290,128]{1,0:T(8,128)S(1)}, u32[]{:S(2)}, u32[]{:S(2)}) collective-permute-start(f32[290,128]{1,0:T(8,128)S(1)} %maximum_select_fusion.3), channel_id=1, source_target_pairs={{0,4},{1,3},{2,6},{3,1},{4,0},{5,7},{6,2},{7,5},{8,12},{9,11},{10,... | collective-permute-start | bytes 445448 | tf_op jit(solution)/shard_map/ppermute | solution.py:328
  57.9 5.6 %shard_map.104 = (bf16[8,512,128]{2,1,0:T(8,128)(2,1)}, bf16[8,512,128]{2,1,0:T(8,128)(2,1)}) custom-call(bf16[8,512,128]{2,1,0:T(8,128)(2,1)} %x_hbm.7, bf16[8,512,128]{2,1,0:T(8,128)(2,1)} %c_hbm.7, bf16[10,512,128]{2,1,0:T(8,128)(2,1)} %get-tuple-element.37.hid_hbm, ...), custom_call_target="tpu_custom_call", output_to_operand_aliasing={{0}: (6, {}), {1}: (7, {})} | custom-call | flops 1207959552 | bytes 2097152 | tf_op jit(solution)/shard_map/pallas_call | solution.py:330
  63.6 1.2 %collective-permute-start.8 = (f32[580,128]{1,0:T(8,128)S(1)}, f32[580,128]{1,0:T(8,128)S(1)}, u32[]{:S(2)}, u32[]{:S(2)}) collective-permute-start(f32[580,128]{1,0:T(8,128)S(1)} %maximum_select_fusion.2), channel_id=1, source_target_pairs={{0,2},{1,5},{2,0},{3,7},{4,6},{5,1},{6,4},{7,3},{8,10},{9,13},{10,... | collective-permute-start | bytes 890888 | tf_op jit(solution)/shard_map/ppermute | solution.py:328
  64.8 5.6 %collective-permute-done.8 = f32[580,128]{1,0:T(8,128)S(1)} collective-permute-done((f32[580,128]{1,0:T(8,128)S(1)}, f32[580,128]{1,0:T(8,128)S(1)}, u32[]{:S(2)}, u32[]{:S(2)}) %collective-permute-start.8) | collective-permute-done | bytes 296992 | tf_op jit(solution)/shard_map/ppermute | solution.py:328
  70.4 0.1 maximum_select_fusion.1
  70.5 0.1 collective-permute-start.9
  70.6 2.0 %collective-permute-done.9 = f32[1160,128]{1,0:T(8,128)S(1)} collective-permute-done((f32[1160,128]{1,0:T(8,128)S(1)}, f32[1160,128]{1,0:T(8,128)S(1)}, u32[]{:S(2)}, u32[]{:S(2)}) %collective-permute-start.9) | collective-permute-done | bytes 593952 | tf_op jit(solution)/shard_map/ppermute | solution.py:328
  72.6 0.1 maximum_select_fusion
  72.8 1.1 %fusion = (f32[1152,128]{1,0:T(8,128)}, f32[1152,128]{1,0:T(8,128)}) fusion(f32[2320,128]{1,0:T(8,128)S(1)} %maximum_select_fusion), kind=kLoop, calls=%fused_computation.14 | loop fusion | bytes 2359296 | tf_op jit(solution)/shard_map/slice | solution.py:360
  73.8 0.6 slice.68
  (15 shorter events, 0.3 us)
Async XLA Ops:
  2.0 14.0 %collective-permute-start.1 = (bf16[4,512,128]{2,1,0:T(8,128)(2,1)S(1)}, bf16[4,512,128]{2,1,0:T(8,128)(2,1)S(1)}, u32[]{:S(2)}, u32[]{:S(2)}) collective-permute-start(bf16[4,512,128]{2,1,0:T(8,128)(2,1)S(1)} %pad_maximum_fusion.1), channel_id=1, source_target_pairs={{1,0},{2,1},{3,2},{4,3},{5,4},{6,5},{7,6},{8,7},{9,8},{10,9},{11,1... | collective-permute-start | bytes 1572872 | tf_op jit(solution)/shard_map/ppermute | solution.py:347
  3.3 12.6 %collective-permute-start = (bf16[4,512,128]{2,1,0:T(8,128)(2,1)S(1)}, bf16[4,512,128]{2,1,0:T(8,128)(2,1)S(1)}, u32[]{:S(2)}, u32[]{:S(2)}) collective-permute-start(bf16[4,512,128]{2,1,0:T(8,128)(2,1)S(1)} %pad_maximum_fusion), channel_id=1, source_target_pairs={{0,1},{1,2},{2,3},{3,4},{4,5},{5,6},{6,7},{7,8},{8,9},{9,10},{10,1... | collective-permute-start | bytes 1572872 | tf_op jit(solution)/shard_map/ppermute | solution.py:346
  15.9 0.8 %copy-start.1 = (bf16[4,512,128]{2,1,0:T(8,128)(2,1)}, bf16[4,512,128]{2,1,0:T(8,128)(2,1)S(1)}, u32[]{:S(2)}) copy-start(bf16[4,512,128]{2,1,0:T(8,128)(2,1)S(1)} %collective-permute-done.1.after_hbm) | copy-start | bytes 1572868
  16.0 0.9 %copy-start.2 = (bf16[4,512,128]{2,1,0:T(8,128)(2,1)}, bf16[4,512,128]{2,1,0:T(8,128)(2,1)S(1)}, u32[]{:S(2)}) copy-start(bf16[4,512,128]{2,1,0:T(8,128)(2,1)S(1)} %collective-permute-done.before_hbm) | copy-start | bytes 1572868
  25.0 6.6 %copy-start = (f32[2320,128]{1,0:T(8,128)S(1)}, f32[2320,128]{1,0:T(8,128)}, u32[]{:S(2)}) copy-start(f32[2320,128]{1,0:T(8,128)} %get-tuple-element.36) | copy-start | bytes 3563524
  26.4 5.2 %collective-permute-start.2 = (f32[1160,128]{1,0:T(8,128)S(1)}, f32[1160,128]{1,0:T(8,128)S(1)}, u32[]{:S(2)}, u32[]{:S(2)}) collective-permute-start(f32[1160,128]{1,0:T(8,128)S(1)} %slice_select_fusion), channel_id=1, source_target_pairs={{0,1},{1,0},{2,3},{3,2},{4,5},{5,4},{6,7},{7,6},{8,9},{9,8},{10,11... | collective-permute-start | bytes 1781768 | tf_op jit(solution)/shard_map/ppermute | solution.py:321
  31.7 8.4 %collective-permute-start.3 = (f32[580,128]{1,0:T(8,128)S(1)}, f32[580,128]{1,0:T(8,128)S(1)}, u32[]{:S(2)}, u32[]{:S(2)}) collective-permute-start(f32[580,128]{1,0:T(8,128)S(1)} %slice_select_fusion.1), channel_id=1, source_target_pairs={{0,2},{1,5},{2,0},{3,7},{4,6},{5,1},{6,4},{7,3},{8,10},{9,13},{10,... | collective-permute-start | bytes 890888 | tf_op jit(solution)/shard_map/ppermute | solution.py:321
  40.2 5.3 %collective-permute-start.4 = (f32[290,128]{1,0:T(8,128)S(1)}, f32[290,128]{1,0:T(8,128)S(1)}, u32[]{:S(2)}, u32[]{:S(2)}) collective-permute-start(f32[290,128]{1,0:T(8,128)S(1)} %slice_select_fusion.2), channel_id=1, source_target_pairs={{0,4},{1,3},{2,6},{3,1},{4,0},{5,7},{6,2},{7,5},{8,12},{9,11},{10,... | collective-permute-start | bytes 445448 | tf_op jit(solution)/shard_map/ppermute | solution.py:321
  45.5 5.4 %collective-permute-start.5 = (f32[145,128]{1,0:T(8,128)S(1)}, f32[145,128]{1,0:T(8,128)S(1)}, u32[]{:S(2)}, u32[]{:S(2)}) collective-permute-start(f32[145,128]{1,0:T(8,128)S(1)} %slice_select_fusion.3), channel_id=1, source_target_pairs={{0,8},{1,9},{2,10},{3,11},{4,12},{5,13},{6,14},{7,15},{8,0},{9,1},... | collective-permute-start | bytes 222728 | tf_op jit(solution)/shard_map/ppermute | solution.py:321
  50.9 5.4 %collective-permute-start.6 = (f32[145,128]{1,0:T(8,128)S(1)}, f32[145,128]{1,0:T(8,128)S(1)}, u32[]{:S(2)}, u32[]{:S(2)}) collective-permute-start(f32[145,128]{1,0:T(8,128)S(1)} %select_add_fusion.3), channel_id=1, source_target_pairs={{0,8},{1,9},{2,10},{3,11},{4,12},{5,13},{6,14},{7,15},{8,0},{9,1},... | collective-permute-start | bytes 222728 | tf_op jit(solution)/shard_map/ppermute | solution.py:328
  56.3 7.3 %collective-permute-start.7 = (f32[290,128]{1,0:T(8,128)S(1)}, f32[290,128]{1,0:T(8,128)S(1)}, u32[]{:S(2)}, u32[]{:S(2)}) collective-permute-start(f32[290,128]{1,0:T(8,128)S(1)} %maximum_select_fusion.3), channel_id=1, source_target_pairs={{0,4},{1,3},{2,6},{3,1},{4,0},{5,7},{6,2},{7,5},{8,12},{9,11},{10,... | collective-permute-start | bytes 445448 | tf_op jit(solution)/shard_map/ppermute | solution.py:328
  63.6 6.8 %collective-permute-start.8 = (f32[580,128]{1,0:T(8,128)S(1)}, f32[580,128]{1,0:T(8,128)S(1)}, u32[]{:S(2)}, u32[]{:S(2)}) collective-permute-start(f32[580,128]{1,0:T(8,128)S(1)} %maximum_select_fusion.2), channel_id=1, source_target_pairs={{0,2},{1,5},{2,0},{3,7},{4,6},{5,1},{6,4},{7,3},{8,10},{9,13},{10,... | collective-permute-start | bytes 890888 | tf_op jit(solution)/shard_map/ppermute | solution.py:328
  70.5 2.1 %collective-permute-start.9 = (f32[1160,128]{1,0:T(8,128)S(1)}, f32[1160,128]{1,0:T(8,128)S(1)}, u32[]{:S(2)}, u32[]{:S(2)}) collective-permute-start(f32[1160,128]{1,0:T(8,128)S(1)} %maximum_select_fusion.1), channel_id=1, source_target_pairs={{0,1},{1,0},{2,3},{3,2},{4,5},{5,4},{6,7},{7,6},{8,9},{9,8},{10,11... | collective-permute-start | bytes 1781768 | tf_op jit(solution)/shard_map/ppermute | solution.py:328

commit v14 on v12

--- a/solution.py
+++ b/solution.py
@@ -164,15 +164,16 @@
     for i in (0, count - 1):
         g1_row(i, xt_ref, bf_ref, acc1)
 
+    half = grad_ref.shape[0] // 2
+    base = 9 * ch
+    grad_ref[base:half, :] = jnp.zeros((half - base, ch), jnp.float32)
+    grad_ref[half + base :, :] = jnp.zeros((grad_ref.shape[0] - half - base, ch), jnp.float32)
     for a in range(3):
         for b in range(3):
             t = 3 * a + b
             blk = (slice(a * ch, (a + 1) * ch), slice(b * ch, (b + 1) * ch))
             grad_ref[t * ch : (t + 1) * ch, :] = acc1[blk] * norm
-            grad_ref[(9 + t) * ch : (10 + t) * ch, :] = acc2[blk] * norm
-    base = 18 * ch
-    tail = grad_ref.shape[0] - base
-    grad_ref[base:, :] = jnp.zeros((tail, ch), jnp.float32)
+            grad_ref[half + t * ch : half + (t + 1) * ch, :] = acc2[blk] * norm
     grad_ref[base : base + 1, :] = lv0 * norm
     grad_ref[base + 1 : base + 2, :] = lv1 * norm
 
@@ -329,8 +330,9 @@
         if count in riders:
             got, state = lax.optimization_barrier((got, riders[count](*state)))
         count += 1
-        piece = jnp.where(low, jnp.concatenate([piece, got]), jnp.concatenate([got, piece]))
-    return piece, state
+        if count < 2 * len(orders):
+            piece = jnp.where(low, jnp.concatenate([piece, got]), jnp.concatenate([got, piece]))
+    return (jnp.where(low, piece, got), jnp.where(low, got, piece)), state
 
 
 def local(inputs, cotangent, first_kernel, second_kernel, level_table, level_index):
@@ -347,18 +349,19 @@
     after = lax.ppermute(jnp.concatenate([inputs[:2], cotangent[:2]]), "rows", down)
     halo = lambda: (before, after)
 
-    used = 18 * ch + 2
-    packed_rows = used + (-used % size)
+    used = 9 * ch + 2
+    half_rows = used + (-used % max(size // 2, 1))
+    packed_rows = 2 * half_rows
     chunks, packed = section(
         norm, packed_rows, level_index, level_table, inputs, cotangent, halo,
         first_kernel, second_kernel,
     )
     steps = 2 * (size.bit_length() - 1)
     places = [1, steps - 2] if len(chunks) == 2 and steps >= 4 else list(range(len(chunks)))
-    total, (outputs, input_grad) = butterfly_sum(packed, dict(zip(places, chunks)))
-    first_sum = total[: 9 * ch].reshape(9, ch, ch)
-    second_sum = total[9 * ch : 18 * ch].reshape(9, ch, ch)
-    level_sum = total[18 * ch : 18 * ch + 2]
+    (lower, upper), (outputs, input_grad) = butterfly_sum(packed, dict(zip(places, chunks)))
+    first_sum = lower[: 9 * ch].reshape(9, ch, ch)
+    level_sum = lower[9 * ch : 9 * ch + 2]
+    second_sum = upper[: 9 * ch].reshape(9, ch, ch)
     return (outputs, input_grad, first_sum, second_sum, level_sum)
 
 

time: 73.5 us -> 74.1 us (level)
  other arithmetic: 2.09 us -> 2.9 us
    select_n x0 -> x2, other arithmetic: none -> 0.96 us  [butterfly_sum(): return ((jnp.where(low, piece, got), jnp.where(low, got, piece)), state)]
where the time goes in v14:
time: 74.1 us; the launch traced here: 73.7 us
  Pallas kernels  28.1 us (38%)
  starting transfers between devices  20.1 us (27%)
  waiting for transfers between devices  17.5 us (24%)
  local copies, waits for them, and re-layouts  3.62 us (5%)
  other arithmetic  2.9 us (4%)
  between operations  1.47 us (2%)
    pallas_call x2, Pallas kernels, butterfly_sum(): got, state = lax.optimization_barrier((got, riders[count](*state)))  11.2 us
    ppermute x4, starting transfers between devices, butterfly_sum(): got = lax.ppermute(send, 'rows', perm)  10.6 us
    ppermute x4, waiting for transfers between devices, butterfly_sum(): got = lax.ppermute(piece, 'rows', perm)  9.5 us
    pallas_call x1, Pallas kernels, section(): pl.pallas_call(interior_kernel, out_shape=(frame, frame, frame_t, square,...  8.87 us
    pallas_call x1, Pallas kernels, section(): pl.pallas_call(functools.partial(edge_kernel, norm), out_shape=(jax.Shape...  8.04 us
    ppermute x4, waiting for transfers between devices, butterfly_sum(): got = lax.ppermute(send, 'rows', perm)  7.97 us
    ppermute x4, starting transfers between devices, butterfly_sum(): got = lax.ppermute(piece, 'rows', perm)  5.12 us
    ppermute x1, starting transfers between devices, local(): lax.ppermute(jnp.concatenate([inputs[-2:], cotangent[-2:]]), 'rows', up)  3.06 us
  transfers between devices with their start and end apart: 10, of which 7 were waited for; matrix products, arithmetic and copies ran while one was open for 0% of the time, Pallas kernels for 27%

profile of v14, /device:TPU:0, one launch (start us, length us, event | category | flops | bytes accessed | tf_op | source)
XLA Modules:
  0.0 73.7 jit_solution(4199650449428810130)
XLA Ops:
  0.6 1.3 %fusion = (bf16[2,512,128]{2,1,0:T(8,128)(2,1)S(1)}, bf16[2,512,128]{2,1,0:T(8,128)(2,1)S(1)}, bf16[2,512,128]{2,1,0:T(8,128)(2,1)S(1)}, bf16[2,512,128]{2,1,0:T(8,128)(2,1)S(1)}) fusion(bf16[8,512,128]{2,1,0:T(8,128)(2,1)} %x_hbm.7, bf16[8,512,128]{2,1,0:T(8,128)(2,1)} %c_hbm.7), kind=kLoop, calls=%fused_computation.15 | loop fusion | bytes 2097152 | tf_op jit(solution)/shard_map/slice | solution.py:349
  2.0 1.3 %collective-permute-start.1 = (bf16[4,512,128]{2,1,0:T(8,128)(2,1)S(1)}, bf16[4,512,128]{2,1,0:T(8,128)(2,1)S(1)}, u32[]{:S(2)}, u32[]{:S(2)}) collective-permute-start(bf16[4,512,128]{2,1,0:T(8,128)(2,1)S(1)} %pad_maximum_fusion.1), channel_id=1, source_target_pairs={{1,0},{2,1},{3,2},{4,3},{5,4},{6,5},{7,6},{8,7},{9,8},{10,9},{11,1... | collective-permute-start | bytes 1572872 | tf_op jit(solution)/shard_map/ppermute | solution.py:349
  3.3 3.1 %collective-permute-start = (bf16[4,512,128]{2,1,0:T(8,128)(2,1)S(1)}, bf16[4,512,128]{2,1,0:T(8,128)(2,1)S(1)}, u32[]{:S(2)}, u32[]{:S(2)}) collective-permute-start(bf16[4,512,128]{2,1,0:T(8,128)(2,1)S(1)} %pad_maximum_fusion), channel_id=1, source_target_pairs={{0,1},{1,2},{2,3},{3,4},{4,5},{5,6},{6,7},{7,8},{8,9},{9,10},{10,1... | collective-permute-start | bytes 1572872 | tf_op jit(solution)/shard_map/ppermute | solution.py:348
  7.0 8.9 %shard_map.101 = (bf16[10,512,128]{2,1,0:T(8,128)(2,1)}, bf16[10,512,128]{2,1,0:T(8,128)(2,1)}, bf16[10,128,512]{2,1,0:T(8,128)(2,1)}, f32[384,384]{1,0:T(8,128)...) custom-call(s32[1]{0:T(128)S(6)} %copy.15.idx_ref, ...), custom_call_target="tpu_custom_call" | custom-call | flops 3925868544 | bytes 4194304 | tf_op jit(solution)/shard_map/pallas_call | solution.py:226
  16.0 0.8 %copy-done.1 = bf16[4,512,128]{2,1,0:T(8,128)(2,1)} copy-done((bf16[4,512,128]{2,1,0:T(8,128)(2,1)}, bf16[4,512,128]{2,1,0:T(8,128)(2,1)S(1)}, u32[]{:S(2)}) %copy-start.1) | copy-done | bytes 524312
  16.7 0.2 copy-done.2
  16.9 8.0 %shard_map.102 = (f32[2320,128]{1,0:T(8,128)}, bf16[10,512,128]{2,1,0:T(8,128)(2,1)}, bf16[10,512,128]{2,1,0:T(8,128)(2,1)}) custom-call(s32[1]{0:T(128)S(6)} %copy.15.idx_ref, f32[16,2,128]{2,1,0:T(2,128)} %lt_ref.3, bf16[8,512,128]{2,1,0:T(8,128)(2,1)} %x_hbm.7, bf16[8,512,128]{2,1,0:T(8,128)(2,1)} %c_hbm.7, bf16[4,512,128]{2,1,0:T(8,128)(2,1)} %copy-done.2, ...), custom_call_target="tpu_custom_call" | custom-call | flops 2113929216 | bytes 5242880 | tf_op jit(solution)/shard_map/pallas_call | solution.py:244
  25.0 1.4 %slice_select_fusion.1 = f32[1160,128]{1,0:T(8,128)S(1)} fusion(f32[2320,128]{1,0:T(8,128)} %get-tuple-element.36, pred[]{:T(512)S(6)} %eq.35), kind=kLoop, calls=%fused_computation.3 | loop fusion | flops 148480 | bytes 1781761 | tf_op jit(solution)/shard_map/jit(_where)/select_n | solution.py:321
  26.4 3.5 %collective-permute-start.2 = (f32[1160,128]{1,0:T(8,128)S(1)}, f32[1160,128]{1,0:T(8,128)S(1)}, u32[]{:S(2)}, u32[]{:S(2)}) collective-permute-start(f32[1160,128]{1,0:T(8,128)S(1)} %slice_select_fusion.1), channel_id=1, source_target_pairs={{0,1},{1,0},{2,3},{3,2},{4,5},{5,4},{6,7},{7,6},{8,9},{9,8},{10,11... | collective-permute-start | bytes 1781768 | tf_op jit(solution)/shard_map/ppermute | solution.py:322
  29.9 1.6 %collective-permute-done.2 = f32[1160,128]{1,0:T(8,128)S(1)} collective-permute-done((f32[1160,128]{1,0:T(8,128)S(1)}, f32[1160,128]{1,0:T(8,128)S(1)}, u32[]{:S(2)}, u32[]{:S(2)}) %collective-permute-start.2) | collective-permute-done | bytes 593952 | tf_op jit(solution)/shard_map/ppermute | solution.py:322
  31.5 0.1 select_add_fusion
  31.7 2.8 %collective-permute-start.3 = (f32[580,128]{1,0:T(8,128)S(1)}, f32[580,128]{1,0:T(8,128)S(1)}, u32[]{:S(2)}, u32[]{:S(2)}) collective-permute-start(f32[580,128]{1,0:T(8,128)S(1)} %slice_select_fusion.2), channel_id=1, source_target_pairs={{0,2},{1,5},{2,0},{3,7},{4,6},{5,1},{6,4},{7,3},{8,10},{9,13},{10,... | collective-permute-start | bytes 890888 | tf_op jit(solution)/shard_map/ppermute | solution.py:322
  34.5 5.6 %shard_map.103 = (bf16[8,512,128]{2,1,0:T(8,128)(2,1)}, bf16[8,512,128]{2,1,0:T(8,128)(2,1)}) custom-call(bf16[8,512,128]{2,1,0:T(8,128)(2,1)} %x_hbm.7, bf16[8,512,128]{2,1,0:T(8,128)(2,1)} %c_hbm.7, bf16[10,512,128]{2,1,0:T(8,128)(2,1)} %get-tuple-element.37.hid_hbm, bf16[10,512,128]{2,1,0:T(8,128)(2,1)} %get-tuple-element.38.bf_hbm, ...), custom_call_target="tpu_custom_call" | custom-call | flops 1207959552 | bytes 2097152 | tf_op jit(solution)/shard_map/pallas_call | solution.py:324
  40.1 0.1 select_add_fusion.1
  40.2 1.6 %collective-permute-start.4 = (f32[290,128]{1,0:T(8,128)S(1)}, f32[290,128]{1,0:T(8,128)S(1)}, u32[]{:S(2)}, u32[]{:S(2)}) collective-permute-start(f32[290,128]{1,0:T(8,128)S(1)} %slice_select_fusion.3), channel_id=1, source_target_pairs={{0,4},{1,3},{2,6},{3,1},{4,0},{5,7},{6,2},{7,5},{8,12},{9,11},{10,... | collective-permute-start | bytes 445448 | tf_op jit(solution)/shard_map/ppermute | solution.py:322
  41.9 3.6 %collective-permute-done.4 = f32[290,128]{1,0:T(8,128)S(1)} collective-permute-done((f32[290,128]{1,0:T(8,128)S(1)}, f32[290,128]{1,0:T(8,128)S(1)}, u32[]{:S(2)}, u32[]{:S(2)}) %collective-permute-start.4) | collective-permute-done | bytes 148512 | tf_op jit(solution)/shard_map/ppermute | solution.py:322
  45.5 2.6 %collective-permute-start.5 = (f32[145,128]{1,0:T(8,128)S(1)}, f32[145,128]{1,0:T(8,128)S(1)}, u32[]{:S(2)}, u32[]{:S(2)}) collective-permute-start(f32[145,128]{1,0:T(8,128)S(1)} %slice_select_fusion.4), channel_id=1, source_target_pairs={{0,8},{1,9},{2,10},{3,11},{4,12},{5,13},{6,14},{7,15},{8,0},{9,1},... | collective-permute-start | bytes 222728 | tf_op jit(solution)/shard_map/ppermute | solution.py:322
  48.2 2.7 %collective-permute-done.5 = f32[145,128]{1,0:T(8,128)S(1)} collective-permute-done((f32[145,128]{1,0:T(8,128)S(1)}, f32[145,128]{1,0:T(8,128)S(1)}, u32[]{:S(2)}, u32[]{:S(2)}) %collective-permute-start.5) | collective-permute-done | bytes 74272 | tf_op jit(solution)/shard_map/ppermute | solution.py:322
  50.9 2.6 %collective-permute-start.6 = (f32[145,128]{1,0:T(8,128)S(1)}, f32[145,128]{1,0:T(8,128)S(1)}, u32[]{:S(2)}, u32[]{:S(2)}) collective-permute-start(f32[145,128]{1,0:T(8,128)S(1)} %select_add_fusion.3), channel_id=1, source_target_pairs={{0,8},{1,9},{2,10},{3,11},{4,12},{5,13},{6,14},{7,15},{8,0},{9,1},... | collective-permute-start | bytes 222728 | tf_op jit(solution)/shard_map/ppermute | solution.py:329
  53.6 2.7 %collective-permute-done.6 = f32[145,128]{1,0:T(8,128)S(1)} collective-permute-done((f32[145,128]{1,0:T(8,128)S(1)}, f32[145,128]{1,0:T(8,128)S(1)}, u32[]{:S(2)}, u32[]{:S(2)}) %collective-permute-start.6) | collective-permute-done | bytes 74272 | tf_op jit(solution)/shard_map/ppermute | solution.py:329
  56.3 1.6 %collective-permute-start.7 = (f32[290,128]{1,0:T(8,128)S(1)}, f32[290,128]{1,0:T(8,128)S(1)}, u32[]{:S(2)}, u32[]{:S(2)}) collective-permute-start(f32[290,128]{1,0:T(8,128)S(1)} %maximum_select_fusion.2), channel_id=1, source_target_pairs={{0,4},{1,3},{2,6},{3,1},{4,0},{5,7},{6,2},{7,5},{8,12},{9,11},{10,... | collective-permute-start | bytes 445448 | tf_op jit(solution)/shard_map/ppermute | solution.py:329
  57.9 4.3 %collective-permute-done.7 = f32[290,128]{1,0:T(8,128)S(1)} collective-permute-done((f32[290,128]{1,0:T(8,128)S(1)}, f32[290,128]{1,0:T(8,128)S(1)}, u32[]{:S(2)}, u32[]{:S(2)}) %collective-permute-start.7) | collective-permute-done | bytes 148512 | tf_op jit(solution)/shard_map/ppermute | solution.py:329
  62.3 0.8 %collective-permute-start.8 = (f32[580,128]{1,0:T(8,128)S(1)}, f32[580,128]{1,0:T(8,128)S(1)}, u32[]{:S(2)}, u32[]{:S(2)}) collective-permute-start(f32[580,128]{1,0:T(8,128)S(1)} %maximum_select_fusion.1), channel_id=1, source_target_pairs={{0,2},{1,5},{2,0},{3,7},{4,6},{5,1},{6,4},{7,3},{8,10},{9,13},{10,... | collective-permute-start | bytes 890888 | tf_op jit(solution)/shard_map/ppermute | solution.py:329
  63.1 5.6 %shard_map.104 = (bf16[8,512,128]{2,1,0:T(8,128)(2,1)}, bf16[8,512,128]{2,1,0:T(8,128)(2,1)}) custom-call(bf16[8,512,128]{2,1,0:T(8,128)(2,1)} %x_hbm.7, bf16[8,512,128]{2,1,0:T(8,128)(2,1)} %c_hbm.7, bf16[10,512,128]{2,1,0:T(8,128)(2,1)} %get-tuple-element.37.hid_hbm, ...), custom_call_target="tpu_custom_call", output_to_operand_aliasing={{0}: (6, {}), {1}: (7, {})} | custom-call | flops 1207959552 | bytes 2097152 | tf_op jit(solution)/shard_map/pallas_call | solution.py:331
  68.7 0.5 collective-permute-done.8
  69.2 0.1 maximum_select_fusion
  69.2 0.1 collective-permute-start.9
  69.3 2.0 %collective-permute-done.9 = f32[1160,128]{1,0:T(8,128)S(1)} collective-permute-done((f32[1160,128]{1,0:T(8,128)S(1)}, f32[1160,128]{1,0:T(8,128)S(1)}, u32[]{:S(2)}, u32[]{:S(2)}) %collective-permute-start.9) | collective-permute-done | bytes 593952 | tf_op jit(solution)/shard_map/ppermute | solution.py:329
  71.3 0.1 broadcast_select_fusion
  71.4 0.9 %slice.66 = f32[1152,128]{1,0:T(8,128)} slice(f32[1160,128]{1,0:T(8,128)S(1)} %broadcast_select_fusion), slice={[0:1152], [0:128]} | slice | bytes 1179648 | tf_op jit(solution)/shard_map/slice | solution.py:362
  72.3 0.6 slice.69
  72.8 0.9 %slice_select_fusion = f32[1152,128]{1,0:T(8,128)} fusion(f32[1160,128]{1,0:T(8,128)S(1)} %maximum_select_fusion, f32[1160,128]{1,0:T(8,128)S(1)} %collective-permute-done.9, pred[]{:T(512)S(6)} %eq.35), kind=kLoop, calls=%fused_computation.2 | loop fusion | flops 147456 | bytes 1769473 | tf_op jit(solution)/shard_map/jit(_where)/select_n | solution.py:335
  (16 shorter events, 0.3 us)
Async XLA Ops:
  2.0 14.0 %collective-permute-start.1 = (bf16[4,512,128]{2,1,0:T(8,128)(2,1)S(1)}, bf16[4,512,128]{2,1,0:T(8,128)(2,1)S(1)}, u32[]{:S(2)}, u32[]{:S(2)}) collective-permute-start(bf16[4,512,128]{2,1,0:T(8,128)(2,1)S(1)} %pad_maximum_fusion.1), channel_id=1, source_target_pairs={{1,0},{2,1},{3,2},{4,3},{5,4},{6,5},{7,6},{8,7},{9,8},{10,9},{11,1... | collective-permute-start | bytes 1572872 | tf_op jit(solution)/shard_map/ppermute | solution.py:349
  3.3 12.6 %collective-permute-start = (bf16[4,512,128]{2,1,0:T(8,128)(2,1)S(1)}, bf16[4,512,128]{2,1,0:T(8,128)(2,1)S(1)}, u32[]{:S(2)}, u32[]{:S(2)}) collective-permute-start(bf16[4,512,128]{2,1,0:T(8,128)(2,1)S(1)} %pad_maximum_fusion), channel_id=1, source_target_pairs={{0,1},{1,2},{2,3},{3,4},{4,5},{5,6},{6,7},{7,8},{8,9},{9,10},{10,1... | collective-permute-start | bytes 1572872 | tf_op jit(solution)/shard_map/ppermute | solution.py:348
  15.9 0.8 %copy-start.1 = (bf16[4,512,128]{2,1,0:T(8,128)(2,1)}, bf16[4,512,128]{2,1,0:T(8,128)(2,1)S(1)}, u32[]{:S(2)}) copy-start(bf16[4,512,128]{2,1,0:T(8,128)(2,1)S(1)} %collective-permute-done.1.after_hbm) | copy-start | bytes 1572868
  16.0 0.9 %copy-start.2 = (bf16[4,512,128]{2,1,0:T(8,128)(2,1)}, bf16[4,512,128]{2,1,0:T(8,128)(2,1)S(1)}, u32[]{:S(2)}) copy-start(bf16[4,512,128]{2,1,0:T(8,128)(2,1)S(1)} %collective-permute-done.before_hbm) | copy-start | bytes 1572868
  25.0 6.6 %copy-start = (f32[2320,128]{1,0:T(8,128)S(1)}, f32[2320,128]{1,0:T(8,128)}, u32[]{:S(2)}) copy-start(f32[2320,128]{1,0:T(8,128)} %get-tuple-element.36) | copy-start | bytes 3563524
  26.4 5.2 %collective-permute-start.2 = (f32[1160,128]{1,0:T(8,128)S(1)}, f32[1160,128]{1,0:T(8,128)S(1)}, u32[]{:S(2)}, u32[]{:S(2)}) collective-permute-start(f32[1160,128]{1,0:T(8,128)S(1)} %slice_select_fusion.1), channel_id=1, source_target_pairs={{0,1},{1,0},{2,3},{3,2},{4,5},{5,4},{6,7},{7,6},{8,9},{9,8},{10,11... | collective-permute-start | bytes 1781768 | tf_op jit(solution)/shard_map/ppermute | solution.py:322
  31.7 8.4 %collective-permute-start.3 = (f32[580,128]{1,0:T(8,128)S(1)}, f32[580,128]{1,0:T(8,128)S(1)}, u32[]{:S(2)}, u32[]{:S(2)}) collective-permute-start(f32[580,128]{1,0:T(8,128)S(1)} %slice_select_fusion.2), channel_id=1, source_target_pairs={{0,2},{1,5},{2,0},{3,7},{4,6},{5,1},{6,4},{7,3},{8,10},{9,13},{10,... | collective-permute-start | bytes 890888 | tf_op jit(solution)/shard_map/ppermute | solution.py:322
  40.2 5.3 %collective-permute-start.4 = (f32[290,128]{1,0:T(8,128)S(1)}, f32[290,128]{1,0:T(8,128)S(1)}, u32[]{:S(2)}, u32[]{:S(2)}) collective-permute-start(f32[290,128]{1,0:T(8,128)S(1)} %slice_select_fusion.3), channel_id=1, source_target_pairs={{0,4},{1,3},{2,6},{3,1},{4,0},{5,7},{6,2},{7,5},{8,12},{9,11},{10,... | collective-permute-start | bytes 445448 | tf_op jit(solution)/shard_map/ppermute | solution.py:322
  45.5 5.4 %collective-permute-start.5 = (f32[145,128]{1,0:T(8,128)S(1)}, f32[145,128]{1,0:T(8,128)S(1)}, u32[]{:S(2)}, u32[]{:S(2)}) collective-permute-start(f32[145,128]{1,0:T(8,128)S(1)} %slice_select_fusion.4), channel_id=1, source_target_pairs={{0,8},{1,9},{2,10},{3,11},{4,12},{5,13},{6,14},{7,15},{8,0},{9,1},... | collective-permute-start | bytes 222728 | tf_op jit(solution)/shard_map/ppermute | solution.py:322
  50.9 5.4 %collective-permute-start.6 = (f32[145,128]{1,0:T(8,128)S(1)}, f32[145,128]{1,0:T(8,128)S(1)}, u32[]{:S(2)}, u32[]{:S(2)}) collective-permute-start(f32[145,128]{1,0:T(8,128)S(1)} %select_add_fusion.3), channel_id=1, source_target_pairs={{0,8},{1,9},{2,10},{3,11},{4,12},{5,13},{6,14},{7,15},{8,0},{9,1},... | collective-permute-start | bytes 222728 | tf_op jit(solution)/shard_map/ppermute | solution.py:329
  56.3 6.0 %collective-permute-start.7 = (f32[290,128]{1,0:T(8,128)S(1)}, f32[290,128]{1,0:T(8,128)S(1)}, u32[]{:S(2)}, u32[]{:S(2)}) collective-permute-start(f32[290,128]{1,0:T(8,128)S(1)} %maximum_select_fusion.2), channel_id=1, source_target_pairs={{0,4},{1,3},{2,6},{3,1},{4,0},{5,7},{6,2},{7,5},{8,12},{9,11},{10,... | collective-permute-start | bytes 445448 | tf_op jit(solution)/shard_map/ppermute | solution.py:329
  62.3 6.8 %collective-permute-start.8 = (f32[580,128]{1,0:T(8,128)S(1)}, f32[580,128]{1,0:T(8,128)S(1)}, u32[]{:S(2)}, u32[]{:S(2)}) collective-permute-start(f32[580,128]{1,0:T(8,128)S(1)} %maximum_select_fusion.1), channel_id=1, source_target_pairs={{0,2},{1,5},{2,0},{3,7},{4,6},{5,1},{6,4},{7,3},{8,10},{9,13},{10,... | collective-permute-start | bytes 890888 | tf_op jit(solution)/shard_map/ppermute | solution.py:329
  69.2 2.1 %collective-permute-start.9 = (f32[1160,128]{1,0:T(8,128)S(1)}, f32[1160,128]{1,0:T(8,128)S(1)}, u32[]{:S(2)}, u32[]{:S(2)}) collective-permute-start(f32[1160,128]{1,0:T(8,128)S(1)} %maximum_select_fusion), channel_id=1, source_target_pairs={{0,1},{1,0},{2,3},{3,2},{4,5},{5,4},{6,7},{7,6},{8,9},{9,8},{10,11... | collective-permute-start | bytes 1781768 | tf_op jit(solution)/shard_map/ppermute | solution.py:329

commit v15 on v12

--- a/solution.py
+++ b/solution.py
@@ -51,13 +51,15 @@
         out_ref[i] = (x_ref[i + 2].astype(jnp.float32) + conv_row(hid_ref, i, k2f_ref)).astype(out_ref.dtype)
         ig_ref[i] = (c_ref[i + 2].astype(jnp.float32) + conv_row(bf_ref, i, k1b_ref)).astype(ig_ref.dtype)
 
-    def g1_row(i, xt_ref, bf_ref, acc1):
+    def g1_row(i, xt_ref, bf_ref, acc1, fresh=False):
         xs = jnp.concatenate([xt_ref[i + 1], xt_ref[i + 2], xt_ref[i + 3]], axis=0)
-        acc1[...] += jnp.dot(xs, shifted(bf_ref[i + 1]), preferred_element_type=jnp.float32)
-
-    def g2_row(i, hidt_ref, c_ref, acc2):
+        term = jnp.dot(xs, shifted(bf_ref[i + 1]), preferred_element_type=jnp.float32)
+        acc1[...] = term if fresh else acc1[...] + term
+
+    def g2_row(i, hidt_ref, c_ref, acc2, fresh=False):
         hs = jnp.concatenate([hidt_ref[i], hidt_ref[i + 1], hidt_ref[i + 2]], axis=0)
-        acc2[...] += jnp.dot(hs, shifted(c_ref[i + 2]), preferred_element_type=jnp.float32)
+        term = jnp.dot(hs, shifted(c_ref[i + 2]), preferred_element_type=jnp.float32)
+        acc2[...] = term if fresh else acc2[...] + term
 
     return phase_one, out_row, g1_row, g2_row, conv_row
 
@@ -146,8 +148,6 @@
         cp.start()
     scale, shift, top, bottom = level_and_edges(idx_ref, lt_ref)
     phase_one, out_row, g1_row, g2_row, _ = row_ops(width, ch, scale, shift, top, bottom, count)
-    acc1[...] = acc1a_ref[...]
-    acc2[...] = acc2a_ref[...]
     for cp in copies:
         cp.wait()
 
@@ -159,17 +159,17 @@
         cp.wait()
     for r in (1, 2, 3, count, count + 1, count + 2):
         xt_ref[r] = x_ref[r].astype(jnp.float32).T.astype(xt_ref.dtype)
-    for i in (0, 1, count - 2, count - 1):
-        g2_row(i, hidt_ref, c_ref, acc2)
-    for i in (0, count - 1):
-        g1_row(i, xt_ref, bf_ref, acc1)
+    for n, i in enumerate((0, 1, count - 2, count - 1)):
+        g2_row(i, hidt_ref, c_ref, acc2, n == 0)
+    for n, i in enumerate((0, count - 1)):
+        g1_row(i, xt_ref, bf_ref, acc1, n == 0)
 
     for a in range(3):
         for b in range(3):
             t = 3 * a + b
             blk = (slice(a * ch, (a + 1) * ch), slice(b * ch, (b + 1) * ch))
-            grad_ref[t * ch : (t + 1) * ch, :] = acc1[blk] * norm
-            grad_ref[(9 + t) * ch : (10 + t) * ch, :] = acc2[blk] * norm
+            grad_ref[t * ch : (t + 1) * ch, :] = (acc1a_ref[blk] + acc1[blk]) * norm
+            grad_ref[(9 + t) * ch : (10 + t) * ch, :] = (acc2a_ref[blk] + acc2[blk]) * norm
     base = 18 * ch
     tail = grad_ref.shape[0] - base
     grad_ref[base:, :] = jnp.zeros((tail, ch), jnp.float32)

time: 73.5 us -> 73.5 us (level)
  no operation moved by 1% of the time
where the time goes in v15:
time: 73.5 us; the launch traced here: 73.1 us
  Pallas kernels  28.1 us (38%)
  starting transfers between devices  20.1 us (27%)
  waiting for transfers between devices  17.4 us (24%)
  local copies, waits for them, and re-layouts  3.86 us (5%)
  other arithmetic  2.09 us (3%)
  between operations  1.47 us (2%)
    pallas_call x2, Pallas kernels, butterfly_sum(): got, state = lax.optimization_barrier((got, riders[count](*state)))  11.2 us
    ppermute x4, starting transfers between devices, butterfly_sum(): got = lax.ppermute(send, 'rows', perm)  10.6 us
    ppermute x4, waiting for transfers between devices, butterfly_sum(): got = lax.ppermute(piece, 'rows', perm)  9.49 us
    pallas_call x1, Pallas kernels, section(): pl.pallas_call(interior_kernel, out_shape=(frame, frame, frame_t, square,...  8.87 us
    pallas_call x1, Pallas kernels, section(): pl.pallas_call(functools.partial(edge_kernel, norm), out_shape=(jax.Shape...  8.06 us
    ppermute x4, waiting for transfers between devices, butterfly_sum(): got = lax.ppermute(send, 'rows', perm)  7.95 us
    ppermute x4, starting transfers between devices, butterfly_sum(): got = lax.ppermute(piece, 'rows', perm)  5.14 us
    ppermute x1, starting transfers between devices, local(): lax.ppermute(jnp.concatenate([inputs[-2:], cotangent[-2:]]), 'rows', up)  3.06 us
  transfers between devices with their start and end apart: 10, of which 7 were waited for; matrix products, arithmetic and copies ran while one was open for 0% of the time, Pallas kernels for 27%

profile of v15, /device:TPU:0, one launch (start us, length us, event | category | flops | bytes accessed | tf_op | source)
XLA Modules:
  0.0 73.1 jit_solution(12689888942279494992)
XLA Ops:
  0.6 1.3 %fusion.1 = (bf16[2,512,128]{2,1,0:T(8,128)(2,1)S(1)}, bf16[2,512,128]{2,1,0:T(8,128)(2,1)S(1)}, bf16[2,512,128]{2,1,0:T(8,128)(2,1)S(1)}, bf16[2,512,128]{2,1,0:T(8,128)(2,1)S(1)}) fusion(bf16[8,512,128]{2,1,0:T(8,128)(2,1)} %x_hbm.7, bf16[8,512,128]{2,1,0:T(8,128)(2,1)} %c_hbm.7), kind=kLoop, calls=%fused_computation.15 | loop fusion | bytes 2097152 | tf_op jit(solution)/shard_map/slice | solution.py:347
  2.0 1.3 %collective-permute-start.1 = (bf16[4,512,128]{2,1,0:T(8,128)(2,1)S(1)}, bf16[4,512,128]{2,1,0:T(8,128)(2,1)S(1)}, u32[]{:S(2)}, u32[]{:S(2)}) collective-permute-start(bf16[4,512,128]{2,1,0:T(8,128)(2,1)S(1)} %pad_maximum_fusion.1), channel_id=1, source_target_pairs={{1,0},{2,1},{3,2},{4,3},{5,4},{6,5},{7,6},{8,7},{9,8},{10,9},{11,1... | collective-permute-start | bytes 1572872 | tf_op jit(solution)/shard_map/ppermute | solution.py:347
  3.3 3.1 %collective-permute-start = (bf16[4,512,128]{2,1,0:T(8,128)(2,1)S(1)}, bf16[4,512,128]{2,1,0:T(8,128)(2,1)S(1)}, u32[]{:S(2)}, u32[]{:S(2)}) collective-permute-start(bf16[4,512,128]{2,1,0:T(8,128)(2,1)S(1)} %pad_maximum_fusion), channel_id=1, source_target_pairs={{0,1},{1,2},{2,3},{3,4},{4,5},{5,6},{6,7},{7,8},{8,9},{9,10},{10,1... | collective-permute-start | bytes 1572872 | tf_op jit(solution)/shard_map/ppermute | solution.py:346
  7.0 8.9 %shard_map.101 = (bf16[10,512,128]{2,1,0:T(8,128)(2,1)}, bf16[10,512,128]{2,1,0:T(8,128)(2,1)}, bf16[10,128,512]{2,1,0:T(8,128)(2,1)}, f32[384,384]{1,0:T(8,128)...) custom-call(s32[1]{0:T(128)S(6)} %copy.15.idx_ref, ...), custom_call_target="tpu_custom_call" | custom-call | flops 3925868544 | bytes 4194304 | tf_op jit(solution)/shard_map/pallas_call | solution.py:225
  15.9 0.0 copy-start.1
  16.0 0.8 %copy-done.1 = bf16[4,512,128]{2,1,0:T(8,128)(2,1)} copy-done((bf16[4,512,128]{2,1,0:T(8,128)(2,1)}, bf16[4,512,128]{2,1,0:T(8,128)(2,1)S(1)}, u32[]{:S(2)}) %copy-start.1) | copy-done | bytes 524312
  16.7 0.2 copy-done.2
  16.9 8.1 %shard_map.102 = (f32[2320,128]{1,0:T(8,128)}, bf16[10,512,128]{2,1,0:T(8,128)(2,1)}, bf16[10,512,128]{2,1,0:T(8,128)(2,1)}) custom-call(s32[1]{0:T(128)S(6)} %copy.15.idx_ref, f32[16,2,128]{2,1,0:T(2,128)} %lt_ref.3, bf16[8,512,128]{2,1,0:T(8,128)(2,1)} %x_hbm.7, bf16[8,512,128]{2,1,0:T(8,128)(2,1)} %c_hbm.7, bf16[4,512,128]{2,1,0:T(8,128)(2,1)} %copy-done.2, ...), custom_call_target="tpu_custom_call" | custom-call | flops 2113929216 | bytes 5242880 | tf_op jit(solution)/shard_map/pallas_call | solution.py:243
  25.0 1.4 %slice_select_fusion = f32[1160,128]{1,0:T(8,128)S(1)} fusion(f32[2320,128]{1,0:T(8,128)} %get-tuple-element.36, pred[]{:T(512)S(6)} %eq.35), kind=kLoop, calls=%fused_computation.3 | loop fusion | flops 148480 | bytes 1781761 | tf_op jit(solution)/shard_map/jit(_where)/select_n | solution.py:320
  26.4 3.5 %collective-permute-start.2 = (f32[1160,128]{1,0:T(8,128)S(1)}, f32[1160,128]{1,0:T(8,128)S(1)}, u32[]{:S(2)}, u32[]{:S(2)}) collective-permute-start(f32[1160,128]{1,0:T(8,128)S(1)} %slice_select_fusion), channel_id=1, source_target_pairs={{0,1},{1,0},{2,3},{3,2},{4,5},{5,4},{6,7},{7,6},{8,9},{9,8},{10,11... | collective-permute-start | bytes 1781768 | tf_op jit(solution)/shard_map/ppermute | solution.py:321
  29.9 1.6 %collective-permute-done.2 = f32[1160,128]{1,0:T(8,128)S(1)} collective-permute-done((f32[1160,128]{1,0:T(8,128)S(1)}, f32[1160,128]{1,0:T(8,128)S(1)}, u32[]{:S(2)}, u32[]{:S(2)}) %collective-permute-start.2) | collective-permute-done | bytes 593952 | tf_op jit(solution)/shard_map/ppermute | solution.py:321
  31.6 0.1 select_add_fusion
  31.7 2.8 %collective-permute-start.3 = (f32[580,128]{1,0:T(8,128)S(1)}, f32[580,128]{1,0:T(8,128)S(1)}, u32[]{:S(2)}, u32[]{:S(2)}) collective-permute-start(f32[580,128]{1,0:T(8,128)S(1)} %slice_select_fusion.1), channel_id=1, source_target_pairs={{0,2},{1,5},{2,0},{3,7},{4,6},{5,1},{6,4},{7,3},{8,10},{9,13},{10,... | collective-permute-start | bytes 890888 | tf_op jit(solution)/shard_map/ppermute | solution.py:321
  34.5 5.6 %shard_map.103 = (bf16[8,512,128]{2,1,0:T(8,128)(2,1)}, bf16[8,512,128]{2,1,0:T(8,128)(2,1)}) custom-call(bf16[8,512,128]{2,1,0:T(8,128)(2,1)} %x_hbm.7, bf16[8,512,128]{2,1,0:T(8,128)(2,1)} %c_hbm.7, bf16[10,512,128]{2,1,0:T(8,128)(2,1)} %get-tuple-element.37.hid_hbm, bf16[10,512,128]{2,1,0:T(8,128)(2,1)} %get-tuple-element.38.bf_hbm, ...), custom_call_target="tpu_custom_call" | custom-call | flops 1207959552 | bytes 2097152 | tf_op jit(solution)/shard_map/pallas_call | solution.py:323
  40.2 0.1 select_add_fusion.1
  40.2 1.6 %collective-permute-start.4 = (f32[290,128]{1,0:T(8,128)S(1)}, f32[290,128]{1,0:T(8,128)S(1)}, u32[]{:S(2)}, u32[]{:S(2)}) collective-permute-start(f32[290,128]{1,0:T(8,128)S(1)} %slice_select_fusion.2), channel_id=1, source_target_pairs={{0,4},{1,3},{2,6},{3,1},{4,0},{5,7},{6,2},{7,5},{8,12},{9,11},{10,... | collective-permute-start | bytes 445448 | tf_op jit(solution)/shard_map/ppermute | solution.py:321
  41.9 3.6 %collective-permute-done.4 = f32[290,128]{1,0:T(8,128)S(1)} collective-permute-done((f32[290,128]{1,0:T(8,128)S(1)}, f32[290,128]{1,0:T(8,128)S(1)}, u32[]{:S(2)}, u32[]{:S(2)}) %collective-permute-start.4) | collective-permute-done | bytes 148512 | tf_op jit(solution)/shard_map/ppermute | solution.py:321
  45.6 2.7 %collective-permute-start.5 = (f32[145,128]{1,0:T(8,128)S(1)}, f32[145,128]{1,0:T(8,128)S(1)}, u32[]{:S(2)}, u32[]{:S(2)}) collective-permute-start(f32[145,128]{1,0:T(8,128)S(1)} %slice_select_fusion.3), channel_id=1, source_target_pairs={{0,8},{1,9},{2,10},{3,11},{4,12},{5,13},{6,14},{7,15},{8,0},{9,1},... | collective-permute-start | bytes 222728 | tf_op jit(solution)/shard_map/ppermute | solution.py:321
  48.2 2.7 %collective-permute-done.5 = f32[145,128]{1,0:T(8,128)S(1)} collective-permute-done((f32[145,128]{1,0:T(8,128)S(1)}, f32[145,128]{1,0:T(8,128)S(1)}, u32[]{:S(2)}, u32[]{:S(2)}) %collective-permute-start.5) | collective-permute-done | bytes 74272 | tf_op jit(solution)/shard_map/ppermute | solution.py:321
  50.9 2.7 %collective-permute-start.6 = (f32[145,128]{1,0:T(8,128)S(1)}, f32[145,128]{1,0:T(8,128)S(1)}, u32[]{:S(2)}, u32[]{:S(2)}) collective-permute-start(f32[145,128]{1,0:T(8,128)S(1)} %select_add_fusion.3), channel_id=1, source_target_pairs={{0,8},{1,9},{2,10},{3,11},{4,12},{5,13},{6,14},{7,15},{8,0},{9,1},... | collective-permute-start | bytes 222728 | tf_op jit(solution)/shard_map/ppermute | solution.py:328
  53.6 2.7 %collective-permute-done.6 = f32[145,128]{1,0:T(8,128)S(1)} collective-permute-done((f32[145,128]{1,0:T(8,128)S(1)}, f32[145,128]{1,0:T(8,128)S(1)}, u32[]{:S(2)}, u32[]{:S(2)}) %collective-permute-start.6) | collective-permute-done | bytes 74272 | tf_op jit(solution)/shard_map/ppermute | solution.py:328
  56.3 1.6 %collective-permute-start.7 = (f32[290,128]{1,0:T(8,128)S(1)}, f32[290,128]{1,0:T(8,128)S(1)}, u32[]{:S(2)}, u32[]{:S(2)}) collective-permute-start(f32[290,128]{1,0:T(8,128)S(1)} %maximum_select_fusion.3), channel_id=1, source_target_pairs={{0,4},{1,3},{2,6},{3,1},{4,0},{5,7},{6,2},{7,5},{8,12},{9,11},{10,... | collective-permute-start | bytes 445448 | tf_op jit(solution)/shard_map/ppermute | solution.py:328
  58.0 4.3 %collective-permute-done.7 = f32[290,128]{1,0:T(8,128)S(1)} collective-permute-done((f32[290,128]{1,0:T(8,128)S(1)}, f32[290,128]{1,0:T(8,128)S(1)}, u32[]{:S(2)}, u32[]{:S(2)}) %collective-permute-start.7) | collective-permute-done | bytes 148512 | tf_op jit(solution)/shard_map/ppermute | solution.py:328
  62.3 0.8 %collective-permute-start.8 = (f32[580,128]{1,0:T(8,128)S(1)}, f32[580,128]{1,0:T(8,128)S(1)}, u32[]{:S(2)}, u32[]{:S(2)}) collective-permute-start(f32[580,128]{1,0:T(8,128)S(1)} %maximum_select_fusion.2), channel_id=1, source_target_pairs={{0,2},{1,5},{2,0},{3,7},{4,6},{5,1},{6,4},{7,3},{8,10},{9,13},{10,... | collective-permute-start | bytes 890888 | tf_op jit(solution)/shard_map/ppermute | solution.py:328
  63.1 5.6 %shard_map.104 = (bf16[8,512,128]{2,1,0:T(8,128)(2,1)}, bf16[8,512,128]{2,1,0:T(8,128)(2,1)}) custom-call(bf16[8,512,128]{2,1,0:T(8,128)(2,1)} %x_hbm.7, bf16[8,512,128]{2,1,0:T(8,128)(2,1)} %c_hbm.7, bf16[10,512,128]{2,1,0:T(8,128)(2,1)} %get-tuple-element.37.hid_hbm, ...), custom_call_target="tpu_custom_call", output_to_operand_aliasing={{0}: (6, {}), {1}: (7, {})} | custom-call | flops 1207959552 | bytes 2097152 | tf_op jit(solution)/shard_map/pallas_call | solution.py:330
  68.7 0.5 collective-permute-done.8
  69.2 0.1 maximum_select_fusion.1
  69.3 0.1 collective-permute-start.9
  69.3 2.0 %collective-permute-done.9 = f32[1160,128]{1,0:T(8,128)S(1)} collective-permute-done((f32[1160,128]{1,0:T(8,128)S(1)}, f32[1160,128]{1,0:T(8,128)S(1)}, u32[]{:S(2)}, u32[]{:S(2)}) %collective-permute-start.9) | collective-permute-done | bytes 593952 | tf_op jit(solution)/shard_map/ppermute | solution.py:328
  71.3 0.1 maximum_select_fusion
  71.5 1.1 %fusion = (f32[1152,128]{1,0:T(8,128)}, f32[1152,128]{1,0:T(8,128)}) fusion(f32[2320,128]{1,0:T(8,128)S(1)} %maximum_select_fusion), kind=kLoop, calls=%fused_computation.14 | loop fusion | bytes 2359296 | tf_op jit(solution)/shard_map/slice | solution.py:360
  72.6 0.6 slice.68
  (15 shorter events, 0.3 us)
Async XLA Ops:
  2.0 14.0 %collective-permute-start.1 = (bf16[4,512,128]{2,1,0:T(8,128)(2,1)S(1)}, bf16[4,512,128]{2,1,0:T(8,128)(2,1)S(1)}, u32[]{:S(2)}, u32[]{:S(2)}) collective-permute-start(bf16[4,512,128]{2,1,0:T(8,128)(2,1)S(1)} %pad_maximum_fusion.1), channel_id=1, source_target_pairs={{1,0},{2,1},{3,2},{4,3},{5,4},{6,5},{7,6},{8,7},{9,8},{10,9},{11,1... | collective-permute-start | bytes 1572872 | tf_op jit(solution)/shard_map/ppermute | solution.py:347
  3.3 12.6 %collective-permute-start = (bf16[4,512,128]{2,1,0:T(8,128)(2,1)S(1)}, bf16[4,512,128]{2,1,0:T(8,128)(2,1)S(1)}, u32[]{:S(2)}, u32[]{:S(2)}) collective-permute-start(bf16[4,512,128]{2,1,0:T(8,128)(2,1)S(1)} %pad_maximum_fusion), channel_id=1, source_target_pairs={{0,1},{1,2},{2,3},{3,4},{4,5},{5,6},{6,7},{7,8},{8,9},{9,10},{10,1... | collective-permute-start | bytes 1572872 | tf_op jit(solution)/shard_map/ppermute | solution.py:346
  15.9 0.8 %copy-start.1 = (bf16[4,512,128]{2,1,0:T(8,128)(2,1)}, bf16[4,512,128]{2,1,0:T(8,128)(2,1)S(1)}, u32[]{:S(2)}) copy-start(bf16[4,512,128]{2,1,0:T(8,128)(2,1)S(1)} %collective-permute-done.1.after_hbm) | copy-start | bytes 1572868
  16.0 0.9 %copy-start.2 = (bf16[4,512,128]{2,1,0:T(8,128)(2,1)}, bf16[4,512,128]{2,1,0:T(8,128)(2,1)S(1)}, u32[]{:S(2)}) copy-start(bf16[4,512,128]{2,1,0:T(8,128)(2,1)S(1)} %collective-permute-done.before_hbm) | copy-start | bytes 1572868
  25.0 6.6 %copy-start = (f32[2320,128]{1,0:T(8,128)S(1)}, f32[2320,128]{1,0:T(8,128)}, u32[]{:S(2)}) copy-start(f32[2320,128]{1,0:T(8,128)} %get-tuple-element.36) | copy-start | bytes 3563524
  26.4 5.2 %collective-permute-start.2 = (f32[1160,128]{1,0:T(8,128)S(1)}, f32[1160,128]{1,0:T(8,128)S(1)}, u32[]{:S(2)}, u32[]{:S(2)}) collective-permute-start(f32[1160,128]{1,0:T(8,128)S(1)} %slice_select_fusion), channel_id=1, source_target_pairs={{0,1},{1,0},{2,3},{3,2},{4,5},{5,4},{6,7},{7,6},{8,9},{9,8},{10,11... | collective-permute-start | bytes 1781768 | tf_op jit(solution)/shard_map/ppermute | solution.py:321
  31.7 8.4 %collective-permute-start.3 = (f32[580,128]{1,0:T(8,128)S(1)}, f32[580,128]{1,0:T(8,128)S(1)}, u32[]{:S(2)}, u32[]{:S(2)}) collective-permute-start(f32[580,128]{1,0:T(8,128)S(1)} %slice_select_fusion.1), channel_id=1, source_target_pairs={{0,2},{1,5},{2,0},{3,7},{4,6},{5,1},{6,4},{7,3},{8,10},{9,13},{10,... | collective-permute-start | bytes 890888 | tf_op jit(solution)/shard_map/ppermute | solution.py:321
  40.2 5.3 %collective-permute-start.4 = (f32[290,128]{1,0:T(8,128)S(1)}, f32[290,128]{1,0:T(8,128)S(1)}, u32[]{:S(2)}, u32[]{:S(2)}) collective-permute-start(f32[290,128]{1,0:T(8,128)S(1)} %slice_select_fusion.2), channel_id=1, source_target_pairs={{0,4},{1,3},{2,6},{3,1},{4,0},{5,7},{6,2},{7,5},{8,12},{9,11},{10,... | collective-permute-start | bytes 445448 | tf_op jit(solution)/shard_map/ppermute | solution.py:321
  45.6 5.4 %collective-permute-start.5 = (f32[145,128]{1,0:T(8,128)S(1)}, f32[145,128]{1,0:T(8,128)S(1)}, u32[]{:S(2)}, u32[]{:S(2)}) collective-permute-start(f32[145,128]{1,0:T(8,128)S(1)} %slice_select_fusion.3), channel_id=1, source_target_pairs={{0,8},{1,9},{2,10},{3,11},{4,12},{5,13},{6,14},{7,15},{8,0},{9,1},... | collective-permute-start | bytes 222728 | tf_op jit(solution)/shard_map/ppermute | solution.py:321
  50.9 5.4 %collective-permute-start.6 = (f32[145,128]{1,0:T(8,128)S(1)}, f32[145,128]{1,0:T(8,128)S(1)}, u32[]{:S(2)}, u32[]{:S(2)}) collective-permute-start(f32[145,128]{1,0:T(8,128)S(1)} %select_add_fusion.3), channel_id=1, source_target_pairs={{0,8},{1,9},{2,10},{3,11},{4,12},{5,13},{6,14},{7,15},{8,0},{9,1},... | collective-permute-start | bytes 222728 | tf_op jit(solution)/shard_map/ppermute | solution.py:328
  56.3 6.0 %collective-permute-start.7 = (f32[290,128]{1,0:T(8,128)S(1)}, f32[290,128]{1,0:T(8,128)S(1)}, u32[]{:S(2)}, u32[]{:S(2)}) collective-permute-start(f32[290,128]{1,0:T(8,128)S(1)} %maximum_select_fusion.3), channel_id=1, source_target_pairs={{0,4},{1,3},{2,6},{3,1},{4,0},{5,7},{6,2},{7,5},{8,12},{9,11},{10,... | collective-permute-start | bytes 445448 | tf_op jit(solution)/shard_map/ppermute | solution.py:328
  62.3 6.8 %collective-permute-start.8 = (f32[580,128]{1,0:T(8,128)S(1)}, f32[580,128]{1,0:T(8,128)S(1)}, u32[]{:S(2)}, u32[]{:S(2)}) collective-permute-start(f32[580,128]{1,0:T(8,128)S(1)} %maximum_select_fusion.2), channel_id=1, source_target_pairs={{0,2},{1,5},{2,0},{3,7},{4,6},{5,1},{6,4},{7,3},{8,10},{9,13},{10,... | collective-permute-start | bytes 890888 | tf_op jit(solution)/shard_map/ppermute | solution.py:328
  69.3 2.1 %collective-permute-start.9 = (f32[1160,128]{1,0:T(8,128)S(1)}, f32[1160,128]{1,0:T(8,128)S(1)}, u32[]{:S(2)}, u32[]{:S(2)}) collective-permute-start(f32[1160,128]{1,0:T(8,128)S(1)} %maximum_select_fusion.1), channel_id=1, source_target_pairs={{0,1},{1,0},{2,3},{3,2},{4,5},{5,4},{6,7},{7,6},{8,9},{9,8},{10,11... | collective-permute-start | bytes 1781768 | tf_op jit(solution)/shard_map/ppermute | solution.py:328

commit v16 on v12

--- a/solution.py
+++ b/solution.py
@@ -125,8 +125,8 @@
 
 def edge_kernel(norm, idx_ref, lt_ref, x_hbm, c_hbm, before_hbm, after_hbm, hida_hbm, bfa_hbm, hidta_hbm,
                 acc1a_ref, acc2a_ref, lva_ref, k1f, k2b,
-                grad_ref, hid_ref, bf_ref,
-                x_ref, c_ref, hidt_ref, xt_ref, acc1, acc2, sems):
+                keep_ref, send_ref, hid_ref, bf_ref,
+                x_ref, c_ref, hidt_ref, xt_ref, acc1, acc2, sems, grad_ref):
     count = hid_ref.shape[0] - 2
     width, ch = hid_ref.shape[1], hid_ref.shape[2]
     copies = [
@@ -175,6 +175,11 @@
     grad_ref[base:, :] = jnp.zeros((tail, ch), jnp.float32)
     grad_ref[base : base + 1, :] = lv0 * norm
     grad_ref[base + 1 : base + 2, :] = lv1 * norm
+    half = keep_ref.shape[0]
+    even = lax.axis_index("rows") % 2 == 0
+    lo, hi = grad_ref[0:half, :], grad_ref[half:, :]
+    keep_ref[...] = jnp.where(even, lo, hi)
+    send_ref[...] = jnp.where(even, hi, lo)
 
 
 def out_kernel(first_row, aliased, x_hbm, c_hbm, hid_hbm, bf_hbm, k2f, k1b, *refs):
@@ -240,11 +245,12 @@
         ),
     )(level_index, level_table, inputs, cotangent, k1, k2)
     before, after = before_fn()
-    packed, hid, bf = pl.pallas_call(
+    halfrows = jax.ShapeDtypeStruct((packed_rows // 2, ch), jnp.float32)
+    keep, send, hid, bf = pl.pallas_call(
         functools.partial(edge_kernel, norm),
-        out_shape=(jax.ShapeDtypeStruct((packed_rows, ch), jnp.float32), frame, frame),
+        out_shape=(halfrows, halfrows, frame, frame),
         in_specs=[smem, spec] + [anywhere] * 7 + [spec] * 5,
-        out_specs=(spec, spec, spec),
+        out_specs=(spec, spec, spec, spec),
         scratch_shapes=[
             pltpu.VMEM((count + 4, width, ch), jnp.bfloat16),
             pltpu.VMEM((count + 4, width, ch), jnp.bfloat16),
@@ -253,6 +259,7 @@
             pltpu.VMEM((big, big), jnp.float32),
             pltpu.VMEM((big, big), jnp.float32),
             pltpu.SemaphoreType.DMA((9,)),
+            pltpu.VMEM((packed_rows, ch), jnp.float32),
         ],
         compiler_params=params,
         cost_estimate=pl.CostEstimate(
@@ -287,10 +294,10 @@
             ),
             inputs, cotangent, hid, bf, k2f, k1b,
         ))
-    return chunks, packed
-
-
-def butterfly_sum(block, riders):
+    return chunks, (keep, send)
+
+
+def butterfly_sum(first_step, riders):
     n = lax.axis_size("rows")
     me = lax.axis_index("rows")
     bits = []
@@ -311,13 +318,15 @@
 
     state = ()
     count = 0
-    piece = block
     for k0, k1 in orders:
         perm, low = step_of(k0, k1)
-        half = piece.shape[0] // 2
-        lo, hi = piece[:half], piece[half:]
-        keep = jnp.where(low, lo, hi)
-        send = jnp.where(low, hi, lo)
+        if count == 0:
+            keep, send = first_step
+        else:
+            half = piece.shape[0] // 2
+            lo, hi = piece[:half], piece[half:]
+            keep = jnp.where(low, lo, hi)
+            send = jnp.where(low, hi, lo)
         got = lax.ppermute(send, "rows", perm)
         if count in riders:
             got, state = lax.optimization_barrier((got, riders[count](*state)))

time: 73.5 us -> 73.7 us (level)
    select_n x4 -> x3, other arithmetic: 1.47 us -> 0.06 us  [butterfly_sum(): send = jnp.where(low, hi, lo)]
    add x4, other arithmetic: 0.24 us -> 1.26 us  [butterfly_sum(): piece = keep + got]
where the time goes in v16:
time: 73.7 us; the launch traced here: 73.3 us
  Pallas kernels  28.5 us (39%)
  starting transfers between devices  20.2 us (27%)
  waiting for transfers between devices  17.7 us (24%)
  local copies, waits for them, and re-layouts  3.86 us (5%)
  other arithmetic  1.71 us (2%)
  between operations  1.45 us (2%)
    pallas_call x2, Pallas kernels, butterfly_sum(): got, state = lax.optimization_barrier((got, riders[count](*state)))  11.2 us
    ppermute x4, starting transfers between devices, butterfly_sum(): got = lax.ppermute(send, 'rows', perm)  10.7 us
    ppermute x4, waiting for transfers between devices, butterfly_sum(): got = lax.ppermute(piece, 'rows', perm)  9.48 us
    pallas_call x1, Pallas kernels, section(): pl.pallas_call(interior_kernel, out_shape=(frame, frame, frame_t, square,...  8.87 us
    pallas_call x1, Pallas kernels, section(): pl.pallas_call(functools.partial(edge_kernel, norm), out_shape=(halfrows,...  8.4 us
    ppermute x4, waiting for transfers between devices, butterfly_sum(): got = lax.ppermute(send, 'rows', perm)  8.16 us
    ppermute x4, starting transfers between devices, butterfly_sum(): got = lax.ppermute(piece, 'rows', perm)  5.14 us
    ppermute x1, starting transfers between devices, local(): lax.ppermute(jnp.concatenate([inputs[-2:], cotangent[-2:]]), 'rows', up)  3.06 us
  transfers between devices with their start and end apart: 10, of which 7 were waited for; matrix products, arithmetic and copies ran while one was open for 0% of the time, Pallas kernels for 27%

profile of v16, /device:TPU:0, one launch (start us, length us, event | category | flops | bytes accessed | tf_op | source)
XLA Modules:
  0.0 73.3 jit_solution(13099443494854795964)
XLA Ops:
  0.6 1.3 %fusion.1 = (bf16[2,512,128]{2,1,0:T(8,128)(2,1)S(1)}, bf16[2,512,128]{2,1,0:T(8,128)(2,1)S(1)}, bf16[2,512,128]{2,1,0:T(8,128)(2,1)S(1)}, bf16[2,512,128]{2,1,0:T(8,128)(2,1)S(1)}) fusion(bf16[8,512,128]{2,1,0:T(8,128)(2,1)} %x_hbm.7, bf16[8,512,128]{2,1,0:T(8,128)(2,1)} %c_hbm.7), kind=kLoop, calls=%fused_computation.13 | loop fusion | bytes 2097152 | tf_op jit(solution)/shard_map/slice | solution.py:356
  2.0 1.3 %collective-permute-start.1 = (bf16[4,512,128]{2,1,0:T(8,128)(2,1)S(1)}, bf16[4,512,128]{2,1,0:T(8,128)(2,1)S(1)}, u32[]{:S(2)}, u32[]{:S(2)}) collective-permute-start(bf16[4,512,128]{2,1,0:T(8,128)(2,1)S(1)} %pad_maximum_fusion.1), channel_id=1, source_target_pairs={{1,0},{2,1},{3,2},{4,3},{5,4},{6,5},{7,6},{8,7},{9,8},{10,9},{11,1... | collective-permute-start | bytes 1572872 | tf_op jit(solution)/shard_map/ppermute | solution.py:356
  3.3 3.1 %collective-permute-start = (bf16[4,512,128]{2,1,0:T(8,128)(2,1)S(1)}, bf16[4,512,128]{2,1,0:T(8,128)(2,1)S(1)}, u32[]{:S(2)}, u32[]{:S(2)}) collective-permute-start(bf16[4,512,128]{2,1,0:T(8,128)(2,1)S(1)} %pad_maximum_fusion), channel_id=1, source_target_pairs={{0,1},{1,2},{2,3},{3,4},{4,5},{5,6},{6,7},{7,8},{8,9},{9,10},{10,1... | collective-permute-start | bytes 1572872 | tf_op jit(solution)/shard_map/ppermute | solution.py:355
  7.0 8.9 %shard_map.101 = (bf16[10,512,128]{2,1,0:T(8,128)(2,1)}, bf16[10,512,128]{2,1,0:T(8,128)(2,1)}, bf16[10,128,512]{2,1,0:T(8,128)(2,1)}, f32[384,384]{1,0:T(8,128)...) custom-call(s32[1]{0:T(128)S(6)} %copy.15.idx_ref, ...), custom_call_target="tpu_custom_call" | custom-call | flops 3925868544 | bytes 4194304 | tf_op jit(solution)/shard_map/pallas_call | solution.py:230
  15.9 0.0 collective-permute-done.before_hbm
  16.0 0.7 %copy-done = bf16[4,512,128]{2,1,0:T(8,128)(2,1)} copy-done((bf16[4,512,128]{2,1,0:T(8,128)(2,1)}, bf16[4,512,128]{2,1,0:T(8,128)(2,1)S(1)}, u32[]{:S(2)}) %copy-start) | copy-done | bytes 524312
  16.7 0.2 copy-done.1
  16.9 8.4 %shard_map.102 = (f32[1160,128]{1,0:T(8,128)}, f32[1160,128]{1,0:T(8,128)}, bf16[10,512,128]{2,1,0:T(8,128)(2,1)}, bf16[10,512,128]{2,1,0:T(8,128)(2,1)}) custom-call(s32[1]{0:T(128)S(6)} %copy.15.idx_ref, f32[16,2,128]{2,1,0:T(2,128)} %lt_ref.3, bf16[8,512,128]{2,1,0:T(8,128)(2,1)} %x_hbm.7, bf16[8,512,128]{2,1,0:T(8,128)(2,1)} %c_hbm.7, ...), custom_call_target="tpu_custom_call" | custom-call | flops 2113929216 | bytes 5242880 | tf_op jit(solution)/shard_map/pallas_call | solution.py:249
  25.3 3.6 %collective-permute-start.2 = (f32[1160,128]{1,0:T(8,128)}, f32[1160,128]{1,0:T(8,128)S(1)}, u32[]{:S(2)}, u32[]{:S(2)}) collective-permute-start(f32[1160,128]{1,0:T(8,128)} %get-tuple-element.38), channel_id=1, source_target_pairs={{0,1},{1,0},{2,3},{3,2},{4,5},{5,4},{6,7},{7,6},{8,9},{9,8},{10,11... | collective-permute-start | bytes 1781768 | tf_op jit(solution)/shard_map/ppermute | solution.py:330
  28.9 1.8 %collective-permute-done.2 = f32[1160,128]{1,0:T(8,128)S(1)} collective-permute-done((f32[1160,128]{1,0:T(8,128)}, f32[1160,128]{1,0:T(8,128)S(1)}, u32[]{:S(2)}, u32[]{:S(2)}) %collective-permute-start.2) | collective-permute-done | bytes 593952 | tf_op jit(solution)/shard_map/ppermute | solution.py:330
  30.7 1.2 %add.44 = f32[1160,128]{1,0:T(8,128)S(1)} add(f32[1160,128]{1,0:T(8,128)} %get-tuple-element.37, f32[1160,128]{1,0:T(8,128)S(1)} %collective-permute-done.2) | non-fusion elementwise | flops 148480 | bytes 1781760 | tf_op jit(solution)/shard_map/add | solution.py:334
  31.9 2.8 %collective-permute-start.3 = (f32[580,128]{1,0:T(8,128)S(1)}, f32[580,128]{1,0:T(8,128)S(1)}, u32[]{:S(2)}, u32[]{:S(2)}) collective-permute-start(f32[580,128]{1,0:T(8,128)S(1)} %slice_select_fusion), channel_id=1, source_target_pairs={{0,2},{1,5},{2,0},{3,7},{4,6},{5,1},{6,4},{7,3},{8,10},{9,13},{10,... | collective-permute-start | bytes 890888 | tf_op jit(solution)/shard_map/ppermute | solution.py:330
  34.7 5.6 %shard_map.103 = (bf16[8,512,128]{2,1,0:T(8,128)(2,1)}, bf16[8,512,128]{2,1,0:T(8,128)(2,1)}) custom-call(bf16[8,512,128]{2,1,0:T(8,128)(2,1)} %x_hbm.7, bf16[8,512,128]{2,1,0:T(8,128)(2,1)} %c_hbm.7, bf16[10,512,128]{2,1,0:T(8,128)(2,1)} %get-tuple-element.39.hid_hbm, bf16[10,512,128]{2,1,0:T(8,128)(2,1)} %get-tuple-element.40.bf_hbm, ...), custom_call_target="tpu_custom_call" | custom-call | flops 1207959552 | bytes 2097152 | tf_op jit(solution)/shard_map/pallas_call | solution.py:332
  40.3 0.0 collective-permute-done.3
  40.3 0.1 select_add_fusion
  40.4 1.6 %collective-permute-start.4 = (f32[290,128]{1,0:T(8,128)S(1)}, f32[290,128]{1,0:T(8,128)S(1)}, u32[]{:S(2)}, u32[]{:S(2)}) collective-permute-start(f32[290,128]{1,0:T(8,128)S(1)} %slice_select_fusion.1), channel_id=1, source_target_pairs={{0,4},{1,3},{2,6},{3,1},{4,0},{5,7},{6,2},{7,5},{8,12},{9,11},{10,... | collective-permute-start | bytes 445448 | tf_op jit(solution)/shard_map/ppermute | solution.py:330
  42.1 3.6 %collective-permute-done.4 = f32[290,128]{1,0:T(8,128)S(1)} collective-permute-done((f32[290,128]{1,0:T(8,128)S(1)}, f32[290,128]{1,0:T(8,128)S(1)}, u32[]{:S(2)}, u32[]{:S(2)}) %collective-permute-start.4) | collective-permute-done | bytes 148512 | tf_op jit(solution)/shard_map/ppermute | solution.py:330
  45.7 2.7 %collective-permute-start.5 = (f32[145,128]{1,0:T(8,128)S(1)}, f32[145,128]{1,0:T(8,128)S(1)}, u32[]{:S(2)}, u32[]{:S(2)}) collective-permute-start(f32[145,128]{1,0:T(8,128)S(1)} %slice_select_fusion.2), channel_id=1, source_target_pairs={{0,8},{1,9},{2,10},{3,11},{4,12},{5,13},{6,14},{7,15},{8,0},{9,1},... | collective-permute-start | bytes 222728 | tf_op jit(solution)/shard_map/ppermute | solution.py:330
  48.4 2.7 %collective-permute-done.5 = f32[145,128]{1,0:T(8,128)S(1)} collective-permute-done((f32[145,128]{1,0:T(8,128)S(1)}, f32[145,128]{1,0:T(8,128)S(1)}, u32[]{:S(2)}, u32[]{:S(2)}) %collective-permute-start.5) | collective-permute-done | bytes 74272 | tf_op jit(solution)/shard_map/ppermute | solution.py:330
  51.1 2.7 %collective-permute-start.6 = (f32[145,128]{1,0:T(8,128)S(1)}, f32[145,128]{1,0:T(8,128)S(1)}, u32[]{:S(2)}, u32[]{:S(2)}) collective-permute-start(f32[145,128]{1,0:T(8,128)S(1)} %select_add_fusion.2), channel_id=1, source_target_pairs={{0,8},{1,9},{2,10},{3,11},{4,12},{5,13},{6,14},{7,15},{8,0},{9,1},... | collective-permute-start | bytes 222728 | tf_op jit(solution)/shard_map/ppermute | solution.py:337
  53.8 2.7 %collective-permute-done.6 = f32[145,128]{1,0:T(8,128)S(1)} collective-permute-done((f32[145,128]{1,0:T(8,128)S(1)}, f32[145,128]{1,0:T(8,128)S(1)}, u32[]{:S(2)}, u32[]{:S(2)}) %collective-permute-start.6) | collective-permute-done | bytes 74272 | tf_op jit(solution)/shard_map/ppermute | solution.py:337
  56.5 1.6 %collective-permute-start.7 = (f32[290,128]{1,0:T(8,128)S(1)}, f32[290,128]{1,0:T(8,128)S(1)}, u32[]{:S(2)}, u32[]{:S(2)}) collective-permute-start(f32[290,128]{1,0:T(8,128)S(1)} %maximum_select_fusion.3), channel_id=1, source_target_pairs={{0,4},{1,3},{2,6},{3,1},{4,0},{5,7},{6,2},{7,5},{8,12},{9,11},{10,... | collective-permute-start | bytes 445448 | tf_op jit(solution)/shard_map/ppermute | solution.py:337
  58.1 4.3 %collective-permute-done.7 = f32[290,128]{1,0:T(8,128)S(1)} collective-permute-done((f32[290,128]{1,0:T(8,128)S(1)}, f32[290,128]{1,0:T(8,128)S(1)}, u32[]{:S(2)}, u32[]{:S(2)}) %collective-permute-start.7) | collective-permute-done | bytes 148512 | tf_op jit(solution)/shard_map/ppermute | solution.py:337
  62.5 0.8 %collective-permute-start.8 = (f32[580,128]{1,0:T(8,128)S(1)}, f32[580,128]{1,0:T(8,128)S(1)}, u32[]{:S(2)}, u32[]{:S(2)}) collective-permute-start(f32[580,128]{1,0:T(8,128)S(1)} %maximum_select_fusion.2), channel_id=1, source_target_pairs={{0,2},{1,5},{2,0},{3,7},{4,6},{5,1},{6,4},{7,3},{8,10},{9,13},{10,... | collective-permute-start | bytes 890888 | tf_op jit(solution)/shard_map/ppermute | solution.py:337
  63.3 5.6 %shard_map.104 = (bf16[8,512,128]{2,1,0:T(8,128)(2,1)}, bf16[8,512,128]{2,1,0:T(8,128)(2,1)}) custom-call(bf16[8,512,128]{2,1,0:T(8,128)(2,1)} %x_hbm.7, bf16[8,512,128]{2,1,0:T(8,128)(2,1)} %c_hbm.7, bf16[10,512,128]{2,1,0:T(8,128)(2,1)} %get-tuple-element.39.hid_hbm, ...), custom_call_target="tpu_custom_call", output_to_operand_aliasing={{0}: (6, {}), {1}: (7, {})} | custom-call | flops 1207959552 | bytes 2097152 | tf_op jit(solution)/shard_map/pallas_call | solution.py:339
  68.9 0.5 collective-permute-done.8
  69.3 0.1 maximum_select_fusion.1
  69.4 0.1 collective-permute-start.9
  69.5 2.0 %collective-permute-done.9 = f32[1160,128]{1,0:T(8,128)S(1)} collective-permute-done((f32[1160,128]{1,0:T(8,128)S(1)}, f32[1160,128]{1,0:T(8,128)S(1)}, u32[]{:S(2)}, u32[]{:S(2)}) %collective-permute-start.9) | collective-permute-done | bytes 593952 | tf_op jit(solution)/shard_map/ppermute | solution.py:337
  71.5 0.1 maximum_select_fusion
  71.6 1.1 %fusion = (f32[1152,128]{1,0:T(8,128)}, f32[1152,128]{1,0:T(8,128)}) fusion(f32[2320,128]{1,0:T(8,128)S(1)} %maximum_select_fusion), kind=kLoop, calls=%fused_computation.12 | loop fusion | bytes 2359296 | tf_op jit(solution)/shard_map/slice | solution.py:369
  72.7 0.6 slice.60
  (12 shorter events, 0.3 us)
Async XLA Ops:
  2.0 14.0 %collective-permute-start.1 = (bf16[4,512,128]{2,1,0:T(8,128)(2,1)S(1)}, bf16[4,512,128]{2,1,0:T(8,128)(2,1)S(1)}, u32[]{:S(2)}, u32[]{:S(2)}) collective-permute-start(bf16[4,512,128]{2,1,0:T(8,128)(2,1)S(1)} %pad_maximum_fusion.1), channel_id=1, source_target_pairs={{1,0},{2,1},{3,2},{4,3},{5,4},{6,5},{7,6},{8,7},{9,8},{10,9},{11,1... | collective-permute-start | bytes 1572872 | tf_op jit(solution)/shard_map/ppermute | solution.py:356
  3.3 12.6 %collective-permute-start = (bf16[4,512,128]{2,1,0:T(8,128)(2,1)S(1)}, bf16[4,512,128]{2,1,0:T(8,128)(2,1)S(1)}, u32[]{:S(2)}, u32[]{:S(2)}) collective-permute-start(bf16[4,512,128]{2,1,0:T(8,128)(2,1)S(1)} %pad_maximum_fusion), channel_id=1, source_target_pairs={{0,1},{1,2},{2,3},{3,4},{4,5},{5,6},{6,7},{7,8},{8,9},{9,10},{10,1... | collective-permute-start | bytes 1572872 | tf_op jit(solution)/shard_map/ppermute | solution.py:355
  15.9 0.8 %copy-start = (bf16[4,512,128]{2,1,0:T(8,128)(2,1)}, bf16[4,512,128]{2,1,0:T(8,128)(2,1)S(1)}, u32[]{:S(2)}) copy-start(bf16[4,512,128]{2,1,0:T(8,128)(2,1)S(1)} %collective-permute-done.1.after_hbm) | copy-start | bytes 1572868
  15.9 1.0 %copy-start.1 = (bf16[4,512,128]{2,1,0:T(8,128)(2,1)}, bf16[4,512,128]{2,1,0:T(8,128)(2,1)S(1)}, u32[]{:S(2)}) copy-start(bf16[4,512,128]{2,1,0:T(8,128)(2,1)S(1)} %collective-permute-done.before_hbm) | copy-start | bytes 1572868
  25.3 5.4 %collective-permute-start.2 = (f32[1160,128]{1,0:T(8,128)}, f32[1160,128]{1,0:T(8,128)S(1)}, u32[]{:S(2)}, u32[]{:S(2)}) collective-permute-start(f32[1160,128]{1,0:T(8,128)} %get-tuple-element.38), channel_id=1, source_target_pairs={{0,1},{1,0},{2,3},{3,2},{4,5},{5,4},{6,7},{7,6},{8,9},{9,8},{10,11... | collective-permute-start | bytes 1781768 | tf_op jit(solution)/shard_map/ppermute | solution.py:330
  31.9 8.4 %collective-permute-start.3 = (f32[580,128]{1,0:T(8,128)S(1)}, f32[580,128]{1,0:T(8,128)S(1)}, u32[]{:S(2)}, u32[]{:S(2)}) collective-permute-start(f32[580,128]{1,0:T(8,128)S(1)} %slice_select_fusion), channel_id=1, source_target_pairs={{0,2},{1,5},{2,0},{3,7},{4,6},{5,1},{6,4},{7,3},{8,10},{9,13},{10,... | collective-permute-start | bytes 890888 | tf_op jit(solution)/shard_map/ppermute | solution.py:330
  40.4 5.3 %collective-permute-start.4 = (f32[290,128]{1,0:T(8,128)S(1)}, f32[290,128]{1,0:T(8,128)S(1)}, u32[]{:S(2)}, u32[]{:S(2)}) collective-permute-start(f32[290,128]{1,0:T(8,128)S(1)} %slice_select_fusion.1), channel_id=1, source_target_pairs={{0,4},{1,3},{2,6},{3,1},{4,0},{5,7},{6,2},{7,5},{8,12},{9,11},{10,... | collective-permute-start | bytes 445448 | tf_op jit(solution)/shard_map/ppermute | solution.py:330
  45.7 5.4 %collective-permute-start.5 = (f32[145,128]{1,0:T(8,128)S(1)}, f32[145,128]{1,0:T(8,128)S(1)}, u32[]{:S(2)}, u32[]{:S(2)}) collective-permute-start(f32[145,128]{1,0:T(8,128)S(1)} %slice_select_fusion.2), channel_id=1, source_target_pairs={{0,8},{1,9},{2,10},{3,11},{4,12},{5,13},{6,14},{7,15},{8,0},{9,1},... | collective-permute-start | bytes 222728 | tf_op jit(solution)/shard_map/ppermute | solution.py:330
  51.1 5.4 %collective-permute-start.6 = (f32[145,128]{1,0:T(8,128)S(1)}, f32[145,128]{1,0:T(8,128)S(1)}, u32[]{:S(2)}, u32[]{:S(2)}) collective-permute-start(f32[145,128]{1,0:T(8,128)S(1)} %select_add_fusion.2), channel_id=1, source_target_pairs={{0,8},{1,9},{2,10},{3,11},{4,12},{5,13},{6,14},{7,15},{8,0},{9,1},... | collective-permute-start | bytes 222728 | tf_op jit(solution)/shard_map/ppermute | solution.py:337
  56.5 6.0 %collective-permute-start.7 = (f32[290,128]{1,0:T(8,128)S(1)}, f32[290,128]{1,0:T(8,128)S(1)}, u32[]{:S(2)}, u32[]{:S(2)}) collective-permute-start(f32[290,128]{1,0:T(8,128)S(1)} %maximum_select_fusion.3), channel_id=1, source_target_pairs={{0,4},{1,3},{2,6},{3,1},{4,0},{5,7},{6,2},{7,5},{8,12},{9,11},{10,... | collective-permute-start | bytes 445448 | tf_op jit(solution)/shard_map/ppermute | solution.py:337
  62.5 6.8 %collective-permute-start.8 = (f32[580,128]{1,0:T(8,128)S(1)}, f32[580,128]{1,0:T(8,128)S(1)}, u32[]{:S(2)}, u32[]{:S(2)}) collective-permute-start(f32[580,128]{1,0:T(8,128)S(1)} %maximum_select_fusion.2), channel_id=1, source_target_pairs={{0,2},{1,5},{2,0},{3,7},{4,6},{5,1},{6,4},{7,3},{8,10},{9,13},{10,... | collective-permute-start | bytes 890888 | tf_op jit(solution)/shard_map/ppermute | solution.py:337
  69.4 2.1 %collective-permute-start.9 = (f32[1160,128]{1,0:T(8,128)S(1)}, f32[1160,128]{1,0:T(8,128)S(1)}, u32[]{:S(2)}, u32[]{:S(2)}) collective-permute-start(f32[1160,128]{1,0:T(8,128)S(1)} %maximum_select_fusion.1), channel_id=1, source_target_pairs={{0,1},{1,0},{2,3},{3,2},{4,5},{5,4},{6,7},{7,6},{8,9},{9,8},{10,11... | collective-permute-start | bytes 1781768 | tf_op jit(solution)/shard_map/ppermute | solution.py:337

commit v17 on v12

--- a/solution.py
+++ b/solution.py
@@ -70,8 +70,8 @@
 
 
 def interior_kernel(idx_ref, lt_ref, x_hbm, c_hbm, k1_ref, k2_ref,
-                    hid_ref, bf_ref, hidt_ref, acc1, acc2, lv_ref, k1f, k2f, k2b, k1b,
-                    x_ref, c_ref, xt_ref, sems):
+                    hid_ref, bf_ref, hidt_ref, acc1, acc2, lv_ref, k1f, k2f, k2b, k1b, xt_ref,
+                    x_ref, c_ref, sems):
     count = hid_ref.shape[0] - 2
     width, ch = hid_ref.shape[1], hid_ref.shape[2]
     copies = [
@@ -124,9 +124,9 @@
 
 
 def edge_kernel(norm, idx_ref, lt_ref, x_hbm, c_hbm, before_hbm, after_hbm, hida_hbm, bfa_hbm, hidta_hbm,
-                acc1a_ref, acc2a_ref, lva_ref, k1f, k2b,
+                xta_hbm, acc1a_ref, acc2a_ref, lva_ref, k1f, k2b,
                 grad_ref, hid_ref, bf_ref,
-                x_ref, c_ref, hidt_ref, xt_ref, acc1, acc2, sems):
+                x_ref, c_ref, hidt_ref, xt_ref, acc1, acc2, sems, xt_sem):
     count = hid_ref.shape[0] - 2
     width, ch = hid_ref.shape[1], hid_ref.shape[2]
     copies = [
@@ -142,7 +142,8 @@
         pltpu.make_async_copy(bfa_hbm.at[2:count], bf_ref.at[2:count], sems.at[7]),
         pltpu.make_async_copy(hidta_hbm.at[2:count], hidt_ref.at[2:count], sems.at[8]),
     ]
-    for cp in copies + inner:
+    xt_copy = pltpu.make_async_copy(xta_hbm.at[2 : count + 2], xt_ref.at[2 : count + 2], xt_sem.at[0])
+    for cp in copies + inner + [xt_copy]:
         cp.start()
     scale, shift, top, bottom = level_and_edges(idx_ref, lt_ref)
     phase_one, out_row, g1_row, g2_row, _ = row_ops(width, ch, scale, shift, top, bottom, count)
@@ -157,8 +158,9 @@
     lv0, lv1 = carry
     for cp in inner:
         cp.wait()
-    for r in (1, 2, 3, count, count + 1, count + 2):
+    for r in (1, count + 2):
         xt_ref[r] = x_ref[r].astype(jnp.float32).T.astype(xt_ref.dtype)
+    xt_copy.wait()
     for i in (0, 1, count - 2, count - 1):
         g2_row(i, hidt_ref, c_ref, acc2)
     for i in (0, count - 1):
@@ -222,16 +224,16 @@
     square = jax.ShapeDtypeStruct((big, big), jnp.float32)
     params = pltpu.CompilerParams(vmem_limit_bytes=60 * 1024 * 1024)
     matrix = jax.ShapeDtypeStruct((big, big), jnp.bfloat16)
-    hid, bf, hidt, acc1, acc2, lv, k1f, k2f, k2b, k1b = pl.pallas_call(
+    hid, bf, hidt, acc1, acc2, lv, k1f, k2f, k2b, k1b, xt = pl.pallas_call(
         interior_kernel,
         out_shape=(frame, frame, frame_t, square, square,
-                   jax.ShapeDtypeStruct((2, ch), jnp.float32), matrix, matrix, matrix, matrix),
+                   jax.ShapeDtypeStruct((2, ch), jnp.float32), matrix, matrix, matrix, matrix,
+                   jax.ShapeDtypeStruct((count + 4, ch, width), jnp.bfloat16)),
         in_specs=[smem, spec, anywhere, anywhere, spec, spec],
-        out_specs=(spec,) * 10,
+        out_specs=(spec,) * 11,
         scratch_shapes=[
             pltpu.VMEM((count + 4, width, ch), jnp.bfloat16),
             pltpu.VMEM((count + 4, width, ch), jnp.bfloat16),
-            pltpu.VMEM((count + 4, ch, width), jnp.bfloat16),
             pltpu.SemaphoreType.DMA((2,)),
         ],
         compiler_params=params,
@@ -243,7 +245,7 @@
     packed, hid, bf = pl.pallas_call(
         functools.partial(edge_kernel, norm),
         out_shape=(jax.ShapeDtypeStruct((packed_rows, ch), jnp.float32), frame, frame),
-        in_specs=[smem, spec] + [anywhere] * 7 + [spec] * 5,
+        in_specs=[smem, spec] + [anywhere] * 8 + [spec] * 5,
         out_specs=(spec, spec, spec),
         scratch_shapes=[
             pltpu.VMEM((count + 4, width, ch), jnp.bfloat16),
@@ -253,12 +255,13 @@
             pltpu.VMEM((big, big), jnp.float32),
             pltpu.VMEM((big, big), jnp.float32),
             pltpu.SemaphoreType.DMA((9,)),
+            pltpu.SemaphoreType.DMA((1,)),
         ],
         compiler_params=params,
         cost_estimate=pl.CostEstimate(
             flops=14 * unit, transcendentals=4 * width * ch, bytes_accessed=10 * count * width * ch
         ),
-    )(level_index, level_table, inputs, cotangent, before, after, hid, bf, hidt, acc1, acc2, lv, k1f, k2b)
+    )(level_index, level_table, inputs, cotangent, before, after, hid, bf, hidt, xt, acc1, acc2, lv, k1f, k2b)
     step = count // 2 if count % 2 == 0 else count
     whole = jax.ShapeDtypeStruct((count, width, ch), jnp.bfloat16)
     chunks = []

time: 73.5 us -> 73.6 us (level)
  transfers between devices with their start and end apart: 10 -> 10, of which waited for: 7 -> 7; matrix products, arithmetic and copies ran while one was open for 0% -> 0% of each run, Pallas kernels for 27% -> 28%
where the time goes in v17:
time: 73.6 us; the launch traced here: 73.2 us
  Pallas kernels  28.5 us (39%)
  starting transfers between devices  19.8 us (27%)
  waiting for transfers between devices  17.5 us (24%)
  local copies, waits for them, and re-layouts  3.86 us (5%)
  other arithmetic  2.09 us (3%)
  between operations  1.47 us (2%)
    pallas_call x2, Pallas kernels, butterfly_sum(): got, state = lax.optimization_barrier((got, riders[count](*state)))  11.2 us
    ppermute x4, starting transfers between devices, butterfly_sum(): got = lax.ppermute(send, 'rows', perm)  10.3 us
    ppermute x4, waiting for transfers between devices, butterfly_sum(): got = lax.ppermute(piece, 'rows', perm)  9.5 us
    pallas_call x1, Pallas kernels, section(): pl.pallas_call(interior_kernel, out_shape=(frame, frame, frame_t, square,...  9.15 us
    pallas_call x1, Pallas kernels, section(): pl.pallas_call(functools.partial(edge_kernel, norm), out_shape=(jax.Shape...  8.11 us
    ppermute x4, waiting for transfers between devices, butterfly_sum(): got = lax.ppermute(send, 'rows', perm)  7.97 us
    ppermute x4, starting transfers between devices, butterfly_sum(): got = lax.ppermute(piece, 'rows', perm)  5.12 us
    ppermute x1, starting transfers between devices, local(): lax.ppermute(jnp.concatenate([inputs[-2:], cotangent[-2:]]), 'rows', up)  3.06 us
  transfers between devices with their start and end apart: 10, of which 7 were waited for; matrix products, arithmetic and copies ran while one was open for 0% of the time, Pallas kernels for 28%

profile of v17, /device:TPU:0, one launch (start us, length us, event | category | flops | bytes accessed | tf_op | source)
XLA Modules:
  0.0 73.2 jit_solution(480907929265603703)
XLA Ops:
  0.6 1.3 %fusion.1 = (bf16[2,512,128]{2,1,0:T(8,128)(2,1)S(1)}, bf16[2,512,128]{2,1,0:T(8,128)(2,1)S(1)}, bf16[2,512,128]{2,1,0:T(8,128)(2,1)S(1)}, bf16[2,512,128]{2,1,0:T(8,128)(2,1)S(1)}) fusion(bf16[8,512,128]{2,1,0:T(8,128)(2,1)} %x_hbm.7, bf16[8,512,128]{2,1,0:T(8,128)(2,1)} %c_hbm.7), kind=kLoop, calls=%fused_computation.15 | loop fusion | bytes 2097152 | tf_op jit(solution)/shard_map/slice | solution.py:350
  2.0 1.3 %collective-permute-start.1 = (bf16[4,512,128]{2,1,0:T(8,128)(2,1)S(1)}, bf16[4,512,128]{2,1,0:T(8,128)(2,1)S(1)}, u32[]{:S(2)}, u32[]{:S(2)}) collective-permute-start(bf16[4,512,128]{2,1,0:T(8,128)(2,1)S(1)} %pad_maximum_fusion.1), channel_id=1, source_target_pairs={{1,0},{2,1},{3,2},{4,3},{5,4},{6,5},{7,6},{8,7},{9,8},{10,9},{11,1... | collective-permute-start | bytes 1572872 | tf_op jit(solution)/shard_map/ppermute | solution.py:350
  3.3 3.1 %collective-permute-start = (bf16[4,512,128]{2,1,0:T(8,128)(2,1)S(1)}, bf16[4,512,128]{2,1,0:T(8,128)(2,1)S(1)}, u32[]{:S(2)}, u32[]{:S(2)}) collective-permute-start(bf16[4,512,128]{2,1,0:T(8,128)(2,1)S(1)} %pad_maximum_fusion), channel_id=1, source_target_pairs={{0,1},{1,2},{2,3},{3,4},{4,5},{5,6},{6,7},{7,8},{8,9},{9,10},{10,1... | collective-permute-start | bytes 1572872 | tf_op jit(solution)/shard_map/ppermute | solution.py:349
  7.0 9.2 %shard_map.101 = (bf16[10,512,128]{2,1,0:T(8,128)(2,1)}, bf16[10,512,128]{2,1,0:T(8,128)(2,1)}, bf16[10,128,512]{2,1,0:T(8,128)(2,1)}, f32[384,384]{1,0:T(8,128)...) custom-call(s32[1]{0:T(128)S(6)} %copy.15.idx_ref, ...), custom_call_target="tpu_custom_call" | custom-call | flops 3925868544 | bytes 4194304 | tf_op jit(solution)/shard_map/pallas_call | solution.py:227
  16.2 0.0 copy-start.2
  16.3 0.8 %copy-done.1 = bf16[4,512,128]{2,1,0:T(8,128)(2,1)} copy-done((bf16[4,512,128]{2,1,0:T(8,128)(2,1)}, bf16[4,512,128]{2,1,0:T(8,128)(2,1)S(1)}, u32[]{:S(2)}) %copy-start.1) | copy-done | bytes 524312
  17.0 0.2 copy-done.2
  17.2 8.1 %shard_map.102 = (f32[2320,128]{1,0:T(8,128)}, bf16[10,512,128]{2,1,0:T(8,128)(2,1)}, bf16[10,512,128]{2,1,0:T(8,128)(2,1)}) custom-call(s32[1]{0:T(128)S(6)} %copy.15.idx_ref, f32[16,2,128]{2,1,0:T(2,128)} %lt_ref.3, bf16[8,512,128]{2,1,0:T(8,128)(2,1)} %x_hbm.7, bf16[8,512,128]{2,1,0:T(8,128)(2,1)} %c_hbm.7, bf16[4,512,128]{2,1,0:T(8,128)(2,1)} %copy-done.2, ...), custom_call_target="tpu_custom_call" | custom-call | flops 2113929216 | bytes 5242880 | tf_op jit(solution)/shard_map/pallas_call | solution.py:245
  25.3 1.4 %slice_select_fusion = f32[1160,128]{1,0:T(8,128)S(1)} fusion(f32[2320,128]{1,0:T(8,128)} %get-tuple-element.38, pred[]{:T(512)S(6)} %eq.35), kind=kLoop, calls=%fused_computation.3 | loop fusion | flops 148480 | bytes 1781761 | tf_op jit(solution)/shard_map/jit(_where)/select_n | solution.py:323
  26.7 3.3 %collective-permute-start.2 = (f32[1160,128]{1,0:T(8,128)S(1)}, f32[1160,128]{1,0:T(8,128)S(1)}, u32[]{:S(2)}, u32[]{:S(2)}) collective-permute-start(f32[1160,128]{1,0:T(8,128)S(1)} %slice_select_fusion), channel_id=1, source_target_pairs={{0,1},{1,0},{2,3},{3,2},{4,5},{5,4},{6,7},{7,6},{8,9},{9,8},{10,11... | collective-permute-start | bytes 1781768 | tf_op jit(solution)/shard_map/ppermute | solution.py:324
  30.0 1.6 %collective-permute-done.2 = f32[1160,128]{1,0:T(8,128)S(1)} collective-permute-done((f32[1160,128]{1,0:T(8,128)S(1)}, f32[1160,128]{1,0:T(8,128)S(1)}, u32[]{:S(2)}, u32[]{:S(2)}) %collective-permute-start.2) | collective-permute-done | bytes 593952 | tf_op jit(solution)/shard_map/ppermute | solution.py:324
  31.6 0.1 select_add_fusion
  31.8 2.8 %collective-permute-start.3 = (f32[580,128]{1,0:T(8,128)S(1)}, f32[580,128]{1,0:T(8,128)S(1)}, u32[]{:S(2)}, u32[]{:S(2)}) collective-permute-start(f32[580,128]{1,0:T(8,128)S(1)} %slice_select_fusion.1), channel_id=1, source_target_pairs={{0,2},{1,5},{2,0},{3,7},{4,6},{5,1},{6,4},{7,3},{8,10},{9,13},{10,... | collective-permute-start | bytes 890888 | tf_op jit(solution)/shard_map/ppermute | solution.py:324
  34.6 5.6 %shard_map.103 = (bf16[8,512,128]{2,1,0:T(8,128)(2,1)}, bf16[8,512,128]{2,1,0:T(8,128)(2,1)}) custom-call(bf16[8,512,128]{2,1,0:T(8,128)(2,1)} %x_hbm.7, bf16[8,512,128]{2,1,0:T(8,128)(2,1)} %c_hbm.7, bf16[10,512,128]{2,1,0:T(8,128)(2,1)} %get-tuple-element.39.hid_hbm, bf16[10,512,128]{2,1,0:T(8,128)(2,1)} %get-tuple-element.40.bf_hbm, ...), custom_call_target="tpu_custom_call" | custom-call | flops 1207959552 | bytes 2097152 | tf_op jit(solution)/shard_map/pallas_call | solution.py:326
  40.2 0.1 select_add_fusion.1
  40.3 1.6 %collective-permute-start.4 = (f32[290,128]{1,0:T(8,128)S(1)}, f32[290,128]{1,0:T(8,128)S(1)}, u32[]{:S(2)}, u32[]{:S(2)}) collective-permute-start(f32[290,128]{1,0:T(8,128)S(1)} %slice_select_fusion.2), channel_id=1, source_target_pairs={{0,4},{1,3},{2,6},{3,1},{4,0},{5,7},{6,2},{7,5},{8,12},{9,11},{10,... | collective-permute-start | bytes 445448 | tf_op jit(solution)/shard_map/ppermute | solution.py:324
  41.9 3.6 %collective-permute-done.4 = f32[290,128]{1,0:T(8,128)S(1)} collective-permute-done((f32[290,128]{1,0:T(8,128)S(1)}, f32[290,128]{1,0:T(8,128)S(1)}, u32[]{:S(2)}, u32[]{:S(2)}) %collective-permute-start.4) | collective-permute-done | bytes 148512 | tf_op jit(solution)/shard_map/ppermute | solution.py:324
  45.6 2.6 %collective-permute-start.5 = (f32[145,128]{1,0:T(8,128)S(1)}, f32[145,128]{1,0:T(8,128)S(1)}, u32[]{:S(2)}, u32[]{:S(2)}) collective-permute-start(f32[145,128]{1,0:T(8,128)S(1)} %slice_select_fusion.3), channel_id=1, source_target_pairs={{0,8},{1,9},{2,10},{3,11},{4,12},{5,13},{6,14},{7,15},{8,0},{9,1},... | collective-permute-start | bytes 222728 | tf_op jit(solution)/shard_map/ppermute | solution.py:324
  48.3 2.7 %collective-permute-done.5 = f32[145,128]{1,0:T(8,128)S(1)} collective-permute-done((f32[145,128]{1,0:T(8,128)S(1)}, f32[145,128]{1,0:T(8,128)S(1)}, u32[]{:S(2)}, u32[]{:S(2)}) %collective-permute-start.5) | collective-permute-done | bytes 74272 | tf_op jit(solution)/shard_map/ppermute | solution.py:324
  51.0 2.6 %collective-permute-start.6 = (f32[145,128]{1,0:T(8,128)S(1)}, f32[145,128]{1,0:T(8,128)S(1)}, u32[]{:S(2)}, u32[]{:S(2)}) collective-permute-start(f32[145,128]{1,0:T(8,128)S(1)} %select_add_fusion.3), channel_id=1, source_target_pairs={{0,8},{1,9},{2,10},{3,11},{4,12},{5,13},{6,14},{7,15},{8,0},{9,1},... | collective-permute-start | bytes 222728 | tf_op jit(solution)/shard_map/ppermute | solution.py:331
  53.6 2.7 %collective-permute-done.6 = f32[145,128]{1,0:T(8,128)S(1)} collective-permute-done((f32[145,128]{1,0:T(8,128)S(1)}, f32[145,128]{1,0:T(8,128)S(1)}, u32[]{:S(2)}, u32[]{:S(2)}) %collective-permute-start.6) | collective-permute-done | bytes 74272 | tf_op jit(solution)/shard_map/ppermute | solution.py:331
  56.4 1.6 %collective-permute-start.7 = (f32[290,128]{1,0:T(8,128)S(1)}, f32[290,128]{1,0:T(8,128)S(1)}, u32[]{:S(2)}, u32[]{:S(2)}) collective-permute-start(f32[290,128]{1,0:T(8,128)S(1)} %maximum_select_fusion.3), channel_id=1, source_target_pairs={{0,4},{1,3},{2,6},{3,1},{4,0},{5,7},{6,2},{7,5},{8,12},{9,11},{10,... | collective-permute-start | bytes 445448 | tf_op jit(solution)/shard_map/ppermute | solution.py:331
  58.0 4.3 %collective-permute-done.7 = f32[290,128]{1,0:T(8,128)S(1)} collective-permute-done((f32[290,128]{1,0:T(8,128)S(1)}, f32[290,128]{1,0:T(8,128)S(1)}, u32[]{:S(2)}, u32[]{:S(2)}) %collective-permute-start.7) | collective-permute-done | bytes 148512 | tf_op jit(solution)/shard_map/ppermute | solution.py:331
  62.4 0.8 %collective-permute-start.8 = (f32[580,128]{1,0:T(8,128)S(1)}, f32[580,128]{1,0:T(8,128)S(1)}, u32[]{:S(2)}, u32[]{:S(2)}) collective-permute-start(f32[580,128]{1,0:T(8,128)S(1)} %maximum_select_fusion.2), channel_id=1, source_target_pairs={{0,2},{1,5},{2,0},{3,7},{4,6},{5,1},{6,4},{7,3},{8,10},{9,13},{10,... | collective-permute-start | bytes 890888 | tf_op jit(solution)/shard_map/ppermute | solution.py:331
  63.2 5.6 %shard_map.104 = (bf16[8,512,128]{2,1,0:T(8,128)(2,1)}, bf16[8,512,128]{2,1,0:T(8,128)(2,1)}) custom-call(bf16[8,512,128]{2,1,0:T(8,128)(2,1)} %x_hbm.7, bf16[8,512,128]{2,1,0:T(8,128)(2,1)} %c_hbm.7, bf16[10,512,128]{2,1,0:T(8,128)(2,1)} %get-tuple-element.39.hid_hbm, ...), custom_call_target="tpu_custom_call", output_to_operand_aliasing={{0}: (6, {}), {1}: (7, {})} | custom-call | flops 1207959552 | bytes 2097152 | tf_op jit(solution)/shard_map/pallas_call | solution.py:333
  68.8 0.5 collective-permute-done.8
  69.2 0.1 maximum_select_fusion.1
  69.3 0.1 collective-permute-start.9
  69.4 2.0 %collective-permute-done.9 = f32[1160,128]{1,0:T(8,128)S(1)} collective-permute-done((f32[1160,128]{1,0:T(8,128)S(1)}, f32[1160,128]{1,0:T(8,128)S(1)}, u32[]{:S(2)}, u32[]{:S(2)}) %collective-permute-start.9) | collective-permute-done | bytes 593952 | tf_op jit(solution)/shard_map/ppermute | solution.py:331
  71.4 0.1 maximum_select_fusion
  71.5 1.1 %fusion = (f32[1152,128]{1,0:T(8,128)}, f32[1152,128]{1,0:T(8,128)}) fusion(f32[2320,128]{1,0:T(8,128)S(1)} %maximum_select_fusion), kind=kLoop, calls=%fused_computation.14 | loop fusion | bytes 2359296 | tf_op jit(solution)/shard_map/slice | solution.py:363
  72.6 0.6 slice.68
  (15 shorter events, 0.3 us)
Async XLA Ops:
  2.0 14.3 %collective-permute-start.1 = (bf16[4,512,128]{2,1,0:T(8,128)(2,1)S(1)}, bf16[4,512,128]{2,1,0:T(8,128)(2,1)S(1)}, u32[]{:S(2)}, u32[]{:S(2)}) collective-permute-start(bf16[4,512,128]{2,1,0:T(8,128)(2,1)S(1)} %pad_maximum_fusion.1), channel_id=1, source_target_pairs={{1,0},{2,1},{3,2},{4,3},{5,4},{6,5},{7,6},{8,7},{9,8},{10,9},{11,1... | collective-permute-start | bytes 1572872 | tf_op jit(solution)/shard_map/ppermute | solution.py:350
  3.3 12.9 %collective-permute-start = (bf16[4,512,128]{2,1,0:T(8,128)(2,1)S(1)}, bf16[4,512,128]{2,1,0:T(8,128)(2,1)S(1)}, u32[]{:S(2)}, u32[]{:S(2)}) collective-permute-start(bf16[4,512,128]{2,1,0:T(8,128)(2,1)S(1)} %pad_maximum_fusion), channel_id=1, source_target_pairs={{0,1},{1,2},{2,3},{3,4},{4,5},{5,6},{6,7},{7,8},{8,9},{9,10},{10,1... | collective-permute-start | bytes 1572872 | tf_op jit(solution)/shard_map/ppermute | solution.py:349
  16.2 0.8 %copy-start.1 = (bf16[4,512,128]{2,1,0:T(8,128)(2,1)}, bf16[4,512,128]{2,1,0:T(8,128)(2,1)S(1)}, u32[]{:S(2)}) copy-start(bf16[4,512,128]{2,1,0:T(8,128)(2,1)S(1)} %collective-permute-done.1.after_hbm) | copy-start | bytes 1572868
  16.2 0.9 %copy-start.2 = (bf16[4,512,128]{2,1,0:T(8,128)(2,1)}, bf16[4,512,128]{2,1,0:T(8,128)(2,1)S(1)}, u32[]{:S(2)}) copy-start(bf16[4,512,128]{2,1,0:T(8,128)(2,1)S(1)} %collective-permute-done.before_hbm) | copy-start | bytes 1572868
  25.3 6.3 %copy-start = (f32[2320,128]{1,0:T(8,128)S(1)}, f32[2320,128]{1,0:T(8,128)}, u32[]{:S(2)}) copy-start(f32[2320,128]{1,0:T(8,128)} %get-tuple-element.38) | copy-start | bytes 3563524
  26.7 4.9 %collective-permute-start.2 = (f32[1160,128]{1,0:T(8,128)S(1)}, f32[1160,128]{1,0:T(8,128)S(1)}, u32[]{:S(2)}, u32[]{:S(2)}) collective-permute-start(f32[1160,128]{1,0:T(8,128)S(1)} %slice_select_fusion), channel_id=1, source_target_pairs={{0,1},{1,0},{2,3},{3,2},{4,5},{5,4},{6,7},{7,6},{8,9},{9,8},{10,11... | collective-permute-start | bytes 1781768 | tf_op jit(solution)/shard_map/ppermute | solution.py:324
  31.8 8.4 %collective-permute-start.3 = (f32[580,128]{1,0:T(8,128)S(1)}, f32[580,128]{1,0:T(8,128)S(1)}, u32[]{:S(2)}, u32[]{:S(2)}) collective-permute-start(f32[580,128]{1,0:T(8,128)S(1)} %slice_select_fusion.1), channel_id=1, source_target_pairs={{0,2},{1,5},{2,0},{3,7},{4,6},{5,1},{6,4},{7,3},{8,10},{9,13},{10,... | collective-permute-start | bytes 890888 | tf_op jit(solution)/shard_map/ppermute | solution.py:324
  40.3 5.3 %collective-permute-start.4 = (f32[290,128]{1,0:T(8,128)S(1)}, f32[290,128]{1,0:T(8,128)S(1)}, u32[]{:S(2)}, u32[]{:S(2)}) collective-permute-start(f32[290,128]{1,0:T(8,128)S(1)} %slice_select_fusion.2), channel_id=1, source_target_pairs={{0,4},{1,3},{2,6},{3,1},{4,0},{5,7},{6,2},{7,5},{8,12},{9,11},{10,... | collective-permute-start | bytes 445448 | tf_op jit(solution)/shard_map/ppermute | solution.py:324
  45.6 5.4 %collective-permute-start.5 = (f32[145,128]{1,0:T(8,128)S(1)}, f32[145,128]{1,0:T(8,128)S(1)}, u32[]{:S(2)}, u32[]{:S(2)}) collective-permute-start(f32[145,128]{1,0:T(8,128)S(1)} %slice_select_fusion.3), channel_id=1, source_target_pairs={{0,8},{1,9},{2,10},{3,11},{4,12},{5,13},{6,14},{7,15},{8,0},{9,1},... | collective-permute-start | bytes 222728 | tf_op jit(solution)/shard_map/ppermute | solution.py:324
  51.0 5.4 %collective-permute-start.6 = (f32[145,128]{1,0:T(8,128)S(1)}, f32[145,128]{1,0:T(8,128)S(1)}, u32[]{:S(2)}, u32[]{:S(2)}) collective-permute-start(f32[145,128]{1,0:T(8,128)S(1)} %select_add_fusion.3), channel_id=1, source_target_pairs={{0,8},{1,9},{2,10},{3,11},{4,12},{5,13},{6,14},{7,15},{8,0},{9,1},... | collective-permute-start | bytes 222728 | tf_op jit(solution)/shard_map/ppermute | solution.py:331
  56.4 6.0 %collective-permute-start.7 = (f32[290,128]{1,0:T(8,128)S(1)}, f32[290,128]{1,0:T(8,128)S(1)}, u32[]{:S(2)}, u32[]{:S(2)}) collective-permute-start(f32[290,128]{1,0:T(8,128)S(1)} %maximum_select_fusion.3), channel_id=1, source_target_pairs={{0,4},{1,3},{2,6},{3,1},{4,0},{5,7},{6,2},{7,5},{8,12},{9,11},{10,... | collective-permute-start | bytes 445448 | tf_op jit(solution)/shard_map/ppermute | solution.py:331
  62.4 6.8 %collective-permute-start.8 = (f32[580,128]{1,0:T(8,128)S(1)}, f32[580,128]{1,0:T(8,128)S(1)}, u32[]{:S(2)}, u32[]{:S(2)}) collective-permute-start(f32[580,128]{1,0:T(8,128)S(1)} %maximum_select_fusion.2), channel_id=1, source_target_pairs={{0,2},{1,5},{2,0},{3,7},{4,6},{5,1},{6,4},{7,3},{8,10},{9,13},{10,... | collective-permute-start | bytes 890888 | tf_op jit(solution)/shard_map/ppermute | solution.py:331
  69.3 2.1 %collective-permute-start.9 = (f32[1160,128]{1,0:T(8,128)S(1)}, f32[1160,128]{1,0:T(8,128)S(1)}, u32[]{:S(2)}, u32[]{:S(2)}) collective-permute-start(f32[1160,128]{1,0:T(8,128)S(1)} %maximum_select_fusion.1), channel_id=1, source_target_pairs={{0,1},{1,0},{2,3},{3,2},{4,5},{5,4},{6,7},{7,6},{8,9},{9,8},{10,11... | collective-permute-start | bytes 1781768 | tf_op jit(solution)/shard_map/ppermute | solution.py:331
